TPU v7x, 32 devices: a whole 2x2x4 slice. The times are simulated.
32 devices in a mesh: groups: 2 (over y), tok: 4 (over z), span: 2 (over x), head: 2 (over core).
Axes of the slice: x: 2, y: 2, z: 4, core: 2. Of those that a mesh axis runs over, the one named last changes fastest.
Arguments:
- key_rows: bfloat16 [6, 2, 2048, 2, 256], P('groups', 'span', 'tok', 'head'), parts along dimension 0, may hold values from -6 to 6
- value_rows: bfloat16 [6, 2, 2048, 2, 256], P('groups', 'span', 'tok', 'head'), parts along dimension 0, may hold values from -6 to 6
- query_rows: bfloat16 [6, 2, 2048, 2, 256], P('groups', 'span', 'tok', 'head'), parts along dimension 0, may hold values from -6 to 6
- step_rates: float32 [6, 2, 2, 2048], P('groups', 'span', 'head', 'tok'), parts along dimension 0, may hold values from 0.4 to 3
- states_in: float32 [4, 2, 3, 256, 256], P(('groups', 'span'), 'head', None, None, 'tok'), parts along dimension 0, may hold values from -0.375 to 0.375
- init_weights: bfloat16 [2, 3, 256, 256], P('head'), may hold values from -0.375 to 0.375
Outputs:
- outputs: bfloat16 [6, 2, 2048, 2, 256], P('groups', 'span', 'tok', 'head'), parts along dimension 0
- states_out: float32 [4, 2, 3, 256, 256], P(('groups', 'span'), 'head', None, None, 'tok'), parts along dimension 0
There are 2 independent parts, one for each index of `groups`. A program takes and returns all parts, laid end to end along the dimension named above; an argument that names none is the same for every part. Nothing has to cross between parts.
All inputs are finite; a program needn't handle non-finite values.
Results may differ from a plain program's by a relative error of at most 0.039.
Values may be sent and summed in bfloat16 or wider, within the bound.
No kernel may reach another device: no remote copies, remote signals or barrier semaphores. Data moves between devices by JAX's collectives and lax.ppermute only.
A program may use at most 64 MiB of HBM per device.

v0:
```python
import math

import jax
import jax.numpy as jnp
from jax import lax
from jax.sharding import PartitionSpec as P

ITERS = 2


def shortened(value):

    def short(part):
        return part.astype(jnp.bfloat16) if part.dtype == jnp.float32 else part

    return jax.tree.map(short, value)


def shifted(value, axis, by):
    devices = lax.axis_size(axis)
    pairs = [(i, i + by) for i in range(devices) if 0 <= i + by < devices]
    return lax.ppermute(value, axis, pairs)


def renormalize(matrices, init_norms):
    column_norms = jnp.sqrt(jnp.sum(matrices * matrices, axis=-2) + 1e-06)
    return matrices * (init_norms / column_norms)[..., None, :]


def fast_grads(fast, key_block, scaled):
    gate_pre = jnp.einsum("ted,edh->teh", key_block, fast[:, 0], preferred_element_type=jnp.float32)
    up_pre = jnp.einsum("ted,edh->teh", key_block, fast[:, 1], preferred_element_type=jnp.float32)
    sigmoid_gate = jax.nn.sigmoid(gate_pre)
    gated = gate_pre * sigmoid_gate
    hidden = (gated * up_pre).astype(jnp.bfloat16)
    back_grad = jnp.einsum("ted,ehd->teh", scaled, fast[:, 2], preferred_element_type=jnp.float32)
    grad_gate = (
        back_grad * up_pre * sigmoid_gate * (1.0 + gate_pre * (1.0 - sigmoid_gate))
    ).astype(jnp.bfloat16)
    grad_up = (back_grad * gated).astype(jnp.bfloat16)
    first = jnp.einsum("ted,teh->edh", key_block, grad_gate, preferred_element_type=jnp.float32)
    second = jnp.einsum("ted,teh->edh", key_block, grad_up, preferred_element_type=jnp.float32)
    third = jnp.einsum("teh,ted->ehd", hidden, scaled, preferred_element_type=jnp.float32)
    return jnp.stack([first, second, third], axis=1)


def apply_fast(fast, query_block):
    query_gate = jnp.einsum(
        "ted,edh->teh", query_block, fast[:, 0], preferred_element_type=jnp.float32
    )
    query_up = jnp.einsum(
        "ted,edh->teh", query_block, fast[:, 1], preferred_element_type=jnp.float32
    )
    applied = (query_gate * jax.nn.sigmoid(query_gate) * query_up).astype(jnp.bfloat16)
    return jnp.einsum(
        "teh,ehd->ted", applied, fast[:, 2], preferred_element_type=jnp.float32
    ).astype(jnp.bfloat16)


def on_device(key_rows, value_rows, query_rows, step_rates, states_in, init_weights):
    tok_count = lax.axis_size("tok")
    feature_width = init_weights.shape[-1]
    part_cols = feature_width // tok_count
    rate_scale = 1.0 / math.sqrt(key_rows.shape[2] * tok_count * feature_width)
    section_index = lax.axis_index("span")
    tok_index = lax.axis_index("tok")
    init_full = init_weights.astype(jnp.float32)
    init_norms = jnp.sqrt(jnp.sum(init_full * init_full, axis=-2) + 1e-06)
    tick_count = key_rows.shape[0]
    results = []
    weights = lax.all_gather(states_in[0].astype(jnp.bfloat16), "tok", axis=3, tiled=True).astype(
        jnp.float32
    )
    for tick_number in range(tick_count):
        if tick_number > 0:
            arrived = shifted(shortened(weights), "span", 1).astype(weights.dtype)
            weights = jnp.where(section_index == 0, init_full, arrived)
        key_block = key_rows[tick_number, 0]
        scaled = (
            (step_rates[tick_number, 0].T * rate_scale)[:, :, None] * value_rows[tick_number, 0]
        ).astype(jnp.bfloat16)
        for update_step in range(ITERS):
            partial_value = fast_grads(weights.astype(jnp.bfloat16), key_block, scaled)
            summed = lax.psum(partial_value.astype(jnp.bfloat16), "tok").astype(jnp.float32)
            weights = renormalize(weights + summed, init_norms)
        results.append(apply_fast(weights.astype(jnp.bfloat16), query_rows[tick_number, 0]))
    final_cols = lax.dynamic_slice_in_dim(weights, tok_index * part_cols, part_cols, 3)
    return (jnp.stack(results)[:, None], final_cols[None])


def solution(mesh):
    placed = (
        P("groups", "span", "tok", "head", None),
        P("groups", "span", "tok", "head", None),
        P("groups", "span", "tok", "head", None),
        P("groups", "span", "head", "tok"),
        P(("groups", "span"), "head", None, None, "tok"),
        P("head", None, None, None),
    )
    return jax.shard_map(
        on_device,
        mesh=mesh,
        in_specs=placed,
        out_specs=(
            P("groups", "span", "tok", "head", None),
            P(("groups", "span"), "head", None, None, "tok"),
        ),
        check_vma=False,
    )
```

profile of v0, /device:TPU:0, one launch (start us, length us, event | category | flops | bytes accessed | tf_op | source)
XLA Modules:
  0.0 308.3 jit_solution(12860910622639942270)
XLA Ops:
  7.2 1.0 convert_element_type.434
  8.2 16.3 %all-gather = bf16[1,1,3,256,256]{3,4,2,1,0:T(8,128)(2,1)S(1)} all-gather(bf16[1,1,3,256,64]{3,4,2,1,0:T(8,128)(2,1)S(1)} %convert_element_type.434), channel_id=2, replica_groups=mesh['groups'=2,'tok'=4,'span'=2,'head'=2] {'tok'}, dimensions={4}, use_global_device_ids=true | all-gather | bytes 491520 | tf_op jit(solution)/shard_map/all_gather | solution.py:71
  27.2 0.8 pad_maximum_fusion
  28.0 0.9 copy-done.14
  29.3 37.6 %all-reduce.7.cloned.1.call-done = bf16[1,3,256,256]{2,3,1,0:T(8,128)(2,1)} async-done(((bf16[1,3,256,256]{2,3,1,0:T(8,128)(2,1)}), bf16[1,3,256,256]{2,3,1,0:T(8,128)(2,1)}) %all-reduce.7.cloned.1.call-update) | async-done | bytes 393232 | tf_op jit(solution)/shard_map/psum | solution.py:84
  66.9 1.3 multiply_reduce_fusion.5
  70.4 0.8 pad_maximum_fusion.1
  71.3 36.8 %all-reduce.9.cloned.1.call-done = bf16[1,3,256,256]{2,3,1,0:T(8,128)(2,1)} async-done(((bf16[1,3,256,256]{2,3,1,0:T(8,128)(2,1)}), bf16[1,3,256,256]{2,3,1,0:T(8,128)(2,1)}) %all-reduce.9.cloned.1.call-update) | async-done | bytes 393232 | tf_op jit(solution)/shard_map/psum | solution.py:84
  108.1 1.4 multiply_reduce_fusion.4
  109.8 3.3 %collective-permute-start = (bf16[1,3,256,256]{2,3,1,0:T(8,128)(2,1)S(1)}, bf16[1,3,256,256]{2,3,1,0:T(8,128)(2,1)S(1)}, u32[]{:S(2)}, u32[]{:S(2)}) collective-permute-start(bf16[1,3,256,256]{2,3,1,0:T(8,128)(2,1)S(1)} %multiply_convert_fusion.1), channel_id=1, source_target_pairs={{0,2},{1,3},{4,6},{5,7},{8,10},{9,11},{12,14},{13,15},{16,18},{17,... | collective-permute-start | bytes 1179656 | tf_op jit(solution)/shard_map/ppermute | solution.py:22
  113.1 6.9 %collective-permute-done = bf16[1,3,256,256]{2,3,1,0:T(8,128)(2,1)S(1)} collective-permute-done((bf16[1,3,256,256]{2,3,1,0:T(8,128)(2,1)S(1)}, bf16[1,3,256,256]{2,3,1,0:T(8,128)(2,1)S(1)}, u32[]{:S(2)}, u32[]{:S(2)}) %collective-permute-start) | collective-permute-done | bytes 393248 | tf_op jit(solution)/shard_map/ppermute | solution.py:22
  122.2 0.8 pad_maximum_fusion.2
  123.0 37.3 %all-reduce.11.cloned.1.call-done = bf16[1,3,256,256]{2,3,1,0:T(8,128)(2,1)} async-done(((bf16[1,3,256,256]{2,3,1,0:T(8,128)(2,1)}), bf16[1,3,256,256]{2,3,1,0:T(8,128)(2,1)}) %all-reduce.11.cloned.1.call-update) | async-done | bytes 393232 | tf_op jit(solution)/shard_map/psum | solution.py:84
  160.3 1.3 multiply_reduce_fusion.3
  163.9 0.8 pad_maximum_fusion.3
  164.8 36.8 %all-reduce.13.cloned.1.call-done = bf16[1,3,256,256]{2,3,1,0:T(8,128)(2,1)} async-done(((bf16[1,3,256,256]{2,3,1,0:T(8,128)(2,1)}), bf16[1,3,256,256]{2,3,1,0:T(8,128)(2,1)}) %all-reduce.13.cloned.1.call-update) | async-done | bytes 393232 | tf_op jit(solution)/shard_map/psum | solution.py:84
  201.6 1.4 multiply_reduce_fusion.2
  203.5 3.3 %collective-permute-start.1 = (bf16[1,3,256,256]{2,3,1,0:T(8,128)(2,1)S(1)}, bf16[1,3,256,256]{2,3,1,0:T(8,128)(2,1)S(1)}, u32[]{:S(2)}, u32[]{:S(2)}) collective-permute-start(bf16[1,3,256,256]{2,3,1,0:T(8,128)(2,1)S(1)} %multiply_convert_fusion), channel_id=1, source_target_pairs={{0,2},{1,3},{4,6},{5,7},{8,10},{9,11},{12,14},{13,15},{16,18},{17,... | collective-permute-start | bytes 1179656 | tf_op jit(solution)/shard_map/ppermute | solution.py:22
  206.8 6.9 %collective-permute-done.1 = bf16[1,3,256,256]{2,3,1,0:T(8,128)(2,1)S(1)} collective-permute-done((bf16[1,3,256,256]{2,3,1,0:T(8,128)(2,1)S(1)}, bf16[1,3,256,256]{2,3,1,0:T(8,128)(2,1)S(1)}, u32[]{:S(2)}, u32[]{:S(2)}) %collective-permute-start.1) | collective-permute-done | bytes 393248 | tf_op jit(solution)/shard_map/ppermute | solution.py:22
  215.8 0.8 pad_maximum_fusion.4
  217.1 2.0 convolution_bitcast_fusion.18
  219.0 35.0 %all-reduce.15.cloned.1.call-done = bf16[1,3,256,256]{2,3,1,0:T(8,128)(2,1)} async-done(((bf16[1,3,256,256]{2,3,1,0:T(8,128)(2,1)}), bf16[1,3,256,256]{2,3,1,0:T(8,128)(2,1)}) %all-reduce.15.cloned.1.call-update) | async-done | bytes 393232 | tf_op jit(solution)/shard_map/psum | solution.py:84
  254.0 1.3 multiply_reduce_fusion.1
  257.6 0.8 pad_maximum_fusion.5
  259.4 1.2 fusion.9
  260.9 1.2 fusion.10
  262.1 33.2 %all-reduce.17.cloned.1.call-done = bf16[1,3,256,256]{2,3,1,0:T(8,128)(2,1)} async-done(((bf16[1,3,256,256]{2,3,1,0:T(8,128)(2,1)}), bf16[1,3,256,256]{2,3,1,0:T(8,128)(2,1)}) %all-reduce.17.cloned.1.call-update) | async-done | bytes 393232 | tf_op jit(solution)/shard_map/psum | solution.py:84
  295.3 1.5 multiply_reduce_fusion
  297.4 1.2 fusion.11
  298.6 1.0 maximum_bitcast_fusion
  299.7 1.2 copy.38
  300.8 0.7 dynamic-slice_bitcast_fusion
  (102 shorter events, 17.2 us)
Async XLA Ops:
  7.2 17.3 %copy-start = (bf16[3,1,512,1,256]{4,2,3,1,0:T(8,128)(2,1)S(1)}, bf16[3,1,512,1,256]{4,2,3,1,0:T(8,128)(2,1)}, u32[]{:S(2)}) copy-start(bf16[3,1,512,1,256]{4,2,3,1,0:T(8,128)(2,1)} %param.6) | copy-start | bytes 2359300
  7.2 59.7 %all-reduce.7.cloned.1.call-start = ((), (), s32[]{:S(2)}) async-start(), calls=%async_computation | async-start | bytes 786432 | tf_op jit(solution)/shard_map/psum | solution.py:84
  24.5 1.1 copy-start.4
  24.8 0.7 copy-start.17
  27.9 1.0 copy-start.14
  28.0 80.1 %all-reduce.9.cloned.1.call-start = ((), (), s32[]{:S(2)}) async-start(), calls=%async_computation.1 | async-start | bytes 786432 | tf_op jit(solution)/shard_map/psum | solution.py:84
  66.9 1.3 copy-start.2
  71.2 89.1 %all-reduce.11.cloned.1.call-start = ((), (), s32[]{:S(2)}) async-start(), calls=%async_computation.2 | async-start | bytes 786432 | tf_op jit(solution)/shard_map/psum | solution.py:84
  108.1 1.4 copy-start.6
  109.8 10.3 %copy-start.9 = (bf16[1,3,256,256]{2,3,1,0:T(8,128)(2,1)}, bf16[1,3,256,256]{2,3,1,0:T(8,128)(2,1)S(1)}, u32[]{:S(2)}) copy-start(bf16[1,3,256,256]{2,3,1,0:T(8,128)(2,1)S(1)} %multiply_convert_fusion.1) | copy-start | bytes 1179652
  109.8 10.2 %collective-permute-start = (bf16[1,3,256,256]{2,3,1,0:T(8,128)(2,1)S(1)}, bf16[1,3,256,256]{2,3,1,0:T(8,128)(2,1)S(1)}, u32[]{:S(2)}, u32[]{:S(2)}) collective-permute-start(bf16[1,3,256,256]{2,3,1,0:T(8,128)(2,1)S(1)} %multiply_convert_fusion.1), channel_id=1, source_target_pairs={{0,2},{1,3},{4,6},{5,7},{8,10},{9,11},{12,14},{13,15},{16,18},{17,... | collective-permute-start | bytes 1179656 | tf_op jit(solution)/shard_map/ppermute | solution.py:22
  123.0 78.6 %all-reduce.13.cloned.1.call-start = ((), (), s32[]{:S(2)}) async-start(), calls=%async_computation.3 | async-start | bytes 786432 | tf_op jit(solution)/shard_map/psum | solution.py:84
  160.3 1.3 copy-start.3
  164.7 89.3 %all-reduce.15.cloned.1.call-start = ((), (), s32[]{:S(2)}) async-start(), calls=%async_computation.4 | async-start | bytes 786432 | tf_op jit(solution)/shard_map/psum | solution.py:84
  201.6 1.5 copy-start.7
  203.4 10.3 %copy-start.11 = (bf16[1,3,256,256]{2,3,1,0:T(8,128)(2,1)}, bf16[1,3,256,256]{2,3,1,0:T(8,128)(2,1)S(1)}, u32[]{:S(2)}) copy-start(bf16[1,3,256,256]{2,3,1,0:T(8,128)(2,1)S(1)} %multiply_convert_fusion) | copy-start | bytes 1179652
  203.5 10.2 %collective-permute-start.1 = (bf16[1,3,256,256]{2,3,1,0:T(8,128)(2,1)S(1)}, bf16[1,3,256,256]{2,3,1,0:T(8,128)(2,1)S(1)}, u32[]{:S(2)}, u32[]{:S(2)}) collective-permute-start(bf16[1,3,256,256]{2,3,1,0:T(8,128)(2,1)S(1)} %multiply_convert_fusion), channel_id=1, source_target_pairs={{0,2},{1,3},{4,6},{5,7},{8,10},{9,11},{12,14},{13,15},{16,18},{17,... | collective-permute-start | bytes 1179656 | tf_op jit(solution)/shard_map/ppermute | solution.py:22
  215.8 1.3 copy-start.8
  216.7 78.6 %all-reduce.17.cloned.1.call-start = ((), (), s32[]{:S(2)}) async-start(), calls=%async_computation.5 | async-start | bytes 786432 | tf_op jit(solution)/shard_map/psum | solution.py:84
  254.0 1.3 copy-start.1
  257.6 1.2 copy-start.13
  258.4 1.0 copy-start.10
  259.4 1.2 copy-start.12
  295.3 1.5 copy-start.5
  297.4 1.2 copy-start.15
  297.4 1.2 copy-start.16
Sparse Core Ops, SparseCore 0:
  28.1 38.7 all-reduce.6
  71.3 36.6 all-reduce.8
  123.1 37.1 all-reduce.10
  164.9 36.6 all-reduce.12
  216.8 37.1 all-reduce.14
  258.5 36.6 all-reduce.16
where the time goes:
time: 309 us; the launch traced here: 308 us
  waiting for transfers between devices  230 us (74%)
  matrix products  18.2 us (6%)
  other arithmetic  17 us (6%)
  blocking collectives  16.3 us (5%)
  between operations  14.5 us (5%)
  starting transfers between devices  7.01 us (2%)
  local copies, waits for them, and re-layouts  4.79 us (2%)
    psum x6, waiting for transfers between devices, on_device(): lax.psum(partial_value.astype(jnp.bfloat16), 'tok').astype(jnp.float32)  217 us
    all_gather x1, blocking collectives, on_device(): lax.all_gather(states_in[0].astype(jnp.bfloat16), 'tok', axis=3, tiled=True)  16.3 us
    ppermute x2, waiting for transfers between devices, shifted(): return lax.ppermute(value, axis, pairs)  13.8 us
    reduce_sum x6, other arithmetic, renormalize(): column_norms = jnp.sqrt(jnp.sum(matrices * matrices, axis=-2) + 1e-06)  8.22 us
    ppermute x2, starting transfers between devices, shifted(): return lax.ppermute(value, axis, pairs)  6.59 us
  transfers between devices with their start and end apart: 8, of which 8 were waited for; matrix products, arithmetic and copies ran while one was open for 2% of the time, Pallas kernels for 0%

commit v1 on v0

v1 whole, which is shorter than its diff:
```python
import math

import jax
import jax.numpy as jnp
from jax import lax
from jax.sharding import PartitionSpec as P

ITERS = 2


def shifted(value, axis, by):
    devices = lax.axis_size(axis)
    pairs = [(i, i + by) for i in range(devices) if 0 <= i + by < devices]
    return lax.ppermute(value, axis, pairs)


def rotated(value, axis, by):
    devices = lax.axis_size(axis)
    return lax.ppermute(value, axis, [(i, (i + by) % devices) for i in range(devices)])


def scatter_sum(partial, part_cols):
    tok_count = lax.axis_size("tok")
    me = lax.axis_index("tok")
    total = lax.dynamic_slice_in_dim(partial, me * part_cols, part_cols, 2).astype(jnp.float32)
    for by in range(1, tok_count):
        chunk = lax.dynamic_slice_in_dim(partial, ((me + by) % tok_count) * part_cols, part_cols, 2)
        total = total + rotated(chunk, "tok", by).astype(jnp.float32)
    return total


def gather_cols(own, part_cols):
    tok_count = lax.axis_size("tok")
    me = lax.axis_index("tok")
    full = jnp.zeros(own.shape[:2] + (part_cols * tok_count,), own.dtype)
    full = lax.dynamic_update_slice_in_dim(full, own, me * part_cols, 2)
    for by in range(1, tok_count):
        got = rotated(own, "tok", by)
        full = lax.dynamic_update_slice_in_dim(full, got, ((me - by) % tok_count) * part_cols, 2)
    return full


def renormalize(matrices, init_norms):
    column_norms = jnp.sqrt(jnp.sum(matrices * matrices, axis=-2) + 1e-06)
    return matrices * (init_norms / column_norms)[..., None, :]


def fast_grads(fast, key_block, scaled):
    gate_pre = jnp.einsum("td,dh->th", key_block, fast[0], preferred_element_type=jnp.float32)
    up_pre = jnp.einsum("td,dh->th", key_block, fast[1], preferred_element_type=jnp.float32)
    sigmoid_gate = jax.nn.sigmoid(gate_pre)
    gated = gate_pre * sigmoid_gate
    hidden = (gated * up_pre).astype(jnp.bfloat16)
    back_grad = jnp.einsum("td,hd->th", scaled, fast[2], preferred_element_type=jnp.float32)
    grad_gate = (
        back_grad * up_pre * sigmoid_gate * (1.0 + gate_pre * (1.0 - sigmoid_gate))
    ).astype(jnp.bfloat16)
    grad_up = (back_grad * gated).astype(jnp.bfloat16)
    first = jnp.einsum("td,th->dh", key_block, grad_gate, preferred_element_type=jnp.float32)
    second = jnp.einsum("td,th->dh", key_block, grad_up, preferred_element_type=jnp.float32)
    third = jnp.einsum("th,td->hd", hidden, scaled, preferred_element_type=jnp.float32)
    return jnp.stack([first, second, third], axis=0).astype(jnp.bfloat16)


def apply_fast(fast, query_block):
    query_gate = jnp.einsum("td,dh->th", query_block, fast[0], preferred_element_type=jnp.float32)
    query_up = jnp.einsum("td,dh->th", query_block, fast[1], preferred_element_type=jnp.float32)
    applied = (query_gate * jax.nn.sigmoid(query_gate) * query_up).astype(jnp.bfloat16)
    return jnp.einsum(
        "th,hd->td", applied, fast[2], preferred_element_type=jnp.float32
    ).astype(jnp.bfloat16)


def on_device(key_rows, value_rows, query_rows, step_rates, states_in, init_weights):
    tok_count = lax.axis_size("tok")
    feature_width = init_weights.shape[-1]
    part_cols = feature_width // tok_count
    rate_scale = 1.0 / math.sqrt(key_rows.shape[2] * tok_count * feature_width)
    section_index = lax.axis_index("span")
    tok_index = lax.axis_index("tok")
    init_fast = init_weights[0]
    init_full = init_fast.astype(jnp.float32)
    init_norms = jnp.sqrt(jnp.sum(init_full * init_full, axis=-2) + 1e-06)
    own_norms = lax.dynamic_slice_in_dim(init_norms, tok_index * part_cols, part_cols, 1)
    tick_count = key_rows.shape[0]
    results = []
    weights = states_in[0, 0]
    fast = gather_cols(weights.astype(jnp.bfloat16), part_cols)
    for tick_number in range(tick_count):
        if tick_number > 0:
            arrived = shifted(fast, "span", 1)
            fast = jnp.where(section_index == 0, init_fast, arrived)
            weights = lax.dynamic_slice_in_dim(fast, tok_index * part_cols, part_cols, 2).astype(
                jnp.float32
            )
        key_block = key_rows[tick_number, 0, :, 0]
        scaled = (
            (step_rates[tick_number, 0, 0] * rate_scale)[:, None]
            * value_rows[tick_number, 0, :, 0].astype(jnp.float32)
        ).astype(jnp.bfloat16)
        for update_step in range(ITERS):
            if update_step > 0:
                fast = gather_cols(weights.astype(jnp.bfloat16), part_cols)
            summed = scatter_sum(fast_grads(fast, key_block, scaled), part_cols)
            weights = renormalize(weights + summed, own_norms)
        fast = gather_cols(weights.astype(jnp.bfloat16), part_cols)
        results.append(apply_fast(fast, query_rows[tick_number, 0, :, 0]))
    outputs = jnp.stack(results)[:, None, :, None]
    return (outputs, weights[None, None])


def solution(mesh):
    placed = (
        P("groups", "span", "tok", "head", None),
        P("groups", "span", "tok", "head", None),
        P("groups", "span", "tok", "head", None),
        P("groups", "span", "head", "tok"),
        P(("groups", "span"), "head", None, None, "tok"),
        P("head", None, None, None),
    )
    return jax.shard_map(
        on_device,
        mesh=mesh,
        in_specs=placed,
        out_specs=(
            P("groups", "span", "tok", "head", None),
            P(("groups", "span"), "head", None, None, "tok"),
        ),
        check_vma=False,
    )
```

time: 309 us -> 186 us (0.60)
  waiting for transfers between devices: 230 us -> 83.4 us
  starting transfers between devices: 7.01 us -> 73.6 us
  blocking collectives: 16.3 us -> 0 us
  between operations: 14.5 us -> 1.54 us
  other arithmetic: 17 us -> 5.37 us
    psum x6 -> x0, waiting for transfers between devices: 217 us -> none  [on_device(): lax.psum(partial_value.astype(jnp.bfloat16), 'tok').astype(jnp.float32)]
    ppermute x0 -> x39, waiting for transfers between devices: none -> 70 us  [rotated(): lax.ppermute(value, axis, [(i, (i + by) % devices) for i in range(devices)])]
    ppermute x0 -> x39, starting transfers between devices: none -> 65.7 us  [rotated(): lax.ppermute(value, axis, [(i, (i + by) % devices) for i in range(devices)])]
    all_gather x1 -> x0, blocking collectives: 16.3 us -> none  [on_device(): lax.all_gather(states_in[0].astype(jnp.bfloat16), 'tok', axis=3, tiled=True)]
    reduce_sum x6, other arithmetic: 8.22 us -> 1.98 us  [renormalize(): column_norms = jnp.sqrt(jnp.sum(matrices * matrices, axis=-2) + 1e-06)]
    another operation x6, other arithmetic: 4.79 us -> 0.28 us  [fast_grads(): return jnp.stack([first, second, third], axis=0).astype(jnp.bfloat16)]
  transfers between devices with their start and end apart: 8 -> 41, of which waited for: 8 -> 30; matrix products, arithmetic and copies ran while one was open for 2% -> 3% of each run, Pallas kernels for 0% -> 0%
where the time goes in v1:
time: 186 us; the launch traced here: 185 us
  waiting for transfers between devices  83.4 us (45%)
  starting transfers between devices  73.6 us (40%)
  matrix products  17.5 us (9%)
  other arithmetic  5.37 us (3%)
  local copies, waits for them, and re-layouts  3.54 us (2%)
    ppermute x39, waiting for transfers between devices, rotated(): lax.ppermute(value, axis, [(i, (i + by) % devices) for i in range(devices)])  70 us
    ppermute x39, starting transfers between devices, rotated(): lax.ppermute(value, axis, [(i, (i + by) % devices) for i in range(devices)])  65.7 us
    ppermute x2, waiting for transfers between devices, shifted(): return lax.ppermute(value, axis, pairs)  13.4 us
    ppermute x2, starting transfers between devices, shifted(): return lax.ppermute(value, axis, pairs)  7.9 us
  transfers between devices with their start and end apart: 41, of which 30 were waited for; matrix products, arithmetic and copies ran while one was open for 3% of the time, Pallas kernels for 0%

profile of v1, /device:TPU:0, one launch (start us, length us, event | category | flops | bytes accessed | tf_op | source)
XLA Modules:
  0.0 185.0 jit_solution(7128895249527814382)
XLA Ops:
  1.6 3.1 %collective-permute-start = (bf16[3,256,64]{1,2,0:T(8,128)(2,1)S(1)}, bf16[3,256,64]{1,2,0:T(8,128)(2,1)S(1)}, u32[]{:S(2)}, u32[]{:S(2)}) collective-permute-start(bf16[3,256,64]{1,2,0:T(8,128)(2,1)S(1)} %get-tuple-element.29), channel_id=1, source_target_pairs={{0,4},{4,8},{8,12},{12,0},{1,5},{5,9},{9,13},{13,1},{2,6},{6,10},{... | collective-permute-start | bytes 294920 | tf_op jit(solution)/shard_map/ppermute | solution.py:19
  4.7 2.6 %collective-permute-start.1 = (bf16[3,256,64]{1,2,0:T(8,128)(2,1)S(1)}, bf16[3,256,64]{1,2,0:T(8,128)(2,1)S(1)}, u32[]{:S(2)}, u32[]{:S(2)}) collective-permute-start(bf16[3,256,64]{1,2,0:T(8,128)(2,1)S(1)} %get-tuple-element.29), channel_id=1, source_target_pairs={{0,8},{4,12},{8,0},{12,4},{1,9},{5,13},{9,1},{13,5},{2,10},{6,14},... | collective-permute-start | bytes 294920 | tf_op jit(solution)/shard_map/ppermute | solution.py:19
  10.4 3.5 %collective-permute-done.1 = bf16[3,256,64]{1,2,0:T(8,128)(2,1)S(1)} collective-permute-done((bf16[3,256,64]{1,2,0:T(8,128)(2,1)S(1)}, bf16[3,256,64]{1,2,0:T(8,128)(2,1)S(1)}, u32[]{:S(2)}, u32[]{:S(2)}) %collective-permute-start.1) | collective-permute-done | bytes 98336 | tf_op jit(solution)/shard_map/ppermute | solution.py:19
  16.7 2.6 %collective-permute-start.3 = (bf16[3,256,64]{1,2,0:T(8,128)(2,1)S(1)}, bf16[3,256,64]{1,2,0:T(8,128)(2,1)S(1)}, u32[]{:S(2)}, u32[]{:S(2)}) collective-permute-start(bf16[3,256,64]{1,2,0:T(8,128)(2,1)S(1)} %get-tuple-element.45), channel_id=1, source_target_pairs={{0,4},{4,8},{8,12},{12,0},{1,5},{5,9},{9,13},{13,1},{2,6},{6,10},{... | collective-permute-start | bytes 294920 | tf_op jit(solution)/shard_map/ppermute | solution.py:19
  24.1 3.4 %collective-permute-done.4 = bf16[3,256,64]{1,2,0:T(8,128)(2,1)S(1)} collective-permute-done((bf16[3,256,64]{1,2,0:T(8,128)(2,1)S(1)}, bf16[3,256,64]{1,2,0:T(8,128)(2,1)S(1)}, u32[]{:S(2)}, u32[]{:S(2)}) %collective-permute-start.4) | collective-permute-done | bytes 98336 | tf_op jit(solution)/shard_map/ppermute | solution.py:19
  27.9 2.6 %collective-permute-start.6 = (bf16[3,256,64]{1,2,0:T(8,128)(2,1)S(1)}, bf16[3,256,64]{1,2,0:T(8,128)(2,1)S(1)}, u32[]{:S(2)}, u32[]{:S(2)}) collective-permute-start(bf16[3,256,64]{1,2,0:T(8,128)(2,1)S(1)} %get-tuple-element.25), channel_id=1, source_target_pairs={{0,4},{4,8},{8,12},{12,0},{1,5},{5,9},{9,13},{13,1},{2,6},{6,10},{... | collective-permute-start | bytes 294920 | tf_op jit(solution)/shard_map/ppermute | solution.py:19
  33.0 2.4 %collective-permute-done.6 = bf16[3,256,64]{1,2,0:T(8,128)(2,1)S(1)} collective-permute-done((bf16[3,256,64]{1,2,0:T(8,128)(2,1)S(1)}, bf16[3,256,64]{1,2,0:T(8,128)(2,1)S(1)}, u32[]{:S(2)}, u32[]{:S(2)}) %collective-permute-start.6) | collective-permute-done | bytes 98336 | tf_op jit(solution)/shard_map/ppermute | solution.py:19
  35.4 3.3 %collective-permute-done.7 = bf16[3,256,64]{1,2,0:T(8,128)(2,1)S(1)} collective-permute-done((bf16[3,256,64]{1,2,0:T(8,128)(2,1)S(1)}, bf16[3,256,64]{1,2,0:T(8,128)(2,1)S(1)}, u32[]{:S(2)}, u32[]{:S(2)}) %collective-permute-start.7) | collective-permute-done | bytes 98336 | tf_op jit(solution)/shard_map/ppermute | solution.py:19
  42.5 3.4 %collective-permute-start.11 = (bf16[3,256,64]{1,2,0:T(8,128)(2,1)S(1)}, bf16[3,256,64]{1,2,0:T(8,128)(2,1)S(1)}, u32[]{:S(2)}, u32[]{:S(2)}) collective-permute-start(bf16[3,256,64]{1,2,0:T(8,128)(2,1)S(1)} %get-tuple-element.43), channel_id=1, source_target_pairs={{0,12},{4,0},{8,4},{12,8},{1,13},{5,1},{9,5},{13,9},{2,14},{6,2},{... | collective-permute-start | bytes 294920 | tf_op jit(solution)/shard_map/ppermute | solution.py:19
  49.0 3.8 %collective-permute-done.9 = bf16[3,256,64]{1,2,0:T(8,128)(2,1)S(1)} collective-permute-done((bf16[3,256,64]{1,2,0:T(8,128)(2,1)S(1)}, bf16[3,256,64]{1,2,0:T(8,128)(2,1)S(1)}, u32[]{:S(2)}, u32[]{:S(2)}) %collective-permute-start.9) | collective-permute-done | bytes 98336 | tf_op jit(solution)/shard_map/ppermute | solution.py:19
  57.9 2.9 %collective-permute-done.12 = bf16[3,256,64]{1,2,0:T(8,128)(2,1)S(1)} collective-permute-done((bf16[3,256,64]{1,2,0:T(8,128)(2,1)S(1)}, bf16[3,256,64]{1,2,0:T(8,128)(2,1)S(1)}, u32[]{:S(2)}, u32[]{:S(2)}) %collective-permute-start.12) | collective-permute-done | bytes 98336 | tf_op jit(solution)/shard_map/ppermute | solution.py:19
  60.8 2.5 %collective-permute-done.13 = bf16[3,256,64]{1,2,0:T(8,128)(2,1)S(1)} collective-permute-done((bf16[3,256,64]{1,2,0:T(8,128)(2,1)S(1)}, bf16[3,256,64]{1,2,0:T(8,128)(2,1)S(1)}, u32[]{:S(2)}, u32[]{:S(2)}) %collective-permute-start.13) | collective-permute-done | bytes 98336 | tf_op jit(solution)/shard_map/ppermute | solution.py:19
  63.3 3.4 %collective-permute-start.15 = (bf16[3,256,256]{1,2,0:T(8,128)(2,1)S(1)}, bf16[3,256,256]{1,2,0:T(8,128)(2,1)S(1)}, u32[]{:S(2)}, u32[]{:S(2)}) collective-permute-start(bf16[3,256,256]{1,2,0:T(8,128)(2,1)S(1)} %constant_dynamic-update-slice_fusion.16), channel_id=1, source_target_pairs={{0,2},{1,3},{4,6},{5,7},{8,10},{9,11},{12,14},{13,15},{16,18},{17,... | collective-permute-start | bytes 1179656 | tf_op jit(solution)/shard_map/ppermute | solution.py:14
  66.7 6.5 %collective-permute-done.15 = bf16[3,256,256]{1,2,0:T(8,128)(2,1)S(1)} collective-permute-done((bf16[3,256,256]{1,2,0:T(8,128)(2,1)S(1)}, bf16[3,256,256]{1,2,0:T(8,128)(2,1)S(1)}, u32[]{:S(2)}, u32[]{:S(2)}) %collective-permute-start.15) | collective-permute-done | bytes 393248 | tf_op jit(solution)/shard_map/ppermute | solution.py:14
  75.5 3.4 %collective-permute-start.16 = (bf16[3,256,64]{1,2,0:T(8,128)(2,1)S(1)}, bf16[3,256,64]{1,2,0:T(8,128)(2,1)S(1)}, u32[]{:S(2)}, u32[]{:S(2)}) collective-permute-start(bf16[3,256,64]{1,2,0:T(8,128)(2,1)S(1)} %get-tuple-element.39), channel_id=1, source_target_pairs={{0,4},{4,8},{8,12},{12,0},{1,5},{5,9},{9,13},{13,1},{2,6},{6,10},{... | collective-permute-start | bytes 294920 | tf_op jit(solution)/shard_map/ppermute | solution.py:19
  81.3 2.6 %collective-permute-done.16 = bf16[3,256,64]{1,2,0:T(8,128)(2,1)S(1)} collective-permute-done((bf16[3,256,64]{1,2,0:T(8,128)(2,1)S(1)}, bf16[3,256,64]{1,2,0:T(8,128)(2,1)S(1)}, u32[]{:S(2)}, u32[]{:S(2)}) %collective-permute-start.16) | collective-permute-done | bytes 98336 | tf_op jit(solution)/shard_map/ppermute | solution.py:19
  83.9 2.9 %collective-permute-done.17 = bf16[3,256,64]{1,2,0:T(8,128)(2,1)S(1)} collective-permute-done((bf16[3,256,64]{1,2,0:T(8,128)(2,1)S(1)}, bf16[3,256,64]{1,2,0:T(8,128)(2,1)S(1)}, u32[]{:S(2)}, u32[]{:S(2)}) %collective-permute-start.17) | collective-permute-done | bytes 98336 | tf_op jit(solution)/shard_map/ppermute | solution.py:19
  91.3 3.2 %collective-permute-done.19 = bf16[3,256,64]{1,2,0:T(8,128)(2,1)S(1)} collective-permute-done((bf16[3,256,64]{1,2,0:T(8,128)(2,1)S(1)}, bf16[3,256,64]{1,2,0:T(8,128)(2,1)S(1)}, u32[]{:S(2)}, u32[]{:S(2)}) %collective-permute-start.19) | collective-permute-done | bytes 98336 | tf_op jit(solution)/shard_map/ppermute | solution.py:19
  94.6 2.6 %collective-permute-done.20 = bf16[3,256,64]{1,2,0:T(8,128)(2,1)S(1)} collective-permute-done((bf16[3,256,64]{1,2,0:T(8,128)(2,1)S(1)}, bf16[3,256,64]{1,2,0:T(8,128)(2,1)S(1)}, u32[]{:S(2)}, u32[]{:S(2)}) %collective-permute-start.20) | collective-permute-done | bytes 98336 | tf_op jit(solution)/shard_map/ppermute | solution.py:19
  103.6 3.3 %collective-permute-done.22 = bf16[3,256,64]{1,2,0:T(8,128)(2,1)S(1)} collective-permute-done((bf16[3,256,64]{1,2,0:T(8,128)(2,1)S(1)}, bf16[3,256,64]{1,2,0:T(8,128)(2,1)S(1)}, u32[]{:S(2)}, u32[]{:S(2)}) %collective-permute-start.22) | collective-permute-done | bytes 98336 | tf_op jit(solution)/shard_map/ppermute | solution.py:19
  106.9 2.5 %collective-permute-done.23 = bf16[3,256,64]{1,2,0:T(8,128)(2,1)S(1)} collective-permute-done((bf16[3,256,64]{1,2,0:T(8,128)(2,1)S(1)}, bf16[3,256,64]{1,2,0:T(8,128)(2,1)S(1)}, u32[]{:S(2)}, u32[]{:S(2)}) %collective-permute-start.23) | collective-permute-done | bytes 98336 | tf_op jit(solution)/shard_map/ppermute | solution.py:19
  114.2 2.9 %collective-permute-done.25 = bf16[3,256,64]{1,2,0:T(8,128)(2,1)S(1)} collective-permute-done((bf16[3,256,64]{1,2,0:T(8,128)(2,1)S(1)}, bf16[3,256,64]{1,2,0:T(8,128)(2,1)S(1)}, u32[]{:S(2)}, u32[]{:S(2)}) %collective-permute-start.25) | collective-permute-done | bytes 98336 | tf_op jit(solution)/shard_map/ppermute | solution.py:19
  117.1 2.7 %collective-permute-done.26 = bf16[3,256,64]{1,2,0:T(8,128)(2,1)S(1)} collective-permute-done((bf16[3,256,64]{1,2,0:T(8,128)(2,1)S(1)}, bf16[3,256,64]{1,2,0:T(8,128)(2,1)S(1)}, u32[]{:S(2)}, u32[]{:S(2)}) %collective-permute-start.26) | collective-permute-done | bytes 98336 | tf_op jit(solution)/shard_map/ppermute | solution.py:19
  119.9 4.5 %collective-permute-start.28 = (bf16[3,256,256]{1,2,0:T(8,128)(2,1)S(1)}, bf16[3,256,256]{1,2,0:T(8,128)(2,1)S(1)}, u32[]{:S(2)}, u32[]{:S(2)}) collective-permute-start(bf16[3,256,256]{1,2,0:T(8,128)(2,1)S(1)} %constant_dynamic-update-slice_fusion.7), channel_id=1, source_target_pairs={{0,2},{1,3},{4,6},{5,7},{8,10},{9,11},{12,14},{13,15},{16,18},{17,... | collective-permute-start | bytes 1179656 | tf_op jit(solution)/shard_map/ppermute | solution.py:14
  125.4 6.9 %collective-permute-done.28 = bf16[3,256,256]{1,2,0:T(8,128)(2,1)S(1)} collective-permute-done((bf16[3,256,256]{1,2,0:T(8,128)(2,1)S(1)}, bf16[3,256,256]{1,2,0:T(8,128)(2,1)S(1)}, u32[]{:S(2)}, u32[]{:S(2)}) %collective-permute-start.28) | collective-permute-done | bytes 393248 | tf_op jit(solution)/shard_map/ppermute | solution.py:14
  135.2 2.6 %collective-permute-start.29 = (bf16[3,256,64]{1,2,0:T(8,128)(2,1)}, bf16[3,256,64]{1,2,0:T(8,128)(2,1)}, u32[]{:S(2)}, u32[]{:S(2)}) collective-permute-start(bf16[3,256,64]{1,2,0:T(8,128)(2,1)} %get-tuple-element.33), channel_id=1, source_target_pairs={{0,4},{4,8},{8,12},{12,0},{1,5},{5,9},{9,13},{13,1},{2,6},{6,10},{... | collective-permute-start | bytes 294920 | tf_op jit(solution)/shard_map/ppermute | solution.py:19
  142.9 3.0 %collective-permute-done.30 = bf16[3,256,64]{1,2,0:T(8,128)(2,1)} collective-permute-done((bf16[3,256,64]{1,2,0:T(8,128)(2,1)}, bf16[3,256,64]{1,2,0:T(8,128)(2,1)}, u32[]{:S(2)}, u32[]{:S(2)}) %collective-permute-start.30) | collective-permute-done | bytes 98336 | tf_op jit(solution)/shard_map/ppermute | solution.py:19
  153.9 4.2 %collective-permute-done.33 = bf16[3,256,64]{1,2,0:T(8,128)(2,1)S(1)} collective-permute-done((bf16[3,256,64]{1,2,0:T(8,128)(2,1)S(1)}, bf16[3,256,64]{1,2,0:T(8,128)(2,1)S(1)}, u32[]{:S(2)}, u32[]{:S(2)}) %collective-permute-start.33) | collective-permute-done | bytes 98336 | tf_op jit(solution)/shard_map/ppermute | solution.py:19
  160.3 2.6 %collective-permute-start.35 = (bf16[3,256,64]{1,2,0:T(8,128)(2,1)S(1)}, bf16[3,256,64]{1,2,0:T(8,128)(2,1)S(1)}, u32[]{:S(2)}, u32[]{:S(2)}) collective-permute-start(bf16[3,256,64]{1,2,0:T(8,128)(2,1)S(1)} %get-tuple-element.30), channel_id=1, source_target_pairs={{0,4},{4,8},{8,12},{12,0},{1,5},{5,9},{9,13},{13,1},{2,6},{6,10},{... | collective-permute-start | bytes 294920 | tf_op jit(solution)/shard_map/ppermute | solution.py:19
  167.7 3.4 %collective-permute-done.36 = bf16[3,256,64]{1,2,0:T(8,128)(2,1)S(1)} collective-permute-done((bf16[3,256,64]{1,2,0:T(8,128)(2,1)S(1)}, bf16[3,256,64]{1,2,0:T(8,128)(2,1)S(1)}, u32[]{:S(2)}, u32[]{:S(2)}) %collective-permute-start.36) | collective-permute-done | bytes 98336 | tf_op jit(solution)/shard_map/ppermute | solution.py:19
  171.5 2.6 %collective-permute-start.38 = (bf16[3,256,64]{1,2,0:T(8,128)(2,1)S(1)}, bf16[3,256,64]{1,2,0:T(8,128)(2,1)S(1)}, u32[]{:S(2)}, u32[]{:S(2)}) collective-permute-start(bf16[3,256,64]{1,2,0:T(8,128)(2,1)S(1)} %get-tuple-element.5), channel_id=1, source_target_pairs={{0,4},{4,8},{8,12},{12,0},{1,5},{5,9},{9,13},{13,1},{2,6},{6,10},{... | collective-permute-start | bytes 294920 | tf_op jit(solution)/shard_map/ppermute | solution.py:19
  178.1 4.2 %collective-permute-done.39 = bf16[3,256,64]{1,2,0:T(8,128)(2,1)S(1)} collective-permute-done((bf16[3,256,64]{1,2,0:T(8,128)(2,1)S(1)}, bf16[3,256,64]{1,2,0:T(8,128)(2,1)S(1)}, u32[]{:S(2)}, u32[]{:S(2)}) %collective-permute-start.39) | collective-permute-done | bytes 98336 | tf_op jit(solution)/shard_map/ppermute | solution.py:19
  (182 shorter events, 77.4 us)
Async XLA Ops:
  1.6 8.8 %collective-permute-start = (bf16[3,256,64]{1,2,0:T(8,128)(2,1)S(1)}, bf16[3,256,64]{1,2,0:T(8,128)(2,1)S(1)}, u32[]{:S(2)}, u32[]{:S(2)}) collective-permute-start(bf16[3,256,64]{1,2,0:T(8,128)(2,1)S(1)} %get-tuple-element.29), channel_id=1, source_target_pairs={{0,4},{4,8},{8,12},{12,0},{1,5},{5,9},{9,13},{13,1},{2,6},{6,10},{... | collective-permute-start | bytes 294920 | tf_op jit(solution)/shard_map/ppermute | solution.py:19
  4.7 9.2 %collective-permute-start.1 = (bf16[3,256,64]{1,2,0:T(8,128)(2,1)S(1)}, bf16[3,256,64]{1,2,0:T(8,128)(2,1)S(1)}, u32[]{:S(2)}, u32[]{:S(2)}) collective-permute-start(bf16[3,256,64]{1,2,0:T(8,128)(2,1)S(1)} %get-tuple-element.29), channel_id=1, source_target_pairs={{0,8},{4,12},{8,0},{12,4},{1,9},{5,13},{9,1},{13,5},{2,10},{6,14},... | collective-permute-start | bytes 294920 | tf_op jit(solution)/shard_map/ppermute | solution.py:19
  16.7 7.4 %collective-permute-start.3 = (bf16[3,256,64]{1,2,0:T(8,128)(2,1)S(1)}, bf16[3,256,64]{1,2,0:T(8,128)(2,1)S(1)}, u32[]{:S(2)}, u32[]{:S(2)}) collective-permute-start(bf16[3,256,64]{1,2,0:T(8,128)(2,1)S(1)} %get-tuple-element.45), channel_id=1, source_target_pairs={{0,4},{4,8},{8,12},{12,0},{1,5},{5,9},{9,13},{13,1},{2,6},{6,10},{... | collective-permute-start | bytes 294920 | tf_op jit(solution)/shard_map/ppermute | solution.py:19
  19.3 8.2 %collective-permute-start.4 = (bf16[3,256,64]{1,2,0:T(8,128)(2,1)S(1)}, bf16[3,256,64]{1,2,0:T(8,128)(2,1)S(1)}, u32[]{:S(2)}, u32[]{:S(2)}) collective-permute-start(bf16[3,256,64]{1,2,0:T(8,128)(2,1)S(1)} %get-tuple-element.47), channel_id=1, source_target_pairs={{0,8},{4,12},{8,0},{12,4},{1,9},{5,13},{9,1},{13,5},{2,10},{6,14},... | collective-permute-start | bytes 294920 | tf_op jit(solution)/shard_map/ppermute | solution.py:19
  27.9 7.4 %collective-permute-start.6 = (bf16[3,256,64]{1,2,0:T(8,128)(2,1)S(1)}, bf16[3,256,64]{1,2,0:T(8,128)(2,1)S(1)}, u32[]{:S(2)}, u32[]{:S(2)}) collective-permute-start(bf16[3,256,64]{1,2,0:T(8,128)(2,1)S(1)} %get-tuple-element.25), channel_id=1, source_target_pairs={{0,4},{4,8},{8,12},{12,0},{1,5},{5,9},{9,13},{13,1},{2,6},{6,10},{... | collective-permute-start | bytes 294920 | tf_op jit(solution)/shard_map/ppermute | solution.py:19
  30.5 8.2 %collective-permute-start.7 = (bf16[3,256,64]{1,2,0:T(8,128)(2,1)S(1)}, bf16[3,256,64]{1,2,0:T(8,128)(2,1)S(1)}, u32[]{:S(2)}, u32[]{:S(2)}) collective-permute-start(bf16[3,256,64]{1,2,0:T(8,128)(2,1)S(1)} %get-tuple-element.25), channel_id=1, source_target_pairs={{0,8},{4,12},{8,0},{12,4},{1,9},{5,13},{9,1},{13,5},{2,10},{6,14},... | collective-permute-start | bytes 294920 | tf_op jit(solution)/shard_map/ppermute | solution.py:19
  31.9 6.8 %collective-permute-start.8 = (bf16[3,256,64]{1,2,0:T(8,128)(2,1)S(1)}, bf16[3,256,64]{1,2,0:T(8,128)(2,1)S(1)}, u32[]{:S(2)}, u32[]{:S(2)}) collective-permute-start(bf16[3,256,64]{1,2,0:T(8,128)(2,1)S(1)} %get-tuple-element.25), channel_id=1, source_target_pairs={{0,12},{4,0},{8,4},{12,8},{1,13},{5,1},{9,5},{13,9},{2,14},{6,2},{... | collective-permute-start | bytes 294920 | tf_op jit(solution)/shard_map/ppermute | solution.py:19
  40.9 7.3 %collective-permute-start.10 = (bf16[3,256,64]{1,2,0:T(8,128)(2,1)S(1)}, bf16[3,256,64]{1,2,0:T(8,128)(2,1)S(1)}, u32[]{:S(2)}, u32[]{:S(2)}) collective-permute-start(bf16[3,256,64]{1,2,0:T(8,128)(2,1)S(1)} %get-tuple-element.44), channel_id=1, source_target_pairs={{0,8},{4,12},{8,0},{12,4},{1,9},{5,13},{9,1},{13,5},{2,10},{6,14},... | collective-permute-start | bytes 294920 | tf_op jit(solution)/shard_map/ppermute | solution.py:19
  45.9 6.9 %collective-permute-start.9 = (bf16[3,256,64]{1,2,0:T(8,128)(2,1)S(1)}, bf16[3,256,64]{1,2,0:T(8,128)(2,1)S(1)}, u32[]{:S(2)}, u32[]{:S(2)}) collective-permute-start(bf16[3,256,64]{1,2,0:T(8,128)(2,1)S(1)} %get-tuple-element.42), channel_id=1, source_target_pairs={{0,4},{4,8},{8,12},{12,0},{1,5},{5,9},{9,13},{13,1},{2,6},{6,10},{... | collective-permute-start | bytes 294920 | tf_op jit(solution)/shard_map/ppermute | solution.py:19
  53.2 7.5 %collective-permute-start.12 = (bf16[3,256,64]{1,2,0:T(8,128)(2,1)S(1)}, bf16[3,256,64]{1,2,0:T(8,128)(2,1)S(1)}, u32[]{:S(2)}, u32[]{:S(2)}) collective-permute-start(bf16[3,256,64]{1,2,0:T(8,128)(2,1)S(1)} %get-tuple-element.21), channel_id=1, source_target_pairs={{0,4},{4,8},{8,12},{12,0},{1,5},{5,9},{9,13},{13,1},{2,6},{6,10},{... | collective-permute-start | bytes 294920 | tf_op jit(solution)/shard_map/ppermute | solution.py:19
  53.3 9.9 %collective-permute-start.13 = (bf16[3,256,64]{1,2,0:T(8,128)(2,1)S(1)}, bf16[3,256,64]{1,2,0:T(8,128)(2,1)S(1)}, u32[]{:S(2)}, u32[]{:S(2)}) collective-permute-start(bf16[3,256,64]{1,2,0:T(8,128)(2,1)S(1)} %get-tuple-element.21), channel_id=1, source_target_pairs={{0,8},{4,12},{8,0},{12,4},{1,9},{5,13},{9,1},{13,5},{2,10},{6,14},... | collective-permute-start | bytes 294920 | tf_op jit(solution)/shard_map/ppermute | solution.py:19
  55.5 7.8 %collective-permute-start.14 = (bf16[3,256,64]{1,2,0:T(8,128)(2,1)S(1)}, bf16[3,256,64]{1,2,0:T(8,128)(2,1)S(1)}, u32[]{:S(2)}, u32[]{:S(2)}) collective-permute-start(bf16[3,256,64]{1,2,0:T(8,128)(2,1)S(1)} %get-tuple-element.21), channel_id=1, source_target_pairs={{0,12},{4,0},{8,4},{12,8},{1,13},{5,1},{9,5},{13,9},{2,14},{6,2},{... | collective-permute-start | bytes 294920 | tf_op jit(solution)/shard_map/ppermute | solution.py:19
  63.3 10.0 %collective-permute-start.15 = (bf16[3,256,256]{1,2,0:T(8,128)(2,1)S(1)}, bf16[3,256,256]{1,2,0:T(8,128)(2,1)S(1)}, u32[]{:S(2)}, u32[]{:S(2)}) collective-permute-start(bf16[3,256,256]{1,2,0:T(8,128)(2,1)S(1)} %constant_dynamic-update-slice_fusion.16), channel_id=1, source_target_pairs={{0,2},{1,3},{4,6},{5,7},{8,10},{9,11},{12,14},{13,15},{16,18},{17,... | collective-permute-start | bytes 1179656 | tf_op jit(solution)/shard_map/ppermute | solution.py:14
  75.5 8.5 %collective-permute-start.16 = (bf16[3,256,64]{1,2,0:T(8,128)(2,1)S(1)}, bf16[3,256,64]{1,2,0:T(8,128)(2,1)S(1)}, u32[]{:S(2)}, u32[]{:S(2)}) collective-permute-start(bf16[3,256,64]{1,2,0:T(8,128)(2,1)S(1)} %get-tuple-element.39), channel_id=1, source_target_pairs={{0,4},{4,8},{8,12},{12,0},{1,5},{5,9},{9,13},{13,1},{2,6},{6,10},{... | collective-permute-start | bytes 294920 | tf_op jit(solution)/shard_map/ppermute | solution.py:19
  78.9 7.9 %collective-permute-start.17 = (bf16[3,256,64]{1,2,0:T(8,128)(2,1)S(1)}, bf16[3,256,64]{1,2,0:T(8,128)(2,1)S(1)}, u32[]{:S(2)}, u32[]{:S(2)}) collective-permute-start(bf16[3,256,64]{1,2,0:T(8,128)(2,1)S(1)} %get-tuple-element.41), channel_id=1, source_target_pairs={{0,8},{4,12},{8,0},{12,4},{1,9},{5,13},{9,1},{13,5},{2,10},{6,14},... | collective-permute-start | bytes 294920 | tf_op jit(solution)/shard_map/ppermute | solution.py:19
  87.2 7.4 %collective-permute-start.19 = (bf16[3,256,64]{1,2,0:T(8,128)(2,1)S(1)}, bf16[3,256,64]{1,2,0:T(8,128)(2,1)S(1)}, u32[]{:S(2)}, u32[]{:S(2)}) collective-permute-start(bf16[3,256,64]{1,2,0:T(8,128)(2,1)S(1)} %get-tuple-element.17), channel_id=1, source_target_pairs={{0,4},{4,8},{8,12},{12,0},{1,5},{5,9},{9,13},{13,1},{2,6},{6,10},{... | collective-permute-start | bytes 294920 | tf_op jit(solution)/shard_map/ppermute | solution.py:19
  88.9 8.3 %collective-permute-start.20 = (bf16[3,256,64]{1,2,0:T(8,128)(2,1)S(1)}, bf16[3,256,64]{1,2,0:T(8,128)(2,1)S(1)}, u32[]{:S(2)}, u32[]{:S(2)}) collective-permute-start(bf16[3,256,64]{1,2,0:T(8,128)(2,1)S(1)} %get-tuple-element.17), channel_id=1, source_target_pairs={{0,8},{4,12},{8,0},{12,4},{1,9},{5,13},{9,1},{13,5},{2,10},{6,14},... | collective-permute-start | bytes 294920 | tf_op jit(solution)/shard_map/ppermute | solution.py:19
  99.4 7.6 %collective-permute-start.22 = (bf16[3,256,64]{1,2,0:T(8,128)(2,1)S(1)}, bf16[3,256,64]{1,2,0:T(8,128)(2,1)S(1)}, u32[]{:S(2)}, u32[]{:S(2)}) collective-permute-start(bf16[3,256,64]{1,2,0:T(8,128)(2,1)S(1)} %get-tuple-element.36), channel_id=1, source_target_pairs={{0,4},{4,8},{8,12},{12,0},{1,5},{5,9},{9,13},{13,1},{2,6},{6,10},{... | collective-permute-start | bytes 294920 | tf_op jit(solution)/shard_map/ppermute | solution.py:19
  101.2 8.3 %collective-permute-start.23 = (bf16[3,256,64]{1,2,0:T(8,128)(2,1)S(1)}, bf16[3,256,64]{1,2,0:T(8,128)(2,1)S(1)}, u32[]{:S(2)}, u32[]{:S(2)}) collective-permute-start(bf16[3,256,64]{1,2,0:T(8,128)(2,1)S(1)} %get-tuple-element.38), channel_id=1, source_target_pairs={{0,8},{4,12},{8,0},{12,4},{1,9},{5,13},{9,1},{13,5},{2,10},{6,14},... | collective-permute-start | bytes 294920 | tf_op jit(solution)/shard_map/ppermute | solution.py:19
  102.5 7.0 %collective-permute-start.24 = (bf16[3,256,64]{1,2,0:T(8,128)(2,1)S(1)}, bf16[3,256,64]{1,2,0:T(8,128)(2,1)S(1)}, u32[]{:S(2)}, u32[]{:S(2)}) collective-permute-start(bf16[3,256,64]{1,2,0:T(8,128)(2,1)S(1)} %get-tuple-element.37), channel_id=1, source_target_pairs={{0,12},{4,0},{8,4},{12,8},{1,13},{5,1},{9,5},{13,9},{2,14},{6,2},{... | collective-permute-start | bytes 294920 | tf_op jit(solution)/shard_map/ppermute | solution.py:19
  109.8 7.3 %collective-permute-start.25 = (bf16[3,256,64]{1,2,0:T(8,128)(2,1)S(1)}, bf16[3,256,64]{1,2,0:T(8,128)(2,1)S(1)}, u32[]{:S(2)}, u32[]{:S(2)}) collective-permute-start(bf16[3,256,64]{1,2,0:T(8,128)(2,1)S(1)} %get-tuple-element.13), channel_id=1, source_target_pairs={{0,4},{4,8},{8,12},{12,0},{1,5},{5,9},{9,13},{13,1},{2,6},{6,10},{... | collective-permute-start | bytes 294920 | tf_op jit(solution)/shard_map/ppermute | solution.py:19
  111.8 8.0 %collective-permute-start.26 = (bf16[3,256,64]{1,2,0:T(8,128)(2,1)S(1)}, bf16[3,256,64]{1,2,0:T(8,128)(2,1)S(1)}, u32[]{:S(2)}, u32[]{:S(2)}) collective-permute-start(bf16[3,256,64]{1,2,0:T(8,128)(2,1)S(1)} %get-tuple-element.13), channel_id=1, source_target_pairs={{0,8},{4,12},{8,0},{12,4},{1,9},{5,13},{9,1},{13,5},{2,10},{6,14},... | collective-permute-start | bytes 294920 | tf_op jit(solution)/shard_map/ppermute | solution.py:19
  113.1 6.8 %collective-permute-start.27 = (bf16[3,256,64]{1,2,0:T(8,128)(2,1)S(1)}, bf16[3,256,64]{1,2,0:T(8,128)(2,1)S(1)}, u32[]{:S(2)}, u32[]{:S(2)}) collective-permute-start(bf16[3,256,64]{1,2,0:T(8,128)(2,1)S(1)} %get-tuple-element.13), channel_id=1, source_target_pairs={{0,12},{4,0},{8,4},{12,8},{1,13},{5,1},{9,5},{13,9},{2,14},{6,2},{... | collective-permute-start | bytes 294920 | tf_op jit(solution)/shard_map/ppermute | solution.py:19
  119.9 12.4 %collective-permute-start.28 = (bf16[3,256,256]{1,2,0:T(8,128)(2,1)S(1)}, bf16[3,256,256]{1,2,0:T(8,128)(2,1)S(1)}, u32[]{:S(2)}, u32[]{:S(2)}) collective-permute-start(bf16[3,256,256]{1,2,0:T(8,128)(2,1)S(1)} %constant_dynamic-update-slice_fusion.7), channel_id=1, source_target_pairs={{0,2},{1,3},{4,6},{5,7},{8,10},{9,11},{12,14},{13,15},{16,18},{17,... | collective-permute-start | bytes 1179656 | tf_op jit(solution)/shard_map/ppermute | solution.py:14
  135.2 7.7 %collective-permute-start.29 = (bf16[3,256,64]{1,2,0:T(8,128)(2,1)}, bf16[3,256,64]{1,2,0:T(8,128)(2,1)}, u32[]{:S(2)}, u32[]{:S(2)}) collective-permute-start(bf16[3,256,64]{1,2,0:T(8,128)(2,1)} %get-tuple-element.33), channel_id=1, source_target_pairs={{0,4},{4,8},{8,12},{12,0},{1,5},{5,9},{9,13},{13,1},{2,6},{6,10},{... | collective-permute-start | bytes 294920 | tf_op jit(solution)/shard_map/ppermute | solution.py:19
  137.9 8.0 %collective-permute-start.30 = (bf16[3,256,64]{1,2,0:T(8,128)(2,1)}, bf16[3,256,64]{1,2,0:T(8,128)(2,1)}, u32[]{:S(2)}, u32[]{:S(2)}) collective-permute-start(bf16[3,256,64]{1,2,0:T(8,128)(2,1)} %get-tuple-element.35), channel_id=1, source_target_pairs={{0,8},{4,12},{8,0},{12,4},{1,9},{5,13},{9,1},{13,5},{2,10},{6,14},... | collective-permute-start | bytes 294920 | tf_op jit(solution)/shard_map/ppermute | solution.py:19
  137.9 8.0 %collective-permute-start.31 = (bf16[3,256,64]{1,2,0:T(8,128)(2,1)}, bf16[3,256,64]{1,2,0:T(8,128)(2,1)}, u32[]{:S(2)}, u32[]{:S(2)}) collective-permute-start(bf16[3,256,64]{1,2,0:T(8,128)(2,1)} %get-tuple-element.34), channel_id=1, source_target_pairs={{0,12},{4,0},{8,4},{12,8},{1,13},{5,1},{9,5},{13,9},{2,14},{6,2},{... | collective-permute-start | bytes 294920 | tf_op jit(solution)/shard_map/ppermute | solution.py:19
  150.5 7.6 %collective-permute-start.33 = (bf16[3,256,64]{1,2,0:T(8,128)(2,1)S(1)}, bf16[3,256,64]{1,2,0:T(8,128)(2,1)S(1)}, u32[]{:S(2)}, u32[]{:S(2)}) collective-permute-start(bf16[3,256,64]{1,2,0:T(8,128)(2,1)S(1)} %get-tuple-element.9), channel_id=1, source_target_pairs={{0,8},{4,12},{8,0},{12,4},{1,9},{5,13},{9,1},{13,5},{2,10},{6,14},... | collective-permute-start | bytes 294920 | tf_op jit(solution)/shard_map/ppermute | solution.py:19
  160.3 7.4 %collective-permute-start.35 = (bf16[3,256,64]{1,2,0:T(8,128)(2,1)S(1)}, bf16[3,256,64]{1,2,0:T(8,128)(2,1)S(1)}, u32[]{:S(2)}, u32[]{:S(2)}) collective-permute-start(bf16[3,256,64]{1,2,0:T(8,128)(2,1)S(1)} %get-tuple-element.30), channel_id=1, source_target_pairs={{0,4},{4,8},{8,12},{12,0},{1,5},{5,9},{9,13},{13,1},{2,6},{6,10},{... | collective-permute-start | bytes 294920 | tf_op jit(solution)/shard_map/ppermute | solution.py:19
  162.9 8.2 %collective-permute-start.36 = (bf16[3,256,64]{1,2,0:T(8,128)(2,1)S(1)}, bf16[3,256,64]{1,2,0:T(8,128)(2,1)S(1)}, u32[]{:S(2)}, u32[]{:S(2)}) collective-permute-start(bf16[3,256,64]{1,2,0:T(8,128)(2,1)S(1)} %get-tuple-element.32), channel_id=1, source_target_pairs={{0,8},{4,12},{8,0},{12,4},{1,9},{5,13},{9,1},{13,5},{2,10},{6,14},... | collective-permute-start | bytes 294920 | tf_op jit(solution)/shard_map/ppermute | solution.py:19
  163.7 7.4 %collective-permute-start.37 = (bf16[3,256,64]{1,2,0:T(8,128)(2,1)S(1)}, bf16[3,256,64]{1,2,0:T(8,128)(2,1)S(1)}, u32[]{:S(2)}, u32[]{:S(2)}) collective-permute-start(bf16[3,256,64]{1,2,0:T(8,128)(2,1)S(1)} %get-tuple-element.31), channel_id=1, source_target_pairs={{0,12},{4,0},{8,4},{12,8},{1,13},{5,1},{9,5},{13,9},{2,14},{6,2},{... | collective-permute-start | bytes 294920 | tf_op jit(solution)/shard_map/ppermute | solution.py:19
  174.9 7.4 %collective-permute-start.39 = (bf16[3,256,64]{1,2,0:T(8,128)(2,1)S(1)}, bf16[3,256,64]{1,2,0:T(8,128)(2,1)S(1)}, u32[]{:S(2)}, u32[]{:S(2)}) collective-permute-start(bf16[3,256,64]{1,2,0:T(8,128)(2,1)S(1)} %get-tuple-element.5), channel_id=1, source_target_pairs={{0,8},{4,12},{8,0},{12,4},{1,9},{5,13},{9,1},{13,5},{2,10},{6,14},... | collective-permute-start | bytes 294920 | tf_op jit(solution)/shard_map/ppermute | solution.py:19
  (21 other events, 176.4 us)

commit v2 on v1

v2 whole, which is shorter than its diff:
```python
import math

import jax
import jax.numpy as jnp
from jax import lax
from jax.sharding import PartitionSpec as P

ITERS = 2


def shifted(value, axis, by):
    devices = lax.axis_size(axis)
    pairs = [(i, i + by) for i in range(devices) if 0 <= i + by < devices]
    return lax.ppermute(value, axis, pairs)


def rotated(value, axis, by):
    devices = lax.axis_size(axis)
    return lax.ppermute(value, axis, [(i, (i + by) % devices) for i in range(devices)])


def gathered(value):
    tok_count = lax.axis_size("tok")
    return jnp.stack([value] + [rotated(value, "tok", by) for by in range(1, tok_count)])


def summed_over_tok(value):
    tok_count = lax.axis_size("tok")
    total = value
    for by in range(1, tok_count):
        total = total + rotated(value, "tok", by)
    return total


def to_rows(cols):
    tok_count = lax.axis_size("tok")
    part = cols.shape[1]
    pieces = cols.reshape(tok_count, part, part)
    got = lax.all_to_all(pieces, "tok", 0, 0, tiled=False)
    return jnp.transpose(got, (0, 2, 1)).reshape(tok_count * part, part)


def to_cols(rows_t):
    tok_count = lax.axis_size("tok")
    part = rows_t.shape[1]
    pieces = jnp.transpose(rows_t.reshape(tok_count, part, part), (0, 2, 1))
    got = lax.all_to_all(pieces, "tok", 0, 0, tiled=False)
    return got.reshape(tok_count * part, part)


def update(weights, keys, scaled, own_norms):
    fast = weights.astype(jnp.bfloat16)
    gate_pre = jnp.einsum("btd,dh->bth", keys, fast[0], preferred_element_type=jnp.float32)
    up_pre = jnp.einsum("btd,dh->bth", keys, fast[1], preferred_element_type=jnp.float32)
    back_grad = jnp.einsum("btd,dh->bth", scaled, fast[2], preferred_element_type=jnp.float32)
    sigmoid_gate = jax.nn.sigmoid(gate_pre)
    gated = gate_pre * sigmoid_gate
    hidden = (gated * up_pre).astype(jnp.bfloat16)
    grad_gate = (
        back_grad * up_pre * sigmoid_gate * (1.0 + gate_pre * (1.0 - sigmoid_gate))
    ).astype(jnp.bfloat16)
    grad_up = (back_grad * gated).astype(jnp.bfloat16)
    first = jnp.einsum("btd,bth->bdh", keys, grad_gate, preferred_element_type=jnp.float32)
    second = jnp.einsum("btd,bth->bdh", keys, grad_up, preferred_element_type=jnp.float32)
    third = jnp.einsum("btd,bth->bdh", scaled, hidden, preferred_element_type=jnp.float32)
    partial = jnp.stack([first, second, third], axis=1).astype(jnp.bfloat16)
    weights = weights + jnp.sum(partial.astype(jnp.float32), axis=0)
    squares = jnp.sum(weights * weights, axis=1)
    first_two = jnp.sqrt(squares[:2] + 1e-06)
    w2_squares = summed_over_tok(jnp.sum(weights[2] * weights[2], axis=1))
    w2_norms = jnp.sqrt(w2_squares + 1e-06)
    top = weights[:2] * (own_norms[0] / first_two)[:, None, :]
    last = weights[2] * (own_norms[1] / w2_norms)[:, None]
    return jnp.concatenate([top, last[None]], axis=0)


def apply_fast(weights, query_block):
    fast = jnp.concatenate(gathered(weights.astype(jnp.bfloat16)), axis=-1)
    query_gate = jnp.einsum("td,dh->th", query_block, fast[0], preferred_element_type=jnp.float32)
    query_up = jnp.einsum("td,dh->th", query_block, fast[1], preferred_element_type=jnp.float32)
    applied = (query_gate * jax.nn.sigmoid(query_gate) * query_up).astype(jnp.bfloat16)
    return jnp.einsum(
        "th,dh->td", applied, fast[2], preferred_element_type=jnp.float32
    ).astype(jnp.bfloat16)


def on_device(key_rows, value_rows, query_rows, step_rates, states_in, init_weights):
    tok_count = lax.axis_size("tok")
    feature_width = init_weights.shape[-1]
    part = feature_width // tok_count
    rate_scale = 1.0 / math.sqrt(key_rows.shape[2] * tok_count * feature_width)
    section_index = lax.axis_index("span")
    tok_index = lax.axis_index("tok")
    init_full = init_weights[0].astype(jnp.float32)
    init_norms = jnp.sqrt(jnp.sum(init_full * init_full, axis=-2) + 1e-06)
    own_hidden = lambda m: lax.dynamic_slice_in_dim(m, tok_index * part, part, m.ndim - 1)
    own_norms = (jnp.stack([own_hidden(init_norms[0]), own_hidden(init_norms[1])]), init_norms[2])
    init_own = jnp.stack(
        [own_hidden(init_full[0]), own_hidden(init_full[1]), own_hidden(init_full[2].T)]
    )
    tick_count = key_rows.shape[0]
    blocks = []
    for tick_number in range(tick_count):
        scaled = (
            (step_rates[tick_number, 0, 0] * rate_scale)[:, None]
            * value_rows[tick_number, 0, :, 0].astype(jnp.float32)
        ).astype(jnp.bfloat16)
        blocks.append(gathered(jnp.stack([key_rows[tick_number, 0, :, 0], scaled])))
    start = states_in[0, 0]
    weights = jnp.stack([start[0], start[1], to_rows(start[2])])
    results = []
    for tick_number in range(tick_count):
        if tick_number > 0:
            arrived = shifted(weights, "span", 1)
            weights = jnp.where(section_index == 0, init_own, arrived)
        keys, scaled = blocks[tick_number][:, 0], blocks[tick_number][:, 1]
        for update_step in range(ITERS):
            weights = update(weights, keys, scaled, own_norms)
        results.append(apply_fast(weights, query_rows[tick_number, 0, :, 0]))
    outputs = jnp.stack(results)[:, None, :, None]
    final = jnp.stack([weights[0], weights[1], to_cols(weights[2])])
    return (outputs, final[None, None])


def solution(mesh):
    placed = (
        P("groups", "span", "tok", "head", None),
        P("groups", "span", "tok", "head", None),
        P("groups", "span", "tok", "head", None),
        P("groups", "span", "head", "tok"),
        P(("groups", "span"), "head", None, None, "tok"),
        P("head", None, None, None),
    )
    return jax.shard_map(
        on_device,
        mesh=mesh,
        in_specs=placed,
        out_specs=(
            P("groups", "span", "tok", "head", None),
            P(("groups", "span"), "head", None, None, "tok"),
        ),
        check_vma=False,
    )
```

time: 186 us -> 242 us (1.30)
  waiting for transfers between devices: 83.4 us -> 123 us
  other arithmetic: 5.37 us -> 12.9 us
  local copies, waits for them, and re-layouts: 3.54 us -> 7.61 us
  matrix products: 17.5 us -> 20.5 us
  starting transfers between devices: 73.6 us -> 76.1 us
    all_to_all x0 -> x2, waiting for transfers between devices: none -> 75.4 us  [the longest x1 70.3 us: to_rows(): got = lax.all_to_all(pieces, 'tok', 0, 0, tiled=False)]
    ppermute x39 -> x36, waiting for transfers between devices: 70 us -> 47.4 us  [rotated(): lax.ppermute(value, axis, [(i, (i + by) % devices) for i in range(devices)])]
    ppermute x2, waiting for transfers between devices: 13.4 us -> 0.01 us  [shifted(): return lax.ppermute(value, axis, pairs)]
    all_to_all x0 -> x2, starting transfers between devices: none -> 7.93 us  [the longest x1 4.64 us: to_rows(): got = lax.all_to_all(pieces, 'tok', 0, 0, tiled=False)]
    another operation x6 -> x7, other arithmetic: 0.28 us -> 5.75 us  [the longest x6 5.67 us: gathered(): jnp.stack([value] + [rotated(value, 'tok', by) for by in range(1, tok_cou...]
    ppermute x39 -> x36, starting transfers between devices: 65.7 us -> 61.4 us  [rotated(): lax.ppermute(value, axis, [(i, (i + by) % devices) for i in range(devices)])]
    dot_general x39, matrix products: 15.2 us -> 18.2 us  [the longest x6 3.97 us: update(): jnp.einsum('btd,dh->bth', scaled, fast[2], preferred_element_type=jnp.flo...]
  transfers between devices with their start and end apart: 41 -> 40, of which waited for: 30 -> 21; matrix products, arithmetic and copies ran while one was open for 3% -> 9% of each run, Pallas kernels for 0% -> 0%
where the time goes in v2:
time: 242 us; the launch traced here: 241 us
  waiting for transfers between devices  123 us (51%)
  starting transfers between devices  76.1 us (31%)
  matrix products  20.5 us (8%)
  other arithmetic  12.9 us (5%)
  local copies, waits for them, and re-layouts  7.61 us (3%)
    all_to_all x1, waiting for transfers between devices, to_rows(): got = lax.all_to_all(pieces, 'tok', 0, 0, tiled=False)  70.3 us
    ppermute x36, starting transfers between devices, rotated(): lax.ppermute(value, axis, [(i, (i + by) % devices) for i in range(devices)])  61.4 us
    ppermute x36, waiting for transfers between devices, rotated(): lax.ppermute(value, axis, [(i, (i + by) % devices) for i in range(devices)])  47.4 us
    ppermute x2, starting transfers between devices, shifted(): return lax.ppermute(value, axis, pairs)  6.8 us
    another operation x6, other arithmetic, gathered(): jnp.stack([value] + [rotated(value, 'tok', by) for by in range(1, tok_cou...  5.67 us
    all_to_all x1, waiting for transfers between devices, to_cols(): got = lax.all_to_all(pieces, 'tok', 0, 0, tiled=False)  5.17 us
  transfers between devices with their start and end apart: 40, of which 21 were waited for; matrix products, arithmetic and copies ran while one was open for 9% of the time, Pallas kernels for 0%

profile of v2, /device:TPU:0, one launch (start us, length us, event | category | flops | bytes accessed | tf_op | source)
XLA Modules:
  0.0 241.3 jit_solution(10408193030183219823)
XLA Ops:
  3.8 3.1 %collective-permute-start = (bf16[2,512,256]{2,1,0:T(8,128)(2,1)}, bf16[2,512,256]{2,1,0:T(8,128)(2,1)}, u32[]{:S(2)}, u32[]{:S(2)}) collective-permute-start(bf16[2,512,256]{2,1,0:T(8,128)(2,1)} %get-tuple-element.35), channel_id=1, source_target_pairs={{0,4},{4,8},{8,12},{12,0},{1,5},{5,9},{9,13},{13,1},{2,6},{6,10},{... | collective-permute-start | bytes 1572872 | tf_op jit(solution)/shard_map/ppermute | solution.py:19
  6.8 2.6 %collective-permute-start.1 = (bf16[2,512,256]{2,1,0:T(8,128)(2,1)}, bf16[2,512,256]{2,1,0:T(8,128)(2,1)}, u32[]{:S(2)}, u32[]{:S(2)}) collective-permute-start(bf16[2,512,256]{2,1,0:T(8,128)(2,1)} %get-tuple-element.35), channel_id=1, source_target_pairs={{0,8},{4,12},{8,0},{12,4},{1,9},{5,13},{9,1},{13,5},{2,10},{6,14},... | collective-permute-start | bytes 1572872 | tf_op jit(solution)/shard_map/ppermute | solution.py:19
  12.8 4.6 %all-to-all-start = ((f32[4,1,4096]{2,1,0:T(1,128)}), f32[4,1,4096]{2,1,0:T(1,128)S(1)}, u32[]{:S(2)}, u32[]{:S(2)}) async-start(f32[4,1,4096]{2,1,0:T(1,128)} %reshape.361), calls=%async_computation | async-start | bytes 131072 | tf_op jit(solution)/shard_map/all_to_all | solution.py:39
  19.6 70.3 %all-to-all-done = f32[4,1,4096]{2,1,0:T(1,128)S(1)} async-done(((f32[4,1,4096]{2,1,0:T(1,128)}), f32[4,1,4096]{2,1,0:T(1,128)S(1)}, u32[]{:S(2)}, u32[]{:S(2)}) %all-to-all-start) | async-done | bytes 65568 | tf_op jit(solution)/shard_map/all_to_all | solution.py:39
  91.6 1.6 collective-permute-start.15
  94.2 1.6 pad_maximum_fusion
  98.4 2.9 %collective-permute-start.28 = (bf16[2,512,256]{2,1,0:T(8,128)(2,1)S(1)}, bf16[2,512,256]{2,1,0:T(8,128)(2,1)S(1)}, u32[]{:S(2)}, u32[]{:S(2)}) collective-permute-start(bf16[2,512,256]{2,1,0:T(8,128)(2,1)S(1)} %get-tuple-element.39), channel_id=1, source_target_pairs={{0,12},{4,0},{8,4},{12,8},{1,13},{5,1},{9,5},{13,9},{2,14},{6,2},{... | collective-permute-start | bytes 1572872 | tf_op jit(solution)/shard_map/ppermute | solution.py:19
  102.0 15.9 %collective-permute-done.15 = bf16[2,512,256]{2,1,0:T(8,128)(2,1)S(1)} collective-permute-done((bf16[2,512,256]{2,1,0:T(8,128)(2,1)S(1)}, bf16[2,512,256]{2,1,0:T(8,128)(2,1)S(1)}, u32[]{:S(2)}, u32[]{:S(2)}) %collective-permute-start.15) | collective-permute-done | bytes 524320 | tf_op jit(solution)/shard_map/ppermute | solution.py:19
  117.9 9.5 %collective-permute-start.4 = (f32[256]{0:T(256)S(1)}, f32[256]{0:T(256)S(1)}, u32[]{:S(2)}, u32[]{:S(2)}) collective-permute-start(f32[256]{0:T(256)S(1)} %multiply_reduce_fusion.12), channel_id=1, source_target_pairs={{0,8},{4,12},{8,0},{12,4},{1,9},{5,13},{9,1},{13,5},{2,10},{6,14},... | collective-permute-start | bytes 3080 | tf_op jit(solution)/shard_map/ppermute | solution.py:19
  127.4 2.8 %pad_maximum_fusion.1 = bf16[4,2,512,256]{3,2,0,1:T(8,128)(2,1)} fusion(bf16[1,2,512,256]{3,2,0,1:T(8,128)(2,1)S(1)} %bitcast.355, bf16[1,2,512,256]{3,2,0,1:T(8,128)(2,1)} %bitcast.61, bf16[1,2,512,256]{3,2,0,1:T(8,128)(2,1)} %bitcast.59, bf16[1,2,512,256]{3,2,0,1:T(8,128)(2,1)S(1)} %get-tuple-element.36), kind=kLoop, calls=%fused_computation.1 | loop fusion | flops 3145728 | bytes 4194304 | tf_op jit(solution)/shard_map/stack | solution.py:24
  130.3 3.9 %collective-permute-start.5 = (f32[256]{0:T(256)S(1)}, f32[256]{0:T(256)S(1)}, u32[]{:S(2)}, u32[]{:S(2)}) collective-permute-start(f32[256]{0:T(256)S(1)} %multiply_reduce_fusion.12), channel_id=1, source_target_pairs={{0,12},{4,0},{8,4},{12,8},{1,13},{5,1},{9,5},{13,9},{2,14},{6,2},{... | collective-permute-start | bytes 3080 | tf_op jit(solution)/shard_map/ppermute | solution.py:19
  134.3 5.7 %collective-permute-done.27 = bf16[2,512,256]{2,1,0:T(8,128)(2,1)S(1)} collective-permute-done((bf16[2,512,256]{2,1,0:T(8,128)(2,1)S(1)}, bf16[2,512,256]{2,1,0:T(8,128)(2,1)S(1)}, u32[]{:S(2)}, u32[]{:S(2)}) %collective-permute-start.27) | collective-permute-done | bytes 524320 | tf_op jit(solution)/shard_map/ppermute | solution.py:19
  140.3 9.9 %collective-permute-done.4 = f32[256]{0:T(256)S(1)} collective-permute-done((f32[256]{0:T(256)S(1)}, f32[256]{0:T(256)S(1)}, u32[]{:S(2)}, u32[]{:S(2)}) %collective-permute-start.4) | collective-permute-done | bytes 1056 | tf_op jit(solution)/shard_map/ppermute | solution.py:19
  153.8 2.7 %collective-permute-start.7 = (f32[256]{0:T(256)S(1)}, f32[256]{0:T(256)S(1)}, u32[]{:S(2)}, u32[]{:S(2)}) collective-permute-start(f32[256]{0:T(256)S(1)} %multiply_reduce_fusion.11), channel_id=1, source_target_pairs={{0,8},{4,12},{8,0},{12,4},{1,9},{5,13},{9,1},{13,5},{2,10},{6,14},... | collective-permute-start | bytes 3080 | tf_op jit(solution)/shard_map/ppermute | solution.py:19
  158.3 1.7 collective-permute-done.8
  161.0 2.7 %collective-permute-start.10 = (bf16[3,256,64]{1,2,0:T(8,128)(2,1)S(1)}, bf16[3,256,64]{1,2,0:T(8,128)(2,1)S(1)}, u32[]{:S(2)}, u32[]{:S(2)}) collective-permute-start(bf16[3,256,64]{1,2,0:T(8,128)(2,1)S(1)} %fusion.145), channel_id=1, source_target_pairs={{0,8},{4,12},{8,0},{12,4},{1,9},{5,13},{9,1},{13,5},{2,10},{6,14},... | collective-permute-start | bytes 294920 | tf_op jit(solution)/shard_map/ppermute | solution.py:19
  164.7 3.4 %collective-permute-start.12 = (f32[3,256,64]{1,2,0:T(8,128)}, f32[3,256,64]{1,2,0:T(8,128)S(1)}, u32[]{:S(2)}, u32[]{:S(2)}) collective-permute-start(f32[3,256,64]{1,2,0:T(8,128)} %pad_maximum_fusion.8), channel_id=1, source_target_pairs={{0,2},{1,3},{4,6},{5,7},{8,10},{9,11},{12,14},{13,15},{16,18},{17,... | collective-permute-start | bytes 589832 | tf_op jit(solution)/shard_map/ppermute | solution.py:14
  171.4 1.6 fusion.6
  173.1 1.8 fusion.30
  177.0 1.7 collective-permute-start.16
  178.7 2.3 collective-permute-start.17
  187.7 2.2 collective-permute-start.20
  193.6 1.9 collective-permute-start.22
  195.4 1.7 collective-permute-start.23
  197.9 3.4 %collective-permute-start.25 = (f32[3,256,64]{1,2,0:T(8,128)S(1)}, f32[3,256,64]{1,2,0:T(8,128)S(1)}, u32[]{:S(2)}, u32[]{:S(2)}) collective-permute-start(f32[3,256,64]{1,2,0:T(8,128)S(1)} %pad_maximum_fusion.11), channel_id=1, source_target_pairs={{0,2},{1,3},{4,6},{5,7},{8,10},{9,11},{12,14},{13,15},{16,18},{17,... | collective-permute-start | bytes 589832 | tf_op jit(solution)/shard_map/ppermute | solution.py:14
  208.4 1.7 collective-permute-start.30
  210.1 1.5 collective-permute-start.31
  216.3 1.5 collective-permute-start.32
  217.8 2.4 %collective-permute-start.33 = (f32[256]{0:T(256)S(1)}, f32[256]{0:T(256)S(1)}, u32[]{:S(2)}, u32[]{:S(2)}) collective-permute-start(f32[256]{0:T(256)S(1)} %multiply_reduce_fusion.7), channel_id=1, source_target_pairs={{0,8},{4,12},{8,0},{12,4},{1,9},{5,13},{9,1},{13,5},{2,10},{6,14},... | collective-permute-start | bytes 3080 | tf_op jit(solution)/shard_map/ppermute | solution.py:19
  224.5 2.1 collective-permute-start.36
  228.7 3.3 %all-to-all-start.1 = ((f32[4,1,4096]{2,1,0:T(1,128)}), f32[4,1,4096]{2,1,0:T(1,128)S(1)}, u32[]{:S(2)}, u32[]{:S(2)}) async-start(f32[4,1,4096]{2,1,0:T(1,128)} %reshape.363), calls=%async_computation.1 | async-start | bytes 131072 | tf_op jit(solution)/shard_map/all_to_all | solution.py:47
  232.6 5.2 %all-to-all-done.1 = f32[4,1,4096]{2,1,0:T(1,128)S(1)} async-done(((f32[4,1,4096]{2,1,0:T(1,128)}), f32[4,1,4096]{2,1,0:T(1,128)S(1)}, u32[]{:S(2)}, u32[]{:S(2)}) %all-to-all-start.1) | async-done | bytes 65568 | tf_op jit(solution)/shard_map/all_to_all | solution.py:47
  (200 shorter events, 60.6 us)
Async XLA Ops:
  3.8 87.8 %collective-permute-start = (bf16[2,512,256]{2,1,0:T(8,128)(2,1)}, bf16[2,512,256]{2,1,0:T(8,128)(2,1)}, u32[]{:S(2)}, u32[]{:S(2)}) collective-permute-start(bf16[2,512,256]{2,1,0:T(8,128)(2,1)} %get-tuple-element.35), channel_id=1, source_target_pairs={{0,4},{4,8},{8,12},{12,0},{1,5},{5,9},{9,13},{13,1},{2,6},{6,10},{... | collective-permute-start | bytes 1572872 | tf_op jit(solution)/shard_map/ppermute | solution.py:19
  6.8 86.4 %collective-permute-start.1 = (bf16[2,512,256]{2,1,0:T(8,128)(2,1)}, bf16[2,512,256]{2,1,0:T(8,128)(2,1)}, u32[]{:S(2)}, u32[]{:S(2)}) collective-permute-start(bf16[2,512,256]{2,1,0:T(8,128)(2,1)} %get-tuple-element.35), channel_id=1, source_target_pairs={{0,8},{4,12},{8,0},{12,4},{1,9},{5,13},{9,1},{13,5},{2,10},{6,14},... | collective-permute-start | bytes 1572872 | tf_op jit(solution)/shard_map/ppermute | solution.py:19
  9.4 84.3 %collective-permute-start.2 = (bf16[2,512,256]{2,1,0:T(8,128)(2,1)}, bf16[2,512,256]{2,1,0:T(8,128)(2,1)}, u32[]{:S(2)}, u32[]{:S(2)}) collective-permute-start(bf16[2,512,256]{2,1,0:T(8,128)(2,1)} %get-tuple-element.35), channel_id=1, source_target_pairs={{0,12},{4,0},{8,4},{12,8},{1,13},{5,1},{9,5},{13,9},{2,14},{6,2},{... | collective-permute-start | bytes 1572872 | tf_op jit(solution)/shard_map/ppermute | solution.py:19
  10.8 87.6 %collective-permute-start.13 = (bf16[2,512,256]{2,1,0:T(8,128)(2,1)S(1)}, bf16[2,512,256]{2,1,0:T(8,128)(2,1)}, u32[]{:S(2)}, u32[]{:S(2)}) collective-permute-start(bf16[2,512,256]{2,1,0:T(8,128)(2,1)S(1)} %get-tuple-element.37), channel_id=1, source_target_pairs={{0,4},{4,8},{8,12},{12,0},{1,5},{5,9},{9,13},{13,1},{2,6},{6,10},{... | collective-permute-start | bytes 1572872 | tf_op jit(solution)/shard_map/ppermute | solution.py:19
  11.6 89.8 %collective-permute-start.14 = (bf16[2,512,256]{2,1,0:T(8,128)(2,1)S(1)}, bf16[2,512,256]{2,1,0:T(8,128)(2,1)}, u32[]{:S(2)}, u32[]{:S(2)}) collective-permute-start(bf16[2,512,256]{2,1,0:T(8,128)(2,1)S(1)} %get-tuple-element.37), channel_id=1, source_target_pairs={{0,8},{4,12},{8,0},{12,4},{1,9},{5,13},{9,1},{13,5},{2,10},{6,14},... | collective-permute-start | bytes 1572872 | tf_op jit(solution)/shard_map/ppermute | solution.py:19
  12.8 77.1 %all-to-all-start = ((f32[4,1,4096]{2,1,0:T(1,128)}), f32[4,1,4096]{2,1,0:T(1,128)S(1)}, u32[]{:S(2)}, u32[]{:S(2)}) async-start(f32[4,1,4096]{2,1,0:T(1,128)} %reshape.361), calls=%async_computation | async-start | bytes 131072 | tf_op jit(solution)/shard_map/all_to_all | solution.py:39
  91.6 26.3 %collective-permute-start.15 = (bf16[2,512,256]{2,1,0:T(8,128)(2,1)S(1)}, bf16[2,512,256]{2,1,0:T(8,128)(2,1)S(1)}, u32[]{:S(2)}, u32[]{:S(2)}) collective-permute-start(bf16[2,512,256]{2,1,0:T(8,128)(2,1)S(1)} %get-tuple-element.37), channel_id=1, source_target_pairs={{0,12},{4,0},{8,4},{12,8},{1,13},{5,1},{9,5},{13,9},{2,14},{6,2},{... | collective-permute-start | bytes 1572872 | tf_op jit(solution)/shard_map/ppermute | solution.py:19
  93.2 37.1 %collective-permute-start.26 = (bf16[2,512,256]{2,1,0:T(8,128)(2,1)S(1)}, bf16[2,512,256]{2,1,0:T(8,128)(2,1)S(1)}, u32[]{:S(2)}, u32[]{:S(2)}) collective-permute-start(bf16[2,512,256]{2,1,0:T(8,128)(2,1)S(1)} %get-tuple-element.39), channel_id=1, source_target_pairs={{0,4},{4,8},{8,12},{12,0},{1,5},{5,9},{9,13},{13,1},{2,6},{6,10},{... | collective-permute-start | bytes 1572872 | tf_op jit(solution)/shard_map/ppermute | solution.py:19
  93.7 46.3 %collective-permute-start.27 = (bf16[2,512,256]{2,1,0:T(8,128)(2,1)S(1)}, bf16[2,512,256]{2,1,0:T(8,128)(2,1)S(1)}, u32[]{:S(2)}, u32[]{:S(2)}) collective-permute-start(bf16[2,512,256]{2,1,0:T(8,128)(2,1)S(1)} %get-tuple-element.39), channel_id=1, source_target_pairs={{0,8},{4,12},{8,0},{12,4},{1,9},{5,13},{9,1},{13,5},{2,10},{6,14},... | collective-permute-start | bytes 1572872 | tf_op jit(solution)/shard_map/ppermute | solution.py:19
  98.4 41.5 %collective-permute-start.28 = (bf16[2,512,256]{2,1,0:T(8,128)(2,1)S(1)}, bf16[2,512,256]{2,1,0:T(8,128)(2,1)S(1)}, u32[]{:S(2)}, u32[]{:S(2)}) collective-permute-start(bf16[2,512,256]{2,1,0:T(8,128)(2,1)S(1)} %get-tuple-element.39), channel_id=1, source_target_pairs={{0,12},{4,0},{8,4},{12,8},{1,13},{5,1},{9,5},{13,9},{2,14},{6,2},{... | collective-permute-start | bytes 1572872 | tf_op jit(solution)/shard_map/ppermute | solution.py:19
  101.4 38.9 %collective-permute-start.3 = (f32[256]{0:T(256)S(1)}, f32[256]{0:T(256)S(1)}, u32[]{:S(2)}, u32[]{:S(2)}) collective-permute-start(f32[256]{0:T(256)S(1)} %multiply_reduce_fusion.12), channel_id=1, source_target_pairs={{0,4},{4,8},{8,12},{12,0},{1,5},{5,9},{9,13},{13,1},{2,6},{6,10},{... | collective-permute-start | bytes 3080 | tf_op jit(solution)/shard_map/ppermute | solution.py:19
  117.9 32.3 %collective-permute-start.4 = (f32[256]{0:T(256)S(1)}, f32[256]{0:T(256)S(1)}, u32[]{:S(2)}, u32[]{:S(2)}) collective-permute-start(f32[256]{0:T(256)S(1)} %multiply_reduce_fusion.12), channel_id=1, source_target_pairs={{0,8},{4,12},{8,0},{12,4},{1,9},{5,13},{9,1},{13,5},{2,10},{6,14},... | collective-permute-start | bytes 3080 | tf_op jit(solution)/shard_map/ppermute | solution.py:19
  130.3 19.9 %collective-permute-start.5 = (f32[256]{0:T(256)S(1)}, f32[256]{0:T(256)S(1)}, u32[]{:S(2)}, u32[]{:S(2)}) collective-permute-start(f32[256]{0:T(256)S(1)} %multiply_reduce_fusion.12), channel_id=1, source_target_pairs={{0,12},{4,0},{8,4},{12,8},{1,13},{5,1},{9,5},{13,9},{2,14},{6,2},{... | collective-permute-start | bytes 3080 | tf_op jit(solution)/shard_map/ppermute | solution.py:19
  152.9 5.4 %collective-permute-start.6 = (f32[256]{0:T(256)S(1)}, f32[256]{0:T(256)S(1)}, u32[]{:S(2)}, u32[]{:S(2)}) collective-permute-start(f32[256]{0:T(256)S(1)} %multiply_reduce_fusion.11), channel_id=1, source_target_pairs={{0,4},{4,8},{8,12},{12,0},{1,5},{5,9},{9,13},{13,1},{2,6},{6,10},{... | collective-permute-start | bytes 3080 | tf_op jit(solution)/shard_map/ppermute | solution.py:19
  153.8 4.5 %collective-permute-start.7 = (f32[256]{0:T(256)S(1)}, f32[256]{0:T(256)S(1)}, u32[]{:S(2)}, u32[]{:S(2)}) collective-permute-start(f32[256]{0:T(256)S(1)} %multiply_reduce_fusion.11), channel_id=1, source_target_pairs={{0,8},{4,12},{8,0},{12,4},{1,9},{5,13},{9,1},{13,5},{2,10},{6,14},... | collective-permute-start | bytes 3080 | tf_op jit(solution)/shard_map/ppermute | solution.py:19
  160.1 8.0 %collective-permute-start.9 = (bf16[3,256,64]{1,2,0:T(8,128)(2,1)S(1)}, bf16[3,256,64]{1,2,0:T(8,128)(2,1)S(1)}, u32[]{:S(2)}, u32[]{:S(2)}) collective-permute-start(bf16[3,256,64]{1,2,0:T(8,128)(2,1)S(1)} %fusion.145), channel_id=1, source_target_pairs={{0,4},{4,8},{8,12},{12,0},{1,5},{5,9},{9,13},{13,1},{2,6},{6,10},{... | collective-permute-start | bytes 294920 | tf_op jit(solution)/shard_map/ppermute | solution.py:19
  161.0 8.5 %collective-permute-start.10 = (bf16[3,256,64]{1,2,0:T(8,128)(2,1)S(1)}, bf16[3,256,64]{1,2,0:T(8,128)(2,1)S(1)}, u32[]{:S(2)}, u32[]{:S(2)}) collective-permute-start(bf16[3,256,64]{1,2,0:T(8,128)(2,1)S(1)} %fusion.145), channel_id=1, source_target_pairs={{0,8},{4,12},{8,0},{12,4},{1,9},{5,13},{9,1},{13,5},{2,10},{6,14},... | collective-permute-start | bytes 294920 | tf_op jit(solution)/shard_map/ppermute | solution.py:19
  163.7 5.9 %collective-permute-start.11 = (bf16[3,256,64]{1,2,0:T(8,128)(2,1)S(1)}, bf16[3,256,64]{1,2,0:T(8,128)(2,1)S(1)}, u32[]{:S(2)}, u32[]{:S(2)}) collective-permute-start(bf16[3,256,64]{1,2,0:T(8,128)(2,1)S(1)} %fusion.145), channel_id=1, source_target_pairs={{0,12},{4,0},{8,4},{12,8},{1,13},{5,1},{9,5},{13,9},{2,14},{6,2},{... | collective-permute-start | bytes 294920 | tf_op jit(solution)/shard_map/ppermute | solution.py:19
  164.7 8.4 %collective-permute-start.12 = (f32[3,256,64]{1,2,0:T(8,128)}, f32[3,256,64]{1,2,0:T(8,128)S(1)}, u32[]{:S(2)}, u32[]{:S(2)}) collective-permute-start(f32[3,256,64]{1,2,0:T(8,128)} %pad_maximum_fusion.8), channel_id=1, source_target_pairs={{0,2},{1,3},{4,6},{5,7},{8,10},{9,11},{12,14},{13,15},{16,18},{17,... | collective-permute-start | bytes 589832 | tf_op jit(solution)/shard_map/ppermute | solution.py:14
  177.0 5.4 %collective-permute-start.16 = (f32[256]{0:T(256)S(1)}, f32[256]{0:T(256)S(1)}, u32[]{:S(2)}, u32[]{:S(2)}) collective-permute-start(f32[256]{0:T(256)S(1)} %multiply_reduce_fusion.10), channel_id=1, source_target_pairs={{0,4},{4,8},{8,12},{12,0},{1,5},{5,9},{9,13},{13,1},{2,6},{6,10},{... | collective-permute-start | bytes 3080 | tf_op jit(solution)/shard_map/ppermute | solution.py:19
  187.2 5.4 %collective-permute-start.19 = (f32[256]{0:T(256)S(1)}, f32[256]{0:T(256)S(1)}, u32[]{:S(2)}, u32[]{:S(2)}) collective-permute-start(f32[256]{0:T(256)S(1)} %multiply_reduce_fusion.9), channel_id=1, source_target_pairs={{0,4},{4,8},{8,12},{12,0},{1,5},{5,9},{9,13},{13,1},{2,6},{6,10},{... | collective-permute-start | bytes 3080 | tf_op jit(solution)/shard_map/ppermute | solution.py:19
  187.7 4.9 %collective-permute-start.20 = (f32[256]{0:T(256)S(1)}, f32[256]{0:T(256)S(1)}, u32[]{:S(2)}, u32[]{:S(2)}) collective-permute-start(f32[256]{0:T(256)S(1)} %multiply_reduce_fusion.9), channel_id=1, source_target_pairs={{0,8},{4,12},{8,0},{12,4},{1,9},{5,13},{9,1},{13,5},{2,10},{6,14},... | collective-permute-start | bytes 3080 | tf_op jit(solution)/shard_map/ppermute | solution.py:19
  193.6 7.8 %collective-permute-start.22 = (bf16[3,256,64]{1,2,0:T(8,128)(2,1)S(1)}, bf16[3,256,64]{1,2,0:T(8,128)(2,1)S(1)}, u32[]{:S(2)}, u32[]{:S(2)}) collective-permute-start(bf16[3,256,64]{1,2,0:T(8,128)(2,1)S(1)} %fusion.144), channel_id=1, source_target_pairs={{0,4},{4,8},{8,12},{12,0},{1,5},{5,9},{9,13},{13,1},{2,6},{6,10},{... | collective-permute-start | bytes 294920 | tf_op jit(solution)/shard_map/ppermute | solution.py:19
  195.4 6.8 %collective-permute-start.23 = (bf16[3,256,64]{1,2,0:T(8,128)(2,1)S(1)}, bf16[3,256,64]{1,2,0:T(8,128)(2,1)S(1)}, u32[]{:S(2)}, u32[]{:S(2)}) collective-permute-start(bf16[3,256,64]{1,2,0:T(8,128)(2,1)S(1)} %fusion.144), channel_id=1, source_target_pairs={{0,8},{4,12},{8,0},{12,4},{1,9},{5,13},{9,1},{13,5},{2,10},{6,14},... | collective-permute-start | bytes 294920 | tf_op jit(solution)/shard_map/ppermute | solution.py:19
  197.1 5.6 %collective-permute-start.24 = (bf16[3,256,64]{1,2,0:T(8,128)(2,1)S(1)}, bf16[3,256,64]{1,2,0:T(8,128)(2,1)S(1)}, u32[]{:S(2)}, u32[]{:S(2)}) collective-permute-start(bf16[3,256,64]{1,2,0:T(8,128)(2,1)S(1)} %fusion.144), channel_id=1, source_target_pairs={{0,12},{4,0},{8,4},{12,8},{1,13},{5,1},{9,5},{13,9},{2,14},{6,2},{... | collective-permute-start | bytes 294920 | tf_op jit(solution)/shard_map/ppermute | solution.py:19
  197.9 6.6 %collective-permute-start.25 = (f32[3,256,64]{1,2,0:T(8,128)S(1)}, f32[3,256,64]{1,2,0:T(8,128)S(1)}, u32[]{:S(2)}, u32[]{:S(2)}) collective-permute-start(f32[3,256,64]{1,2,0:T(8,128)S(1)} %pad_maximum_fusion.11), channel_id=1, source_target_pairs={{0,2},{1,3},{4,6},{5,7},{8,10},{9,11},{12,14},{13,15},{16,18},{17,... | collective-permute-start | bytes 589832 | tf_op jit(solution)/shard_map/ppermute | solution.py:14
  207.1 5.4 %collective-permute-start.29 = (f32[256]{0:T(256)S(1)}, f32[256]{0:T(256)S(1)}, u32[]{:S(2)}, u32[]{:S(2)}) collective-permute-start(f32[256]{0:T(256)S(1)} %multiply_reduce_fusion.8), channel_id=1, source_target_pairs={{0,4},{4,8},{8,12},{12,0},{1,5},{5,9},{9,13},{13,1},{2,6},{6,10},{... | collective-permute-start | bytes 3080 | tf_op jit(solution)/shard_map/ppermute | solution.py:19
  216.3 5.4 %collective-permute-start.32 = (f32[256]{0:T(256)S(1)}, f32[256]{0:T(256)S(1)}, u32[]{:S(2)}, u32[]{:S(2)}) collective-permute-start(f32[256]{0:T(256)S(1)} %multiply_reduce_fusion.7), channel_id=1, source_target_pairs={{0,4},{4,8},{8,12},{12,0},{1,5},{5,9},{9,13},{13,1},{2,6},{6,10},{... | collective-permute-start | bytes 3080 | tf_op jit(solution)/shard_map/ppermute | solution.py:19
  223.9 14.8 %collective-permute-start.35 = (bf16[3,256,64]{1,2,0:T(8,128)(2,1)S(1)}, bf16[3,256,64]{1,2,0:T(8,128)(2,1)S(1)}, u32[]{:S(2)}, u32[]{:S(2)}) collective-permute-start(bf16[3,256,64]{1,2,0:T(8,128)(2,1)S(1)} %pad_maximum_fusion.13), channel_id=1, source_target_pairs={{0,4},{4,8},{8,12},{12,0},{1,5},{5,9},{9,13},{13,1},{2,6},{6,10},{... | collective-permute-start | bytes 294920 | tf_op jit(solution)/shard_map/ppermute | solution.py:19
  224.5 14.3 %collective-permute-start.36 = (bf16[3,256,64]{1,2,0:T(8,128)(2,1)S(1)}, bf16[3,256,64]{1,2,0:T(8,128)(2,1)S(1)}, u32[]{:S(2)}, u32[]{:S(2)}) collective-permute-start(bf16[3,256,64]{1,2,0:T(8,128)(2,1)S(1)} %pad_maximum_fusion.13), channel_id=1, source_target_pairs={{0,8},{4,12},{8,0},{12,4},{1,9},{5,13},{9,1},{13,5},{2,10},{6,14},... | collective-permute-start | bytes 294920 | tf_op jit(solution)/shard_map/ppermute | solution.py:19
  226.6 12.2 %collective-permute-start.37 = (bf16[3,256,64]{1,2,0:T(8,128)(2,1)S(1)}, bf16[3,256,64]{1,2,0:T(8,128)(2,1)S(1)}, u32[]{:S(2)}, u32[]{:S(2)}) collective-permute-start(bf16[3,256,64]{1,2,0:T(8,128)(2,1)S(1)} %pad_maximum_fusion.13), channel_id=1, source_target_pairs={{0,12},{4,0},{8,4},{12,8},{1,13},{5,1},{9,5},{13,9},{2,14},{6,2},{... | collective-permute-start | bytes 294920 | tf_op jit(solution)/shard_map/ppermute | solution.py:19
  228.7 9.0 %all-to-all-start.1 = ((f32[4,1,4096]{2,1,0:T(1,128)}), f32[4,1,4096]{2,1,0:T(1,128)S(1)}, u32[]{:S(2)}, u32[]{:S(2)}) async-start(f32[4,1,4096]{2,1,0:T(1,128)} %reshape.363), calls=%async_computation.1 | async-start | bytes 131072 | tf_op jit(solution)/shard_map/all_to_all | solution.py:47
  (16 other events, 124.5 us)

commit v3 on v1

--- a/solution.py
+++ b/solution.py
@@ -19,25 +19,53 @@
     return lax.ppermute(value, axis, [(i, (i + by) % devices) for i in range(devices)])
 
 
+def _halving_bits(tok_count):
+    bits = tok_count.bit_length() - 1
+    return bits if (1 << bits) == tok_count else None
+
+
 def scatter_sum(partial, part_cols):
     tok_count = lax.axis_size("tok")
     me = lax.axis_index("tok")
-    total = lax.dynamic_slice_in_dim(partial, me * part_cols, part_cols, 2).astype(jnp.float32)
-    for by in range(1, tok_count):
-        chunk = lax.dynamic_slice_in_dim(partial, ((me + by) % tok_count) * part_cols, part_cols, 2)
-        total = total + rotated(chunk, "tok", by).astype(jnp.float32)
-    return total
+    bits = _halving_bits(tok_count)
+    if bits is None:
+        total = lax.dynamic_slice_in_dim(partial, me * part_cols, part_cols, 2).astype(jnp.float32)
+        for by in range(1, tok_count):
+            chunk = lax.dynamic_slice_in_dim(partial, ((me + by) % tok_count) * part_cols, part_cols, 2)
+            total = total + rotated(chunk, "tok", by).astype(jnp.float32)
+        return total
+    held = partial.reshape(partial.shape[:2] + (2,) * bits + (part_cols,))
+    for bit in range(bits):
+        axis = 2 + (bits - 1 - bit)
+        mine = (me >> bit) & 1
+        keep = lax.dynamic_index_in_dim(held, mine, axis, keepdims=False)
+        send = lax.dynamic_index_in_dim(held, 1 - mine, axis, keepdims=False)
+        got = lax.ppermute(
+            send.astype(jnp.bfloat16), "tok", [(i, i ^ (1 << bit)) for i in range(tok_count)]
+        )
+        held = keep.astype(jnp.float32) + got.astype(jnp.float32)
+    return held
 
 
 def gather_cols(own, part_cols):
     tok_count = lax.axis_size("tok")
     me = lax.axis_index("tok")
-    full = jnp.zeros(own.shape[:2] + (part_cols * tok_count,), own.dtype)
-    full = lax.dynamic_update_slice_in_dim(full, own, me * part_cols, 2)
-    for by in range(1, tok_count):
-        got = rotated(own, "tok", by)
-        full = lax.dynamic_update_slice_in_dim(full, got, ((me - by) % tok_count) * part_cols, 2)
-    return full
+    bits = _halving_bits(tok_count)
+    if bits is None:
+        full = jnp.zeros(own.shape[:2] + (part_cols * tok_count,), own.dtype)
+        full = lax.dynamic_update_slice_in_dim(full, own, me * part_cols, 2)
+        for by in range(1, tok_count):
+            got = rotated(own, "tok", by)
+            full = lax.dynamic_update_slice_in_dim(full, got, ((me - by) % tok_count) * part_cols, 2)
+        return full
+    held = own
+    for bit in reversed(range(bits)):
+        mine = (me >> bit) & 1
+        got = lax.ppermute(held, "tok", [(i, i ^ (1 << bit)) for i in range(tok_count)])
+        low = jnp.where(mine == 0, held, got)
+        high = jnp.where(mine == 0, got, held)
+        held = jnp.stack([low, high], axis=-2)
+    return held.reshape(own.shape[:2] + (part_cols * tok_count,))
 
 
 def renormalize(matrices, init_norms):

time: 186 us -> 205 us (1.10)
  waiting for transfers between devices: 83.4 us -> 120 us
  starting transfers between devices: 73.6 us -> 57.2 us
  matrix products: 17.5 us -> 13.6 us
  other arithmetic: 5.37 us -> 7.54 us
    ppermute x39 -> x26, waiting for transfers between devices: 70 us -> 110 us  [the longest x14 60.8 us: gather_cols(): lax.ppermute(held, 'tok', [(i, i ^ 1 << bit) for i in range(tok_count)])]
    ppermute x39 -> x26, starting transfers between devices: 65.7 us -> 49.2 us  [the longest x14 26 us: gather_cols(): lax.ppermute(held, 'tok', [(i, i ^ 1 << bit) for i in range(tok_count)])]
    ppermute x2, waiting for transfers between devices: 13.4 us -> 9.92 us  [shifted(): return lax.ppermute(value, axis, pairs)]
    slice x0 -> x22, local copies, waits for them, and re-layouts: none -> 2.69 us  [the longest x1 1.16 us: on_device(): value_rows[tick_number, 0, :, 0].astype(jnp.float32)]
  transfers between devices with their start and end apart: 41 -> 28, of which waited for: 30 -> 28; matrix products, arithmetic and copies ran while one was open for 3% -> 2% of each run, Pallas kernels for 0% -> 0%
where the time goes in v3:
time: 205 us; the launch traced here: 204 us
  waiting for transfers between devices  120 us (59%)
  starting transfers between devices  57.2 us (28%)
  matrix products  13.6 us (7%)
  other arithmetic  7.54 us (4%)
  local copies, waits for them, and re-layouts  4.44 us (2%)
    ppermute x14, waiting for transfers between devices, gather_cols(): lax.ppermute(held, 'tok', [(i, i ^ 1 << bit) for i in range(tok_count)])  60.8 us
    ppermute x12, waiting for transfers between devices, scatter_sum(): lax.ppermute(send.astype(jnp.bfloat16), 'tok', [(i, i ^ 1 << bit) for i i...  49.2 us
    ppermute x14, starting transfers between devices, gather_cols(): lax.ppermute(held, 'tok', [(i, i ^ 1 << bit) for i in range(tok_count)])  26 us
    ppermute x12, starting transfers between devices, scatter_sum(): lax.ppermute(send.astype(jnp.bfloat16), 'tok', [(i, i ^ 1 << bit) for i i...  23.3 us
    ppermute x2, waiting for transfers between devices, shifted(): return lax.ppermute(value, axis, pairs)  9.92 us
    ppermute x2, starting transfers between devices, shifted(): return lax.ppermute(value, axis, pairs)  8.01 us
  transfers between devices with their start and end apart: 28, of which 28 were waited for; matrix products, arithmetic and copies ran while one was open for 2% of the time, Pallas kernels for 0%

profile of v3, /device:TPU:0, one launch (start us, length us, event | category | flops | bytes accessed | tf_op | source)
XLA Modules:
  0.0 204.4 jit_solution(7613810912957024892)
XLA Ops:
  1.6 4.1 %collective-permute-start = (bf16[3,256,64]{1,2,0:T(8,128)(2,1)S(1)}, bf16[3,256,64]{1,2,0:T(8,128)(2,1)S(1)}, u32[]{:S(2)}, u32[]{:S(2)}) collective-permute-start(bf16[3,256,64]{1,2,0:T(8,128)(2,1)S(1)} %bitcast_convert_fusion), channel_id=1, source_target_pairs={{0,8},{4,12},{8,0},{12,4},{1,9},{5,13},{9,1},{13,5},{2,10},{6,14},... | collective-permute-start | bytes 294920 | tf_op jit(solution)/shard_map/ppermute | solution.py:64
  7.1 3.5 %collective-permute-done = bf16[3,256,64]{1,2,0:T(8,128)(2,1)S(1)} collective-permute-done((bf16[3,256,64]{1,2,0:T(8,128)(2,1)S(1)}, bf16[3,256,64]{1,2,0:T(8,128)(2,1)S(1)}, u32[]{:S(2)}, u32[]{:S(2)}) %collective-permute-start) | collective-permute-done | bytes 98336 | tf_op jit(solution)/shard_map/ppermute | solution.py:64
  11.5 5.3 %collective-permute-done.1 = bf16[3,256,2,64]{1,3,0,2:T(8,128)(2,1)S(1)} collective-permute-done((bf16[3,256,2,64]{1,3,0,2:T(8,128)(2,1)S(1)}, bf16[3,256,2,64]{1,3,0,2:T(8,128)(2,1)S(1)}, u32[]{:S(2)}, u32[]{:S(2)}) %collective-permute-start.1) | collective-permute-done | bytes 196640 | tf_op jit(solution)/shard_map/ppermute | solution.py:64
  21.5 4.2 %collective-permute-done.2 = bf16[3,256,2,64]{1,3,2,0:T(8,128)(2,1)} collective-permute-done((bf16[3,256,2,64]{1,3,2,0:T(8,128)(2,1)S(1)}, bf16[3,256,2,64]{1,3,2,0:T(8,128)(2,1)}, u32[]{:S(2)}, u32[]{:S(2)}) %collective-permute-start.2) | collective-permute-done | bytes 196640 | tf_op jit(solution)/shard_map/ppermute | solution.py:43
  26.7 3.7 %collective-permute-start.3 = (bf16[3,256,64]{1,2,0:T(8,128)(2,1)S(1)}, bf16[3,256,64]{1,2,0:T(8,128)(2,1)S(1)}, u32[]{:S(2)}, u32[]{:S(2)}) collective-permute-start(bf16[3,256,64]{1,2,0:T(8,128)(2,1)S(1)} %fusion.144), channel_id=1, source_target_pairs={{0,8},{4,12},{8,0},{12,4},{1,9},{5,13},{9,1},{13,5},{2,10},{6,14},... | collective-permute-start | bytes 294920 | tf_op jit(solution)/shard_map/ppermute | solution.py:43
  30.6 3.5 %collective-permute-done.3 = bf16[3,256,64]{1,2,0:T(8,128)(2,1)S(1)} collective-permute-done((bf16[3,256,64]{1,2,0:T(8,128)(2,1)S(1)}, bf16[3,256,64]{1,2,0:T(8,128)(2,1)S(1)}, u32[]{:S(2)}, u32[]{:S(2)}) %collective-permute-start.3) | collective-permute-done | bytes 98336 | tf_op jit(solution)/shard_map/ppermute | solution.py:43
  36.4 4.7 %collective-permute-done.4 = bf16[3,256,64]{1,2,0:T(8,128)(2,1)S(1)} collective-permute-done((bf16[3,256,64]{1,2,0:T(8,128)(2,1)S(1)}, bf16[3,256,64]{1,2,0:T(8,128)(2,1)S(1)}, u32[]{:S(2)}, u32[]{:S(2)}) %collective-permute-start.4) | collective-permute-done | bytes 98336 | tf_op jit(solution)/shard_map/ppermute | solution.py:64
  41.7 5.3 %collective-permute-done.5 = bf16[3,256,2,64]{1,3,0,2:T(8,128)(2,1)S(1)} collective-permute-done((bf16[3,256,2,64]{1,3,0,2:T(8,128)(2,1)S(1)}, bf16[3,256,2,64]{1,3,0,2:T(8,128)(2,1)S(1)}, u32[]{:S(2)}, u32[]{:S(2)}) %collective-permute-start.5) | collective-permute-done | bytes 196640 | tf_op jit(solution)/shard_map/ppermute | solution.py:64
  49.6 6.3 %collective-permute-done.6 = bf16[3,256,2,64]{1,3,0,2:T(8,128)(2,1)S(1)} collective-permute-done((bf16[3,256,2,64]{1,3,0,2:T(8,128)(2,1)S(1)}, bf16[3,256,2,64]{1,3,0,2:T(8,128)(2,1)S(1)}, u32[]{:S(2)}, u32[]{:S(2)}) %collective-permute-start.6) | collective-permute-done | bytes 196640 | tf_op jit(solution)/shard_map/ppermute | solution.py:43
  57.5 5.2 %collective-permute-done.7 = bf16[3,256,64]{1,2,0:T(8,128)(2,1)S(1)} collective-permute-done((bf16[3,256,64]{1,2,0:T(8,128)(2,1)S(1)}, bf16[3,256,64]{1,2,0:T(8,128)(2,1)S(1)}, u32[]{:S(2)}, u32[]{:S(2)}) %collective-permute-start.7) | collective-permute-done | bytes 98336 | tf_op jit(solution)/shard_map/ppermute | solution.py:43
  63.6 5.6 %collective-permute-done.8 = bf16[3,256,64]{1,2,0:T(8,128)(2,1)S(1)} collective-permute-done((bf16[3,256,64]{1,2,0:T(8,128)(2,1)S(1)}, bf16[3,256,64]{1,2,0:T(8,128)(2,1)S(1)}, u32[]{:S(2)}, u32[]{:S(2)}) %collective-permute-start.8) | collective-permute-done | bytes 98336 | tf_op jit(solution)/shard_map/ppermute | solution.py:64
  70.8 4.1 %collective-permute-done.9 = bf16[3,256,2,64]{1,3,0,2:T(8,128)(2,1)S(1)} collective-permute-done((bf16[3,256,2,64]{1,3,0,2:T(8,128)(2,1)S(1)}, bf16[3,256,2,64]{1,3,0,2:T(8,128)(2,1)S(1)}, u32[]{:S(2)}, u32[]{:S(2)}) %collective-permute-start.9) | collective-permute-done | bytes 196640 | tf_op jit(solution)/shard_map/ppermute | solution.py:64
  75.1 3.4 %collective-permute-start.10 = (bf16[3,256,256]{1,2,0:T(8,128)(2,1)S(1)}, bf16[3,256,256]{1,2,0:T(8,128)(2,1)S(1)}, u32[]{:S(2)}, u32[]{:S(2)}) collective-permute-start(bf16[3,256,256]{1,2,0:T(8,128)(2,1)S(1)} %bitcast.473), channel_id=1, source_target_pairs={{0,2},{1,3},{4,6},{5,7},{8,10},{9,11},{12,14},{13,15},{16,18},{17,... | collective-permute-start | bytes 1179656 | tf_op jit(solution)/shard_map/ppermute | solution.py:14
  78.7 5.0 %collective-permute-done.10 = bf16[3,256,256]{1,2,0:T(8,128)(2,1)S(1)} collective-permute-done((bf16[3,256,256]{1,2,0:T(8,128)(2,1)S(1)}, bf16[3,256,256]{1,2,0:T(8,128)(2,1)S(1)}, u32[]{:S(2)}, u32[]{:S(2)}) %collective-permute-start.10) | collective-permute-done | bytes 393248 | tf_op jit(solution)/shard_map/ppermute | solution.py:14
  87.4 4.1 %collective-permute-done.11 = bf16[3,256,2,64]{1,3,0,2:T(8,128)(2,1)S(1)} collective-permute-done((bf16[3,256,2,64]{1,3,0,2:T(8,128)(2,1)S(1)}, bf16[3,256,2,64]{1,3,0,2:T(8,128)(2,1)S(1)}, u32[]{:S(2)}, u32[]{:S(2)}) %collective-permute-start.11) | collective-permute-done | bytes 196640 | tf_op jit(solution)/shard_map/ppermute | solution.py:43
  93.4 3.9 %collective-permute-done.12 = bf16[3,256,64]{1,2,0:T(8,128)(2,1)S(1)} collective-permute-done((bf16[3,256,64]{1,2,0:T(8,128)(2,1)S(1)}, bf16[3,256,64]{1,2,0:T(8,128)(2,1)S(1)}, u32[]{:S(2)}, u32[]{:S(2)}) %collective-permute-start.12) | collective-permute-done | bytes 98336 | tf_op jit(solution)/shard_map/ppermute | solution.py:43
  103.3 2.9 %collective-permute-start.14 = (bf16[3,256,2,64]{1,3,0,2:T(8,128)(2,1)S(1)}, bf16[3,256,2,64]{1,3,0,2:T(8,128)(2,1)S(1)}, u32[]{:S(2)}, u32[]{:S(2)}) collective-permute-start(bf16[3,256,2,64]{1,3,0,2:T(8,128)(2,1)S(1)} %pad_maximum_fusion.11), channel_id=1, source_target_pairs={{0,4},{4,0},{8,12},{12,8},{1,5},{5,1},{9,13},{13,9},{2,6},{6,2},{1... | collective-permute-start | bytes 589832 | tf_op jit(solution)/shard_map/ppermute | solution.py:64
  106.2 4.7 %collective-permute-done.14 = bf16[3,256,2,64]{1,3,0,2:T(8,128)(2,1)S(1)} collective-permute-done((bf16[3,256,2,64]{1,3,0,2:T(8,128)(2,1)S(1)}, bf16[3,256,2,64]{1,3,0,2:T(8,128)(2,1)S(1)}, u32[]{:S(2)}, u32[]{:S(2)}) %collective-permute-start.14) | collective-permute-done | bytes 196640 | tf_op jit(solution)/shard_map/ppermute | solution.py:64
  115.1 3.7 %collective-permute-done.15 = bf16[3,256,2,64]{1,3,0,2:T(8,128)(2,1)S(1)} collective-permute-done((bf16[3,256,2,64]{1,3,0,2:T(8,128)(2,1)S(1)}, bf16[3,256,2,64]{1,3,0,2:T(8,128)(2,1)S(1)}, u32[]{:S(2)}, u32[]{:S(2)}) %collective-permute-start.15) | collective-permute-done | bytes 196640 | tf_op jit(solution)/shard_map/ppermute | solution.py:43
  121.4 3.1 %collective-permute-done.16 = bf16[3,256,64]{1,2,0:T(8,128)(2,1)S(1)} collective-permute-done((bf16[3,256,64]{1,2,0:T(8,128)(2,1)S(1)}, bf16[3,256,64]{1,2,0:T(8,128)(2,1)S(1)}, u32[]{:S(2)}, u32[]{:S(2)}) %collective-permute-start.16) | collective-permute-done | bytes 98336 | tf_op jit(solution)/shard_map/ppermute | solution.py:43
  127.4 3.1 %collective-permute-done.17 = bf16[3,256,64]{1,2,0:T(8,128)(2,1)S(1)} collective-permute-done((bf16[3,256,64]{1,2,0:T(8,128)(2,1)S(1)}, bf16[3,256,64]{1,2,0:T(8,128)(2,1)S(1)}, u32[]{:S(2)}, u32[]{:S(2)}) %collective-permute-start.17) | collective-permute-done | bytes 98336 | tf_op jit(solution)/shard_map/ppermute | solution.py:64
  132.6 5.3 %collective-permute-done.18 = bf16[3,256,2,64]{1,3,0,2:T(8,128)(2,1)S(1)} collective-permute-done((bf16[3,256,2,64]{1,3,0,2:T(8,128)(2,1)S(1)}, bf16[3,256,2,64]{1,3,0,2:T(8,128)(2,1)S(1)}, u32[]{:S(2)}, u32[]{:S(2)}) %collective-permute-start.18) | collective-permute-done | bytes 196640 | tf_op jit(solution)/shard_map/ppermute | solution.py:64
  138.0 4.6 %collective-permute-start.19 = (bf16[3,256,256]{1,2,0:T(8,128)(2,1)S(1)}, bf16[3,256,256]{1,2,0:T(8,128)(2,1)S(1)}, u32[]{:S(2)}, u32[]{:S(2)}) collective-permute-start(bf16[3,256,256]{1,2,0:T(8,128)(2,1)S(1)} %bitcast.474), channel_id=1, source_target_pairs={{0,2},{1,3},{4,6},{5,7},{8,10},{9,11},{12,14},{13,15},{16,18},{17,... | collective-permute-start | bytes 1179656 | tf_op jit(solution)/shard_map/ppermute | solution.py:14
  142.8 4.9 %collective-permute-done.19 = bf16[3,256,256]{1,2,0:T(8,128)(2,1)S(1)} collective-permute-done((bf16[3,256,256]{1,2,0:T(8,128)(2,1)S(1)}, bf16[3,256,256]{1,2,0:T(8,128)(2,1)S(1)}, u32[]{:S(2)}, u32[]{:S(2)}) %collective-permute-start.19) | collective-permute-done | bytes 393248 | tf_op jit(solution)/shard_map/ppermute | solution.py:14
  152.1 3.6 %collective-permute-done.20 = bf16[3,256,2,64]{1,3,0,2:T(8,128)(2,1)S(1)} collective-permute-done((bf16[3,256,2,64]{1,3,0,2:T(8,128)(2,1)S(1)}, bf16[3,256,2,64]{1,3,0,2:T(8,128)(2,1)S(1)}, u32[]{:S(2)}, u32[]{:S(2)}) %collective-permute-start.20) | collective-permute-done | bytes 196640 | tf_op jit(solution)/shard_map/ppermute | solution.py:43
  155.9 2.9 %collective-permute-start.21 = (bf16[3,256,64]{1,2,0:T(8,128)(2,1)S(1)}, bf16[3,256,64]{1,2,0:T(8,128)(2,1)S(1)}, u32[]{:S(2)}, u32[]{:S(2)}) collective-permute-start(bf16[3,256,64]{1,2,0:T(8,128)(2,1)S(1)} %fusion.148), channel_id=1, source_target_pairs={{0,8},{4,12},{8,0},{12,4},{1,9},{5,13},{9,1},{13,5},{2,10},{6,14},... | collective-permute-start | bytes 294920 | tf_op jit(solution)/shard_map/ppermute | solution.py:43
  161.7 2.9 %collective-permute-start.22 = (bf16[3,256,64]{1,2,0:T(8,128)(2,1)S(1)}, bf16[3,256,64]{1,2,0:T(8,128)(2,1)S(1)}, u32[]{:S(2)}, u32[]{:S(2)}) collective-permute-start(bf16[3,256,64]{1,2,0:T(8,128)(2,1)S(1)} %multiply_convert_fusion.33), channel_id=1, source_target_pairs={{0,8},{4,12},{8,0},{12,4},{1,9},{5,13},{9,1},{13,5},{2,10},{6,14},... | collective-permute-start | bytes 294920 | tf_op jit(solution)/shard_map/ppermute | solution.py:64
  170.3 4.4 %collective-permute-done.23 = bf16[3,256,2,64]{1,3,0,2:T(8,128)(2,1)S(1)} collective-permute-done((bf16[3,256,2,64]{1,3,0,2:T(8,128)(2,1)S(1)}, bf16[3,256,2,64]{1,3,0,2:T(8,128)(2,1)S(1)}, u32[]{:S(2)}, u32[]{:S(2)}) %collective-permute-start.23) | collective-permute-done | bytes 196640 | tf_op jit(solution)/shard_map/ppermute | solution.py:64
  178.4 4.3 %collective-permute-done.24 = bf16[3,256,2,64]{1,3,0,2:T(8,128)(2,1)S(1)} collective-permute-done((bf16[3,256,2,64]{1,3,0,2:T(8,128)(2,1)S(1)}, bf16[3,256,2,64]{1,3,0,2:T(8,128)(2,1)S(1)}, u32[]{:S(2)}, u32[]{:S(2)}) %collective-permute-start.24) | collective-permute-done | bytes 196640 | tf_op jit(solution)/shard_map/ppermute | solution.py:43
  184.7 4.7 %collective-permute-done.25 = bf16[3,256,64]{1,2,0:T(8,128)(2,1)S(1)} collective-permute-done((bf16[3,256,64]{1,2,0:T(8,128)(2,1)S(1)}, bf16[3,256,64]{1,2,0:T(8,128)(2,1)S(1)}, u32[]{:S(2)}, u32[]{:S(2)}) %collective-permute-start.25) | collective-permute-done | bytes 98336 | tf_op jit(solution)/shard_map/ppermute | solution.py:43
  191.5 5.3 %collective-permute-done.26 = bf16[3,256,64]{1,2,0:T(8,128)(2,1)S(1)} collective-permute-done((bf16[3,256,64]{1,2,0:T(8,128)(2,1)S(1)}, bf16[3,256,64]{1,2,0:T(8,128)(2,1)S(1)}, u32[]{:S(2)}, u32[]{:S(2)}) %collective-permute-start.26) | collective-permute-done | bytes 98336 | tf_op jit(solution)/shard_map/ppermute | solution.py:64
  197.4 5.2 %collective-permute-done.27 = bf16[3,256,2,64]{1,3,0,2:T(8,128)(2,1)S(1)} collective-permute-done((bf16[3,256,2,64]{1,3,0,2:T(8,128)(2,1)S(1)}, bf16[3,256,2,64]{1,3,0,2:T(8,128)(2,1)S(1)}, u32[]{:S(2)}, u32[]{:S(2)}) %collective-permute-start.27) | collective-permute-done | bytes 196640 | tf_op jit(solution)/shard_map/ppermute | solution.py:64
  (189 shorter events, 65.3 us)
Async XLA Ops:
  1.6 5.3 %copy-start.6 = (f32[3,1,1,512]{3,2,1,0:T(1,128)S(1)}, f32[3,1,1,512]{3,2,1,0:T(1,128)}, u32[]{:S(2)}) copy-start(f32[3,1,1,512]{3,2,1,0:T(1,128)} %param.9) | copy-start | bytes 18436
  1.6 9.0 %collective-permute-start = (bf16[3,256,64]{1,2,0:T(8,128)(2,1)S(1)}, bf16[3,256,64]{1,2,0:T(8,128)(2,1)S(1)}, u32[]{:S(2)}, u32[]{:S(2)}) collective-permute-start(bf16[3,256,64]{1,2,0:T(8,128)(2,1)S(1)} %bitcast_convert_fusion), channel_id=1, source_target_pairs={{0,8},{4,12},{8,0},{12,4},{1,9},{5,13},{9,1},{13,5},{2,10},{6,14},... | collective-permute-start | bytes 294920 | tf_op jit(solution)/shard_map/ppermute | solution.py:64
  6.9 3.7 %copy-start.1 = (f32[1,1,3,256,64]{3,4,2,1,0:T(8,128)S(1)}, f32[1,1,3,256,64]{3,4,2,1,0:T(8,128)}, u32[]{:S(2)}) copy-start(f32[1,1,3,256,64]{3,4,2,1,0:T(8,128)} %param.10) | copy-start | bytes 589828
  10.7 6.1 %collective-permute-start.1 = (bf16[3,256,2,64]{1,3,0,2:T(8,128)(2,1)S(1)}, bf16[3,256,2,64]{1,3,0,2:T(8,128)(2,1)S(1)}, u32[]{:S(2)}, u32[]{:S(2)}) collective-permute-start(bf16[3,256,2,64]{1,3,0,2:T(8,128)(2,1)S(1)} %pad_maximum_fusion.8), channel_id=1, source_target_pairs={{0,4},{4,0},{8,12},{12,8},{1,5},{5,1},{9,13},{13,9},{2,6},{6,2},{1... | collective-permute-start | bytes 589832 | tf_op jit(solution)/shard_map/ppermute | solution.py:64
  19.8 1.6 copy-start.3
  19.8 5.9 %collective-permute-start.2 = (bf16[3,256,2,64]{1,3,2,0:T(8,128)(2,1)S(1)}, bf16[3,256,2,64]{1,3,2,0:T(8,128)(2,1)}, u32[]{:S(2)}, u32[]{:S(2)}) collective-permute-start(bf16[3,256,2,64]{1,3,2,0:T(8,128)(2,1)S(1)} %dynamic-slice_bitcast_fusion.5), channel_id=1, source_target_pairs={{0,4},{4,0},{8,12},{12,8},{1,5},{5,1},{9,13},{13,9},{2,6},{6,2},{1... | collective-permute-start | bytes 589832 | tf_op jit(solution)/shard_map/ppermute | solution.py:43
  26.7 7.4 %collective-permute-start.3 = (bf16[3,256,64]{1,2,0:T(8,128)(2,1)S(1)}, bf16[3,256,64]{1,2,0:T(8,128)(2,1)S(1)}, u32[]{:S(2)}, u32[]{:S(2)}) collective-permute-start(bf16[3,256,64]{1,2,0:T(8,128)(2,1)S(1)} %fusion.144), channel_id=1, source_target_pairs={{0,8},{4,12},{8,0},{12,4},{1,9},{5,13},{9,1},{13,5},{2,10},{6,14},... | collective-permute-start | bytes 294920 | tf_op jit(solution)/shard_map/ppermute | solution.py:43
  34.4 6.7 %collective-permute-start.4 = (bf16[3,256,64]{1,2,0:T(8,128)(2,1)S(1)}, bf16[3,256,64]{1,2,0:T(8,128)(2,1)S(1)}, u32[]{:S(2)}, u32[]{:S(2)}) collective-permute-start(bf16[3,256,64]{1,2,0:T(8,128)(2,1)S(1)} %multiply_convert_fusion.35), channel_id=1, source_target_pairs={{0,8},{4,12},{8,0},{12,4},{1,9},{5,13},{9,1},{13,5},{2,10},{6,14},... | collective-permute-start | bytes 294920 | tf_op jit(solution)/shard_map/ppermute | solution.py:64
  41.3 5.7 %collective-permute-start.5 = (bf16[3,256,2,64]{1,3,0,2:T(8,128)(2,1)S(1)}, bf16[3,256,2,64]{1,3,0,2:T(8,128)(2,1)S(1)}, u32[]{:S(2)}, u32[]{:S(2)}) collective-permute-start(bf16[3,256,2,64]{1,3,0,2:T(8,128)(2,1)S(1)} %pad_maximum_fusion.9), channel_id=1, source_target_pairs={{0,4},{4,0},{8,12},{12,8},{1,5},{5,1},{9,13},{13,9},{2,6},{6,2},{1... | collective-permute-start | bytes 589832 | tf_op jit(solution)/shard_map/ppermute | solution.py:64
  49.2 6.8 %collective-permute-start.6 = (bf16[3,256,2,64]{1,3,0,2:T(8,128)(2,1)S(1)}, bf16[3,256,2,64]{1,3,0,2:T(8,128)(2,1)S(1)}, u32[]{:S(2)}, u32[]{:S(2)}) collective-permute-start(bf16[3,256,2,64]{1,3,0,2:T(8,128)(2,1)S(1)} %dynamic-slice_bitcast_fusion.4), channel_id=1, source_target_pairs={{0,4},{4,0},{8,12},{12,8},{1,5},{5,1},{9,13},{13,9},{2,6},{6,2},{1... | collective-permute-start | bytes 589832 | tf_op jit(solution)/shard_map/ppermute | solution.py:43
  56.0 6.6 %collective-permute-start.7 = (bf16[3,256,64]{1,2,0:T(8,128)(2,1)S(1)}, bf16[3,256,64]{1,2,0:T(8,128)(2,1)S(1)}, u32[]{:S(2)}, u32[]{:S(2)}) collective-permute-start(bf16[3,256,64]{1,2,0:T(8,128)(2,1)S(1)} %fusion.145), channel_id=1, source_target_pairs={{0,8},{4,12},{8,0},{12,4},{1,9},{5,13},{9,1},{13,5},{2,10},{6,14},... | collective-permute-start | bytes 294920 | tf_op jit(solution)/shard_map/ppermute | solution.py:43
  63.0 6.1 %collective-permute-start.8 = (bf16[3,256,64]{1,2,0:T(8,128)(2,1)S(1)}, bf16[3,256,64]{1,2,0:T(8,128)(2,1)S(1)}, u32[]{:S(2)}, u32[]{:S(2)}) collective-permute-start(bf16[3,256,64]{1,2,0:T(8,128)(2,1)S(1)} %multiply_convert_fusion.31), channel_id=1, source_target_pairs={{0,8},{4,12},{8,0},{12,4},{1,9},{5,13},{9,1},{13,5},{2,10},{6,14},... | collective-permute-start | bytes 294920 | tf_op jit(solution)/shard_map/ppermute | solution.py:64
  69.2 5.7 %collective-permute-start.9 = (bf16[3,256,2,64]{1,3,0,2:T(8,128)(2,1)S(1)}, bf16[3,256,2,64]{1,3,0,2:T(8,128)(2,1)S(1)}, u32[]{:S(2)}, u32[]{:S(2)}) collective-permute-start(bf16[3,256,2,64]{1,3,0,2:T(8,128)(2,1)S(1)} %pad_maximum_fusion.10), channel_id=1, source_target_pairs={{0,4},{4,0},{8,12},{12,8},{1,5},{5,1},{9,13},{13,9},{2,6},{6,2},{1... | collective-permute-start | bytes 589832 | tf_op jit(solution)/shard_map/ppermute | solution.py:64
  75.1 8.7 %collective-permute-start.10 = (bf16[3,256,256]{1,2,0:T(8,128)(2,1)S(1)}, bf16[3,256,256]{1,2,0:T(8,128)(2,1)S(1)}, u32[]{:S(2)}, u32[]{:S(2)}) collective-permute-start(bf16[3,256,256]{1,2,0:T(8,128)(2,1)S(1)} %bitcast.473), channel_id=1, source_target_pairs={{0,2},{1,3},{4,6},{5,7},{8,10},{9,11},{12,14},{13,15},{16,18},{17,... | collective-permute-start | bytes 1179656 | tf_op jit(solution)/shard_map/ppermute | solution.py:14
  85.8 5.7 %collective-permute-start.11 = (bf16[3,256,2,64]{1,3,0,2:T(8,128)(2,1)S(1)}, bf16[3,256,2,64]{1,3,0,2:T(8,128)(2,1)S(1)}, u32[]{:S(2)}, u32[]{:S(2)}) collective-permute-start(bf16[3,256,2,64]{1,3,0,2:T(8,128)(2,1)S(1)} %dynamic-slice_bitcast_fusion.3), channel_id=1, source_target_pairs={{0,4},{4,0},{8,12},{12,8},{1,5},{5,1},{9,13},{13,9},{2,6},{6,2},{1... | collective-permute-start | bytes 589832 | tf_op jit(solution)/shard_map/ppermute | solution.py:43
  91.7 5.6 %collective-permute-start.12 = (bf16[3,256,64]{1,2,0:T(8,128)(2,1)S(1)}, bf16[3,256,64]{1,2,0:T(8,128)(2,1)S(1)}, u32[]{:S(2)}, u32[]{:S(2)}) collective-permute-start(bf16[3,256,64]{1,2,0:T(8,128)(2,1)S(1)} %fusion.146), channel_id=1, source_target_pairs={{0,8},{4,12},{8,0},{12,4},{1,9},{5,13},{9,1},{13,5},{2,10},{6,14},... | collective-permute-start | bytes 294920 | tf_op jit(solution)/shard_map/ppermute | solution.py:43
  97.6 5.6 %collective-permute-start.13 = (bf16[3,256,64]{1,2,0:T(8,128)(2,1)S(1)}, bf16[3,256,64]{1,2,0:T(8,128)(2,1)S(1)}, u32[]{:S(2)}, u32[]{:S(2)}) collective-permute-start(bf16[3,256,64]{1,2,0:T(8,128)(2,1)S(1)} %multiply_convert_fusion.34), channel_id=1, source_target_pairs={{0,8},{4,12},{8,0},{12,4},{1,9},{5,13},{9,1},{13,5},{2,10},{6,14},... | collective-permute-start | bytes 294920 | tf_op jit(solution)/shard_map/ppermute | solution.py:64
  103.3 7.6 %collective-permute-start.14 = (bf16[3,256,2,64]{1,3,0,2:T(8,128)(2,1)S(1)}, bf16[3,256,2,64]{1,3,0,2:T(8,128)(2,1)S(1)}, u32[]{:S(2)}, u32[]{:S(2)}) collective-permute-start(bf16[3,256,2,64]{1,3,0,2:T(8,128)(2,1)S(1)} %pad_maximum_fusion.11), channel_id=1, source_target_pairs={{0,4},{4,0},{8,12},{12,8},{1,5},{5,1},{9,13},{13,9},{2,6},{6,2},{1... | collective-permute-start | bytes 589832 | tf_op jit(solution)/shard_map/ppermute | solution.py:64
  113.1 5.7 %collective-permute-start.15 = (bf16[3,256,2,64]{1,3,0,2:T(8,128)(2,1)S(1)}, bf16[3,256,2,64]{1,3,0,2:T(8,128)(2,1)S(1)}, u32[]{:S(2)}, u32[]{:S(2)}) collective-permute-start(bf16[3,256,2,64]{1,3,0,2:T(8,128)(2,1)S(1)} %dynamic-slice_bitcast_fusion.2), channel_id=1, source_target_pairs={{0,4},{4,0},{8,12},{12,8},{1,5},{5,1},{9,13},{13,9},{2,6},{6,2},{1... | collective-permute-start | bytes 589832 | tf_op jit(solution)/shard_map/ppermute | solution.py:43
  118.9 5.6 %collective-permute-start.16 = (bf16[3,256,64]{1,2,0:T(8,128)(2,1)S(1)}, bf16[3,256,64]{1,2,0:T(8,128)(2,1)S(1)}, u32[]{:S(2)}, u32[]{:S(2)}) collective-permute-start(bf16[3,256,64]{1,2,0:T(8,128)(2,1)S(1)} %fusion.147), channel_id=1, source_target_pairs={{0,8},{4,12},{8,0},{12,4},{1,9},{5,13},{9,1},{13,5},{2,10},{6,14},... | collective-permute-start | bytes 294920 | tf_op jit(solution)/shard_map/ppermute | solution.py:43
  124.9 5.6 %collective-permute-start.17 = (bf16[3,256,64]{1,2,0:T(8,128)(2,1)S(1)}, bf16[3,256,64]{1,2,0:T(8,128)(2,1)S(1)}, u32[]{:S(2)}, u32[]{:S(2)}) collective-permute-start(bf16[3,256,64]{1,2,0:T(8,128)(2,1)S(1)} %multiply_convert_fusion.30), channel_id=1, source_target_pairs={{0,8},{4,12},{8,0},{12,4},{1,9},{5,13},{9,1},{13,5},{2,10},{6,14},... | collective-permute-start | bytes 294920 | tf_op jit(solution)/shard_map/ppermute | solution.py:64
  130.5 7.4 %collective-permute-start.18 = (bf16[3,256,2,64]{1,3,0,2:T(8,128)(2,1)S(1)}, bf16[3,256,2,64]{1,3,0,2:T(8,128)(2,1)S(1)}, u32[]{:S(2)}, u32[]{:S(2)}) collective-permute-start(bf16[3,256,2,64]{1,3,0,2:T(8,128)(2,1)S(1)} %pad_maximum_fusion.12), channel_id=1, source_target_pairs={{0,4},{4,0},{8,12},{12,8},{1,5},{5,1},{9,13},{13,9},{2,6},{6,2},{1... | collective-permute-start | bytes 589832 | tf_op jit(solution)/shard_map/ppermute | solution.py:64
  138.0 9.7 %collective-permute-start.19 = (bf16[3,256,256]{1,2,0:T(8,128)(2,1)S(1)}, bf16[3,256,256]{1,2,0:T(8,128)(2,1)S(1)}, u32[]{:S(2)}, u32[]{:S(2)}) collective-permute-start(bf16[3,256,256]{1,2,0:T(8,128)(2,1)S(1)} %bitcast.474), channel_id=1, source_target_pairs={{0,2},{1,3},{4,6},{5,7},{8,10},{9,11},{12,14},{13,15},{16,18},{17,... | collective-permute-start | bytes 1179656 | tf_op jit(solution)/shard_map/ppermute | solution.py:14
  149.8 6.0 %collective-permute-start.20 = (bf16[3,256,2,64]{1,3,0,2:T(8,128)(2,1)S(1)}, bf16[3,256,2,64]{1,3,0,2:T(8,128)(2,1)S(1)}, u32[]{:S(2)}, u32[]{:S(2)}) collective-permute-start(bf16[3,256,2,64]{1,3,0,2:T(8,128)(2,1)S(1)} %dynamic-slice_bitcast_fusion.1), channel_id=1, source_target_pairs={{0,4},{4,0},{8,12},{12,8},{1,5},{5,1},{9,13},{13,9},{2,6},{6,2},{1... | collective-permute-start | bytes 589832 | tf_op jit(solution)/shard_map/ppermute | solution.py:43
  155.9 5.6 %collective-permute-start.21 = (bf16[3,256,64]{1,2,0:T(8,128)(2,1)S(1)}, bf16[3,256,64]{1,2,0:T(8,128)(2,1)S(1)}, u32[]{:S(2)}, u32[]{:S(2)}) collective-permute-start(bf16[3,256,64]{1,2,0:T(8,128)(2,1)S(1)} %fusion.148), channel_id=1, source_target_pairs={{0,8},{4,12},{8,0},{12,4},{1,9},{5,13},{9,1},{13,5},{2,10},{6,14},... | collective-permute-start | bytes 294920 | tf_op jit(solution)/shard_map/ppermute | solution.py:43
  161.7 5.9 %collective-permute-start.22 = (bf16[3,256,64]{1,2,0:T(8,128)(2,1)S(1)}, bf16[3,256,64]{1,2,0:T(8,128)(2,1)S(1)}, u32[]{:S(2)}, u32[]{:S(2)}) collective-permute-start(bf16[3,256,64]{1,2,0:T(8,128)(2,1)S(1)} %multiply_convert_fusion.33), channel_id=1, source_target_pairs={{0,8},{4,12},{8,0},{12,4},{1,9},{5,13},{9,1},{13,5},{2,10},{6,14},... | collective-permute-start | bytes 294920 | tf_op jit(solution)/shard_map/ppermute | solution.py:64
  164.7 5.3 %copy-start.2 = (bf16[3,1,512,1,256]{4,2,3,1,0:T(8,128)(2,1)S(1)}, bf16[3,1,512,1,256]{4,2,3,1,0:T(8,128)(2,1)}, u32[]{:S(2)}) copy-start(bf16[3,1,512,1,256]{4,2,3,1,0:T(8,128)(2,1)} %param.8) | copy-start | bytes 2359300
  167.8 7.0 %collective-permute-start.23 = (bf16[3,256,2,64]{1,3,0,2:T(8,128)(2,1)S(1)}, bf16[3,256,2,64]{1,3,0,2:T(8,128)(2,1)S(1)}, u32[]{:S(2)}, u32[]{:S(2)}) collective-permute-start(bf16[3,256,2,64]{1,3,0,2:T(8,128)(2,1)S(1)} %pad_maximum_fusion.13), channel_id=1, source_target_pairs={{0,4},{4,0},{8,12},{12,8},{1,5},{5,1},{9,13},{13,9},{2,6},{6,2},{1... | collective-permute-start | bytes 589832 | tf_op jit(solution)/shard_map/ppermute | solution.py:64
  176.9 5.7 %collective-permute-start.24 = (bf16[3,256,2,64]{1,3,0,2:T(8,128)(2,1)S(1)}, bf16[3,256,2,64]{1,3,0,2:T(8,128)(2,1)S(1)}, u32[]{:S(2)}, u32[]{:S(2)}) collective-permute-start(bf16[3,256,2,64]{1,3,0,2:T(8,128)(2,1)S(1)} %dynamic-slice_bitcast_fusion), channel_id=1, source_target_pairs={{0,4},{4,0},{8,12},{12,8},{1,5},{5,1},{9,13},{13,9},{2,6},{6,2},{1... | collective-permute-start | bytes 589832 | tf_op jit(solution)/shard_map/ppermute | solution.py:43
  182.7 6.6 %collective-permute-start.25 = (bf16[3,256,64]{1,2,0:T(8,128)(2,1)S(1)}, bf16[3,256,64]{1,2,0:T(8,128)(2,1)S(1)}, u32[]{:S(2)}, u32[]{:S(2)}) collective-permute-start(bf16[3,256,64]{1,2,0:T(8,128)(2,1)S(1)} %fusion.149), channel_id=1, source_target_pairs={{0,8},{4,12},{8,0},{12,4},{1,9},{5,13},{9,1},{13,5},{2,10},{6,14},... | collective-permute-start | bytes 294920 | tf_op jit(solution)/shard_map/ppermute | solution.py:43
  190.4 6.4 %collective-permute-start.26 = (bf16[3,256,64]{1,2,0:T(8,128)(2,1)S(1)}, bf16[3,256,64]{1,2,0:T(8,128)(2,1)S(1)}, u32[]{:S(2)}, u32[]{:S(2)}) collective-permute-start(bf16[3,256,64]{1,2,0:T(8,128)(2,1)S(1)} %get-tuple-element.53), channel_id=1, source_target_pairs={{0,8},{4,12},{8,0},{12,4},{1,9},{5,13},{9,1},{13,5},{2,10},{6,14},... | collective-permute-start | bytes 294920 | tf_op jit(solution)/shard_map/ppermute | solution.py:64
  196.8 5.7 %collective-permute-start.27 = (bf16[3,256,2,64]{1,3,0,2:T(8,128)(2,1)S(1)}, bf16[3,256,2,64]{1,3,0,2:T(8,128)(2,1)S(1)}, u32[]{:S(2)}, u32[]{:S(2)}) collective-permute-start(bf16[3,256,2,64]{1,3,0,2:T(8,128)(2,1)S(1)} %pad_maximum_fusion.14), channel_id=1, source_target_pairs={{0,4},{4,0},{8,12},{12,8},{1,5},{5,1},{9,13},{13,9},{2,6},{6,2},{1... | collective-permute-start | bytes 589832 | tf_op jit(solution)/shard_map/ppermute | solution.py:64
  (3 other events, 3.3 us)

commit v4 on v1

v4 whole, which is shorter than its diff:
```python
import math

import jax
import numpy as np
import jax.numpy as jnp
from jax import lax
from jax.sharding import PartitionSpec as P

ITERS = 2


def shifted(value, axis, by):
    devices = lax.axis_size(axis)
    pairs = [(i, i + by) for i in range(devices) if 0 <= i + by < devices]
    return lax.ppermute(value, axis, pairs)


def rotated(value, axis, by):
    devices = lax.axis_size(axis)
    return lax.ppermute(value, axis, [(i, (i + by) % devices) for i in range(devices)])


def scatter_sum(partial, part_cols):
    tok_count = lax.axis_size("tok")
    me = lax.axis_index("tok")
    last = partial.ndim - 1
    total = lax.dynamic_slice_in_dim(partial, me * part_cols, part_cols, last).astype(jnp.float32)
    for by in range(1, tok_count):
        chunk = lax.dynamic_slice_in_dim(partial, ((me + by) % tok_count) * part_cols, part_cols, last)
        total = total + rotated(chunk, "tok", by).astype(jnp.float32)
    return total


def gather_cols(own, part_cols):
    tok_count = lax.axis_size("tok")
    me = lax.axis_index("tok")
    last = own.ndim - 1
    full = jnp.zeros(own.shape[:-1] + (part_cols * tok_count,), own.dtype)
    full = lax.dynamic_update_slice_in_dim(full, own, me * part_cols, last)
    for by in range(1, tok_count):
        got = rotated(own, "tok", by)
        full = lax.dynamic_update_slice_in_dim(full, got, ((me - by) % tok_count) * part_cols, last)
    return full


def renormalize(matrices, init_norms):
    column_norms = jnp.sqrt(jnp.sum(matrices * matrices, axis=-2) + 1e-06)
    return matrices * (init_norms / column_norms)[..., None, :]


def fast_grads(fast, key_block, scaled):
    gate_pre = jnp.einsum("btd,bdh->bth", key_block, fast[:, 0], preferred_element_type=jnp.float32)
    up_pre = jnp.einsum("btd,bdh->bth", key_block, fast[:, 1], preferred_element_type=jnp.float32)
    sigmoid_gate = jax.nn.sigmoid(gate_pre)
    gated = gate_pre * sigmoid_gate
    hidden = (gated * up_pre).astype(jnp.bfloat16)
    back_grad = jnp.einsum("btd,bhd->bth", scaled, fast[:, 2], preferred_element_type=jnp.float32)
    grad_gate = (
        back_grad * up_pre * sigmoid_gate * (1.0 + gate_pre * (1.0 - sigmoid_gate))
    ).astype(jnp.bfloat16)
    grad_up = (back_grad * gated).astype(jnp.bfloat16)
    first = jnp.einsum("btd,bth->bdh", key_block, grad_gate, preferred_element_type=jnp.float32)
    second = jnp.einsum("btd,bth->bdh", key_block, grad_up, preferred_element_type=jnp.float32)
    third = jnp.einsum("bth,btd->bhd", hidden, scaled, preferred_element_type=jnp.float32)
    return jnp.stack([first, second, third], axis=1).astype(jnp.bfloat16)


def apply_fast(fast, query_block):
    query_gate = jnp.einsum(
        "btd,bdh->bth", query_block, fast[:, 0], preferred_element_type=jnp.float32
    )
    query_up = jnp.einsum("btd,bdh->bth", query_block, fast[:, 1], preferred_element_type=jnp.float32)
    applied = (query_gate * jax.nn.sigmoid(query_gate) * query_up).astype(jnp.bfloat16)
    return jnp.einsum(
        "bth,bhd->btd", applied, fast[:, 2], preferred_element_type=jnp.float32
    ).astype(jnp.bfloat16)


def section_plan(sections, ticks):
    depth = min(sections, ticks)
    slots = -(-ticks // depth)
    done = {}
    phases = []
    while len(done) < sections * ticks:
        phase = len(phases)
        chosen = []
        for s in range(sections):
            ready = [
                t
                for t in range(ticks)
                if (s, t) not in done and (t == 0 or s == 0 or (s - 1, t - 1) in done)
            ]
            chosen.append(ready[:slots])
        for s in range(sections):
            for k, t in enumerate(chosen[s]):
                done[(s, t)] = (phase, k)
        phases.append(chosen)
    return slots, phases, done


def on_device(key_rows, value_rows, query_rows, step_rates, states_in, init_weights):
    tok_count = lax.axis_size("tok")
    sections = lax.axis_size("span")
    feature_width = init_weights.shape[-1]
    part_cols = feature_width // tok_count
    rate_scale = 1.0 / math.sqrt(key_rows.shape[2] * tok_count * feature_width)
    section_index = lax.axis_index("span")
    tok_index = lax.axis_index("tok")
    tick_count = key_rows.shape[0]
    slots, phases, done = section_plan(sections, tick_count)

    init_fast = init_weights[0]
    init_full = init_fast.astype(jnp.float32)
    init_norms = jnp.sqrt(jnp.sum(init_full * init_full, axis=-2) + 1e-06)
    own_norms = lax.dynamic_slice_in_dim(init_norms, tok_index * part_cols, part_cols, 1)
    own_cols = lambda m: lax.dynamic_slice_in_dim(m, tok_index * part_cols, part_cols, m.ndim - 1)

    keys = key_rows[:, 0, :, 0]
    queries = query_rows[:, 0, :, 0]
    scaled_all = (
        (step_rates[:, 0, 0] * rate_scale)[:, :, None] * value_rows[:, 0, :, 0].astype(jnp.float32)
    ).astype(jnp.bfloat16)

    start_weights = states_in[0, 0]
    start_fast = gather_cols(start_weights.astype(jnp.bfloat16), part_cols)
    fast_pool = [start_fast, init_fast]
    weight_pool = [start_weights, own_cols(init_full)]
    slot_code = {}
    finals = []
    out_rows = jnp.zeros((tick_count + 1,) + queries.shape[1:], jnp.bfloat16)
    for phase, chosen in enumerate(phases):
        ticks_here = np.full((slots, sections), tick_count, np.int32)
        source = np.ones((slots, sections), np.int32)
        for s in range(sections):
            for k, t in enumerate(chosen[s]):
                ticks_here[k, s] = t
                if t == 0:
                    source[k, s] = 0
                elif s > 0:
                    q, j = done[(s - 1, t - 1)]
                    source[k, s] = slot_code[(q, j)]
        my_ticks = jnp.asarray(ticks_here)[:, section_index]
        my_source = jnp.asarray(source)[:, section_index]
        fast_stack = jnp.stack(fast_pool)
        weight_stack = jnp.stack(weight_pool)
        fast = jnp.stack([lax.dynamic_index_in_dim(fast_stack, my_source[k], 0, False) for k in range(slots)])
        weights = jnp.stack(
            [lax.dynamic_index_in_dim(weight_stack, my_source[k], 0, False) for k in range(slots)]
        )
        row = jnp.minimum(my_ticks, tick_count - 1)
        key_block = jnp.stack([lax.dynamic_index_in_dim(keys, row[k], 0, False) for k in range(slots)])
        scaled = jnp.stack([lax.dynamic_index_in_dim(scaled_all, row[k], 0, False) for k in range(slots)])
        query_block = jnp.stack([lax.dynamic_index_in_dim(queries, row[k], 0, False) for k in range(slots)])
        for update_step in range(ITERS):
            if update_step > 0:
                fast = gather_cols(weights.astype(jnp.bfloat16), part_cols)
            summed = scatter_sum(fast_grads(fast, key_block, scaled), part_cols)
            weights = renormalize(weights + summed, own_norms)
        fast = gather_cols(weights.astype(jnp.bfloat16), part_cols)
        result = apply_fast(fast, query_block)
        for k in range(slots):
            out_rows = lax.dynamic_update_index_in_dim(out_rows, result[k], my_ticks[k], 0)
            finals.append(weights[k])
        if phase + 1 < len(phases):
            arrived = shifted(fast, "span", 1)
            for k in range(slots):
                slot_code[(phase, k)] = len(fast_pool)
                fast_pool.append(arrived[k])
                weight_pool.append(own_cols(arrived[k]).astype(jnp.float32))
    last = np.zeros((sections,), np.int32)
    for s in range(sections):
        q, j = done[(s, tick_count - 1)]
        last[s] = q * slots + j
    final = lax.dynamic_index_in_dim(jnp.stack(finals), jnp.asarray(last)[section_index], 0, False)
    outputs = out_rows[:tick_count][:, None, :, None]
    return (outputs, final[None, None])


def solution(mesh):
    placed = (
        P("groups", "span", "tok", "head", None),
        P("groups", "span", "tok", "head", None),
        P("groups", "span", "tok", "head", None),
        P("groups", "span", "head", "tok"),
        P(("groups", "span"), "head", None, None, "tok"),
        P("head", None, None, None),
    )
    return jax.shard_map(
        on_device,
        mesh=mesh,
        in_specs=placed,
        out_specs=(
            P("groups", "span", "tok", "head", None),
            P(("groups", "span"), "head", None, None, "tok"),
        ),
        check_vma=False,
    )
```

time: 186 us -> 410 us (2.20)
  the two profiles are of different devices: /device:TPU:0 before, /device:TPU:28 now
where the time goes in v4:
time: 410 us; the launch traced here: 408 us
  waiting for transfers between devices  211 us (51%)
  local copies, waits for them, and re-layouts  87.1 us (21%)
  starting transfers between devices  55.4 us (14%)
  between operations  26 us (6%)
  matrix products  20.3 us (5%)
  other arithmetic  8.5 us (2%)
    ppermute x27, waiting for transfers between devices, rotated(): lax.ppermute(value, axis, [(i, (i + by) % devices) for i in range(devices)])  211 us
    dynamic_update_slice x15, local copies, waits for them, and re-layouts, gather_cols(): lax.dynamic_update_slice_in_dim(full, got, (me - by) % tok_count * part_c...  52.6 us
    ppermute x27, starting transfers between devices, rotated(): lax.ppermute(value, axis, [(i, (i + by) % devices) for i in range(devices)])  51.9 us
    dynamic_update_slice x5, local copies, waits for them, and re-layouts, gather_cols(): full = lax.dynamic_update_slice_in_dim(full, own, me * part_cols, last)  17.4 us
  transfers between devices with their start and end apart: 28, of which 14 were waited for; matrix products, arithmetic and copies ran while one was open for 19% of the time, Pallas kernels for 0%

profile of v4, /device:TPU:28, one launch (start us, length us, event | category | flops | bytes accessed | tf_op | source)
XLA Modules:
  0.0 408.0 jit_solution(11487132902037665380)
XLA Ops:
  28.0 3.1 dynamic_update_slice.79
  36.1 3.5 collective-permute-start.3
  41.0 8.1 %collective-permute-done.3 = bf16[2,3,256,64]{3,2,0,1:T(8,128)(2,1)S(1)} collective-permute-done((bf16[2,3,256,64]{3,2,0,1:T(8,128)(2,1)S(1)}, bf16[2,3,256,64]{3,2,0,1:T(8,128)(2,1)S(1)}, u32[]{:S(2)}, u32[]{:S(2)}) %collective-permute-start.3) | collective-permute-done | bytes 196640 | tf_op jit(solution)/shard_map/ppermute | solution.py:20
  49.1 23.2 %collective-permute-done.4 = bf16[2,3,256,64]{3,2,0,1:T(8,128)(2,1)S(1)} collective-permute-done((bf16[2,3,256,64]{3,2,0,1:T(8,128)(2,1)S(1)}, bf16[2,3,256,64]{3,2,0,1:T(8,128)(2,1)S(1)}, u32[]{:S(2)}, u32[]{:S(2)}) %collective-permute-start.4) | collective-permute-done | bytes 196640 | tf_op jit(solution)/shard_map/ppermute | solution.py:20
  73.6 3.0 collective-permute-start.7
  79.5 4.9 %dynamic_update_slice.81 = bf16[2,3,256,256]{3,2,0,1:T(8,128)(2,1)} dynamic-update-slice(bf16[2,3,256,256]{3,2,0,1:T(8,128)(2,1)} %broadcast.63.clone.1, bf16[2,3,256,64]{3,2,0,1:T(8,128)(2,1)} %multiply_convert_fusion.15, s32[]{:T(128)} %constant.184.clone.1, s32[]{:T(128)} %constant.184.clone.1, s32[]{:T(128)} %constant.184.clone.1, s32[]{:T(128)S(6)} %select_n.190) | dynamic-update-slice | bytes 393220 | tf_op jit(solution)/shard_map/dynamic_update_slice | solution.py:39
  84.3 4.0 dynamic_update_slice.82
  88.4 22.5 %collective-permute-done.7 = bf16[2,3,256,64]{3,2,0,1:T(8,128)(2,1)} collective-permute-done((bf16[2,3,256,64]{3,2,0,1:T(8,128)(2,1)}, bf16[2,3,256,64]{3,2,0,1:T(8,128)(2,1)}, u32[]{:S(2)}, u32[]{:S(2)}) %collective-permute-start.7) | collective-permute-done | bytes 196640 | tf_op jit(solution)/shard_map/ppermute | solution.py:20
  110.9 5.5 %dynamic_update_slice.83 = bf16[2,3,256,256]{3,2,0,1:T(8,128)(2,1)} dynamic-update-slice(bf16[2,3,256,256]{3,2,0,1:T(8,128)(2,1)} %dynamic_update_slice.82, bf16[2,3,256,64]{3,2,0,1:T(8,128)(2,1)} %collective-permute-done.7, s32[]{:T(128)} %constant.184.clone.1, s32[]{:T(128)} %constant.184.clone.1, s32[]{:T(128)} %constant.184.clone.1, s32[]{:T(128)S(6)} %select_n.196) | dynamic-update-slice | bytes 393220 | tf_op jit(solution)/shard_map/dynamic_update_slice | solution.py:42
  116.4 4.7 %dynamic_update_slice.84 = bf16[2,3,256,256]{3,2,0,1:T(8,128)(2,1)} dynamic-update-slice(bf16[2,3,256,256]{3,2,0,1:T(8,128)(2,1)} %dynamic_update_slice.83, bf16[2,3,256,64]{3,2,0,1:T(8,128)(2,1)} %collective-permute-done.8, s32[]{:T(128)} %constant.184.clone.1, s32[]{:T(128)} %constant.184.clone.1, s32[]{:T(128)} %constant.184.clone.1, s32[]{:T(128)S(6)} %select_n.198) | dynamic-update-slice | bytes 393220 | tf_op jit(solution)/shard_map/dynamic_update_slice | solution.py:42
  126.0 3.8 collective-permute-start.9
  129.8 16.4 %collective-permute-done.10 = bf16[2,3,256,64]{3,2,0,1:T(8,128)(2,1)S(1)} collective-permute-done((bf16[2,3,256,64]{3,2,0,1:T(8,128)(2,1)S(1)}, bf16[2,3,256,64]{3,2,0,1:T(8,128)(2,1)S(1)}, u32[]{:S(2)}, u32[]{:S(2)}) %collective-permute-start.10) | collective-permute-done | bytes 196640 | tf_op jit(solution)/shard_map/ppermute | solution.py:20
  146.2 7.7 %collective-permute-done.9 = bf16[2,3,256,64]{3,2,0,1:T(8,128)(2,1)S(1)} collective-permute-done((bf16[2,3,256,64]{3,2,0,1:T(8,128)(2,1)S(1)}, bf16[2,3,256,64]{3,2,0,1:T(8,128)(2,1)S(1)}, u32[]{:S(2)}, u32[]{:S(2)}) %collective-permute-start.9) | collective-permute-done | bytes 196640 | tf_op jit(solution)/shard_map/ppermute | solution.py:20
  158.5 4.7 %dynamic_update_slice.85 = bf16[2,3,256,256]{3,2,0,1:T(8,128)(2,1)} dynamic-update-slice(bf16[2,3,256,256]{3,2,0,1:T(8,128)(2,1)} %broadcast.63.clone, bf16[2,3,256,64]{3,2,0,1:T(8,128)(2,1)S(1)} %get-tuple-element.8, s32[]{:T(128)} %constant.184.clone.1, s32[]{:T(128)} %constant.184.clone.1, s32[]{:T(128)} %constant.184.clone.1, s32[]{:T(128)S(6)} %select_n.190) | dynamic-update-slice | bytes 393220 | tf_op jit(solution)/shard_map/dynamic_update_slice | solution.py:39
  163.2 3.0 collective-permute-done.12
  166.2 4.0 dynamic_update_slice.86
  170.2 21.3 %collective-permute-done.13 = bf16[2,3,256,64]{3,2,0,1:T(8,128)(2,1)S(1)} collective-permute-done((bf16[2,3,256,64]{3,2,0,1:T(8,128)(2,1)S(1)}, bf16[2,3,256,64]{3,2,0,1:T(8,128)(2,1)S(1)}, u32[]{:S(2)}, u32[]{:S(2)}) %collective-permute-start.13) | collective-permute-done | bytes 196640 | tf_op jit(solution)/shard_map/ppermute | solution.py:20
  191.5 5.3 %dynamic_update_slice.87 = bf16[2,3,256,256]{3,2,0,1:T(8,128)(2,1)} dynamic-update-slice(bf16[2,3,256,256]{3,2,0,1:T(8,128)(2,1)} %dynamic_update_slice.86, bf16[2,3,256,64]{3,2,0,1:T(8,128)(2,1)S(1)} %collective-permute-done.13, s32[]{:T(128)} %constant.184.clone.1, s32[]{:T(128)} %constant.184.clone.1, s32[]{:T(128)} %constant.184.clone.1, s32[]{:T(128)S(6)} %select_n.196) | dynamic-update-slice | bytes 393220 | tf_op jit(solution)/shard_map/dynamic_update_slice | solution.py:42
  196.8 4.4 %dynamic_update_slice.88 = bf16[2,3,256,256]{3,2,0,1:T(8,128)(2,1)} dynamic-update-slice(bf16[2,3,256,256]{3,2,0,1:T(8,128)(2,1)} %dynamic_update_slice.87, bf16[2,3,256,64]{3,2,0,1:T(8,128)(2,1)S(1)} %collective-permute-done.14, s32[]{:T(128)} %constant.184.clone.1, s32[]{:T(128)} %constant.184.clone.1, s32[]{:T(128)} %constant.184.clone.1, s32[]{:T(128)S(6)} %select_n.198) | dynamic-update-slice | bytes 393220 | tf_op jit(solution)/shard_map/dynamic_update_slice | solution.py:42
  201.2 3.4 collective-permute-start.15
  231.5 9.8 %collective-permute-done.16 = bf16[2,3,256,64]{3,2,0,1:T(8,128)(2,1)S(1)} collective-permute-done((bf16[2,3,256,64]{3,2,0,1:T(8,128)(2,1)S(1)}, bf16[2,3,256,64]{3,2,0,1:T(8,128)(2,1)S(1)}, u32[]{:S(2)}, u32[]{:S(2)}) %collective-permute-start.16) | collective-permute-done | bytes 196640 | tf_op jit(solution)/shard_map/ppermute | solution.py:20
  241.3 19.4 %collective-permute-done.17 = bf16[2,3,256,64]{3,2,0,1:T(8,128)(2,1)S(1)} collective-permute-done((bf16[2,3,256,64]{3,2,0,1:T(8,128)(2,1)S(1)}, bf16[2,3,256,64]{3,2,0,1:T(8,128)(2,1)S(1)}, u32[]{:S(2)}, u32[]{:S(2)}) %collective-permute-start.17) | collective-permute-done | bytes 196640 | tf_op jit(solution)/shard_map/ppermute | solution.py:20
  261.2 13.1 %collective-permute-start.20 = (bf16[2,3,256,64]{3,2,0,1:T(8,128)(2,1)S(1)}, bf16[2,3,256,64]{3,2,0,1:T(8,128)(2,1)}, u32[]{:S(2)}, u32[]{:S(2)}) collective-permute-start(bf16[2,3,256,64]{3,2,0,1:T(8,128)(2,1)S(1)} %multiply_convert_fusion.14), channel_id=1, source_target_pairs={{0,8},{4,12},{8,0},{12,4},{1,9},{5,13},{9,1},{13,5},{2,10},{6,14},... | collective-permute-start | bytes 589832 | tf_op jit(solution)/shard_map/ppermute | solution.py:20
  282.0 3.5 dynamic_update_slice.92
  285.5 23.4 %collective-permute-done.20 = bf16[2,3,256,64]{3,2,0,1:T(8,128)(2,1)} collective-permute-done((bf16[2,3,256,64]{3,2,0,1:T(8,128)(2,1)S(1)}, bf16[2,3,256,64]{3,2,0,1:T(8,128)(2,1)}, u32[]{:S(2)}, u32[]{:S(2)}) %collective-permute-start.20) | collective-permute-done | bytes 196640 | tf_op jit(solution)/shard_map/ppermute | solution.py:20
  308.9 4.7 %dynamic_update_slice.93 = bf16[2,3,256,256]{3,2,0,1:T(8,128)(2,1)S(1)} dynamic-update-slice(bf16[2,3,256,256]{3,2,0,1:T(8,128)(2,1)S(1)} %dynamic_update_slice.92, bf16[2,3,256,64]{3,2,0,1:T(8,128)(2,1)} %collective-permute-done.20, s32[]{:T(128)} %constant.184.clone.1, s32[]{:T(128)} %constant.184.clone.1, s32[]{:T(128)} %constant.184.clone.1, s32[]{:T(128)S(6)} %select_n.196) | dynamic-update-slice | bytes 393220 | tf_op jit(solution)/shard_map/dynamic_update_slice | solution.py:42
  320.7 9.6 %collective-permute-done.22 = bf16[2,3,256,64]{3,2,0,1:T(8,128)(2,1)S(1)} collective-permute-done((bf16[2,3,256,64]{3,2,0,1:T(8,128)(2,1)S(1)}, bf16[2,3,256,64]{3,2,0,1:T(8,128)(2,1)S(1)}, u32[]{:S(2)}, u32[]{:S(2)}) %collective-permute-start.22) | collective-permute-done | bytes 196640 | tf_op jit(solution)/shard_map/ppermute | solution.py:20
  330.3 21.3 %collective-permute-done.23 = bf16[2,3,256,64]{3,2,0,1:T(8,128)(2,1)S(1)} collective-permute-done((bf16[2,3,256,64]{3,2,0,1:T(8,128)(2,1)S(1)}, bf16[2,3,256,64]{3,2,0,1:T(8,128)(2,1)S(1)}, u32[]{:S(2)}, u32[]{:S(2)}) %collective-permute-start.23) | collective-permute-done | bytes 196640 | tf_op jit(solution)/shard_map/ppermute | solution.py:20
  352.3 12.4 %collective-permute-start.26 = (bf16[2,3,256,64]{3,2,0,1:T(8,128)(2,1)S(1)}, bf16[2,3,256,64]{3,2,0,1:T(8,128)(2,1)S(1)}, u32[]{:S(2)}, u32[]{:S(2)}) collective-permute-start(bf16[2,3,256,64]{3,2,0,1:T(8,128)(2,1)S(1)} %get-tuple-element.2), channel_id=1, source_target_pairs={{0,8},{4,12},{8,0},{12,4},{1,9},{5,13},{9,1},{13,5},{2,10},{6,14},... | collective-permute-start | bytes 589832 | tf_op jit(solution)/shard_map/ppermute | solution.py:20
  371.9 3.5 dynamic_update_slice.96
  375.4 23.8 %collective-permute-done.26 = bf16[2,3,256,64]{3,2,0,1:T(8,128)(2,1)S(1)} collective-permute-done((bf16[2,3,256,64]{3,2,0,1:T(8,128)(2,1)S(1)}, bf16[2,3,256,64]{3,2,0,1:T(8,128)(2,1)S(1)}, u32[]{:S(2)}, u32[]{:S(2)}) %collective-permute-start.26) | collective-permute-done | bytes 196640 | tf_op jit(solution)/shard_map/ppermute | solution.py:20
  399.1 3.1 dynamic_update_slice.97
  (169 shorter events, 78.1 us)
Async XLA Ops:
  2.6 23.1 %collective-permute-start = (bf16[3,256,64]{2,1,0:T(8,128)(2,1)}, bf16[3,256,64]{2,1,0:T(8,128)(2,1)}, u32[]{:S(2)}, u32[]{:S(2)}) collective-permute-start(bf16[3,256,64]{2,1,0:T(8,128)(2,1)} %get-tuple-element.48), channel_id=1, source_target_pairs={{0,4},{4,8},{8,12},{12,0},{1,5},{5,9},{9,13},{13,1},{2,6},{6,10},{... | collective-permute-start | bytes 294920 | tf_op jit(solution)/shard_map/ppermute | solution.py:20
  2.8 25.2 %collective-permute-start.1 = (bf16[3,256,64]{2,1,0:T(8,128)(2,1)}, bf16[3,256,64]{2,1,0:T(8,128)(2,1)}, u32[]{:S(2)}, u32[]{:S(2)}) collective-permute-start(bf16[3,256,64]{2,1,0:T(8,128)(2,1)} %get-tuple-element.48), channel_id=1, source_target_pairs={{0,8},{4,12},{8,0},{12,4},{1,9},{5,13},{9,1},{13,5},{2,10},{6,14},... | collective-permute-start | bytes 294920 | tf_op jit(solution)/shard_map/ppermute | solution.py:20
  4.5 26.6 %collective-permute-start.2 = (bf16[3,256,64]{2,1,0:T(8,128)(2,1)}, bf16[3,256,64]{2,1,0:T(8,128)(2,1)S(1)}, u32[]{:S(2)}, u32[]{:S(2)}) collective-permute-start(bf16[3,256,64]{2,1,0:T(8,128)(2,1)} %get-tuple-element.48), channel_id=1, source_target_pairs={{0,12},{4,0},{8,4},{12,8},{1,13},{5,1},{9,5},{13,9},{2,14},{6,2},{... | collective-permute-start | bytes 294920 | tf_op jit(solution)/shard_map/ppermute | solution.py:20
  36.1 13.0 %collective-permute-start.3 = (bf16[2,3,256,64]{3,2,0,1:T(8,128)(2,1)S(1)}, bf16[2,3,256,64]{3,2,0,1:T(8,128)(2,1)S(1)}, u32[]{:S(2)}, u32[]{:S(2)}) collective-permute-start(bf16[2,3,256,64]{3,2,0,1:T(8,128)(2,1)S(1)} %get-tuple-element.43), channel_id=1, source_target_pairs={{0,4},{4,8},{8,12},{12,0},{1,5},{5,9},{9,13},{13,1},{2,6},{6,10},{... | collective-permute-start | bytes 589832 | tf_op jit(solution)/shard_map/ppermute | solution.py:20
  39.6 32.7 %collective-permute-start.4 = (bf16[2,3,256,64]{3,2,0,1:T(8,128)(2,1)S(1)}, bf16[2,3,256,64]{3,2,0,1:T(8,128)(2,1)S(1)}, u32[]{:S(2)}, u32[]{:S(2)}) collective-permute-start(bf16[2,3,256,64]{3,2,0,1:T(8,128)(2,1)S(1)} %get-tuple-element.45), channel_id=1, source_target_pairs={{0,8},{4,12},{8,0},{12,4},{1,9},{5,13},{9,1},{13,5},{2,10},{6,14},... | collective-permute-start | bytes 589832 | tf_op jit(solution)/shard_map/ppermute | solution.py:20
  39.6 32.7 %collective-permute-start.5 = (bf16[2,3,256,64]{3,2,0,1:T(8,128)(2,1)S(1)}, bf16[2,3,256,64]{3,2,0,1:T(8,128)(2,1)S(1)}, u32[]{:S(2)}, u32[]{:S(2)}) collective-permute-start(bf16[2,3,256,64]{3,2,0,1:T(8,128)(2,1)S(1)} %get-tuple-element.44), channel_id=1, source_target_pairs={{0,12},{4,0},{8,4},{12,8},{1,13},{5,1},{9,5},{13,9},{2,14},{6,2},{... | collective-permute-start | bytes 589832 | tf_op jit(solution)/shard_map/ppermute | solution.py:20
  73.6 10.8 %collective-permute-start.6 = (bf16[2,3,256,64]{3,2,0,1:T(8,128)(2,1)}, bf16[2,3,256,64]{3,2,0,1:T(8,128)(2,1)}, u32[]{:S(2)}, u32[]{:S(2)}) collective-permute-start(bf16[2,3,256,64]{3,2,0,1:T(8,128)(2,1)} %multiply_convert_fusion.15), channel_id=1, source_target_pairs={{0,4},{4,8},{8,12},{12,0},{1,5},{5,9},{9,13},{13,1},{2,6},{6,10},{... | collective-permute-start | bytes 589832 | tf_op jit(solution)/shard_map/ppermute | solution.py:20
  73.6 37.3 %collective-permute-start.7 = (bf16[2,3,256,64]{3,2,0,1:T(8,128)(2,1)}, bf16[2,3,256,64]{3,2,0,1:T(8,128)(2,1)}, u32[]{:S(2)}, u32[]{:S(2)}) collective-permute-start(bf16[2,3,256,64]{3,2,0,1:T(8,128)(2,1)} %multiply_convert_fusion.15), channel_id=1, source_target_pairs={{0,8},{4,12},{8,0},{12,4},{1,9},{5,13},{9,1},{13,5},{2,10},{6,14},... | collective-permute-start | bytes 589832 | tf_op jit(solution)/shard_map/ppermute | solution.py:20
  76.5 39.8 %collective-permute-start.8 = (bf16[2,3,256,64]{3,2,0,1:T(8,128)(2,1)}, bf16[2,3,256,64]{3,2,0,1:T(8,128)(2,1)}, u32[]{:S(2)}, u32[]{:S(2)}) collective-permute-start(bf16[2,3,256,64]{3,2,0,1:T(8,128)(2,1)} %multiply_convert_fusion.15), channel_id=1, source_target_pairs={{0,12},{4,0},{8,4},{12,8},{1,13},{5,1},{9,5},{13,9},{2,14},{6,2},{... | collective-permute-start | bytes 589832 | tf_op jit(solution)/shard_map/ppermute | solution.py:20
  125.8 20.3 %collective-permute-start.10 = (bf16[2,3,256,64]{3,2,0,1:T(8,128)(2,1)S(1)}, bf16[2,3,256,64]{3,2,0,1:T(8,128)(2,1)S(1)}, u32[]{:S(2)}, u32[]{:S(2)}) collective-permute-start(bf16[2,3,256,64]{3,2,0,1:T(8,128)(2,1)S(1)} %get-tuple-element.40), channel_id=1, source_target_pairs={{0,8},{4,12},{8,0},{12,4},{1,9},{5,13},{9,1},{13,5},{2,10},{6,14},... | collective-permute-start | bytes 589832 | tf_op jit(solution)/shard_map/ppermute | solution.py:20
  125.9 20.2 %collective-permute-start.11 = (bf16[2,3,256,64]{3,2,0,1:T(8,128)(2,1)S(1)}, bf16[2,3,256,64]{3,2,0,1:T(8,128)(2,1)S(1)}, u32[]{:S(2)}, u32[]{:S(2)}) collective-permute-start(bf16[2,3,256,64]{3,2,0,1:T(8,128)(2,1)S(1)} %get-tuple-element.39), channel_id=1, source_target_pairs={{0,12},{4,0},{8,4},{12,8},{1,13},{5,1},{9,5},{13,9},{2,14},{6,2},{... | collective-permute-start | bytes 589832 | tf_op jit(solution)/shard_map/ppermute | solution.py:20
  126.0 27.9 %collective-permute-start.9 = (bf16[2,3,256,64]{3,2,0,1:T(8,128)(2,1)S(1)}, bf16[2,3,256,64]{3,2,0,1:T(8,128)(2,1)S(1)}, u32[]{:S(2)}, u32[]{:S(2)}) collective-permute-start(bf16[2,3,256,64]{3,2,0,1:T(8,128)(2,1)S(1)} %get-tuple-element.38), channel_id=1, source_target_pairs={{0,4},{4,8},{8,12},{12,0},{1,5},{5,9},{9,13},{13,1},{2,6},{6,10},{... | collective-permute-start | bytes 589832 | tf_op jit(solution)/shard_map/ppermute | solution.py:20
  155.3 10.9 %collective-permute-start.12 = (bf16[2,3,256,64]{3,2,0,1:T(8,128)(2,1)S(1)}, bf16[2,3,256,64]{3,2,0,1:T(8,128)(2,1)}, u32[]{:S(2)}, u32[]{:S(2)}) collective-permute-start(bf16[2,3,256,64]{3,2,0,1:T(8,128)(2,1)S(1)} %get-tuple-element.8), channel_id=1, source_target_pairs={{0,4},{4,8},{8,12},{12,0},{1,5},{5,9},{9,13},{13,1},{2,6},{6,10},{... | collective-permute-start | bytes 589832 | tf_op jit(solution)/shard_map/ppermute | solution.py:20
  156.2 35.3 %collective-permute-start.13 = (bf16[2,3,256,64]{3,2,0,1:T(8,128)(2,1)S(1)}, bf16[2,3,256,64]{3,2,0,1:T(8,128)(2,1)S(1)}, u32[]{:S(2)}, u32[]{:S(2)}) collective-permute-start(bf16[2,3,256,64]{3,2,0,1:T(8,128)(2,1)S(1)} %get-tuple-element.8), channel_id=1, source_target_pairs={{0,8},{4,12},{8,0},{12,4},{1,9},{5,13},{9,1},{13,5},{2,10},{6,14},... | collective-permute-start | bytes 589832 | tf_op jit(solution)/shard_map/ppermute | solution.py:20
  157.6 39.2 %collective-permute-start.14 = (bf16[2,3,256,64]{3,2,0,1:T(8,128)(2,1)S(1)}, bf16[2,3,256,64]{3,2,0,1:T(8,128)(2,1)S(1)}, u32[]{:S(2)}, u32[]{:S(2)}) collective-permute-start(bf16[2,3,256,64]{3,2,0,1:T(8,128)(2,1)S(1)} %get-tuple-element.8), channel_id=1, source_target_pairs={{0,12},{4,0},{8,4},{12,8},{1,13},{5,1},{9,5},{13,9},{2,14},{6,2},{... | collective-permute-start | bytes 589832 | tf_op jit(solution)/shard_map/ppermute | solution.py:20
  158.5 49.1 %copy-start.16 = (s32[2]{0:T(128)S(1)}, s32[2]{0:T(128)}, u32[]{:S(2)}) copy-start(s32[2]{0:T(128)} %constant.205.clone) | copy-start | bytes 28
  158.5 51.0 %copy-start.15 = (s32[2,1]{1,0:T(2,128)S(1)}, s32[2,1]{1,0:T(2,128)}, u32[]{:S(2)}) copy-start(s32[2,1]{1,0:T(2,128)} %get-tuple-element.68) | copy-start | bytes 28
  201.2 23.4 %collective-permute-start.15 = (bf16[2,3,256,256]{3,2,0,1:T(8,128)(2,1)}, bf16[2,3,256,256]{3,2,0,1:T(8,128)(2,1)S(1)}, u32[]{:S(2)}, u32[]{:S(2)}) collective-permute-start(bf16[2,3,256,256]{3,2,0,1:T(8,128)(2,1)} %dynamic_update_slice.88), channel_id=1, source_target_pairs={{0,2},{1,3},{4,6},{5,7},{8,10},{9,11},{12,14},{13,15},{16,18},{17,... | collective-permute-start | bytes 2359304 | tf_op jit(solution)/shard_map/ppermute | solution.py:15
  229.2 12.1 %collective-permute-start.16 = (bf16[2,3,256,64]{3,2,0,1:T(8,128)(2,1)S(1)}, bf16[2,3,256,64]{3,2,0,1:T(8,128)(2,1)S(1)}, u32[]{:S(2)}, u32[]{:S(2)}) collective-permute-start(bf16[2,3,256,64]{3,2,0,1:T(8,128)(2,1)S(1)} %get-tuple-element.23), channel_id=1, source_target_pairs={{0,4},{4,8},{8,12},{12,0},{1,5},{5,9},{9,13},{13,1},{2,6},{6,10},{... | collective-permute-start | bytes 589832 | tf_op jit(solution)/shard_map/ppermute | solution.py:20
  229.2 31.4 %collective-permute-start.17 = (bf16[2,3,256,64]{3,2,0,1:T(8,128)(2,1)S(1)}, bf16[2,3,256,64]{3,2,0,1:T(8,128)(2,1)S(1)}, u32[]{:S(2)}, u32[]{:S(2)}) collective-permute-start(bf16[2,3,256,64]{3,2,0,1:T(8,128)(2,1)S(1)} %get-tuple-element.25), channel_id=1, source_target_pairs={{0,8},{4,12},{8,0},{12,4},{1,9},{5,13},{9,1},{13,5},{2,10},{6,14},... | collective-permute-start | bytes 589832 | tf_op jit(solution)/shard_map/ppermute | solution.py:20
  229.3 31.3 %collective-permute-start.18 = (bf16[2,3,256,64]{3,2,0,1:T(8,128)(2,1)S(1)}, bf16[2,3,256,64]{3,2,0,1:T(8,128)(2,1)S(1)}, u32[]{:S(2)}, u32[]{:S(2)}) collective-permute-start(bf16[2,3,256,64]{3,2,0,1:T(8,128)(2,1)S(1)} %get-tuple-element.24), channel_id=1, source_target_pairs={{0,12},{4,0},{8,4},{12,8},{1,13},{5,1},{9,5},{13,9},{2,14},{6,2},{... | collective-permute-start | bytes 589832 | tf_op jit(solution)/shard_map/ppermute | solution.py:20
  261.1 20.9 %collective-permute-start.19 = (bf16[2,3,256,64]{3,2,0,1:T(8,128)(2,1)S(1)}, bf16[2,3,256,64]{3,2,0,1:T(8,128)(2,1)}, u32[]{:S(2)}, u32[]{:S(2)}) collective-permute-start(bf16[2,3,256,64]{3,2,0,1:T(8,128)(2,1)S(1)} %multiply_convert_fusion.14), channel_id=1, source_target_pairs={{0,4},{4,8},{8,12},{12,0},{1,5},{5,9},{9,13},{13,1},{2,6},{6,10},{... | collective-permute-start | bytes 589832 | tf_op jit(solution)/shard_map/ppermute | solution.py:20
  261.2 47.7 %collective-permute-start.20 = (bf16[2,3,256,64]{3,2,0,1:T(8,128)(2,1)S(1)}, bf16[2,3,256,64]{3,2,0,1:T(8,128)(2,1)}, u32[]{:S(2)}, u32[]{:S(2)}) collective-permute-start(bf16[2,3,256,64]{3,2,0,1:T(8,128)(2,1)S(1)} %multiply_convert_fusion.14), channel_id=1, source_target_pairs={{0,8},{4,12},{8,0},{12,4},{1,9},{5,13},{9,1},{13,5},{2,10},{6,14},... | collective-permute-start | bytes 589832 | tf_op jit(solution)/shard_map/ppermute | solution.py:20
  274.3 39.3 %collective-permute-start.21 = (bf16[2,3,256,64]{3,2,0,1:T(8,128)(2,1)S(1)}, bf16[2,3,256,64]{3,2,0,1:T(8,128)(2,1)S(1)}, u32[]{:S(2)}, u32[]{:S(2)}) collective-permute-start(bf16[2,3,256,64]{3,2,0,1:T(8,128)(2,1)S(1)} %multiply_convert_fusion.14), channel_id=1, source_target_pairs={{0,12},{4,0},{8,4},{12,8},{1,13},{5,1},{9,5},{13,9},{2,14},{6,2},{... | collective-permute-start | bytes 589832 | tf_op jit(solution)/shard_map/ppermute | solution.py:20
  318.5 11.8 %collective-permute-start.22 = (bf16[2,3,256,64]{3,2,0,1:T(8,128)(2,1)S(1)}, bf16[2,3,256,64]{3,2,0,1:T(8,128)(2,1)S(1)}, u32[]{:S(2)}, u32[]{:S(2)}) collective-permute-start(bf16[2,3,256,64]{3,2,0,1:T(8,128)(2,1)S(1)} %get-tuple-element.18), channel_id=1, source_target_pairs={{0,4},{4,8},{8,12},{12,0},{1,5},{5,9},{9,13},{13,1},{2,6},{6,10},{... | collective-permute-start | bytes 589832 | tf_op jit(solution)/shard_map/ppermute | solution.py:20
  318.6 33.1 %collective-permute-start.23 = (bf16[2,3,256,64]{3,2,0,1:T(8,128)(2,1)S(1)}, bf16[2,3,256,64]{3,2,0,1:T(8,128)(2,1)S(1)}, u32[]{:S(2)}, u32[]{:S(2)}) collective-permute-start(bf16[2,3,256,64]{3,2,0,1:T(8,128)(2,1)S(1)} %get-tuple-element.20), channel_id=1, source_target_pairs={{0,8},{4,12},{8,0},{12,4},{1,9},{5,13},{9,1},{13,5},{2,10},{6,14},... | collective-permute-start | bytes 589832 | tf_op jit(solution)/shard_map/ppermute | solution.py:20
  318.6 33.0 %collective-permute-start.24 = (bf16[2,3,256,64]{3,2,0,1:T(8,128)(2,1)S(1)}, bf16[2,3,256,64]{3,2,0,1:T(8,128)(2,1)S(1)}, u32[]{:S(2)}, u32[]{:S(2)}) collective-permute-start(bf16[2,3,256,64]{3,2,0,1:T(8,128)(2,1)S(1)} %get-tuple-element.19), channel_id=1, source_target_pairs={{0,12},{4,0},{8,4},{12,8},{1,13},{5,1},{9,5},{13,9},{2,14},{6,2},{... | collective-permute-start | bytes 589832 | tf_op jit(solution)/shard_map/ppermute | solution.py:20
  352.2 19.7 %collective-permute-start.25 = (bf16[2,3,256,64]{3,2,0,1:T(8,128)(2,1)S(1)}, bf16[2,3,256,64]{3,2,0,1:T(8,128)(2,1)}, u32[]{:S(2)}, u32[]{:S(2)}) collective-permute-start(bf16[2,3,256,64]{3,2,0,1:T(8,128)(2,1)S(1)} %get-tuple-element.2), channel_id=1, source_target_pairs={{0,4},{4,8},{8,12},{12,0},{1,5},{5,9},{9,13},{13,1},{2,6},{6,10},{... | collective-permute-start | bytes 589832 | tf_op jit(solution)/shard_map/ppermute | solution.py:20
  352.3 46.9 %collective-permute-start.26 = (bf16[2,3,256,64]{3,2,0,1:T(8,128)(2,1)S(1)}, bf16[2,3,256,64]{3,2,0,1:T(8,128)(2,1)S(1)}, u32[]{:S(2)}, u32[]{:S(2)}) collective-permute-start(bf16[2,3,256,64]{3,2,0,1:T(8,128)(2,1)S(1)} %get-tuple-element.2), channel_id=1, source_target_pairs={{0,8},{4,12},{8,0},{12,4},{1,9},{5,13},{9,1},{13,5},{2,10},{6,14},... | collective-permute-start | bytes 589832 | tf_op jit(solution)/shard_map/ppermute | solution.py:20
  364.6 37.7 %collective-permute-start.27 = (bf16[2,3,256,64]{3,2,0,1:T(8,128)(2,1)S(1)}, bf16[2,3,256,64]{3,2,0,1:T(8,128)(2,1)S(1)}, u32[]{:S(2)}, u32[]{:S(2)}) collective-permute-start(bf16[2,3,256,64]{3,2,0,1:T(8,128)(2,1)S(1)} %get-tuple-element.2), channel_id=1, source_target_pairs={{0,12},{4,0},{8,4},{12,8},{1,13},{5,1},{9,5},{13,9},{2,14},{6,2},{... | collective-permute-start | bytes 589832 | tf_op jit(solution)/shard_map/ppermute | solution.py:20
  367.6 36.3 %copy-start.10 = (bf16[1,512,256]{2,1,0:T(8,128)(2,1)S(1)}, bf16[1,512,256]{2,1,0:T(8,128)(2,1)}, u32[]{:S(2)}) copy-start(bf16[1,512,256]{2,1,0:T(8,128)(2,1)} %get-tuple-element.34) | copy-start | bytes 786436
  367.6 36.3 %copy-start.11 = (bf16[1,512,256]{2,1,0:T(8,128)(2,1)S(1)}, bf16[1,512,256]{2,1,0:T(8,128)(2,1)}, u32[]{:S(2)}) copy-start(bf16[1,512,256]{2,1,0:T(8,128)(2,1)} %get-tuple-element.37) | copy-start | bytes 786436
  (13 other events, 103.4 us)

commit v5 on v1

--- a/solution.py
+++ b/solution.py
@@ -36,6 +36,22 @@
     full = lax.dynamic_update_slice_in_dim(full, own, me * part_cols, 2)
     for by in range(1, tok_count):
         got = rotated(own, "tok", by)
+        full = lax.dynamic_update_slice_in_dim(full, got, ((me - by) % tok_count) * part_cols, 2)
+    return full
+
+
+def cross_gather(own, part_cols):
+    tok_count = lax.axis_size("tok")
+    sections = lax.axis_size("span")
+    me = lax.axis_index("tok")
+    full = jnp.zeros(own.shape[:2] + (part_cols * tok_count,), own.dtype)
+    for by in range(tok_count):
+        pairs = [
+            (t * sections + s, ((t + by) % tok_count) * sections + s + 1)
+            for t in range(tok_count)
+            for s in range(sections - 1)
+        ]
+        got = lax.ppermute(own, ("tok", "span"), pairs)
         full = lax.dynamic_update_slice_in_dim(full, got, ((me - by) % tok_count) * part_cols, 2)
     return full
 
@@ -86,9 +102,9 @@
     results = []
     weights = states_in[0, 0]
     fast = gather_cols(weights.astype(jnp.bfloat16), part_cols)
+    arrived = None
     for tick_number in range(tick_count):
         if tick_number > 0:
-            arrived = shifted(fast, "span", 1)
             fast = jnp.where(section_index == 0, init_fast, arrived)
             weights = lax.dynamic_slice_in_dim(fast, tok_index * part_cols, part_cols, 2).astype(
                 jnp.float32
@@ -103,7 +119,10 @@
                 fast = gather_cols(weights.astype(jnp.bfloat16), part_cols)
             summed = scatter_sum(fast_grads(fast, key_block, scaled), part_cols)
             weights = renormalize(weights + summed, own_norms)
-        fast = gather_cols(weights.astype(jnp.bfloat16), part_cols)
+        own = weights.astype(jnp.bfloat16)
+        if tick_number + 1 < tick_count:
+            arrived = cross_gather(own, part_cols)
+        fast = gather_cols(own, part_cols)
         results.append(apply_fast(fast, query_rows[tick_number, 0, :, 0]))
     outputs = jnp.stack(results)[:, None, :, None]
     return (outputs, weights[None, None])

time: 186 us -> 184 us (0.989)
  waiting for transfers between devices: 83.4 us -> 60.9 us
  starting transfers between devices: 73.6 us -> 94.4 us
    ppermute x2 -> x8, waiting for transfers between devices: 13.4 us -> 0.02 us  [cross_gather(): got = lax.ppermute(own, ('tok', 'span'), pairs)]
    ppermute x2 -> x8, starting transfers between devices: 7.9 us -> 19.3 us  [cross_gather(): got = lax.ppermute(own, ('tok', 'span'), pairs)]
    ppermute x39, starting transfers between devices: 65.7 us -> 75.1 us  [rotated(): lax.ppermute(value, axis, [(i, (i + by) % devices) for i in range(devices)])]
    ppermute x39, waiting for transfers between devices: 70 us -> 60.9 us  [rotated(): lax.ppermute(value, axis, [(i, (i + by) % devices) for i in range(devices)])]
  transfers between devices with their start and end apart: 41 -> 47, of which waited for: 30 -> 24; matrix products, arithmetic and copies ran while one was open for 3% -> 6% of each run, Pallas kernels for 0% -> 0%
where the time goes in v5:
time: 184 us; the launch traced here: 183 us
  starting transfers between devices  94.4 us (51%)
  waiting for transfers between devices  60.9 us (33%)
  matrix products  17.5 us (10%)
  other arithmetic  5.03 us (3%)
  local copies, waits for them, and re-layouts  3.87 us (2%)
    ppermute x39, starting transfers between devices, rotated(): lax.ppermute(value, axis, [(i, (i + by) % devices) for i in range(devices)])  75.1 us
    ppermute x39, waiting for transfers between devices, rotated(): lax.ppermute(value, axis, [(i, (i + by) % devices) for i in range(devices)])  60.9 us
    ppermute x8, starting transfers between devices, cross_gather(): got = lax.ppermute(own, ('tok', 'span'), pairs)  19.3 us
  transfers between devices with their start and end apart: 47, of which 24 were waited for; matrix products, arithmetic and copies ran while one was open for 6% of the time, Pallas kernels for 0%

profile of v5, /device:TPU:0, one launch (start us, length us, event | category | flops | bytes accessed | tf_op | source)
XLA Modules:
  0.0 183.4 jit_solution(12208774364791603725)
XLA Ops:
  1.6 3.1 %collective-permute-start = (bf16[3,256,64]{1,2,0:T(8,128)(2,1)S(1)}, bf16[3,256,64]{1,2,0:T(8,128)(2,1)S(1)}, u32[]{:S(2)}, u32[]{:S(2)}) collective-permute-start(bf16[3,256,64]{1,2,0:T(8,128)(2,1)S(1)} %get-tuple-element.29), channel_id=1, source_target_pairs={{0,4},{4,8},{8,12},{12,0},{1,5},{5,9},{9,13},{13,1},{2,6},{6,10},{... | collective-permute-start | bytes 294920 | tf_op jit(solution)/shard_map/ppermute | solution.py:19
  4.7 2.6 %collective-permute-start.1 = (bf16[3,256,64]{1,2,0:T(8,128)(2,1)S(1)}, bf16[3,256,64]{1,2,0:T(8,128)(2,1)S(1)}, u32[]{:S(2)}, u32[]{:S(2)}) collective-permute-start(bf16[3,256,64]{1,2,0:T(8,128)(2,1)S(1)} %get-tuple-element.29), channel_id=1, source_target_pairs={{0,8},{4,12},{8,0},{12,4},{1,9},{5,13},{9,1},{13,5},{2,10},{6,14},... | collective-permute-start | bytes 294920 | tf_op jit(solution)/shard_map/ppermute | solution.py:19
  10.4 3.5 %collective-permute-done.1 = bf16[3,256,64]{1,2,0:T(8,128)(2,1)S(1)} collective-permute-done((bf16[3,256,64]{1,2,0:T(8,128)(2,1)S(1)}, bf16[3,256,64]{1,2,0:T(8,128)(2,1)S(1)}, u32[]{:S(2)}, u32[]{:S(2)}) %collective-permute-start.1) | collective-permute-done | bytes 98336 | tf_op jit(solution)/shard_map/ppermute | solution.py:19
  16.7 2.6 %collective-permute-start.3 = (bf16[3,256,64]{1,2,0:T(8,128)(2,1)S(1)}, bf16[3,256,64]{1,2,0:T(8,128)(2,1)S(1)}, u32[]{:S(2)}, u32[]{:S(2)}) collective-permute-start(bf16[3,256,64]{1,2,0:T(8,128)(2,1)S(1)} %get-tuple-element.45), channel_id=1, source_target_pairs={{0,4},{4,8},{8,12},{12,0},{1,5},{5,9},{9,13},{13,1},{2,6},{6,10},{... | collective-permute-start | bytes 294920 | tf_op jit(solution)/shard_map/ppermute | solution.py:19
  21.9 2.2 %collective-permute-done.3 = bf16[3,256,64]{1,2,0:T(8,128)(2,1)S(1)} collective-permute-done((bf16[3,256,64]{1,2,0:T(8,128)(2,1)S(1)}, bf16[3,256,64]{1,2,0:T(8,128)(2,1)S(1)}, u32[]{:S(2)}, u32[]{:S(2)}) %collective-permute-start.3) | collective-permute-done | bytes 98336 | tf_op jit(solution)/shard_map/ppermute | solution.py:19
  24.1 3.4 %collective-permute-done.4 = bf16[3,256,64]{1,2,0:T(8,128)(2,1)S(1)} collective-permute-done((bf16[3,256,64]{1,2,0:T(8,128)(2,1)S(1)}, bf16[3,256,64]{1,2,0:T(8,128)(2,1)S(1)}, u32[]{:S(2)}, u32[]{:S(2)}) %collective-permute-start.4) | collective-permute-done | bytes 98336 | tf_op jit(solution)/shard_map/ppermute | solution.py:19
  27.9 2.6 %collective-permute-start.6 = (bf16[3,256,64]{1,2,0:T(8,128)(2,1)S(1)}, bf16[3,256,64]{1,2,0:T(8,128)(2,1)S(1)}, u32[]{:S(2)}, u32[]{:S(2)}) collective-permute-start(bf16[3,256,64]{1,2,0:T(8,128)(2,1)S(1)} %get-tuple-element.25), channel_id=1, source_target_pairs={{0,4},{4,8},{8,12},{12,0},{1,5},{5,9},{9,13},{13,1},{2,6},{6,10},{... | collective-permute-start | bytes 294920 | tf_op jit(solution)/shard_map/ppermute | solution.py:19
  33.0 2.4 %collective-permute-done.6 = bf16[3,256,64]{1,2,0:T(8,128)(2,1)S(1)} collective-permute-done((bf16[3,256,64]{1,2,0:T(8,128)(2,1)S(1)}, bf16[3,256,64]{1,2,0:T(8,128)(2,1)S(1)}, u32[]{:S(2)}, u32[]{:S(2)}) %collective-permute-start.6) | collective-permute-done | bytes 98336 | tf_op jit(solution)/shard_map/ppermute | solution.py:19
  35.4 3.3 %collective-permute-done.7 = bf16[3,256,64]{1,2,0:T(8,128)(2,1)S(1)} collective-permute-done((bf16[3,256,64]{1,2,0:T(8,128)(2,1)S(1)}, bf16[3,256,64]{1,2,0:T(8,128)(2,1)S(1)}, u32[]{:S(2)}, u32[]{:S(2)}) %collective-permute-start.7) | collective-permute-done | bytes 98336 | tf_op jit(solution)/shard_map/ppermute | solution.py:19
  42.5 3.4 %collective-permute-start.11 = (bf16[3,256,64]{1,2,0:T(8,128)(2,1)S(1)}, bf16[3,256,64]{1,2,0:T(8,128)(2,1)S(1)}, u32[]{:S(2)}, u32[]{:S(2)}) collective-permute-start(bf16[3,256,64]{1,2,0:T(8,128)(2,1)S(1)} %get-tuple-element.43), channel_id=1, source_target_pairs={{0,12},{4,0},{8,4},{12,8},{1,13},{5,1},{9,5},{13,9},{2,14},{6,2},{... | collective-permute-start | bytes 294920 | tf_op jit(solution)/shard_map/ppermute | solution.py:19
  45.9 2.4 %collective-permute-done.10 = bf16[3,256,64]{1,2,0:T(8,128)(2,1)S(1)} collective-permute-done((bf16[3,256,64]{1,2,0:T(8,128)(2,1)S(1)}, bf16[3,256,64]{1,2,0:T(8,128)(2,1)S(1)}, u32[]{:S(2)}, u32[]{:S(2)}) %collective-permute-start.10) | collective-permute-done | bytes 98336 | tf_op jit(solution)/shard_map/ppermute | solution.py:19
  49.0 3.8 %collective-permute-done.9 = bf16[3,256,64]{1,2,0:T(8,128)(2,1)S(1)} collective-permute-done((bf16[3,256,64]{1,2,0:T(8,128)(2,1)S(1)}, bf16[3,256,64]{1,2,0:T(8,128)(2,1)S(1)}, u32[]{:S(2)}, u32[]{:S(2)}) %collective-permute-start.9) | collective-permute-done | bytes 98336 | tf_op jit(solution)/shard_map/ppermute | solution.py:19
  53.2 3.4 %collective-permute-start.15 = (bf16[3,256,64]{1,2,0:T(8,128)(2,1)S(1)}, bf16[3,256,64]{1,2,0:T(8,128)(2,1)S(1)}, u32[]{:S(2)}, u32[]{:S(2)}) collective-permute-start(bf16[3,256,64]{1,2,0:T(8,128)(2,1)S(1)} %get-tuple-element.5), channel_id=1, source_target_pairs={{0,2},{4,6},{8,10},{12,14},{1,3},{5,7},{9,11},{13,15},{16,18},{20,... | collective-permute-start | bytes 294920 | tf_op jit(solution)/shard_map/ppermute | solution.py:54
  58.0 2.4 %collective-permute-start.17 = (bf16[3,256,64]{1,2,0:T(8,128)(2,1)S(1)}, bf16[3,256,64]{1,2,0:T(8,128)(2,1)S(1)}, u32[]{:S(2)}, u32[]{:S(2)}) collective-permute-start(bf16[3,256,64]{1,2,0:T(8,128)(2,1)S(1)} %get-tuple-element.5), channel_id=1, source_target_pairs={{0,10},{4,14},{8,2},{12,6},{1,11},{5,15},{9,3},{13,7},{16,26},{20,... | collective-permute-start | bytes 294920 | tf_op jit(solution)/shard_map/ppermute | solution.py:54
  68.3 6.5 %collective-permute-start.19 = (bf16[3,256,64]{1,2,0:T(8,128)(2,1)S(1)}, bf16[3,256,64]{1,2,0:T(8,128)(2,1)S(1)}, u32[]{:S(2)}, u32[]{:S(2)}) collective-permute-start(bf16[3,256,64]{1,2,0:T(8,128)(2,1)S(1)} %get-tuple-element.39), channel_id=1, source_target_pairs={{0,4},{4,8},{8,12},{12,0},{1,5},{5,9},{9,13},{13,1},{2,6},{6,10},{... | collective-permute-start | bytes 294920 | tf_op jit(solution)/shard_map/ppermute | solution.py:19
  76.7 2.8 %collective-permute-start.21 = (bf16[3,256,64]{1,2,0:T(8,128)(2,1)S(1)}, bf16[3,256,64]{1,2,0:T(8,128)(2,1)S(1)}, u32[]{:S(2)}, u32[]{:S(2)}) collective-permute-start(bf16[3,256,64]{1,2,0:T(8,128)(2,1)S(1)} %get-tuple-element.40), channel_id=1, source_target_pairs={{0,12},{4,0},{8,4},{12,8},{1,13},{5,1},{9,5},{13,9},{2,14},{6,2},{... | collective-permute-start | bytes 294920 | tf_op jit(solution)/shard_map/ppermute | solution.py:19
  79.6 4.8 %collective-permute-done.20 = bf16[3,256,64]{1,2,0:T(8,128)(2,1)S(1)} collective-permute-done((bf16[3,256,64]{1,2,0:T(8,128)(2,1)S(1)}, bf16[3,256,64]{1,2,0:T(8,128)(2,1)S(1)}, u32[]{:S(2)}, u32[]{:S(2)}) %collective-permute-start.20) | collective-permute-done | bytes 98336 | tf_op jit(solution)/shard_map/ppermute | solution.py:19
  84.8 2.5 %collective-permute-start.22 = (bf16[3,256,64]{1,2,0:T(8,128)(2,1)S(1)}, bf16[3,256,64]{1,2,0:T(8,128)(2,1)S(1)}, u32[]{:S(2)}, u32[]{:S(2)}) collective-permute-start(bf16[3,256,64]{1,2,0:T(8,128)(2,1)S(1)} %get-tuple-element.19), channel_id=1, source_target_pairs={{0,4},{4,8},{8,12},{12,0},{1,5},{5,9},{9,13},{13,1},{2,6},{6,10},{... | collective-permute-start | bytes 294920 | tf_op jit(solution)/shard_map/ppermute | solution.py:19
  89.7 2.6 %collective-permute-done.22 = bf16[3,256,64]{1,2,0:T(8,128)(2,1)S(1)} collective-permute-done((bf16[3,256,64]{1,2,0:T(8,128)(2,1)S(1)}, bf16[3,256,64]{1,2,0:T(8,128)(2,1)S(1)}, u32[]{:S(2)}, u32[]{:S(2)}) %collective-permute-start.22) | collective-permute-done | bytes 98336 | tf_op jit(solution)/shard_map/ppermute | solution.py:19
  92.4 3.1 %collective-permute-done.23 = bf16[3,256,64]{1,2,0:T(8,128)(2,1)S(1)} collective-permute-done((bf16[3,256,64]{1,2,0:T(8,128)(2,1)S(1)}, bf16[3,256,64]{1,2,0:T(8,128)(2,1)S(1)}, u32[]{:S(2)}, u32[]{:S(2)}) %collective-permute-start.23) | collective-permute-done | bytes 98336 | tf_op jit(solution)/shard_map/ppermute | solution.py:19
  97.7 2.6 %collective-permute-start.25 = (bf16[3,256,64]{1,2,0:T(8,128)(2,1)S(1)}, bf16[3,256,64]{1,2,0:T(8,128)(2,1)S(1)}, u32[]{:S(2)}, u32[]{:S(2)}) collective-permute-start(bf16[3,256,64]{1,2,0:T(8,128)(2,1)S(1)} %get-tuple-element.36), channel_id=1, source_target_pairs={{0,4},{4,8},{8,12},{12,0},{1,5},{5,9},{9,13},{13,1},{2,6},{6,10},{... | collective-permute-start | bytes 294920 | tf_op jit(solution)/shard_map/ppermute | solution.py:19
  105.1 3.4 %collective-permute-done.26 = bf16[3,256,64]{1,2,0:T(8,128)(2,1)S(1)} collective-permute-done((bf16[3,256,64]{1,2,0:T(8,128)(2,1)S(1)}, bf16[3,256,64]{1,2,0:T(8,128)(2,1)S(1)}, u32[]{:S(2)}, u32[]{:S(2)}) %collective-permute-start.26) | collective-permute-done | bytes 98336 | tf_op jit(solution)/shard_map/ppermute | solution.py:19
  109.5 4.9 %collective-permute-start.31 = (bf16[3,256,64]{1,2,0:T(8,128)(2,1)}, bf16[3,256,64]{1,2,0:T(8,128)(2,1)}, u32[]{:S(2)}, u32[]{:S(2)}) collective-permute-start(bf16[3,256,64]{1,2,0:T(8,128)(2,1)} %get-tuple-element.7), channel_id=1, source_target_pairs={{0,2},{4,6},{8,10},{12,14},{1,3},{5,7},{9,11},{13,15},{16,18},{20,... | collective-permute-start | bytes 294920 | tf_op jit(solution)/shard_map/ppermute | solution.py:54
  116.6 2.7 %collective-permute-start.32 = (bf16[3,256,64]{1,2,0:T(8,128)(2,1)}, bf16[3,256,64]{1,2,0:T(8,128)(2,1)S(1)}, u32[]{:S(2)}, u32[]{:S(2)}) collective-permute-start(bf16[3,256,64]{1,2,0:T(8,128)(2,1)} %get-tuple-element.7), channel_id=1, source_target_pairs={{0,6},{4,10},{8,14},{12,2},{1,7},{5,11},{9,15},{13,3},{16,22},{20,... | collective-permute-start | bytes 294920 | tf_op jit(solution)/shard_map/ppermute | solution.py:54
  130.0 5.8 %collective-permute-start.35 = (bf16[3,256,64]{1,2,0:T(8,128)(2,1)S(1)}, bf16[3,256,64]{1,2,0:T(8,128)(2,1)S(1)}, u32[]{:S(2)}, u32[]{:S(2)}) collective-permute-start(bf16[3,256,64]{1,2,0:T(8,128)(2,1)S(1)} %get-tuple-element.33), channel_id=1, source_target_pairs={{0,4},{4,8},{8,12},{12,0},{1,5},{5,9},{9,13},{13,1},{2,6},{6,10},{... | collective-permute-start | bytes 294920 | tf_op jit(solution)/shard_map/ppermute | solution.py:19
  136.7 2.8 %collective-permute-start.37 = (bf16[3,256,64]{1,2,0:T(8,128)(2,1)S(1)}, bf16[3,256,64]{1,2,0:T(8,128)(2,1)S(1)}, u32[]{:S(2)}, u32[]{:S(2)}) collective-permute-start(bf16[3,256,64]{1,2,0:T(8,128)(2,1)S(1)} %get-tuple-element.34), channel_id=1, source_target_pairs={{0,12},{4,0},{8,4},{12,8},{1,13},{5,1},{9,5},{13,9},{2,14},{6,2},{... | collective-permute-start | bytes 294920 | tf_op jit(solution)/shard_map/ppermute | solution.py:19
  140.0 5.2 %collective-permute-done.36 = bf16[3,256,64]{1,2,0:T(8,128)(2,1)S(1)} collective-permute-done((bf16[3,256,64]{1,2,0:T(8,128)(2,1)S(1)}, bf16[3,256,64]{1,2,0:T(8,128)(2,1)S(1)}, u32[]{:S(2)}, u32[]{:S(2)}) %collective-permute-start.36) | collective-permute-done | bytes 98336 | tf_op jit(solution)/shard_map/ppermute | solution.py:19
  153.0 3.4 %collective-permute-done.39 = bf16[3,256,64]{1,2,0:T(8,128)(2,1)S(1)} collective-permute-done((bf16[3,256,64]{1,2,0:T(8,128)(2,1)S(1)}, bf16[3,256,64]{1,2,0:T(8,128)(2,1)S(1)}, u32[]{:S(2)}, u32[]{:S(2)}) %collective-permute-start.39) | collective-permute-done | bytes 98336 | tf_op jit(solution)/shard_map/ppermute | solution.py:19
  164.1 2.7 %collective-permute-done.41 = bf16[3,256,64]{1,2,0:T(8,128)(2,1)S(1)} collective-permute-done((bf16[3,256,64]{1,2,0:T(8,128)(2,1)S(1)}, bf16[3,256,64]{1,2,0:T(8,128)(2,1)S(1)}, u32[]{:S(2)}, u32[]{:S(2)}) %collective-permute-start.41) | collective-permute-done | bytes 98336 | tf_op jit(solution)/shard_map/ppermute | solution.py:19
  166.8 2.8 %collective-permute-done.42 = bf16[3,256,64]{1,2,0:T(8,128)(2,1)S(1)} collective-permute-done((bf16[3,256,64]{1,2,0:T(8,128)(2,1)S(1)}, bf16[3,256,64]{1,2,0:T(8,128)(2,1)S(1)}, u32[]{:S(2)}, u32[]{:S(2)}) %collective-permute-start.42) | collective-permute-done | bytes 98336 | tf_op jit(solution)/shard_map/ppermute | solution.py:19
  170.0 2.6 %collective-permute-start.44 = (bf16[3,256,64]{1,2,0:T(8,128)(2,1)S(1)}, bf16[3,256,64]{1,2,0:T(8,128)(2,1)S(1)}, u32[]{:S(2)}, u32[]{:S(2)}) collective-permute-start(bf16[3,256,64]{1,2,0:T(8,128)(2,1)S(1)} %get-tuple-element.9), channel_id=1, source_target_pairs={{0,4},{4,8},{8,12},{12,0},{1,5},{5,9},{9,13},{13,1},{2,6},{6,10},{... | collective-permute-start | bytes 294920 | tf_op jit(solution)/shard_map/ppermute | solution.py:19
  176.6 4.2 %collective-permute-done.45 = bf16[3,256,64]{1,2,0:T(8,128)(2,1)S(1)} collective-permute-done((bf16[3,256,64]{1,2,0:T(8,128)(2,1)S(1)}, bf16[3,256,64]{1,2,0:T(8,128)(2,1)S(1)}, u32[]{:S(2)}, u32[]{:S(2)}) %collective-permute-start.45) | collective-permute-done | bytes 98336 | tf_op jit(solution)/shard_map/ppermute | solution.py:19
  (196 shorter events, 75.1 us)
Async XLA Ops:
  1.6 8.8 %collective-permute-start = (bf16[3,256,64]{1,2,0:T(8,128)(2,1)S(1)}, bf16[3,256,64]{1,2,0:T(8,128)(2,1)S(1)}, u32[]{:S(2)}, u32[]{:S(2)}) collective-permute-start(bf16[3,256,64]{1,2,0:T(8,128)(2,1)S(1)} %get-tuple-element.29), channel_id=1, source_target_pairs={{0,4},{4,8},{8,12},{12,0},{1,5},{5,9},{9,13},{13,1},{2,6},{6,10},{... | collective-permute-start | bytes 294920 | tf_op jit(solution)/shard_map/ppermute | solution.py:19
  4.7 9.2 %collective-permute-start.1 = (bf16[3,256,64]{1,2,0:T(8,128)(2,1)S(1)}, bf16[3,256,64]{1,2,0:T(8,128)(2,1)S(1)}, u32[]{:S(2)}, u32[]{:S(2)}) collective-permute-start(bf16[3,256,64]{1,2,0:T(8,128)(2,1)S(1)} %get-tuple-element.29), channel_id=1, source_target_pairs={{0,8},{4,12},{8,0},{12,4},{1,9},{5,13},{9,1},{13,5},{2,10},{6,14},... | collective-permute-start | bytes 294920 | tf_op jit(solution)/shard_map/ppermute | solution.py:19
  16.7 7.4 %collective-permute-start.3 = (bf16[3,256,64]{1,2,0:T(8,128)(2,1)S(1)}, bf16[3,256,64]{1,2,0:T(8,128)(2,1)S(1)}, u32[]{:S(2)}, u32[]{:S(2)}) collective-permute-start(bf16[3,256,64]{1,2,0:T(8,128)(2,1)S(1)} %get-tuple-element.45), channel_id=1, source_target_pairs={{0,4},{4,8},{8,12},{12,0},{1,5},{5,9},{9,13},{13,1},{2,6},{6,10},{... | collective-permute-start | bytes 294920 | tf_op jit(solution)/shard_map/ppermute | solution.py:19
  19.3 8.2 %collective-permute-start.4 = (bf16[3,256,64]{1,2,0:T(8,128)(2,1)S(1)}, bf16[3,256,64]{1,2,0:T(8,128)(2,1)S(1)}, u32[]{:S(2)}, u32[]{:S(2)}) collective-permute-start(bf16[3,256,64]{1,2,0:T(8,128)(2,1)S(1)} %get-tuple-element.47), channel_id=1, source_target_pairs={{0,8},{4,12},{8,0},{12,4},{1,9},{5,13},{9,1},{13,5},{2,10},{6,14},... | collective-permute-start | bytes 294920 | tf_op jit(solution)/shard_map/ppermute | solution.py:19
  27.9 7.4 %collective-permute-start.6 = (bf16[3,256,64]{1,2,0:T(8,128)(2,1)S(1)}, bf16[3,256,64]{1,2,0:T(8,128)(2,1)S(1)}, u32[]{:S(2)}, u32[]{:S(2)}) collective-permute-start(bf16[3,256,64]{1,2,0:T(8,128)(2,1)S(1)} %get-tuple-element.25), channel_id=1, source_target_pairs={{0,4},{4,8},{8,12},{12,0},{1,5},{5,9},{9,13},{13,1},{2,6},{6,10},{... | collective-permute-start | bytes 294920 | tf_op jit(solution)/shard_map/ppermute | solution.py:19
  30.5 8.2 %collective-permute-start.7 = (bf16[3,256,64]{1,2,0:T(8,128)(2,1)S(1)}, bf16[3,256,64]{1,2,0:T(8,128)(2,1)S(1)}, u32[]{:S(2)}, u32[]{:S(2)}) collective-permute-start(bf16[3,256,64]{1,2,0:T(8,128)(2,1)S(1)} %get-tuple-element.25), channel_id=1, source_target_pairs={{0,8},{4,12},{8,0},{12,4},{1,9},{5,13},{9,1},{13,5},{2,10},{6,14},... | collective-permute-start | bytes 294920 | tf_op jit(solution)/shard_map/ppermute | solution.py:19
  53.2 9.1 %collective-permute-start.15 = (bf16[3,256,64]{1,2,0:T(8,128)(2,1)S(1)}, bf16[3,256,64]{1,2,0:T(8,128)(2,1)S(1)}, u32[]{:S(2)}, u32[]{:S(2)}) collective-permute-start(bf16[3,256,64]{1,2,0:T(8,128)(2,1)S(1)} %get-tuple-element.5), channel_id=1, source_target_pairs={{0,2},{4,6},{8,10},{12,14},{1,3},{5,7},{9,11},{13,15},{16,18},{20,... | collective-permute-start | bytes 294920 | tf_op jit(solution)/shard_map/ppermute | solution.py:54
  56.7 7.8 %collective-permute-start.16 = (bf16[3,256,64]{1,2,0:T(8,128)(2,1)S(1)}, bf16[3,256,64]{1,2,0:T(8,128)(2,1)S(1)}, u32[]{:S(2)}, u32[]{:S(2)}) collective-permute-start(bf16[3,256,64]{1,2,0:T(8,128)(2,1)S(1)} %get-tuple-element.5), channel_id=1, source_target_pairs={{0,6},{4,10},{8,14},{12,2},{1,7},{5,11},{9,15},{13,3},{16,22},{20,... | collective-permute-start | bytes 294920 | tf_op jit(solution)/shard_map/ppermute | solution.py:54
  58.0 8.1 %collective-permute-start.17 = (bf16[3,256,64]{1,2,0:T(8,128)(2,1)S(1)}, bf16[3,256,64]{1,2,0:T(8,128)(2,1)S(1)}, u32[]{:S(2)}, u32[]{:S(2)}) collective-permute-start(bf16[3,256,64]{1,2,0:T(8,128)(2,1)S(1)} %get-tuple-element.5), channel_id=1, source_target_pairs={{0,10},{4,14},{8,2},{12,6},{1,11},{5,15},{9,3},{13,7},{16,26},{20,... | collective-permute-start | bytes 294920 | tf_op jit(solution)/shard_map/ppermute | solution.py:54
  61.7 15.0 %collective-permute-start.12 = (bf16[3,256,64]{1,2,0:T(8,128)(2,1)S(1)}, bf16[3,256,64]{1,2,0:T(8,128)(2,1)S(1)}, u32[]{:S(2)}, u32[]{:S(2)}) collective-permute-start(bf16[3,256,64]{1,2,0:T(8,128)(2,1)S(1)} %get-tuple-element.5), channel_id=1, source_target_pairs={{0,4},{4,8},{8,12},{12,0},{1,5},{5,9},{9,13},{13,1},{2,6},{6,10},{... | collective-permute-start | bytes 294920 | tf_op jit(solution)/shard_map/ppermute | solution.py:19
  62.3 17.2 %collective-permute-start.13 = (bf16[3,256,64]{1,2,0:T(8,128)(2,1)S(1)}, bf16[3,256,64]{1,2,0:T(8,128)(2,1)S(1)}, u32[]{:S(2)}, u32[]{:S(2)}) collective-permute-start(bf16[3,256,64]{1,2,0:T(8,128)(2,1)S(1)} %get-tuple-element.5), channel_id=1, source_target_pairs={{0,8},{4,12},{8,0},{12,4},{1,9},{5,13},{9,1},{13,5},{2,10},{6,14},... | collective-permute-start | bytes 294920 | tf_op jit(solution)/shard_map/ppermute | solution.py:19
  64.5 22.7 %collective-permute-start.14 = (bf16[3,256,64]{1,2,0:T(8,128)(2,1)S(1)}, bf16[3,256,64]{1,2,0:T(8,128)(2,1)S(1)}, u32[]{:S(2)}, u32[]{:S(2)}) collective-permute-start(bf16[3,256,64]{1,2,0:T(8,128)(2,1)S(1)} %get-tuple-element.5), channel_id=1, source_target_pairs={{0,12},{4,0},{8,4},{12,8},{1,13},{5,1},{9,5},{13,9},{2,14},{6,2},{... | collective-permute-start | bytes 294920 | tf_op jit(solution)/shard_map/ppermute | solution.py:19
  68.3 11.2 %collective-permute-start.19 = (bf16[3,256,64]{1,2,0:T(8,128)(2,1)S(1)}, bf16[3,256,64]{1,2,0:T(8,128)(2,1)S(1)}, u32[]{:S(2)}, u32[]{:S(2)}) collective-permute-start(bf16[3,256,64]{1,2,0:T(8,128)(2,1)S(1)} %get-tuple-element.39), channel_id=1, source_target_pairs={{0,4},{4,8},{8,12},{12,0},{1,5},{5,9},{9,13},{13,1},{2,6},{6,10},{... | collective-permute-start | bytes 294920 | tf_op jit(solution)/shard_map/ppermute | solution.py:19
  74.8 9.6 %collective-permute-start.20 = (bf16[3,256,64]{1,2,0:T(8,128)(2,1)S(1)}, bf16[3,256,64]{1,2,0:T(8,128)(2,1)S(1)}, u32[]{:S(2)}, u32[]{:S(2)}) collective-permute-start(bf16[3,256,64]{1,2,0:T(8,128)(2,1)S(1)} %get-tuple-element.41), channel_id=1, source_target_pairs={{0,8},{4,12},{8,0},{12,4},{1,9},{5,13},{9,1},{13,5},{2,10},{6,14},... | collective-permute-start | bytes 294920 | tf_op jit(solution)/shard_map/ppermute | solution.py:19
  76.7 7.7 %collective-permute-start.21 = (bf16[3,256,64]{1,2,0:T(8,128)(2,1)S(1)}, bf16[3,256,64]{1,2,0:T(8,128)(2,1)S(1)}, u32[]{:S(2)}, u32[]{:S(2)}) collective-permute-start(bf16[3,256,64]{1,2,0:T(8,128)(2,1)S(1)} %get-tuple-element.40), channel_id=1, source_target_pairs={{0,12},{4,0},{8,4},{12,8},{1,13},{5,1},{9,5},{13,9},{2,14},{6,2},{... | collective-permute-start | bytes 294920 | tf_op jit(solution)/shard_map/ppermute | solution.py:19
  84.8 7.6 %collective-permute-start.22 = (bf16[3,256,64]{1,2,0:T(8,128)(2,1)S(1)}, bf16[3,256,64]{1,2,0:T(8,128)(2,1)S(1)}, u32[]{:S(2)}, u32[]{:S(2)}) collective-permute-start(bf16[3,256,64]{1,2,0:T(8,128)(2,1)S(1)} %get-tuple-element.19), channel_id=1, source_target_pairs={{0,4},{4,8},{8,12},{12,0},{1,5},{5,9},{9,13},{13,1},{2,6},{6,10},{... | collective-permute-start | bytes 294920 | tf_op jit(solution)/shard_map/ppermute | solution.py:19
  87.3 8.2 %collective-permute-start.23 = (bf16[3,256,64]{1,2,0:T(8,128)(2,1)S(1)}, bf16[3,256,64]{1,2,0:T(8,128)(2,1)S(1)}, u32[]{:S(2)}, u32[]{:S(2)}) collective-permute-start(bf16[3,256,64]{1,2,0:T(8,128)(2,1)S(1)} %get-tuple-element.19), channel_id=1, source_target_pairs={{0,8},{4,12},{8,0},{12,4},{1,9},{5,13},{9,1},{13,5},{2,10},{6,14},... | collective-permute-start | bytes 294920 | tf_op jit(solution)/shard_map/ppermute | solution.py:19
  97.7 7.4 %collective-permute-start.25 = (bf16[3,256,64]{1,2,0:T(8,128)(2,1)S(1)}, bf16[3,256,64]{1,2,0:T(8,128)(2,1)S(1)}, u32[]{:S(2)}, u32[]{:S(2)}) collective-permute-start(bf16[3,256,64]{1,2,0:T(8,128)(2,1)S(1)} %get-tuple-element.36), channel_id=1, source_target_pairs={{0,4},{4,8},{8,12},{12,0},{1,5},{5,9},{9,13},{13,1},{2,6},{6,10},{... | collective-permute-start | bytes 294920 | tf_op jit(solution)/shard_map/ppermute | solution.py:19
  100.3 8.2 %collective-permute-start.26 = (bf16[3,256,64]{1,2,0:T(8,128)(2,1)S(1)}, bf16[3,256,64]{1,2,0:T(8,128)(2,1)S(1)}, u32[]{:S(2)}, u32[]{:S(2)}) collective-permute-start(bf16[3,256,64]{1,2,0:T(8,128)(2,1)S(1)} %get-tuple-element.38), channel_id=1, source_target_pairs={{0,8},{4,12},{8,0},{12,4},{1,9},{5,13},{9,1},{13,5},{2,10},{6,14},... | collective-permute-start | bytes 294920 | tf_op jit(solution)/shard_map/ppermute | solution.py:19
  109.5 13.8 %collective-permute-start.31 = (bf16[3,256,64]{1,2,0:T(8,128)(2,1)}, bf16[3,256,64]{1,2,0:T(8,128)(2,1)}, u32[]{:S(2)}, u32[]{:S(2)}) collective-permute-start(bf16[3,256,64]{1,2,0:T(8,128)(2,1)} %get-tuple-element.7), channel_id=1, source_target_pairs={{0,2},{4,6},{8,10},{12,14},{1,3},{5,7},{9,11},{13,15},{16,18},{20,... | collective-permute-start | bytes 294920 | tf_op jit(solution)/shard_map/ppermute | solution.py:54
  116.6 9.2 %collective-permute-start.32 = (bf16[3,256,64]{1,2,0:T(8,128)(2,1)}, bf16[3,256,64]{1,2,0:T(8,128)(2,1)S(1)}, u32[]{:S(2)}, u32[]{:S(2)}) collective-permute-start(bf16[3,256,64]{1,2,0:T(8,128)(2,1)} %get-tuple-element.7), channel_id=1, source_target_pairs={{0,6},{4,10},{8,14},{12,2},{1,7},{5,11},{9,15},{13,3},{16,22},{20,... | collective-permute-start | bytes 294920 | tf_op jit(solution)/shard_map/ppermute | solution.py:54
  119.3 8.4 %collective-permute-start.33 = (bf16[3,256,64]{1,2,0:T(8,128)(2,1)}, bf16[3,256,64]{1,2,0:T(8,128)(2,1)S(1)}, u32[]{:S(2)}, u32[]{:S(2)}) collective-permute-start(bf16[3,256,64]{1,2,0:T(8,128)(2,1)} %get-tuple-element.7), channel_id=1, source_target_pairs={{0,10},{4,14},{8,2},{12,6},{1,11},{5,15},{9,3},{13,7},{16,26},{20,... | collective-permute-start | bytes 294920 | tf_op jit(solution)/shard_map/ppermute | solution.py:54
  122.7 14.0 %collective-permute-start.28 = (bf16[3,256,64]{1,2,0:T(8,128)(2,1)}, bf16[3,256,64]{1,2,0:T(8,128)(2,1)S(1)}, u32[]{:S(2)}, u32[]{:S(2)}) collective-permute-start(bf16[3,256,64]{1,2,0:T(8,128)(2,1)} %get-tuple-element.7), channel_id=1, source_target_pairs={{0,4},{4,8},{8,12},{12,0},{1,5},{5,9},{9,13},{13,1},{2,6},{6,10},{... | collective-permute-start | bytes 294920 | tf_op jit(solution)/shard_map/ppermute | solution.py:19
  123.3 16.6 %collective-permute-start.29 = (bf16[3,256,64]{1,2,0:T(8,128)(2,1)}, bf16[3,256,64]{1,2,0:T(8,128)(2,1)S(1)}, u32[]{:S(2)}, u32[]{:S(2)}) collective-permute-start(bf16[3,256,64]{1,2,0:T(8,128)(2,1)} %get-tuple-element.7), channel_id=1, source_target_pairs={{0,8},{4,12},{8,0},{12,4},{1,9},{5,13},{9,1},{13,5},{2,10},{6,14},... | collective-permute-start | bytes 294920 | tf_op jit(solution)/shard_map/ppermute | solution.py:19
  125.8 14.1 %collective-permute-start.30 = (bf16[3,256,64]{1,2,0:T(8,128)(2,1)}, bf16[3,256,64]{1,2,0:T(8,128)(2,1)S(1)}, u32[]{:S(2)}, u32[]{:S(2)}) collective-permute-start(bf16[3,256,64]{1,2,0:T(8,128)(2,1)} %get-tuple-element.7), channel_id=1, source_target_pairs={{0,12},{4,0},{8,4},{12,8},{1,13},{5,1},{9,5},{13,9},{2,14},{6,2},{... | collective-permute-start | bytes 294920 | tf_op jit(solution)/shard_map/ppermute | solution.py:19
  130.0 10.0 %collective-permute-start.35 = (bf16[3,256,64]{1,2,0:T(8,128)(2,1)S(1)}, bf16[3,256,64]{1,2,0:T(8,128)(2,1)S(1)}, u32[]{:S(2)}, u32[]{:S(2)}) collective-permute-start(bf16[3,256,64]{1,2,0:T(8,128)(2,1)S(1)} %get-tuple-element.33), channel_id=1, source_target_pairs={{0,4},{4,8},{8,12},{12,0},{1,5},{5,9},{9,13},{13,1},{2,6},{6,10},{... | collective-permute-start | bytes 294920 | tf_op jit(solution)/shard_map/ppermute | solution.py:19
  135.8 9.4 %collective-permute-start.36 = (bf16[3,256,64]{1,2,0:T(8,128)(2,1)S(1)}, bf16[3,256,64]{1,2,0:T(8,128)(2,1)S(1)}, u32[]{:S(2)}, u32[]{:S(2)}) collective-permute-start(bf16[3,256,64]{1,2,0:T(8,128)(2,1)S(1)} %get-tuple-element.35), channel_id=1, source_target_pairs={{0,8},{4,12},{8,0},{12,4},{1,9},{5,13},{9,1},{13,5},{2,10},{6,14},... | collective-permute-start | bytes 294920 | tf_op jit(solution)/shard_map/ppermute | solution.py:19
  136.7 8.5 %collective-permute-start.37 = (bf16[3,256,64]{1,2,0:T(8,128)(2,1)S(1)}, bf16[3,256,64]{1,2,0:T(8,128)(2,1)S(1)}, u32[]{:S(2)}, u32[]{:S(2)}) collective-permute-start(bf16[3,256,64]{1,2,0:T(8,128)(2,1)S(1)} %get-tuple-element.34), channel_id=1, source_target_pairs={{0,12},{4,0},{8,4},{12,8},{1,13},{5,1},{9,5},{13,9},{2,14},{6,2},{... | collective-permute-start | bytes 294920 | tf_op jit(solution)/shard_map/ppermute | solution.py:19
  148.8 7.6 %collective-permute-start.39 = (bf16[3,256,64]{1,2,0:T(8,128)(2,1)S(1)}, bf16[3,256,64]{1,2,0:T(8,128)(2,1)S(1)}, u32[]{:S(2)}, u32[]{:S(2)}) collective-permute-start(bf16[3,256,64]{1,2,0:T(8,128)(2,1)S(1)} %get-tuple-element.13), channel_id=1, source_target_pairs={{0,8},{4,12},{8,0},{12,4},{1,9},{5,13},{9,1},{13,5},{2,10},{6,14},... | collective-permute-start | bytes 294920 | tf_op jit(solution)/shard_map/ppermute | solution.py:19
  159.3 7.5 %collective-permute-start.41 = (bf16[3,256,64]{1,2,0:T(8,128)(2,1)S(1)}, bf16[3,256,64]{1,2,0:T(8,128)(2,1)S(1)}, u32[]{:S(2)}, u32[]{:S(2)}) collective-permute-start(bf16[3,256,64]{1,2,0:T(8,128)(2,1)S(1)} %get-tuple-element.30), channel_id=1, source_target_pairs={{0,4},{4,8},{8,12},{12,0},{1,5},{5,9},{9,13},{13,1},{2,6},{6,10},{... | collective-permute-start | bytes 294920 | tf_op jit(solution)/shard_map/ppermute | solution.py:19
  161.2 8.4 %collective-permute-start.42 = (bf16[3,256,64]{1,2,0:T(8,128)(2,1)S(1)}, bf16[3,256,64]{1,2,0:T(8,128)(2,1)S(1)}, u32[]{:S(2)}, u32[]{:S(2)}) collective-permute-start(bf16[3,256,64]{1,2,0:T(8,128)(2,1)S(1)} %get-tuple-element.32), channel_id=1, source_target_pairs={{0,8},{4,12},{8,0},{12,4},{1,9},{5,13},{9,1},{13,5},{2,10},{6,14},... | collective-permute-start | bytes 294920 | tf_op jit(solution)/shard_map/ppermute | solution.py:19
  173.4 7.4 %collective-permute-start.45 = (bf16[3,256,64]{1,2,0:T(8,128)(2,1)S(1)}, bf16[3,256,64]{1,2,0:T(8,128)(2,1)S(1)}, u32[]{:S(2)}, u32[]{:S(2)}) collective-permute-start(bf16[3,256,64]{1,2,0:T(8,128)(2,1)S(1)} %get-tuple-element.9), channel_id=1, source_target_pairs={{0,8},{4,12},{8,0},{12,4},{1,9},{5,13},{9,1},{13,5},{2,10},{6,14},... | collective-permute-start | bytes 294920 | tf_op jit(solution)/shard_map/ppermute | solution.py:19
  (23 other events, 134.1 us)

commit v6 on v2

--- a/solution.py
+++ b/solution.py
@@ -99,15 +99,18 @@
         [own_hidden(init_full[0]), own_hidden(init_full[1]), own_hidden(init_full[2].T)]
     )
     tick_count = key_rows.shape[0]
+    start = states_in[0, 0]
+    weights = jnp.stack([start[0], start[1], to_rows(start[2])])
     blocks = []
+    after = weights
     for tick_number in range(tick_count):
         scaled = (
             (step_rates[tick_number, 0, 0] * rate_scale)[:, None]
             * value_rows[tick_number, 0, :, 0].astype(jnp.float32)
         ).astype(jnp.bfloat16)
-        blocks.append(gathered(jnp.stack([key_rows[tick_number, 0, :, 0], scaled])))
-    start = states_in[0, 0]
-    weights = jnp.stack([start[0], start[1], to_rows(start[2])])
+        rows, _ = lax.optimization_barrier((jnp.stack([key_rows[tick_number, 0, :, 0], scaled]), after))
+        blocks.append(gathered(rows))
+        after = blocks[-1]
     results = []
     for tick_number in range(tick_count):
         if tick_number > 0:

time: 242 us -> 241 us (level)
  waiting for transfers between devices: 123 us -> 126 us
  matrix products: 20.5 us -> 17.8 us
    all_to_all x1, waiting for transfers between devices: 70.3 us -> 38.8 us  [to_rows(): got = lax.all_to_all(pieces, 'tok', 0, 0, tiled=False)]
    ppermute x36, waiting for transfers between devices: 47.4 us -> 78.3 us  [rotated(): lax.ppermute(value, axis, [(i, (i + by) % devices) for i in range(devices)])]
    ppermute x2, waiting for transfers between devices: 0.01 us -> 3.68 us  [shifted(): return lax.ppermute(value, axis, pairs)]
    another operation x6 -> x3, other arithmetic: 5.67 us -> 3.19 us  [gathered(): jnp.stack([value] + [rotated(value, 'tok', by) for by in range(1, tok_cou...]
  transfers between devices with their start and end apart: 40 -> 40, of which waited for: 21 -> 20; matrix products, arithmetic and copies ran while one was open for 9% -> 7% of each run, Pallas kernels for 0% -> 0%
where the time goes in v6:
time: 241 us
  waiting for transfers between devices  126 us (52%)
  starting transfers between devices  78 us (32%)
  matrix products  17.8 us (7%)
  other arithmetic  10.7 us (4%)
  local copies, waits for them, and re-layouts  6.96 us (3%)
    ppermute x36, waiting for transfers between devices, rotated(): lax.ppermute(value, axis, [(i, (i + by) % devices) for i in range(devices)])  78.3 us
    ppermute x36, starting transfers between devices, rotated(): lax.ppermute(value, axis, [(i, (i + by) % devices) for i in range(devices)])  63.8 us
    all_to_all x1, waiting for transfers between devices, to_rows(): got = lax.all_to_all(pieces, 'tok', 0, 0, tiled=False)  38.8 us
    ppermute x2, starting transfers between devices, shifted(): return lax.ppermute(value, axis, pairs)  7.68 us
    all_to_all x1, waiting for transfers between devices, to_cols(): got = lax.all_to_all(pieces, 'tok', 0, 0, tiled=False)  5.17 us
  transfers between devices with their start and end apart: 40, of which 20 were waited for; matrix products, arithmetic and copies ran while one was open for 7% of the time, Pallas kernels for 0%

profile of v6, /device:TPU:0, one launch (start us, length us, event | category | flops | bytes accessed | tf_op | source)
XLA Modules:
  0.0 240.8 jit_solution(6983972508611348184)
XLA Ops:
  3.0 3.1 %collective-permute-start = (bf16[2,512,256]{2,1,0:T(8,128)(2,1)S(1)}, bf16[2,512,256]{2,1,0:T(8,128)(2,1)S(1)}, u32[]{:S(2)}, u32[]{:S(2)}) collective-permute-start(bf16[2,512,256]{2,1,0:T(8,128)(2,1)S(1)} %pad_maximum_fusion.3), channel_id=1, source_target_pairs={{0,4},{4,8},{8,12},{12,0},{1,5},{5,9},{9,13},{13,1},{2,6},{6,10},{... | collective-permute-start | bytes 1572872 | tf_op jit(solution)/shard_map/ppermute | solution.py:19
  6.1 2.6 %collective-permute-start.1 = (bf16[2,512,256]{2,1,0:T(8,128)(2,1)S(1)}, bf16[2,512,256]{2,1,0:T(8,128)(2,1)}, u32[]{:S(2)}, u32[]{:S(2)}) collective-permute-start(bf16[2,512,256]{2,1,0:T(8,128)(2,1)S(1)} %pad_maximum_fusion.3), channel_id=1, source_target_pairs={{0,8},{4,12},{8,0},{12,4},{1,9},{5,13},{9,1},{13,5},{2,10},{6,14},... | collective-permute-start | bytes 1572872 | tf_op jit(solution)/shard_map/ppermute | solution.py:19
  10.9 3.3 %all-to-all-start = ((f32[4,1,4096]{2,1,0:T(1,128)}), f32[4,1,4096]{2,1,0:T(1,128)S(1)}, u32[]{:S(2)}, u32[]{:S(2)}) async-start(f32[4,1,4096]{2,1,0:T(1,128)} %reshape.361), calls=%async_computation | async-start | bytes 131072 | tf_op jit(solution)/shard_map/all_to_all | solution.py:39
  16.5 38.8 %all-to-all-done = f32[4,1,4096]{2,1,0:T(1,128)S(1)} async-done(((f32[4,1,4096]{2,1,0:T(1,128)}), f32[4,1,4096]{2,1,0:T(1,128)S(1)}, u32[]{:S(2)}, u32[]{:S(2)}) %all-to-all-start) | async-done | bytes 65568 | tf_op jit(solution)/shard_map/all_to_all | solution.py:39
  61.6 1.8 collective-permute-start.4
  63.4 1.7 collective-permute-start.5
  69.9 2.4 %collective-permute-start.6 = (f32[256]{0:T(256)S(1)}, f32[256]{0:T(256)S(1)}, u32[]{:S(2)}, u32[]{:S(2)}) collective-permute-start(f32[256]{0:T(256)S(1)} %multiply_reduce_fusion.11), channel_id=1, source_target_pairs={{0,4},{4,8},{8,12},{12,0},{1,5},{5,9},{9,13},{13,1},{2,6},{6,10},{... | collective-permute-start | bytes 3080 | tf_op jit(solution)/shard_map/ppermute | solution.py:19
  74.9 16.7 %collective-permute-done.6 = f32[256]{0:T(256)S(1)} collective-permute-done((f32[256]{0:T(256)S(1)}, f32[256]{0:T(256)S(1)}, u32[]{:S(2)}, u32[]{:S(2)}) %collective-permute-start.6) | collective-permute-done | bytes 1056 | tf_op jit(solution)/shard_map/ppermute | solution.py:19
  91.5 10.7 %collective-permute-done.7 = f32[256]{0:T(256)S(1)} collective-permute-done((f32[256]{0:T(256)S(1)}, f32[256]{0:T(256)S(1)}, u32[]{:S(2)}, u32[]{:S(2)}) %collective-permute-start.7) | collective-permute-done | bytes 1056 | tf_op jit(solution)/shard_map/ppermute | solution.py:19
  104.3 1.8 collective-permute-start.11
  106.8 2.9 %collective-permute-done.9 = bf16[3,256,64]{1,2,0:T(8,128)(2,1)S(1)} collective-permute-done((bf16[3,256,64]{1,2,0:T(8,128)(2,1)S(1)}, bf16[3,256,64]{1,2,0:T(8,128)(2,1)S(1)}, u32[]{:S(2)}, u32[]{:S(2)}) %collective-permute-start.9) | collective-permute-done | bytes 98336 | tf_op jit(solution)/shard_map/ppermute | solution.py:19
  109.8 2.7 %collective-permute-done.10 = bf16[3,256,64]{1,2,0:T(8,128)(2,1)S(1)} collective-permute-done((bf16[3,256,64]{1,2,0:T(8,128)(2,1)S(1)}, bf16[3,256,64]{1,2,0:T(8,128)(2,1)S(1)}, u32[]{:S(2)}, u32[]{:S(2)}) %collective-permute-start.10) | collective-permute-done | bytes 98336 | tf_op jit(solution)/shard_map/ppermute | solution.py:19
  112.5 3.4 %collective-permute-start.12 = (f32[3,256,64]{1,2,0:T(8,128)}, f32[3,256,64]{1,2,0:T(8,128)S(1)}, u32[]{:S(2)}, u32[]{:S(2)}) collective-permute-start(f32[3,256,64]{1,2,0:T(8,128)} %pad_maximum_fusion.8), channel_id=1, source_target_pairs={{0,2},{1,3},{4,6},{5,7},{8,10},{9,11},{12,14},{13,15},{16,18},{17,... | collective-permute-start | bytes 589832 | tf_op jit(solution)/shard_map/ppermute | solution.py:14
  119.5 3.5 %collective-permute-done.15 = bf16[2,512,256]{2,1,0:T(8,128)(2,1)} collective-permute-done((bf16[2,512,256]{2,1,0:T(8,128)(2,1)S(1)}, bf16[2,512,256]{2,1,0:T(8,128)(2,1)}, u32[]{:S(2)}, u32[]{:S(2)}) %collective-permute-start.15) | collective-permute-done | bytes 524320 | tf_op jit(solution)/shard_map/ppermute | solution.py:19
  127.0 8.3 %collective-permute-start.16 = (f32[256]{0:T(256)S(1)}, f32[256]{0:T(256)S(1)}, u32[]{:S(2)}, u32[]{:S(2)}) collective-permute-start(f32[256]{0:T(256)S(1)} %multiply_reduce_fusion.10), channel_id=1, source_target_pairs={{0,4},{4,8},{8,12},{12,0},{1,5},{5,9},{9,13},{13,1},{2,6},{6,10},{... | collective-permute-start | bytes 3080 | tf_op jit(solution)/shard_map/ppermute | solution.py:19
  135.3 2.8 %collective-permute-start.17 = (f32[256]{0:T(256)S(1)}, f32[256]{0:T(256)S(1)}, u32[]{:S(2)}, u32[]{:S(2)}) collective-permute-start(f32[256]{0:T(256)S(1)} %multiply_reduce_fusion.10), channel_id=1, source_target_pairs={{0,8},{4,12},{8,0},{12,4},{1,9},{5,13},{9,1},{13,5},{2,10},{6,14},... | collective-permute-start | bytes 3080 | tf_op jit(solution)/shard_map/ppermute | solution.py:19
  144.5 2.4 %collective-permute-start.19 = (f32[256]{0:T(256)S(1)}, f32[256]{0:T(256)S(1)}, u32[]{:S(2)}, u32[]{:S(2)}) collective-permute-start(f32[256]{0:T(256)S(1)} %multiply_reduce_fusion.9), channel_id=1, source_target_pairs={{0,4},{4,8},{8,12},{12,0},{1,5},{5,9},{9,13},{13,1},{2,6},{6,10},{... | collective-permute-start | bytes 3080 | tf_op jit(solution)/shard_map/ppermute | solution.py:19
  149.5 13.8 %collective-permute-done.19 = f32[256]{0:T(256)S(1)} collective-permute-done((f32[256]{0:T(256)S(1)}, f32[256]{0:T(256)S(1)}, u32[]{:S(2)}, u32[]{:S(2)}) %collective-permute-start.19) | collective-permute-done | bytes 1056 | tf_op jit(solution)/shard_map/ppermute | solution.py:19
  163.4 11.2 %collective-permute-done.20 = f32[256]{0:T(256)S(1)} collective-permute-done((f32[256]{0:T(256)S(1)}, f32[256]{0:T(256)S(1)}, u32[]{:S(2)}, u32[]{:S(2)}) %collective-permute-start.20) | collective-permute-done | bytes 1056 | tf_op jit(solution)/shard_map/ppermute | solution.py:19
  175.9 2.6 %collective-permute-start.24 = (bf16[3,256,64]{1,2,0:T(8,128)(2,1)S(1)}, bf16[3,256,64]{1,2,0:T(8,128)(2,1)S(1)}, u32[]{:S(2)}, u32[]{:S(2)}) collective-permute-start(bf16[3,256,64]{1,2,0:T(8,128)(2,1)S(1)} %fusion.142), channel_id=1, source_target_pairs={{0,12},{4,0},{8,4},{12,8},{1,13},{5,1},{9,5},{13,9},{2,14},{6,2},{... | collective-permute-start | bytes 294920 | tf_op jit(solution)/shard_map/ppermute | solution.py:19
  178.5 3.7 %collective-permute-done.22 = bf16[3,256,64]{1,2,0:T(8,128)(2,1)S(1)} collective-permute-done((bf16[3,256,64]{1,2,0:T(8,128)(2,1)S(1)}, bf16[3,256,64]{1,2,0:T(8,128)(2,1)S(1)}, u32[]{:S(2)}, u32[]{:S(2)}) %collective-permute-start.22) | collective-permute-done | bytes 98336 | tf_op jit(solution)/shard_map/ppermute | solution.py:19
  182.2 3.2 %collective-permute-done.23 = bf16[3,256,64]{1,2,0:T(8,128)(2,1)S(1)} collective-permute-done((bf16[3,256,64]{1,2,0:T(8,128)(2,1)S(1)}, bf16[3,256,64]{1,2,0:T(8,128)(2,1)S(1)}, u32[]{:S(2)}, u32[]{:S(2)}) %collective-permute-start.23) | collective-permute-done | bytes 98336 | tf_op jit(solution)/shard_map/ppermute | solution.py:19
  185.5 4.3 %collective-permute-start.25 = (f32[3,256,64]{1,2,0:T(8,128)S(1)}, f32[3,256,64]{1,2,0:T(8,128)S(1)}, u32[]{:S(2)}, u32[]{:S(2)}) collective-permute-start(f32[3,256,64]{1,2,0:T(8,128)S(1)} %pad_maximum_fusion.11), channel_id=1, source_target_pairs={{0,2},{1,3},{4,6},{5,7},{8,10},{9,11},{12,14},{13,15},{16,18},{17,... | collective-permute-start | bytes 589832 | tf_op jit(solution)/shard_map/ppermute | solution.py:14
  190.1 2.8 %collective-permute-done.25 = f32[3,256,64]{1,2,0:T(8,128)S(1)} collective-permute-done((f32[3,256,64]{1,2,0:T(8,128)S(1)}, f32[3,256,64]{1,2,0:T(8,128)S(1)}, u32[]{:S(2)}, u32[]{:S(2)}) %collective-permute-start.25) | collective-permute-done | bytes 196640 | tf_op jit(solution)/shard_map/ppermute | solution.py:14
  193.0 2.8 %collective-permute-done.28 = bf16[2,512,256]{2,1,0:T(8,128)(2,1)S(1)} collective-permute-done((bf16[2,512,256]{2,1,0:T(8,128)(2,1)S(1)}, bf16[2,512,256]{2,1,0:T(8,128)(2,1)S(1)}, u32[]{:S(2)}, u32[]{:S(2)}) %collective-permute-start.28) | collective-permute-done | bytes 524320 | tf_op jit(solution)/shard_map/ppermute | solution.py:19
  198.7 8.1 %collective-permute-start.29 = (f32[256]{0:T(256)S(1)}, f32[256]{0:T(256)S(1)}, u32[]{:S(2)}, u32[]{:S(2)}) collective-permute-start(f32[256]{0:T(256)S(1)} %multiply_reduce_fusion.8), channel_id=1, source_target_pairs={{0,4},{4,8},{8,12},{12,0},{1,5},{5,9},{9,13},{13,1},{2,6},{6,10},{... | collective-permute-start | bytes 3080 | tf_op jit(solution)/shard_map/ppermute | solution.py:19
  206.8 3.4 %collective-permute-start.30 = (f32[256]{0:T(256)S(1)}, f32[256]{0:T(256)S(1)}, u32[]{:S(2)}, u32[]{:S(2)}) collective-permute-start(f32[256]{0:T(256)S(1)} %multiply_reduce_fusion.8), channel_id=1, source_target_pairs={{0,8},{4,12},{8,0},{12,4},{1,9},{5,13},{9,1},{13,5},{2,10},{6,14},... | collective-permute-start | bytes 3080 | tf_op jit(solution)/shard_map/ppermute | solution.py:19
  211.7 2.0 collective-permute-done.31
  216.6 2.3 collective-permute-start.33
  222.6 2.2 collective-permute-start.35
  228.1 3.3 %all-to-all-start.1 = ((f32[4,1,4096]{2,1,0:T(1,128)}), f32[4,1,4096]{2,1,0:T(1,128)S(1)}, u32[]{:S(2)}, u32[]{:S(2)}) async-start(f32[4,1,4096]{2,1,0:T(1,128)} %reshape.363), calls=%async_computation.1 | async-start | bytes 131072 | tf_op jit(solution)/shard_map/all_to_all | solution.py:47
  231.9 5.2 %all-to-all-done.1 = f32[4,1,4096]{2,1,0:T(1,128)S(1)} async-done(((f32[4,1,4096]{2,1,0:T(1,128)}), f32[4,1,4096]{2,1,0:T(1,128)S(1)}, u32[]{:S(2)}, u32[]{:S(2)}) %all-to-all-start.1) | async-done | bytes 65568 | tf_op jit(solution)/shard_map/all_to_all | solution.py:47
  (192 shorter events, 59.4 us)
Async XLA Ops:
  3.0 54.1 %collective-permute-start = (bf16[2,512,256]{2,1,0:T(8,128)(2,1)S(1)}, bf16[2,512,256]{2,1,0:T(8,128)(2,1)S(1)}, u32[]{:S(2)}, u32[]{:S(2)}) collective-permute-start(bf16[2,512,256]{2,1,0:T(8,128)(2,1)S(1)} %pad_maximum_fusion.3), channel_id=1, source_target_pairs={{0,4},{4,8},{8,12},{12,0},{1,5},{5,9},{9,13},{13,1},{2,6},{6,10},{... | collective-permute-start | bytes 1572872 | tf_op jit(solution)/shard_map/ppermute | solution.py:19
  6.1 51.0 %collective-permute-start.1 = (bf16[2,512,256]{2,1,0:T(8,128)(2,1)S(1)}, bf16[2,512,256]{2,1,0:T(8,128)(2,1)}, u32[]{:S(2)}, u32[]{:S(2)}) collective-permute-start(bf16[2,512,256]{2,1,0:T(8,128)(2,1)S(1)} %pad_maximum_fusion.3), channel_id=1, source_target_pairs={{0,8},{4,12},{8,0},{12,4},{1,9},{5,13},{9,1},{13,5},{2,10},{6,14},... | collective-permute-start | bytes 1572872 | tf_op jit(solution)/shard_map/ppermute | solution.py:19
  8.7 48.4 %collective-permute-start.2 = (bf16[2,512,256]{2,1,0:T(8,128)(2,1)S(1)}, bf16[2,512,256]{2,1,0:T(8,128)(2,1)}, u32[]{:S(2)}, u32[]{:S(2)}) collective-permute-start(bf16[2,512,256]{2,1,0:T(8,128)(2,1)S(1)} %pad_maximum_fusion.3), channel_id=1, source_target_pairs={{0,12},{4,0},{8,4},{12,8},{1,13},{5,1},{9,5},{13,9},{2,14},{6,2},{... | collective-permute-start | bytes 1572872 | tf_op jit(solution)/shard_map/ppermute | solution.py:19
  10.9 44.3 %all-to-all-start = ((f32[4,1,4096]{2,1,0:T(1,128)}), f32[4,1,4096]{2,1,0:T(1,128)S(1)}, u32[]{:S(2)}, u32[]{:S(2)}) async-start(f32[4,1,4096]{2,1,0:T(1,128)} %reshape.361), calls=%async_computation | async-start | bytes 131072 | tf_op jit(solution)/shard_map/all_to_all | solution.py:39
  61.2 6.0 %collective-permute-start.3 = (f32[256]{0:T(256)S(1)}, f32[256]{0:T(256)S(1)}, u32[]{:S(2)}, u32[]{:S(2)}) collective-permute-start(f32[256]{0:T(256)S(1)} %multiply_reduce_fusion.12), channel_id=1, source_target_pairs={{0,4},{4,8},{8,12},{12,0},{1,5},{5,9},{9,13},{13,1},{2,6},{6,10},{... | collective-permute-start | bytes 3080 | tf_op jit(solution)/shard_map/ppermute | solution.py:19
  61.6 5.7 %collective-permute-start.4 = (f32[256]{0:T(256)S(1)}, f32[256]{0:T(256)S(1)}, u32[]{:S(2)}, u32[]{:S(2)}) collective-permute-start(f32[256]{0:T(256)S(1)} %multiply_reduce_fusion.12), channel_id=1, source_target_pairs={{0,8},{4,12},{8,0},{12,4},{1,9},{5,13},{9,1},{13,5},{2,10},{6,14},... | collective-permute-start | bytes 3080 | tf_op jit(solution)/shard_map/ppermute | solution.py:19
  65.1 54.4 %collective-permute-start.13 = (bf16[2,512,256]{2,1,0:T(8,128)(2,1)S(1)}, bf16[2,512,256]{2,1,0:T(8,128)(2,1)S(1)}, u32[]{:S(2)}, u32[]{:S(2)}) collective-permute-start(bf16[2,512,256]{2,1,0:T(8,128)(2,1)S(1)} %pad_maximum_fusion.4), channel_id=1, source_target_pairs={{0,4},{4,8},{8,12},{12,0},{1,5},{5,9},{9,13},{13,1},{2,6},{6,10},{... | collective-permute-start | bytes 1572872 | tf_op jit(solution)/shard_map/ppermute | solution.py:19
  65.6 53.8 %collective-permute-start.14 = (bf16[2,512,256]{2,1,0:T(8,128)(2,1)S(1)}, bf16[2,512,256]{2,1,0:T(8,128)(2,1)}, u32[]{:S(2)}, u32[]{:S(2)}) collective-permute-start(bf16[2,512,256]{2,1,0:T(8,128)(2,1)S(1)} %pad_maximum_fusion.4), channel_id=1, source_target_pairs={{0,8},{4,12},{8,0},{12,4},{1,9},{5,13},{9,1},{13,5},{2,10},{6,14},... | collective-permute-start | bytes 1572872 | tf_op jit(solution)/shard_map/ppermute | solution.py:19
  69.9 21.6 %collective-permute-start.6 = (f32[256]{0:T(256)S(1)}, f32[256]{0:T(256)S(1)}, u32[]{:S(2)}, u32[]{:S(2)}) collective-permute-start(f32[256]{0:T(256)S(1)} %multiply_reduce_fusion.11), channel_id=1, source_target_pairs={{0,4},{4,8},{8,12},{12,0},{1,5},{5,9},{9,13},{13,1},{2,6},{6,10},{... | collective-permute-start | bytes 3080 | tf_op jit(solution)/shard_map/ppermute | solution.py:19
  72.3 29.9 %collective-permute-start.7 = (f32[256]{0:T(256)S(1)}, f32[256]{0:T(256)S(1)}, u32[]{:S(2)}, u32[]{:S(2)}) collective-permute-start(f32[256]{0:T(256)S(1)} %multiply_reduce_fusion.11), channel_id=1, source_target_pairs={{0,8},{4,12},{8,0},{12,4},{1,9},{5,13},{9,1},{13,5},{2,10},{6,14},... | collective-permute-start | bytes 3080 | tf_op jit(solution)/shard_map/ppermute | solution.py:19
  73.8 28.5 %collective-permute-start.8 = (f32[256]{0:T(256)S(1)}, f32[256]{0:T(256)S(1)}, u32[]{:S(2)}, u32[]{:S(2)}) collective-permute-start(f32[256]{0:T(256)S(1)} %multiply_reduce_fusion.11), channel_id=1, source_target_pairs={{0,12},{4,0},{8,4},{12,8},{1,13},{5,1},{9,5},{13,9},{2,14},{6,2},{... | collective-permute-start | bytes 3080 | tf_op jit(solution)/shard_map/ppermute | solution.py:19
  102.3 7.5 %collective-permute-start.9 = (bf16[3,256,64]{1,2,0:T(8,128)(2,1)S(1)}, bf16[3,256,64]{1,2,0:T(8,128)(2,1)S(1)}, u32[]{:S(2)}, u32[]{:S(2)}) collective-permute-start(bf16[3,256,64]{1,2,0:T(8,128)(2,1)S(1)} %fusion.143), channel_id=1, source_target_pairs={{0,4},{4,8},{8,12},{12,0},{1,5},{5,9},{9,13},{13,1},{2,6},{6,10},{... | collective-permute-start | bytes 294920 | tf_op jit(solution)/shard_map/ppermute | solution.py:19
  102.8 9.7 %collective-permute-start.10 = (bf16[3,256,64]{1,2,0:T(8,128)(2,1)S(1)}, bf16[3,256,64]{1,2,0:T(8,128)(2,1)S(1)}, u32[]{:S(2)}, u32[]{:S(2)}) collective-permute-start(bf16[3,256,64]{1,2,0:T(8,128)(2,1)S(1)} %fusion.143), channel_id=1, source_target_pairs={{0,8},{4,12},{8,0},{12,4},{1,9},{5,13},{9,1},{13,5},{2,10},{6,14},... | collective-permute-start | bytes 294920 | tf_op jit(solution)/shard_map/ppermute | solution.py:19
  104.3 11.6 %collective-permute-start.11 = (bf16[3,256,64]{1,2,0:T(8,128)(2,1)S(1)}, bf16[3,256,64]{1,2,0:T(8,128)(2,1)S(1)}, u32[]{:S(2)}, u32[]{:S(2)}) collective-permute-start(bf16[3,256,64]{1,2,0:T(8,128)(2,1)S(1)} %fusion.143), channel_id=1, source_target_pairs={{0,12},{4,0},{8,4},{12,8},{1,13},{5,1},{9,5},{13,9},{2,14},{6,2},{... | collective-permute-start | bytes 294920 | tf_op jit(solution)/shard_map/ppermute | solution.py:19
  109.8 13.2 %collective-permute-start.15 = (bf16[2,512,256]{2,1,0:T(8,128)(2,1)S(1)}, bf16[2,512,256]{2,1,0:T(8,128)(2,1)}, u32[]{:S(2)}, u32[]{:S(2)}) collective-permute-start(bf16[2,512,256]{2,1,0:T(8,128)(2,1)S(1)} %pad_maximum_fusion.4), channel_id=1, source_target_pairs={{0,12},{4,0},{8,4},{12,8},{1,13},{5,1},{9,5},{13,9},{2,14},{6,2},{... | collective-permute-start | bytes 1572872 | tf_op jit(solution)/shard_map/ppermute | solution.py:19
  112.5 6.9 %collective-permute-start.12 = (f32[3,256,64]{1,2,0:T(8,128)}, f32[3,256,64]{1,2,0:T(8,128)S(1)}, u32[]{:S(2)}, u32[]{:S(2)}) collective-permute-start(f32[3,256,64]{1,2,0:T(8,128)} %pad_maximum_fusion.8), channel_id=1, source_target_pairs={{0,2},{1,3},{4,6},{5,7},{8,10},{9,11},{12,14},{13,15},{16,18},{17,... | collective-permute-start | bytes 589832 | tf_op jit(solution)/shard_map/ppermute | solution.py:14
  127.0 13.4 %collective-permute-start.16 = (f32[256]{0:T(256)S(1)}, f32[256]{0:T(256)S(1)}, u32[]{:S(2)}, u32[]{:S(2)}) collective-permute-start(f32[256]{0:T(256)S(1)} %multiply_reduce_fusion.10), channel_id=1, source_target_pairs={{0,4},{4,8},{8,12},{12,0},{1,5},{5,9},{9,13},{13,1},{2,6},{6,10},{... | collective-permute-start | bytes 3080 | tf_op jit(solution)/shard_map/ppermute | solution.py:19
  139.7 53.2 %collective-permute-start.26 = (bf16[2,512,256]{2,1,0:T(8,128)(2,1)S(1)}, bf16[2,512,256]{2,1,0:T(8,128)(2,1)S(1)}, u32[]{:S(2)}, u32[]{:S(2)}) collective-permute-start(bf16[2,512,256]{2,1,0:T(8,128)(2,1)S(1)} %pad_maximum_fusion.5), channel_id=1, source_target_pairs={{0,4},{4,8},{8,12},{12,0},{1,5},{5,9},{9,13},{13,1},{2,6},{6,10},{... | collective-permute-start | bytes 1572872 | tf_op jit(solution)/shard_map/ppermute | solution.py:19
  140.2 52.7 %collective-permute-start.27 = (bf16[2,512,256]{2,1,0:T(8,128)(2,1)S(1)}, bf16[2,512,256]{2,1,0:T(8,128)(2,1)S(1)}, u32[]{:S(2)}, u32[]{:S(2)}) collective-permute-start(bf16[2,512,256]{2,1,0:T(8,128)(2,1)S(1)} %pad_maximum_fusion.5), channel_id=1, source_target_pairs={{0,8},{4,12},{8,0},{12,4},{1,9},{5,13},{9,1},{13,5},{2,10},{6,14},... | collective-permute-start | bytes 1572872 | tf_op jit(solution)/shard_map/ppermute | solution.py:19
  144.5 18.8 %collective-permute-start.19 = (f32[256]{0:T(256)S(1)}, f32[256]{0:T(256)S(1)}, u32[]{:S(2)}, u32[]{:S(2)}) collective-permute-start(f32[256]{0:T(256)S(1)} %multiply_reduce_fusion.9), channel_id=1, source_target_pairs={{0,4},{4,8},{8,12},{12,0},{1,5},{5,9},{9,13},{13,1},{2,6},{6,10},{... | collective-permute-start | bytes 3080 | tf_op jit(solution)/shard_map/ppermute | solution.py:19
  147.0 27.6 %collective-permute-start.20 = (f32[256]{0:T(256)S(1)}, f32[256]{0:T(256)S(1)}, u32[]{:S(2)}, u32[]{:S(2)}) collective-permute-start(f32[256]{0:T(256)S(1)} %multiply_reduce_fusion.9), channel_id=1, source_target_pairs={{0,8},{4,12},{8,0},{12,4},{1,9},{5,13},{9,1},{13,5},{2,10},{6,14},... | collective-permute-start | bytes 3080 | tf_op jit(solution)/shard_map/ppermute | solution.py:19
  148.4 26.2 %collective-permute-start.21 = (f32[256]{0:T(256)S(1)}, f32[256]{0:T(256)S(1)}, u32[]{:S(2)}, u32[]{:S(2)}) collective-permute-start(f32[256]{0:T(256)S(1)} %multiply_reduce_fusion.9), channel_id=1, source_target_pairs={{0,12},{4,0},{8,4},{12,8},{1,13},{5,1},{9,5},{13,9},{2,14},{6,2},{... | collective-permute-start | bytes 3080 | tf_op jit(solution)/shard_map/ppermute | solution.py:19
  174.6 7.6 %collective-permute-start.22 = (bf16[3,256,64]{1,2,0:T(8,128)(2,1)S(1)}, bf16[3,256,64]{1,2,0:T(8,128)(2,1)S(1)}, u32[]{:S(2)}, u32[]{:S(2)}) collective-permute-start(bf16[3,256,64]{1,2,0:T(8,128)(2,1)S(1)} %fusion.142), channel_id=1, source_target_pairs={{0,4},{4,8},{8,12},{12,0},{1,5},{5,9},{9,13},{13,1},{2,6},{6,10},{... | collective-permute-start | bytes 294920 | tf_op jit(solution)/shard_map/ppermute | solution.py:19
  175.2 10.3 %collective-permute-start.23 = (bf16[3,256,64]{1,2,0:T(8,128)(2,1)S(1)}, bf16[3,256,64]{1,2,0:T(8,128)(2,1)S(1)}, u32[]{:S(2)}, u32[]{:S(2)}) collective-permute-start(bf16[3,256,64]{1,2,0:T(8,128)(2,1)S(1)} %fusion.142), channel_id=1, source_target_pairs={{0,8},{4,12},{8,0},{12,4},{1,9},{5,13},{9,1},{13,5},{2,10},{6,14},... | collective-permute-start | bytes 294920 | tf_op jit(solution)/shard_map/ppermute | solution.py:19
  175.9 13.8 %collective-permute-start.24 = (bf16[3,256,64]{1,2,0:T(8,128)(2,1)S(1)}, bf16[3,256,64]{1,2,0:T(8,128)(2,1)S(1)}, u32[]{:S(2)}, u32[]{:S(2)}) collective-permute-start(bf16[3,256,64]{1,2,0:T(8,128)(2,1)S(1)} %fusion.142), channel_id=1, source_target_pairs={{0,12},{4,0},{8,4},{12,8},{1,13},{5,1},{9,5},{13,9},{2,14},{6,2},{... | collective-permute-start | bytes 294920 | tf_op jit(solution)/shard_map/ppermute | solution.py:19
  182.2 13.6 %collective-permute-start.28 = (bf16[2,512,256]{2,1,0:T(8,128)(2,1)S(1)}, bf16[2,512,256]{2,1,0:T(8,128)(2,1)S(1)}, u32[]{:S(2)}, u32[]{:S(2)}) collective-permute-start(bf16[2,512,256]{2,1,0:T(8,128)(2,1)S(1)} %pad_maximum_fusion.5), channel_id=1, source_target_pairs={{0,12},{4,0},{8,4},{12,8},{1,13},{5,1},{9,5},{13,9},{2,14},{6,2},{... | collective-permute-start | bytes 1572872 | tf_op jit(solution)/shard_map/ppermute | solution.py:19
  185.5 7.4 %collective-permute-start.25 = (f32[3,256,64]{1,2,0:T(8,128)S(1)}, f32[3,256,64]{1,2,0:T(8,128)S(1)}, u32[]{:S(2)}, u32[]{:S(2)}) collective-permute-start(f32[3,256,64]{1,2,0:T(8,128)S(1)} %pad_maximum_fusion.11), channel_id=1, source_target_pairs={{0,2},{1,3},{4,6},{5,7},{8,10},{9,11},{12,14},{13,15},{16,18},{17,... | collective-permute-start | bytes 589832 | tf_op jit(solution)/shard_map/ppermute | solution.py:14
  198.7 12.5 %collective-permute-start.29 = (f32[256]{0:T(256)S(1)}, f32[256]{0:T(256)S(1)}, u32[]{:S(2)}, u32[]{:S(2)}) collective-permute-start(f32[256]{0:T(256)S(1)} %multiply_reduce_fusion.8), channel_id=1, source_target_pairs={{0,4},{4,8},{8,12},{12,0},{1,5},{5,9},{9,13},{13,1},{2,6},{6,10},{... | collective-permute-start | bytes 3080 | tf_op jit(solution)/shard_map/ppermute | solution.py:19
  222.6 15.6 %collective-permute-start.35 = (bf16[3,256,64]{1,2,0:T(8,128)(2,1)S(1)}, bf16[3,256,64]{1,2,0:T(8,128)(2,1)S(1)}, u32[]{:S(2)}, u32[]{:S(2)}) collective-permute-start(bf16[3,256,64]{1,2,0:T(8,128)(2,1)S(1)} %pad_maximum_fusion.13), channel_id=1, source_target_pairs={{0,4},{4,8},{8,12},{12,0},{1,5},{5,9},{9,13},{13,1},{2,6},{6,10},{... | collective-permute-start | bytes 294920 | tf_op jit(solution)/shard_map/ppermute | solution.py:19
  224.8 13.4 %collective-permute-start.36 = (bf16[3,256,64]{1,2,0:T(8,128)(2,1)S(1)}, bf16[3,256,64]{1,2,0:T(8,128)(2,1)S(1)}, u32[]{:S(2)}, u32[]{:S(2)}) collective-permute-start(bf16[3,256,64]{1,2,0:T(8,128)(2,1)S(1)} %pad_maximum_fusion.13), channel_id=1, source_target_pairs={{0,8},{4,12},{8,0},{12,4},{1,9},{5,13},{9,1},{13,5},{2,10},{6,14},... | collective-permute-start | bytes 294920 | tf_op jit(solution)/shard_map/ppermute | solution.py:19
  226.4 11.8 %collective-permute-start.37 = (bf16[3,256,64]{1,2,0:T(8,128)(2,1)S(1)}, bf16[3,256,64]{1,2,0:T(8,128)(2,1)S(1)}, u32[]{:S(2)}, u32[]{:S(2)}) collective-permute-start(bf16[3,256,64]{1,2,0:T(8,128)(2,1)S(1)} %pad_maximum_fusion.13), channel_id=1, source_target_pairs={{0,12},{4,0},{8,4},{12,8},{1,13},{5,1},{9,5},{13,9},{2,14},{6,2},{... | collective-permute-start | bytes 294920 | tf_op jit(solution)/shard_map/ppermute | solution.py:19
  228.1 9.0 %all-to-all-start.1 = ((f32[4,1,4096]{2,1,0:T(1,128)}), f32[4,1,4096]{2,1,0:T(1,128)S(1)}, u32[]{:S(2)}, u32[]{:S(2)}) async-start(f32[4,1,4096]{2,1,0:T(1,128)} %reshape.363), calls=%async_computation.1 | async-start | bytes 131072 | tf_op jit(solution)/shard_map/all_to_all | solution.py:47
  (12 other events, 104.7 us)

commit v7 on v5

--- a/solution.py
+++ b/solution.py
@@ -47,9 +47,9 @@
     full = jnp.zeros(own.shape[:2] + (part_cols * tok_count,), own.dtype)
     for by in range(tok_count):
         pairs = [
-            (t * sections + s, ((t + by) % tok_count) * sections + s + 1)
+            (t * sections + s, ((t + by) % tok_count) * sections + (s + 1) % sections)
             for t in range(tok_count)
-            for s in range(sections - 1)
+            for s in range(sections)
         ]
         got = lax.ppermute(own, ("tok", "span"), pairs)
         full = lax.dynamic_update_slice_in_dim(full, got, ((me - by) % tok_count) * part_cols, 2)
@@ -103,6 +103,7 @@
     weights = states_in[0, 0]
     fast = gather_cols(weights.astype(jnp.bfloat16), part_cols)
     arrived = None
+    earlier_queries = rotated(query_rows[: tick_count - 1, 0, :, 0], "span", 1)
     for tick_number in range(tick_count):
         if tick_number > 0:
             fast = jnp.where(section_index == 0, init_fast, arrived)
@@ -122,8 +123,11 @@
         own = weights.astype(jnp.bfloat16)
         if tick_number + 1 < tick_count:
             arrived = cross_gather(own, part_cols)
-        fast = gather_cols(own, part_cols)
-        results.append(apply_fast(fast, query_rows[tick_number, 0, :, 0]))
+            for_previous = apply_fast(arrived, earlier_queries[tick_number])
+            results.append(rotated(for_previous, "span", -1))
+        else:
+            fast = gather_cols(own, part_cols)
+            results.append(apply_fast(fast, query_rows[tick_number, 0, :, 0]))
     outputs = jnp.stack(results)[:, None, :, None]
     return (outputs, weights[None, None])
 

time: 184 us -> 170 us (0.924)
  starting transfers between devices: 94.4 us -> 71.8 us
  waiting for transfers between devices: 60.9 us -> 70.8 us
    ppermute x39 -> x36, starting transfers between devices: 75.1 us -> 57.9 us  [rotated(): lax.ppermute(value, axis, [(i, (i + by) % devices) for i in range(devices)])]
    ppermute x8, waiting for transfers between devices: 0.02 us -> 9.53 us  [cross_gather(): got = lax.ppermute(own, ('tok', 'span'), pairs)]
    ppermute x8, starting transfers between devices: 19.3 us -> 13.8 us  [cross_gather(): got = lax.ppermute(own, ('tok', 'span'), pairs)]
    dot_general x3 -> x1, matrix products: 2.38 us -> 0.26 us  [apply_fast(): jnp.einsum('td,dh->th', query_block, fast[0], preferred_element_type=jnp....]
    ppermute x39 -> x36, waiting for transfers between devices: 60.9 us -> 61.3 us  [rotated(): lax.ppermute(value, axis, [(i, (i + by) % devices) for i in range(devices)])]
  transfers between devices with their start and end apart: 47 -> 44, of which waited for: 24 -> 28; matrix products, arithmetic and copies ran while one was open for 6% -> 6% of each run, Pallas kernels for 0% -> 0%
where the time goes in v7:
time: 170 us
  starting transfers between devices  71.8 us (42%)
  waiting for transfers between devices  70.8 us (42%)
  matrix products  16.8 us (10%)
  other arithmetic  6.22 us (4%)
  local copies, waits for them, and re-layouts  3.02 us (2%)
    ppermute x36, waiting for transfers between devices, rotated(): lax.ppermute(value, axis, [(i, (i + by) % devices) for i in range(devices)])  61.3 us
    ppermute x36, starting transfers between devices, rotated(): lax.ppermute(value, axis, [(i, (i + by) % devices) for i in range(devices)])  57.9 us
    ppermute x8, starting transfers between devices, cross_gather(): got = lax.ppermute(own, ('tok', 'span'), pairs)  13.8 us
    ppermute x8, waiting for transfers between devices, cross_gather(): got = lax.ppermute(own, ('tok', 'span'), pairs)  9.53 us
  transfers between devices with their start and end apart: 44, of which 28 were waited for; matrix products, arithmetic and copies ran while one was open for 6% of the time, Pallas kernels for 0%

profile of v7, /device:TPU:0, one launch (start us, length us, event | category | flops | bytes accessed | tf_op | source)
XLA Modules:
  0.0 170.2 jit_solution(14333771598086443877)
XLA Ops:
  1.6 3.1 %collective-permute-start = (bf16[3,256,64]{1,2,0:T(8,128)(2,1)S(1)}, bf16[3,256,64]{1,2,0:T(8,128)(2,1)S(1)}, u32[]{:S(2)}, u32[]{:S(2)}) collective-permute-start(bf16[3,256,64]{1,2,0:T(8,128)(2,1)S(1)} %get-tuple-element.25), channel_id=1, source_target_pairs={{0,4},{4,8},{8,12},{12,0},{1,5},{5,9},{9,13},{13,1},{2,6},{6,10},{... | collective-permute-start | bytes 294920 | tf_op jit(solution)/shard_map/ppermute | solution.py:19
  4.7 2.6 %collective-permute-start.1 = (bf16[3,256,64]{1,2,0:T(8,128)(2,1)S(1)}, bf16[3,256,64]{1,2,0:T(8,128)(2,1)S(1)}, u32[]{:S(2)}, u32[]{:S(2)}) collective-permute-start(bf16[3,256,64]{1,2,0:T(8,128)(2,1)S(1)} %get-tuple-element.25), channel_id=1, source_target_pairs={{0,8},{4,12},{8,0},{12,4},{1,9},{5,13},{9,1},{13,5},{2,10},{6,14},... | collective-permute-start | bytes 294920 | tf_op jit(solution)/shard_map/ppermute | solution.py:19
  10.4 3.5 %collective-permute-done.1 = bf16[3,256,64]{1,2,0:T(8,128)(2,1)S(1)} collective-permute-done((bf16[3,256,64]{1,2,0:T(8,128)(2,1)S(1)}, bf16[3,256,64]{1,2,0:T(8,128)(2,1)S(1)}, u32[]{:S(2)}, u32[]{:S(2)}) %collective-permute-start.1) | collective-permute-done | bytes 98336 | tf_op jit(solution)/shard_map/ppermute | solution.py:19
  16.7 2.6 %collective-permute-start.3 = (bf16[3,256,64]{1,2,0:T(8,128)(2,1)S(1)}, bf16[3,256,64]{1,2,0:T(8,128)(2,1)S(1)}, u32[]{:S(2)}, u32[]{:S(2)}) collective-permute-start(bf16[3,256,64]{1,2,0:T(8,128)(2,1)S(1)} %get-tuple-element.41), channel_id=1, source_target_pairs={{0,4},{4,8},{8,12},{12,0},{1,5},{5,9},{9,13},{13,1},{2,6},{6,10},{... | collective-permute-start | bytes 294920 | tf_op jit(solution)/shard_map/ppermute | solution.py:19
  21.9 2.2 %collective-permute-done.3 = bf16[3,256,64]{1,2,0:T(8,128)(2,1)S(1)} collective-permute-done((bf16[3,256,64]{1,2,0:T(8,128)(2,1)S(1)}, bf16[3,256,64]{1,2,0:T(8,128)(2,1)S(1)}, u32[]{:S(2)}, u32[]{:S(2)}) %collective-permute-start.3) | collective-permute-done | bytes 98336 | tf_op jit(solution)/shard_map/ppermute | solution.py:19
  24.1 3.4 %collective-permute-done.4 = bf16[3,256,64]{1,2,0:T(8,128)(2,1)S(1)} collective-permute-done((bf16[3,256,64]{1,2,0:T(8,128)(2,1)S(1)}, bf16[3,256,64]{1,2,0:T(8,128)(2,1)S(1)}, u32[]{:S(2)}, u32[]{:S(2)}) %collective-permute-start.4) | collective-permute-done | bytes 98336 | tf_op jit(solution)/shard_map/ppermute | solution.py:19
  27.9 2.6 %collective-permute-start.6 = (bf16[3,256,64]{1,2,0:T(8,128)(2,1)S(1)}, bf16[3,256,64]{1,2,0:T(8,128)(2,1)S(1)}, u32[]{:S(2)}, u32[]{:S(2)}) collective-permute-start(bf16[3,256,64]{1,2,0:T(8,128)(2,1)S(1)} %get-tuple-element.21), channel_id=1, source_target_pairs={{0,4},{4,8},{8,12},{12,0},{1,5},{5,9},{9,13},{13,1},{2,6},{6,10},{... | collective-permute-start | bytes 294920 | tf_op jit(solution)/shard_map/ppermute | solution.py:19
  32.9 2.4 %collective-permute-done.6 = bf16[3,256,64]{1,2,0:T(8,128)(2,1)S(1)} collective-permute-done((bf16[3,256,64]{1,2,0:T(8,128)(2,1)S(1)}, bf16[3,256,64]{1,2,0:T(8,128)(2,1)S(1)}, u32[]{:S(2)}, u32[]{:S(2)}) %collective-permute-start.6) | collective-permute-done | bytes 98336 | tf_op jit(solution)/shard_map/ppermute | solution.py:19
  35.4 3.3 %collective-permute-done.7 = bf16[3,256,64]{1,2,0:T(8,128)(2,1)S(1)} collective-permute-done((bf16[3,256,64]{1,2,0:T(8,128)(2,1)S(1)}, bf16[3,256,64]{1,2,0:T(8,128)(2,1)S(1)}, u32[]{:S(2)}, u32[]{:S(2)}) %collective-permute-start.7) | collective-permute-done | bytes 98336 | tf_op jit(solution)/shard_map/ppermute | solution.py:19
  42.5 3.4 %collective-permute-start.11 = (bf16[3,256,64]{1,2,0:T(8,128)(2,1)S(1)}, bf16[3,256,64]{1,2,0:T(8,128)(2,1)S(1)}, u32[]{:S(2)}, u32[]{:S(2)}) collective-permute-start(bf16[3,256,64]{1,2,0:T(8,128)(2,1)S(1)} %get-tuple-element.39), channel_id=1, source_target_pairs={{0,12},{4,0},{8,4},{12,8},{1,13},{5,1},{9,5},{13,9},{2,14},{6,2},{... | collective-permute-start | bytes 294920 | tf_op jit(solution)/shard_map/ppermute | solution.py:19
  45.9 2.4 %collective-permute-done.10 = bf16[3,256,64]{1,2,0:T(8,128)(2,1)S(1)} collective-permute-done((bf16[3,256,64]{1,2,0:T(8,128)(2,1)S(1)}, bf16[3,256,64]{1,2,0:T(8,128)(2,1)S(1)}, u32[]{:S(2)}, u32[]{:S(2)}) %collective-permute-start.10) | collective-permute-done | bytes 98336 | tf_op jit(solution)/shard_map/ppermute | solution.py:19
  49.0 3.9 %collective-permute-done.9 = bf16[3,256,64]{1,2,0:T(8,128)(2,1)S(1)} collective-permute-done((bf16[3,256,64]{1,2,0:T(8,128)(2,1)S(1)}, bf16[3,256,64]{1,2,0:T(8,128)(2,1)S(1)}, u32[]{:S(2)}, u32[]{:S(2)}) %collective-permute-start.9) | collective-permute-done | bytes 98336 | tf_op jit(solution)/shard_map/ppermute | solution.py:19
  54.7 3.1 %collective-permute-start.14 = (bf16[3,256,64]{1,2,0:T(8,128)(2,1)S(1)}, bf16[3,256,64]{1,2,0:T(8,128)(2,1)S(1)}, u32[]{:S(2)}, u32[]{:S(2)}) collective-permute-start(bf16[3,256,64]{1,2,0:T(8,128)(2,1)S(1)} %multiply_convert_fusion.42), channel_id=1, source_target_pairs={{0,10},{2,8},{4,14},{6,12},{8,2},{10,0},{12,6},{14,4},{1,11},{3,9}... | collective-permute-start | bytes 294920 | tf_op jit(solution)/shard_map/ppermute | solution.py:54
  57.8 2.3 %collective-permute-start.15 = (bf16[3,256,64]{1,2,0:T(8,128)(2,1)S(1)}, bf16[3,256,64]{1,2,0:T(8,128)(2,1)S(1)}, u32[]{:S(2)}, u32[]{:S(2)}) collective-permute-start(bf16[3,256,64]{1,2,0:T(8,128)(2,1)S(1)} %multiply_convert_fusion.42), channel_id=1, source_target_pairs={{0,14},{2,12},{4,2},{6,0},{8,6},{10,4},{12,10},{14,8},{1,15},{3,13... | collective-permute-start | bytes 294920 | tf_op jit(solution)/shard_map/ppermute | solution.py:54
  60.2 2.9 %collective-permute-done.13 = bf16[3,256,64]{1,2,0:T(8,128)(2,1)S(1)} collective-permute-done((bf16[3,256,64]{1,2,0:T(8,128)(2,1)S(1)}, bf16[3,256,64]{1,2,0:T(8,128)(2,1)S(1)}, u32[]{:S(2)}, u32[]{:S(2)}) %collective-permute-start.13) | collective-permute-done | bytes 98336 | tf_op jit(solution)/shard_map/ppermute | solution.py:54
  63.1 2.2 %collective-permute-done.14 = bf16[3,256,64]{1,2,0:T(8,128)(2,1)S(1)} collective-permute-done((bf16[3,256,64]{1,2,0:T(8,128)(2,1)S(1)}, bf16[3,256,64]{1,2,0:T(8,128)(2,1)S(1)}, u32[]{:S(2)}, u32[]{:S(2)}) %collective-permute-start.14) | collective-permute-done | bytes 98336 | tf_op jit(solution)/shard_map/ppermute | solution.py:54
  69.5 2.3 %collective-permute-start.19 = (bf16[3,256,64]{1,2,0:T(8,128)(2,1)S(1)}, bf16[3,256,64]{1,2,0:T(8,128)(2,1)S(1)}, u32[]{:S(2)}, u32[]{:S(2)}) collective-permute-start(bf16[3,256,64]{1,2,0:T(8,128)(2,1)S(1)} %get-tuple-element.37), channel_id=1, source_target_pairs={{0,8},{4,12},{8,0},{12,4},{1,9},{5,13},{9,1},{13,5},{2,10},{6,14},... | collective-permute-start | bytes 294920 | tf_op jit(solution)/shard_map/ppermute | solution.py:19
  72.2 2.7 %collective-permute-done.18 = bf16[3,256,64]{1,2,0:T(8,128)(2,1)S(1)} collective-permute-done((bf16[3,256,64]{1,2,0:T(8,128)(2,1)S(1)}, bf16[3,256,64]{1,2,0:T(8,128)(2,1)S(1)}, u32[]{:S(2)}, u32[]{:S(2)}) %collective-permute-start.18) | collective-permute-done | bytes 98336 | tf_op jit(solution)/shard_map/ppermute | solution.py:19
  74.9 2.7 %collective-permute-done.19 = bf16[3,256,64]{1,2,0:T(8,128)(2,1)S(1)} collective-permute-done((bf16[3,256,64]{1,2,0:T(8,128)(2,1)S(1)}, bf16[3,256,64]{1,2,0:T(8,128)(2,1)S(1)}, u32[]{:S(2)}, u32[]{:S(2)}) %collective-permute-start.19) | collective-permute-done | bytes 98336 | tf_op jit(solution)/shard_map/ppermute | solution.py:19
  82.7 3.0 %collective-permute-done.21 = bf16[3,256,64]{1,2,0:T(8,128)(2,1)S(1)} collective-permute-done((bf16[3,256,64]{1,2,0:T(8,128)(2,1)S(1)}, bf16[3,256,64]{1,2,0:T(8,128)(2,1)S(1)}, u32[]{:S(2)}, u32[]{:S(2)}) %collective-permute-start.21) | collective-permute-done | bytes 98336 | tf_op jit(solution)/shard_map/ppermute | solution.py:19
  85.7 2.7 %collective-permute-done.22 = bf16[3,256,64]{1,2,0:T(8,128)(2,1)S(1)} collective-permute-done((bf16[3,256,64]{1,2,0:T(8,128)(2,1)S(1)}, bf16[3,256,64]{1,2,0:T(8,128)(2,1)S(1)}, u32[]{:S(2)}, u32[]{:S(2)}) %collective-permute-start.22) | collective-permute-done | bytes 98336 | tf_op jit(solution)/shard_map/ppermute | solution.py:19
  90.6 2.5 %collective-permute-start.24 = (bf16[3,256,64]{1,2,0:T(8,128)(2,1)S(1)}, bf16[3,256,64]{1,2,0:T(8,128)(2,1)S(1)}, u32[]{:S(2)}, u32[]{:S(2)}) collective-permute-start(bf16[3,256,64]{1,2,0:T(8,128)(2,1)S(1)} %get-tuple-element.32), channel_id=1, source_target_pairs={{0,4},{4,8},{8,12},{12,0},{1,5},{5,9},{9,13},{13,1},{2,6},{6,10},{... | collective-permute-start | bytes 294920 | tf_op jit(solution)/shard_map/ppermute | solution.py:19
  98.1 3.3 %collective-permute-done.25 = bf16[3,256,64]{1,2,0:T(8,128)(2,1)S(1)} collective-permute-done((bf16[3,256,64]{1,2,0:T(8,128)(2,1)S(1)}, bf16[3,256,64]{1,2,0:T(8,128)(2,1)S(1)}, u32[]{:S(2)}, u32[]{:S(2)}) %collective-permute-start.25) | collective-permute-done | bytes 98336 | tf_op jit(solution)/shard_map/ppermute | solution.py:19
  103.3 6.7 %collective-permute-done.16 = bf16[2,512,256]{2,1,0:T(8,128)(2,1)S(1)} collective-permute-done((bf16[2,512,256]{2,1,0:T(8,128)(2,1)S(1)}, bf16[2,512,256]{2,1,0:T(8,128)(2,1)S(1)}, u32[]{:S(2)}, u32[]{:S(2)}) %collective-permute-start.16) | collective-permute-done | bytes 524320 | tf_op jit(solution)/shard_map/ppermute | solution.py:19
  111.8 2.4 %collective-permute-start.29 = (bf16[3,256,64]{1,2,0:T(8,128)(2,1)S(1)}, bf16[3,256,64]{1,2,0:T(8,128)(2,1)S(1)}, u32[]{:S(2)}, u32[]{:S(2)}) collective-permute-start(bf16[3,256,64]{1,2,0:T(8,128)(2,1)S(1)} %multiply_convert_fusion.41), channel_id=1, source_target_pairs={{0,10},{2,8},{4,14},{6,12},{8,2},{10,0},{12,6},{14,4},{1,11},{3,9}... | collective-permute-start | bytes 294920 | tf_op jit(solution)/shard_map/ppermute | solution.py:54
  118.5 2.3 %collective-permute-done.29 = bf16[3,256,64]{1,2,0:T(8,128)(2,1)S(1)} collective-permute-done((bf16[3,256,64]{1,2,0:T(8,128)(2,1)S(1)}, bf16[3,256,64]{1,2,0:T(8,128)(2,1)S(1)}, u32[]{:S(2)}, u32[]{:S(2)}) %collective-permute-start.29) | collective-permute-done | bytes 98336 | tf_op jit(solution)/shard_map/ppermute | solution.py:54
  127.6 2.3 %convolution_convert_fusion.2 = bf16[512,256]{1,0:T(8,128)(2,1)} fusion(f32[512,256]{1,0:T(8,128)} %convolution_bitcast_fusion.12, bf16[2,512,256]{2,1,0:T(8,128)(2,1)} %copy-done.5, bf16[3,256,256]{1,2,0:T(8,128)(2,1)S(1)} %constant_dynamic-update-slice_fusion.16), kind=kOutput, calls=%fused_computation.20 | convolution fusion | flops 135135232 | bytes 1310720 | tf_op jit(solution)/shard_map/th,hd->td/dot_general | solution.py:85
  139.8 2.3 %collective-permute-done.35 = bf16[3,256,64]{1,2,0:T(8,128)(2,1)S(1)} collective-permute-done((bf16[3,256,64]{1,2,0:T(8,128)(2,1)S(1)}, bf16[3,256,64]{1,2,0:T(8,128)(2,1)S(1)}, u32[]{:S(2)}, u32[]{:S(2)}) %collective-permute-start.35) | collective-permute-done | bytes 98336 | tf_op jit(solution)/shard_map/ppermute | solution.py:19
  142.1 2.6 %collective-permute-done.36 = bf16[3,256,64]{1,2,0:T(8,128)(2,1)S(1)} collective-permute-done((bf16[3,256,64]{1,2,0:T(8,128)(2,1)S(1)}, bf16[3,256,64]{1,2,0:T(8,128)(2,1)S(1)}, u32[]{:S(2)}, u32[]{:S(2)}) %collective-permute-start.36) | collective-permute-done | bytes 98336 | tf_op jit(solution)/shard_map/ppermute | solution.py:19
  153.9 2.7 %collective-permute-done.39 = bf16[3,256,64]{1,2,0:T(8,128)(2,1)S(1)} collective-permute-done((bf16[3,256,64]{1,2,0:T(8,128)(2,1)S(1)}, bf16[3,256,64]{1,2,0:T(8,128)(2,1)S(1)}, u32[]{:S(2)}, u32[]{:S(2)}) %collective-permute-start.39) | collective-permute-done | bytes 98336 | tf_op jit(solution)/shard_map/ppermute | solution.py:19
  157.0 2.7 %collective-permute-start.41 = (bf16[3,256,64]{1,2,0:T(8,128)(2,1)S(1)}, bf16[3,256,64]{1,2,0:T(8,128)(2,1)S(1)}, u32[]{:S(2)}, u32[]{:S(2)}) collective-permute-start(bf16[3,256,64]{1,2,0:T(8,128)(2,1)S(1)} %get-tuple-element.5), channel_id=1, source_target_pairs={{0,4},{4,8},{8,12},{12,0},{1,5},{5,9},{9,13},{13,1},{2,6},{6,10},{... | collective-permute-start | bytes 294920 | tf_op jit(solution)/shard_map/ppermute | solution.py:19
  164.4 3.1 %collective-permute-done.42 = bf16[3,256,64]{1,2,0:T(8,128)(2,1)S(1)} collective-permute-done((bf16[3,256,64]{1,2,0:T(8,128)(2,1)S(1)}, bf16[3,256,64]{1,2,0:T(8,128)(2,1)S(1)}, u32[]{:S(2)}, u32[]{:S(2)}) %collective-permute-start.42) | collective-permute-done | bytes 98336 | tf_op jit(solution)/shard_map/ppermute | solution.py:19
  (185 shorter events, 76.7 us)
Async XLA Ops:
  1.6 8.8 %collective-permute-start = (bf16[3,256,64]{1,2,0:T(8,128)(2,1)S(1)}, bf16[3,256,64]{1,2,0:T(8,128)(2,1)S(1)}, u32[]{:S(2)}, u32[]{:S(2)}) collective-permute-start(bf16[3,256,64]{1,2,0:T(8,128)(2,1)S(1)} %get-tuple-element.25), channel_id=1, source_target_pairs={{0,4},{4,8},{8,12},{12,0},{1,5},{5,9},{9,13},{13,1},{2,6},{6,10},{... | collective-permute-start | bytes 294920 | tf_op jit(solution)/shard_map/ppermute | solution.py:19
  4.7 9.2 %collective-permute-start.1 = (bf16[3,256,64]{1,2,0:T(8,128)(2,1)S(1)}, bf16[3,256,64]{1,2,0:T(8,128)(2,1)S(1)}, u32[]{:S(2)}, u32[]{:S(2)}) collective-permute-start(bf16[3,256,64]{1,2,0:T(8,128)(2,1)S(1)} %get-tuple-element.25), channel_id=1, source_target_pairs={{0,8},{4,12},{8,0},{12,4},{1,9},{5,13},{9,1},{13,5},{2,10},{6,14},... | collective-permute-start | bytes 294920 | tf_op jit(solution)/shard_map/ppermute | solution.py:19
  16.7 7.4 %collective-permute-start.3 = (bf16[3,256,64]{1,2,0:T(8,128)(2,1)S(1)}, bf16[3,256,64]{1,2,0:T(8,128)(2,1)S(1)}, u32[]{:S(2)}, u32[]{:S(2)}) collective-permute-start(bf16[3,256,64]{1,2,0:T(8,128)(2,1)S(1)} %get-tuple-element.41), channel_id=1, source_target_pairs={{0,4},{4,8},{8,12},{12,0},{1,5},{5,9},{9,13},{13,1},{2,6},{6,10},{... | collective-permute-start | bytes 294920 | tf_op jit(solution)/shard_map/ppermute | solution.py:19
  19.3 8.2 %collective-permute-start.4 = (bf16[3,256,64]{1,2,0:T(8,128)(2,1)S(1)}, bf16[3,256,64]{1,2,0:T(8,128)(2,1)S(1)}, u32[]{:S(2)}, u32[]{:S(2)}) collective-permute-start(bf16[3,256,64]{1,2,0:T(8,128)(2,1)S(1)} %get-tuple-element.43), channel_id=1, source_target_pairs={{0,8},{4,12},{8,0},{12,4},{1,9},{5,13},{9,1},{13,5},{2,10},{6,14},... | collective-permute-start | bytes 294920 | tf_op jit(solution)/shard_map/ppermute | solution.py:19
  27.9 7.4 %collective-permute-start.6 = (bf16[3,256,64]{1,2,0:T(8,128)(2,1)S(1)}, bf16[3,256,64]{1,2,0:T(8,128)(2,1)S(1)}, u32[]{:S(2)}, u32[]{:S(2)}) collective-permute-start(bf16[3,256,64]{1,2,0:T(8,128)(2,1)S(1)} %get-tuple-element.21), channel_id=1, source_target_pairs={{0,4},{4,8},{8,12},{12,0},{1,5},{5,9},{9,13},{13,1},{2,6},{6,10},{... | collective-permute-start | bytes 294920 | tf_op jit(solution)/shard_map/ppermute | solution.py:19
  30.5 8.2 %collective-permute-start.7 = (bf16[3,256,64]{1,2,0:T(8,128)(2,1)S(1)}, bf16[3,256,64]{1,2,0:T(8,128)(2,1)S(1)}, u32[]{:S(2)}, u32[]{:S(2)}) collective-permute-start(bf16[3,256,64]{1,2,0:T(8,128)(2,1)S(1)} %get-tuple-element.21), channel_id=1, source_target_pairs={{0,8},{4,12},{8,0},{12,4},{1,9},{5,13},{9,1},{13,5},{2,10},{6,14},... | collective-permute-start | bytes 294920 | tf_op jit(solution)/shard_map/ppermute | solution.py:19
  40.9 7.3 %collective-permute-start.10 = (bf16[3,256,64]{1,2,0:T(8,128)(2,1)S(1)}, bf16[3,256,64]{1,2,0:T(8,128)(2,1)S(1)}, u32[]{:S(2)}, u32[]{:S(2)}) collective-permute-start(bf16[3,256,64]{1,2,0:T(8,128)(2,1)S(1)} %get-tuple-element.40), channel_id=1, source_target_pairs={{0,8},{4,12},{8,0},{12,4},{1,9},{5,13},{9,1},{13,5},{2,10},{6,14},... | collective-permute-start | bytes 294920 | tf_op jit(solution)/shard_map/ppermute | solution.py:19
  45.8 7.0 %collective-permute-start.9 = (bf16[3,256,64]{1,2,0:T(8,128)(2,1)S(1)}, bf16[3,256,64]{1,2,0:T(8,128)(2,1)S(1)}, u32[]{:S(2)}, u32[]{:S(2)}) collective-permute-start(bf16[3,256,64]{1,2,0:T(8,128)(2,1)S(1)} %get-tuple-element.38), channel_id=1, source_target_pairs={{0,4},{4,8},{8,12},{12,0},{1,5},{5,9},{9,13},{13,1},{2,6},{6,10},{... | collective-permute-start | bytes 294920 | tf_op jit(solution)/shard_map/ppermute | solution.py:19
  53.2 7.0 %collective-permute-start.12 = (bf16[3,256,64]{1,2,0:T(8,128)(2,1)S(1)}, bf16[3,256,64]{1,2,0:T(8,128)(2,1)S(1)}, u32[]{:S(2)}, u32[]{:S(2)}) collective-permute-start(bf16[3,256,64]{1,2,0:T(8,128)(2,1)S(1)} %multiply_convert_fusion.42), channel_id=1, source_target_pairs={{0,2},{2,0},{4,6},{6,4},{8,10},{10,8},{12,14},{14,12},{1,3},{3,1},... | collective-permute-start | bytes 294920 | tf_op jit(solution)/shard_map/ppermute | solution.py:54
  54.7 8.4 %collective-permute-start.13 = (bf16[3,256,64]{1,2,0:T(8,128)(2,1)S(1)}, bf16[3,256,64]{1,2,0:T(8,128)(2,1)S(1)}, u32[]{:S(2)}, u32[]{:S(2)}) collective-permute-start(bf16[3,256,64]{1,2,0:T(8,128)(2,1)S(1)} %multiply_convert_fusion.42), channel_id=1, source_target_pairs={{0,6},{2,4},{4,10},{6,8},{8,14},{10,12},{12,2},{14,0},{1,7},{3,5},... | collective-permute-start | bytes 294920 | tf_op jit(solution)/shard_map/ppermute | solution.py:54
  54.7 10.6 %collective-permute-start.14 = (bf16[3,256,64]{1,2,0:T(8,128)(2,1)S(1)}, bf16[3,256,64]{1,2,0:T(8,128)(2,1)S(1)}, u32[]{:S(2)}, u32[]{:S(2)}) collective-permute-start(bf16[3,256,64]{1,2,0:T(8,128)(2,1)S(1)} %multiply_convert_fusion.42), channel_id=1, source_target_pairs={{0,10},{2,8},{4,14},{6,12},{8,2},{10,0},{12,6},{14,4},{1,11},{3,9}... | collective-permute-start | bytes 294920 | tf_op jit(solution)/shard_map/ppermute | solution.py:54
  57.8 7.6 %collective-permute-start.15 = (bf16[3,256,64]{1,2,0:T(8,128)(2,1)S(1)}, bf16[3,256,64]{1,2,0:T(8,128)(2,1)S(1)}, u32[]{:S(2)}, u32[]{:S(2)}) collective-permute-start(bf16[3,256,64]{1,2,0:T(8,128)(2,1)S(1)} %multiply_convert_fusion.42), channel_id=1, source_target_pairs={{0,14},{2,12},{4,2},{6,0},{8,6},{10,4},{12,10},{14,8},{1,15},{3,13... | collective-permute-start | bytes 294920 | tf_op jit(solution)/shard_map/ppermute | solution.py:54
  67.6 7.3 %collective-permute-start.18 = (bf16[3,256,64]{1,2,0:T(8,128)(2,1)S(1)}, bf16[3,256,64]{1,2,0:T(8,128)(2,1)S(1)}, u32[]{:S(2)}, u32[]{:S(2)}) collective-permute-start(bf16[3,256,64]{1,2,0:T(8,128)(2,1)S(1)} %get-tuple-element.35), channel_id=1, source_target_pairs={{0,4},{4,8},{8,12},{12,0},{1,5},{5,9},{9,13},{13,1},{2,6},{6,10},{... | collective-permute-start | bytes 294920 | tf_op jit(solution)/shard_map/ppermute | solution.py:19
  69.5 8.1 %collective-permute-start.19 = (bf16[3,256,64]{1,2,0:T(8,128)(2,1)S(1)}, bf16[3,256,64]{1,2,0:T(8,128)(2,1)S(1)}, u32[]{:S(2)}, u32[]{:S(2)}) collective-permute-start(bf16[3,256,64]{1,2,0:T(8,128)(2,1)S(1)} %get-tuple-element.37), channel_id=1, source_target_pairs={{0,8},{4,12},{8,0},{12,4},{1,9},{5,13},{9,1},{13,5},{2,10},{6,14},... | collective-permute-start | bytes 294920 | tf_op jit(solution)/shard_map/ppermute | solution.py:19
  78.2 7.5 %collective-permute-start.21 = (bf16[3,256,64]{1,2,0:T(8,128)(2,1)S(1)}, bf16[3,256,64]{1,2,0:T(8,128)(2,1)S(1)}, u32[]{:S(2)}, u32[]{:S(2)}) collective-permute-start(bf16[3,256,64]{1,2,0:T(8,128)(2,1)S(1)} %get-tuple-element.15), channel_id=1, source_target_pairs={{0,4},{4,8},{8,12},{12,0},{1,5},{5,9},{9,13},{13,1},{2,6},{6,10},{... | collective-permute-start | bytes 294920 | tf_op jit(solution)/shard_map/ppermute | solution.py:19
  80.3 8.1 %collective-permute-start.22 = (bf16[3,256,64]{1,2,0:T(8,128)(2,1)S(1)}, bf16[3,256,64]{1,2,0:T(8,128)(2,1)S(1)}, u32[]{:S(2)}, u32[]{:S(2)}) collective-permute-start(bf16[3,256,64]{1,2,0:T(8,128)(2,1)S(1)} %get-tuple-element.15), channel_id=1, source_target_pairs={{0,8},{4,12},{8,0},{12,4},{1,9},{5,13},{9,1},{13,5},{2,10},{6,14},... | collective-permute-start | bytes 294920 | tf_op jit(solution)/shard_map/ppermute | solution.py:19
  90.6 7.5 %collective-permute-start.24 = (bf16[3,256,64]{1,2,0:T(8,128)(2,1)S(1)}, bf16[3,256,64]{1,2,0:T(8,128)(2,1)S(1)}, u32[]{:S(2)}, u32[]{:S(2)}) collective-permute-start(bf16[3,256,64]{1,2,0:T(8,128)(2,1)S(1)} %get-tuple-element.32), channel_id=1, source_target_pairs={{0,4},{4,8},{8,12},{12,0},{1,5},{5,9},{9,13},{13,1},{2,6},{6,10},{... | collective-permute-start | bytes 294920 | tf_op jit(solution)/shard_map/ppermute | solution.py:19
  93.1 8.2 %collective-permute-start.25 = (bf16[3,256,64]{1,2,0:T(8,128)(2,1)S(1)}, bf16[3,256,64]{1,2,0:T(8,128)(2,1)S(1)}, u32[]{:S(2)}, u32[]{:S(2)}) collective-permute-start(bf16[3,256,64]{1,2,0:T(8,128)(2,1)S(1)} %get-tuple-element.34), channel_id=1, source_target_pairs={{0,8},{4,12},{8,0},{12,4},{1,9},{5,13},{9,1},{13,5},{2,10},{6,14},... | collective-permute-start | bytes 294920 | tf_op jit(solution)/shard_map/ppermute | solution.py:19
  95.6 14.4 %collective-permute-start.16 = (bf16[2,512,256]{2,1,0:T(8,128)(2,1)S(1)}, bf16[2,512,256]{2,1,0:T(8,128)(2,1)S(1)}, u32[]{:S(2)}, u32[]{:S(2)}) collective-permute-start(bf16[2,512,256]{2,1,0:T(8,128)(2,1)S(1)} %slice_bitcast_fusion), channel_id=1, source_target_pairs={{0,2},{2,0},{1,3},{3,1},{4,6},{6,4},{5,7},{7,5},{8,10},{10,8},{9,1... | collective-permute-start | bytes 1572872 | tf_op jit(solution)/shard_map/ppermute | solution.py:19
  101.7 14.6 %collective-permute-start.27 = (bf16[3,256,64]{1,2,0:T(8,128)(2,1)S(1)}, bf16[3,256,64]{1,2,0:T(8,128)(2,1)S(1)}, u32[]{:S(2)}, u32[]{:S(2)}) collective-permute-start(bf16[3,256,64]{1,2,0:T(8,128)(2,1)S(1)} %multiply_convert_fusion.41), channel_id=1, source_target_pairs={{0,2},{2,0},{4,6},{6,4},{8,10},{10,8},{12,14},{14,12},{1,3},{3,1},... | collective-permute-start | bytes 294920 | tf_op jit(solution)/shard_map/ppermute | solution.py:54
  111.0 7.4 %collective-permute-start.28 = (bf16[3,256,64]{1,2,0:T(8,128)(2,1)S(1)}, bf16[3,256,64]{1,2,0:T(8,128)(2,1)S(1)}, u32[]{:S(2)}, u32[]{:S(2)}) collective-permute-start(bf16[3,256,64]{1,2,0:T(8,128)(2,1)S(1)} %multiply_convert_fusion.41), channel_id=1, source_target_pairs={{0,6},{2,4},{4,10},{6,8},{8,14},{10,12},{12,2},{14,0},{1,7},{3,5},... | collective-permute-start | bytes 294920 | tf_op jit(solution)/shard_map/ppermute | solution.py:54
  111.8 9.0 %collective-permute-start.29 = (bf16[3,256,64]{1,2,0:T(8,128)(2,1)S(1)}, bf16[3,256,64]{1,2,0:T(8,128)(2,1)S(1)}, u32[]{:S(2)}, u32[]{:S(2)}) collective-permute-start(bf16[3,256,64]{1,2,0:T(8,128)(2,1)S(1)} %multiply_convert_fusion.41), channel_id=1, source_target_pairs={{0,10},{2,8},{4,14},{6,12},{8,2},{10,0},{12,6},{14,4},{1,11},{3,9}... | collective-permute-start | bytes 294920 | tf_op jit(solution)/shard_map/ppermute | solution.py:54
  123.7 7.4 %collective-permute-start.32 = (bf16[3,256,64]{1,2,0:T(8,128)(2,1)}, bf16[3,256,64]{1,2,0:T(8,128)(2,1)S(1)}, u32[]{:S(2)}, u32[]{:S(2)}) collective-permute-start(bf16[3,256,64]{1,2,0:T(8,128)(2,1)} %get-tuple-element.29), channel_id=1, source_target_pairs={{0,4},{4,8},{8,12},{12,0},{1,5},{5,9},{9,13},{13,1},{2,6},{6,10},{... | collective-permute-start | bytes 294920 | tf_op jit(solution)/shard_map/ppermute | solution.py:19
  125.2 8.1 %collective-permute-start.33 = (bf16[3,256,64]{1,2,0:T(8,128)(2,1)S(1)}, bf16[3,256,64]{1,2,0:T(8,128)(2,1)S(1)}, u32[]{:S(2)}, u32[]{:S(2)}) collective-permute-start(bf16[3,256,64]{1,2,0:T(8,128)(2,1)S(1)} %get-tuple-element.31), channel_id=1, source_target_pairs={{0,8},{4,12},{8,0},{12,4},{1,9},{5,13},{9,1},{13,5},{2,10},{6,14},... | collective-permute-start | bytes 294920 | tf_op jit(solution)/shard_map/ppermute | solution.py:19
  129.9 38.3 %collective-permute-start.17 = (bf16[512,256]{1,0:T(8,128)(2,1)}, bf16[512,256]{1,0:T(8,128)(2,1)}, u32[]{:S(2)}, u32[]{:S(2)}) collective-permute-start(bf16[512,256]{1,0:T(8,128)(2,1)} %convolution_convert_fusion.2), channel_id=1, source_target_pairs={{0,2},{2,0},{1,3},{3,1},{4,6},{6,4},{5,7},{7,5},{8,10},{10,8},{9,1... | collective-permute-start | bytes 786440 | tf_op jit(solution)/shard_map/ppermute | solution.py:19
  134.6 7.5 %collective-permute-start.35 = (bf16[3,256,64]{1,2,0:T(8,128)(2,1)S(1)}, bf16[3,256,64]{1,2,0:T(8,128)(2,1)S(1)}, u32[]{:S(2)}, u32[]{:S(2)}) collective-permute-start(bf16[3,256,64]{1,2,0:T(8,128)(2,1)S(1)} %get-tuple-element.9), channel_id=1, source_target_pairs={{0,4},{4,8},{8,12},{12,0},{1,5},{5,9},{9,13},{13,1},{2,6},{6,10},{... | collective-permute-start | bytes 294920 | tf_op jit(solution)/shard_map/ppermute | solution.py:19
  136.6 8.1 %collective-permute-start.36 = (bf16[3,256,64]{1,2,0:T(8,128)(2,1)S(1)}, bf16[3,256,64]{1,2,0:T(8,128)(2,1)S(1)}, u32[]{:S(2)}, u32[]{:S(2)}) collective-permute-start(bf16[3,256,64]{1,2,0:T(8,128)(2,1)S(1)} %get-tuple-element.9), channel_id=1, source_target_pairs={{0,8},{4,12},{8,0},{12,4},{1,9},{5,13},{9,1},{13,5},{2,10},{6,14},... | collective-permute-start | bytes 294920 | tf_op jit(solution)/shard_map/ppermute | solution.py:19
  146.9 7.0 %collective-permute-start.38 = (bf16[3,256,64]{1,2,0:T(8,128)(2,1)S(1)}, bf16[3,256,64]{1,2,0:T(8,128)(2,1)S(1)}, u32[]{:S(2)}, u32[]{:S(2)}) collective-permute-start(bf16[3,256,64]{1,2,0:T(8,128)(2,1)S(1)} %get-tuple-element.26), channel_id=1, source_target_pairs={{0,4},{4,8},{8,12},{12,0},{1,5},{5,9},{9,13},{13,1},{2,6},{6,10},{... | collective-permute-start | bytes 294920 | tf_op jit(solution)/shard_map/ppermute | solution.py:19
  148.6 8.0 %collective-permute-start.39 = (bf16[3,256,64]{1,2,0:T(8,128)(2,1)S(1)}, bf16[3,256,64]{1,2,0:T(8,128)(2,1)S(1)}, u32[]{:S(2)}, u32[]{:S(2)}) collective-permute-start(bf16[3,256,64]{1,2,0:T(8,128)(2,1)S(1)} %get-tuple-element.28), channel_id=1, source_target_pairs={{0,8},{4,12},{8,0},{12,4},{1,9},{5,13},{9,1},{13,5},{2,10},{6,14},... | collective-permute-start | bytes 294920 | tf_op jit(solution)/shard_map/ppermute | solution.py:19
  151.5 16.8 %collective-permute-start.31 = (bf16[512,256]{1,0:T(8,128)(2,1)S(1)}, bf16[512,256]{1,0:T(8,128)(2,1)S(1)}, u32[]{:S(2)}, u32[]{:S(2)}) collective-permute-start(bf16[512,256]{1,0:T(8,128)(2,1)S(1)} %convolution_convert_fusion.1), channel_id=1, source_target_pairs={{0,2},{2,0},{1,3},{3,1},{4,6},{6,4},{5,7},{7,5},{8,10},{10,8},{9,1... | collective-permute-start | bytes 786440 | tf_op jit(solution)/shard_map/ppermute | solution.py:19
  157.0 7.3 %collective-permute-start.41 = (bf16[3,256,64]{1,2,0:T(8,128)(2,1)S(1)}, bf16[3,256,64]{1,2,0:T(8,128)(2,1)S(1)}, u32[]{:S(2)}, u32[]{:S(2)}) collective-permute-start(bf16[3,256,64]{1,2,0:T(8,128)(2,1)S(1)} %get-tuple-element.5), channel_id=1, source_target_pairs={{0,4},{4,8},{8,12},{12,0},{1,5},{5,9},{9,13},{13,1},{2,6},{6,10},{... | collective-permute-start | bytes 294920 | tf_op jit(solution)/shard_map/ppermute | solution.py:19
  160.5 7.0 %collective-permute-start.42 = (bf16[3,256,64]{1,2,0:T(8,128)(2,1)S(1)}, bf16[3,256,64]{1,2,0:T(8,128)(2,1)S(1)}, u32[]{:S(2)}, u32[]{:S(2)}) collective-permute-start(bf16[3,256,64]{1,2,0:T(8,128)(2,1)S(1)} %get-tuple-element.5), channel_id=1, source_target_pairs={{0,8},{4,12},{8,0},{12,4},{1,9},{5,13},{9,1},{13,5},{2,10},{6,14},... | collective-permute-start | bytes 294920 | tf_op jit(solution)/shard_map/ppermute | solution.py:19
  (21 other events, 125.5 us)

commit v8 on v7

--- a/solution.py
+++ b/solution.py
@@ -5,13 +5,8 @@
 from jax import lax
 from jax.sharding import PartitionSpec as P
 
+
 ITERS = 2
-
-
-def shifted(value, axis, by):
-    devices = lax.axis_size(axis)
-    pairs = [(i, i + by) for i in range(devices) if 0 <= i + by < devices]
-    return lax.ppermute(value, axis, pairs)
 
 
 def rotated(value, axis, by):
@@ -87,7 +82,7 @@
     ).astype(jnp.bfloat16)
 
 
-def on_device(key_rows, value_rows, query_rows, step_rates, states_in, init_weights):
+def section_chain(key_rows, value_rows, query_rows, step_rates, states_in, init_weights):
     tok_count = lax.axis_size("tok")
     feature_width = init_weights.shape[-1]
     part_cols = feature_width // tok_count
@@ -118,7 +113,8 @@
         for update_step in range(ITERS):
             if update_step > 0:
                 fast = gather_cols(weights.astype(jnp.bfloat16), part_cols)
-            summed = scatter_sum(fast_grads(fast, key_block, scaled), part_cols)
+            partial = fast_grads(fast, key_block, scaled)
+            summed = scatter_sum(partial, part_cols)
             weights = renormalize(weights + summed, own_norms)
         own = weights.astype(jnp.bfloat16)
         if tick_number + 1 < tick_count:
@@ -142,7 +138,7 @@
         P("head", None, None, None),
     )
     return jax.shard_map(
-        on_device,
+        section_chain,
         mesh=mesh,
         in_specs=placed,
         out_specs=(

time: 170 us -> 170 us (level)
  no operation moved by 1% of the time
where the time goes in v8:
time: 170 us
  starting transfers between devices  71.8 us (42%)
  waiting for transfers between devices  70.8 us (42%)
  matrix products  16.8 us (10%)
  other arithmetic  6.22 us (4%)
  local copies, waits for them, and re-layouts  3.02 us (2%)
    ppermute x36, waiting for transfers between devices, rotated(): lax.ppermute(value, axis, [(i, (i + by) % devices) for i in range(devices)])  61.3 us
    ppermute x36, starting transfers between devices, rotated(): lax.ppermute(value, axis, [(i, (i + by) % devices) for i in range(devices)])  57.9 us
    ppermute x8, starting transfers between devices, cross_gather(): got = lax.ppermute(own, ('tok', 'span'), pairs)  13.8 us
    ppermute x8, waiting for transfers between devices, cross_gather(): got = lax.ppermute(own, ('tok', 'span'), pairs)  9.53 us
  transfers between devices with their start and end apart: 44, of which 28 were waited for; matrix products, arithmetic and copies ran while one was open for 6% of the time, Pallas kernels for 0%

profile of v8, /device:TPU:0, one launch (start us, length us, event | category | flops | bytes accessed | tf_op | source)
XLA Modules:
  0.0 170.2 jit_solution(14333771598086443877)
XLA Ops:
  1.6 3.1 %collective-permute-start = (bf16[3,256,64]{1,2,0:T(8,128)(2,1)S(1)}, bf16[3,256,64]{1,2,0:T(8,128)(2,1)S(1)}, u32[]{:S(2)}, u32[]{:S(2)}) collective-permute-start(bf16[3,256,64]{1,2,0:T(8,128)(2,1)S(1)} %get-tuple-element.25), channel_id=1, source_target_pairs={{0,4},{4,8},{8,12},{12,0},{1,5},{5,9},{9,13},{13,1},{2,6},{6,10},{... | collective-permute-start | bytes 294920 | tf_op jit(solution)/shard_map/ppermute | solution.py:14
  4.7 2.6 %collective-permute-start.1 = (bf16[3,256,64]{1,2,0:T(8,128)(2,1)S(1)}, bf16[3,256,64]{1,2,0:T(8,128)(2,1)S(1)}, u32[]{:S(2)}, u32[]{:S(2)}) collective-permute-start(bf16[3,256,64]{1,2,0:T(8,128)(2,1)S(1)} %get-tuple-element.25), channel_id=1, source_target_pairs={{0,8},{4,12},{8,0},{12,4},{1,9},{5,13},{9,1},{13,5},{2,10},{6,14},... | collective-permute-start | bytes 294920 | tf_op jit(solution)/shard_map/ppermute | solution.py:14
  10.4 3.5 %collective-permute-done.1 = bf16[3,256,64]{1,2,0:T(8,128)(2,1)S(1)} collective-permute-done((bf16[3,256,64]{1,2,0:T(8,128)(2,1)S(1)}, bf16[3,256,64]{1,2,0:T(8,128)(2,1)S(1)}, u32[]{:S(2)}, u32[]{:S(2)}) %collective-permute-start.1) | collective-permute-done | bytes 98336 | tf_op jit(solution)/shard_map/ppermute | solution.py:14
  16.7 2.6 %collective-permute-start.3 = (bf16[3,256,64]{1,2,0:T(8,128)(2,1)S(1)}, bf16[3,256,64]{1,2,0:T(8,128)(2,1)S(1)}, u32[]{:S(2)}, u32[]{:S(2)}) collective-permute-start(bf16[3,256,64]{1,2,0:T(8,128)(2,1)S(1)} %get-tuple-element.41), channel_id=1, source_target_pairs={{0,4},{4,8},{8,12},{12,0},{1,5},{5,9},{9,13},{13,1},{2,6},{6,10},{... | collective-permute-start | bytes 294920 | tf_op jit(solution)/shard_map/ppermute | solution.py:14
  21.9 2.2 %collective-permute-done.3 = bf16[3,256,64]{1,2,0:T(8,128)(2,1)S(1)} collective-permute-done((bf16[3,256,64]{1,2,0:T(8,128)(2,1)S(1)}, bf16[3,256,64]{1,2,0:T(8,128)(2,1)S(1)}, u32[]{:S(2)}, u32[]{:S(2)}) %collective-permute-start.3) | collective-permute-done | bytes 98336 | tf_op jit(solution)/shard_map/ppermute | solution.py:14
  24.1 3.4 %collective-permute-done.4 = bf16[3,256,64]{1,2,0:T(8,128)(2,1)S(1)} collective-permute-done((bf16[3,256,64]{1,2,0:T(8,128)(2,1)S(1)}, bf16[3,256,64]{1,2,0:T(8,128)(2,1)S(1)}, u32[]{:S(2)}, u32[]{:S(2)}) %collective-permute-start.4) | collective-permute-done | bytes 98336 | tf_op jit(solution)/shard_map/ppermute | solution.py:14
  27.9 2.6 %collective-permute-start.6 = (bf16[3,256,64]{1,2,0:T(8,128)(2,1)S(1)}, bf16[3,256,64]{1,2,0:T(8,128)(2,1)S(1)}, u32[]{:S(2)}, u32[]{:S(2)}) collective-permute-start(bf16[3,256,64]{1,2,0:T(8,128)(2,1)S(1)} %get-tuple-element.21), channel_id=1, source_target_pairs={{0,4},{4,8},{8,12},{12,0},{1,5},{5,9},{9,13},{13,1},{2,6},{6,10},{... | collective-permute-start | bytes 294920 | tf_op jit(solution)/shard_map/ppermute | solution.py:14
  32.9 2.4 %collective-permute-done.6 = bf16[3,256,64]{1,2,0:T(8,128)(2,1)S(1)} collective-permute-done((bf16[3,256,64]{1,2,0:T(8,128)(2,1)S(1)}, bf16[3,256,64]{1,2,0:T(8,128)(2,1)S(1)}, u32[]{:S(2)}, u32[]{:S(2)}) %collective-permute-start.6) | collective-permute-done | bytes 98336 | tf_op jit(solution)/shard_map/ppermute | solution.py:14
  35.4 3.3 %collective-permute-done.7 = bf16[3,256,64]{1,2,0:T(8,128)(2,1)S(1)} collective-permute-done((bf16[3,256,64]{1,2,0:T(8,128)(2,1)S(1)}, bf16[3,256,64]{1,2,0:T(8,128)(2,1)S(1)}, u32[]{:S(2)}, u32[]{:S(2)}) %collective-permute-start.7) | collective-permute-done | bytes 98336 | tf_op jit(solution)/shard_map/ppermute | solution.py:14
  42.5 3.4 %collective-permute-start.11 = (bf16[3,256,64]{1,2,0:T(8,128)(2,1)S(1)}, bf16[3,256,64]{1,2,0:T(8,128)(2,1)S(1)}, u32[]{:S(2)}, u32[]{:S(2)}) collective-permute-start(bf16[3,256,64]{1,2,0:T(8,128)(2,1)S(1)} %get-tuple-element.39), channel_id=1, source_target_pairs={{0,12},{4,0},{8,4},{12,8},{1,13},{5,1},{9,5},{13,9},{2,14},{6,2},{... | collective-permute-start | bytes 294920 | tf_op jit(solution)/shard_map/ppermute | solution.py:14
  45.9 2.4 %collective-permute-done.10 = bf16[3,256,64]{1,2,0:T(8,128)(2,1)S(1)} collective-permute-done((bf16[3,256,64]{1,2,0:T(8,128)(2,1)S(1)}, bf16[3,256,64]{1,2,0:T(8,128)(2,1)S(1)}, u32[]{:S(2)}, u32[]{:S(2)}) %collective-permute-start.10) | collective-permute-done | bytes 98336 | tf_op jit(solution)/shard_map/ppermute | solution.py:14
  49.0 3.9 %collective-permute-done.9 = bf16[3,256,64]{1,2,0:T(8,128)(2,1)S(1)} collective-permute-done((bf16[3,256,64]{1,2,0:T(8,128)(2,1)S(1)}, bf16[3,256,64]{1,2,0:T(8,128)(2,1)S(1)}, u32[]{:S(2)}, u32[]{:S(2)}) %collective-permute-start.9) | collective-permute-done | bytes 98336 | tf_op jit(solution)/shard_map/ppermute | solution.py:14
  54.7 3.1 %collective-permute-start.14 = (bf16[3,256,64]{1,2,0:T(8,128)(2,1)S(1)}, bf16[3,256,64]{1,2,0:T(8,128)(2,1)S(1)}, u32[]{:S(2)}, u32[]{:S(2)}) collective-permute-start(bf16[3,256,64]{1,2,0:T(8,128)(2,1)S(1)} %multiply_convert_fusion.42), channel_id=1, source_target_pairs={{0,10},{2,8},{4,14},{6,12},{8,2},{10,0},{12,6},{14,4},{1,11},{3,9}... | collective-permute-start | bytes 294920 | tf_op jit(solution)/shard_map/ppermute | solution.py:49
  57.8 2.3 %collective-permute-start.15 = (bf16[3,256,64]{1,2,0:T(8,128)(2,1)S(1)}, bf16[3,256,64]{1,2,0:T(8,128)(2,1)S(1)}, u32[]{:S(2)}, u32[]{:S(2)}) collective-permute-start(bf16[3,256,64]{1,2,0:T(8,128)(2,1)S(1)} %multiply_convert_fusion.42), channel_id=1, source_target_pairs={{0,14},{2,12},{4,2},{6,0},{8,6},{10,4},{12,10},{14,8},{1,15},{3,13... | collective-permute-start | bytes 294920 | tf_op jit(solution)/shard_map/ppermute | solution.py:49
  60.2 2.9 %collective-permute-done.13 = bf16[3,256,64]{1,2,0:T(8,128)(2,1)S(1)} collective-permute-done((bf16[3,256,64]{1,2,0:T(8,128)(2,1)S(1)}, bf16[3,256,64]{1,2,0:T(8,128)(2,1)S(1)}, u32[]{:S(2)}, u32[]{:S(2)}) %collective-permute-start.13) | collective-permute-done | bytes 98336 | tf_op jit(solution)/shard_map/ppermute | solution.py:49
  63.1 2.2 %collective-permute-done.14 = bf16[3,256,64]{1,2,0:T(8,128)(2,1)S(1)} collective-permute-done((bf16[3,256,64]{1,2,0:T(8,128)(2,1)S(1)}, bf16[3,256,64]{1,2,0:T(8,128)(2,1)S(1)}, u32[]{:S(2)}, u32[]{:S(2)}) %collective-permute-start.14) | collective-permute-done | bytes 98336 | tf_op jit(solution)/shard_map/ppermute | solution.py:49
  69.5 2.3 %collective-permute-start.19 = (bf16[3,256,64]{1,2,0:T(8,128)(2,1)S(1)}, bf16[3,256,64]{1,2,0:T(8,128)(2,1)S(1)}, u32[]{:S(2)}, u32[]{:S(2)}) collective-permute-start(bf16[3,256,64]{1,2,0:T(8,128)(2,1)S(1)} %get-tuple-element.37), channel_id=1, source_target_pairs={{0,8},{4,12},{8,0},{12,4},{1,9},{5,13},{9,1},{13,5},{2,10},{6,14},... | collective-permute-start | bytes 294920 | tf_op jit(solution)/shard_map/ppermute | solution.py:14
  72.2 2.7 %collective-permute-done.18 = bf16[3,256,64]{1,2,0:T(8,128)(2,1)S(1)} collective-permute-done((bf16[3,256,64]{1,2,0:T(8,128)(2,1)S(1)}, bf16[3,256,64]{1,2,0:T(8,128)(2,1)S(1)}, u32[]{:S(2)}, u32[]{:S(2)}) %collective-permute-start.18) | collective-permute-done | bytes 98336 | tf_op jit(solution)/shard_map/ppermute | solution.py:14
  74.9 2.7 %collective-permute-done.19 = bf16[3,256,64]{1,2,0:T(8,128)(2,1)S(1)} collective-permute-done((bf16[3,256,64]{1,2,0:T(8,128)(2,1)S(1)}, bf16[3,256,64]{1,2,0:T(8,128)(2,1)S(1)}, u32[]{:S(2)}, u32[]{:S(2)}) %collective-permute-start.19) | collective-permute-done | bytes 98336 | tf_op jit(solution)/shard_map/ppermute | solution.py:14
  82.7 3.0 %collective-permute-done.21 = bf16[3,256,64]{1,2,0:T(8,128)(2,1)S(1)} collective-permute-done((bf16[3,256,64]{1,2,0:T(8,128)(2,1)S(1)}, bf16[3,256,64]{1,2,0:T(8,128)(2,1)S(1)}, u32[]{:S(2)}, u32[]{:S(2)}) %collective-permute-start.21) | collective-permute-done | bytes 98336 | tf_op jit(solution)/shard_map/ppermute | solution.py:14
  85.7 2.7 %collective-permute-done.22 = bf16[3,256,64]{1,2,0:T(8,128)(2,1)S(1)} collective-permute-done((bf16[3,256,64]{1,2,0:T(8,128)(2,1)S(1)}, bf16[3,256,64]{1,2,0:T(8,128)(2,1)S(1)}, u32[]{:S(2)}, u32[]{:S(2)}) %collective-permute-start.22) | collective-permute-done | bytes 98336 | tf_op jit(solution)/shard_map/ppermute | solution.py:14
  90.6 2.5 %collective-permute-start.24 = (bf16[3,256,64]{1,2,0:T(8,128)(2,1)S(1)}, bf16[3,256,64]{1,2,0:T(8,128)(2,1)S(1)}, u32[]{:S(2)}, u32[]{:S(2)}) collective-permute-start(bf16[3,256,64]{1,2,0:T(8,128)(2,1)S(1)} %get-tuple-element.32), channel_id=1, source_target_pairs={{0,4},{4,8},{8,12},{12,0},{1,5},{5,9},{9,13},{13,1},{2,6},{6,10},{... | collective-permute-start | bytes 294920 | tf_op jit(solution)/shard_map/ppermute | solution.py:14
  98.1 3.3 %collective-permute-done.25 = bf16[3,256,64]{1,2,0:T(8,128)(2,1)S(1)} collective-permute-done((bf16[3,256,64]{1,2,0:T(8,128)(2,1)S(1)}, bf16[3,256,64]{1,2,0:T(8,128)(2,1)S(1)}, u32[]{:S(2)}, u32[]{:S(2)}) %collective-permute-start.25) | collective-permute-done | bytes 98336 | tf_op jit(solution)/shard_map/ppermute | solution.py:14
  103.3 6.7 %collective-permute-done.16 = bf16[2,512,256]{2,1,0:T(8,128)(2,1)S(1)} collective-permute-done((bf16[2,512,256]{2,1,0:T(8,128)(2,1)S(1)}, bf16[2,512,256]{2,1,0:T(8,128)(2,1)S(1)}, u32[]{:S(2)}, u32[]{:S(2)}) %collective-permute-start.16) | collective-permute-done | bytes 524320 | tf_op jit(solution)/shard_map/ppermute | solution.py:14
  111.8 2.4 %collective-permute-start.29 = (bf16[3,256,64]{1,2,0:T(8,128)(2,1)S(1)}, bf16[3,256,64]{1,2,0:T(8,128)(2,1)S(1)}, u32[]{:S(2)}, u32[]{:S(2)}) collective-permute-start(bf16[3,256,64]{1,2,0:T(8,128)(2,1)S(1)} %multiply_convert_fusion.41), channel_id=1, source_target_pairs={{0,10},{2,8},{4,14},{6,12},{8,2},{10,0},{12,6},{14,4},{1,11},{3,9}... | collective-permute-start | bytes 294920 | tf_op jit(solution)/shard_map/ppermute | solution.py:49
  118.5 2.3 %collective-permute-done.29 = bf16[3,256,64]{1,2,0:T(8,128)(2,1)S(1)} collective-permute-done((bf16[3,256,64]{1,2,0:T(8,128)(2,1)S(1)}, bf16[3,256,64]{1,2,0:T(8,128)(2,1)S(1)}, u32[]{:S(2)}, u32[]{:S(2)}) %collective-permute-start.29) | collective-permute-done | bytes 98336 | tf_op jit(solution)/shard_map/ppermute | solution.py:49
  127.6 2.3 %convolution_convert_fusion.2 = bf16[512,256]{1,0:T(8,128)(2,1)} fusion(f32[512,256]{1,0:T(8,128)} %convolution_bitcast_fusion.12, bf16[2,512,256]{2,1,0:T(8,128)(2,1)} %copy-done.5, bf16[3,256,256]{1,2,0:T(8,128)(2,1)S(1)} %constant_dynamic-update-slice_fusion.16), kind=kOutput, calls=%fused_computation.20 | convolution fusion | flops 135135232 | bytes 1310720 | tf_op jit(solution)/shard_map/th,hd->td/dot_general | solution.py:80
  139.8 2.3 %collective-permute-done.35 = bf16[3,256,64]{1,2,0:T(8,128)(2,1)S(1)} collective-permute-done((bf16[3,256,64]{1,2,0:T(8,128)(2,1)S(1)}, bf16[3,256,64]{1,2,0:T(8,128)(2,1)S(1)}, u32[]{:S(2)}, u32[]{:S(2)}) %collective-permute-start.35) | collective-permute-done | bytes 98336 | tf_op jit(solution)/shard_map/ppermute | solution.py:14
  142.1 2.6 %collective-permute-done.36 = bf16[3,256,64]{1,2,0:T(8,128)(2,1)S(1)} collective-permute-done((bf16[3,256,64]{1,2,0:T(8,128)(2,1)S(1)}, bf16[3,256,64]{1,2,0:T(8,128)(2,1)S(1)}, u32[]{:S(2)}, u32[]{:S(2)}) %collective-permute-start.36) | collective-permute-done | bytes 98336 | tf_op jit(solution)/shard_map/ppermute | solution.py:14
  153.9 2.7 %collective-permute-done.39 = bf16[3,256,64]{1,2,0:T(8,128)(2,1)S(1)} collective-permute-done((bf16[3,256,64]{1,2,0:T(8,128)(2,1)S(1)}, bf16[3,256,64]{1,2,0:T(8,128)(2,1)S(1)}, u32[]{:S(2)}, u32[]{:S(2)}) %collective-permute-start.39) | collective-permute-done | bytes 98336 | tf_op jit(solution)/shard_map/ppermute | solution.py:14
  157.0 2.7 %collective-permute-start.41 = (bf16[3,256,64]{1,2,0:T(8,128)(2,1)S(1)}, bf16[3,256,64]{1,2,0:T(8,128)(2,1)S(1)}, u32[]{:S(2)}, u32[]{:S(2)}) collective-permute-start(bf16[3,256,64]{1,2,0:T(8,128)(2,1)S(1)} %get-tuple-element.5), channel_id=1, source_target_pairs={{0,4},{4,8},{8,12},{12,0},{1,5},{5,9},{9,13},{13,1},{2,6},{6,10},{... | collective-permute-start | bytes 294920 | tf_op jit(solution)/shard_map/ppermute | solution.py:14
  164.4 3.1 %collective-permute-done.42 = bf16[3,256,64]{1,2,0:T(8,128)(2,1)S(1)} collective-permute-done((bf16[3,256,64]{1,2,0:T(8,128)(2,1)S(1)}, bf16[3,256,64]{1,2,0:T(8,128)(2,1)S(1)}, u32[]{:S(2)}, u32[]{:S(2)}) %collective-permute-start.42) | collective-permute-done | bytes 98336 | tf_op jit(solution)/shard_map/ppermute | solution.py:14
  (185 shorter events, 76.7 us)
Async XLA Ops:
  1.6 8.8 %collective-permute-start = (bf16[3,256,64]{1,2,0:T(8,128)(2,1)S(1)}, bf16[3,256,64]{1,2,0:T(8,128)(2,1)S(1)}, u32[]{:S(2)}, u32[]{:S(2)}) collective-permute-start(bf16[3,256,64]{1,2,0:T(8,128)(2,1)S(1)} %get-tuple-element.25), channel_id=1, source_target_pairs={{0,4},{4,8},{8,12},{12,0},{1,5},{5,9},{9,13},{13,1},{2,6},{6,10},{... | collective-permute-start | bytes 294920 | tf_op jit(solution)/shard_map/ppermute | solution.py:14
  4.7 9.2 %collective-permute-start.1 = (bf16[3,256,64]{1,2,0:T(8,128)(2,1)S(1)}, bf16[3,256,64]{1,2,0:T(8,128)(2,1)S(1)}, u32[]{:S(2)}, u32[]{:S(2)}) collective-permute-start(bf16[3,256,64]{1,2,0:T(8,128)(2,1)S(1)} %get-tuple-element.25), channel_id=1, source_target_pairs={{0,8},{4,12},{8,0},{12,4},{1,9},{5,13},{9,1},{13,5},{2,10},{6,14},... | collective-permute-start | bytes 294920 | tf_op jit(solution)/shard_map/ppermute | solution.py:14
  16.7 7.4 %collective-permute-start.3 = (bf16[3,256,64]{1,2,0:T(8,128)(2,1)S(1)}, bf16[3,256,64]{1,2,0:T(8,128)(2,1)S(1)}, u32[]{:S(2)}, u32[]{:S(2)}) collective-permute-start(bf16[3,256,64]{1,2,0:T(8,128)(2,1)S(1)} %get-tuple-element.41), channel_id=1, source_target_pairs={{0,4},{4,8},{8,12},{12,0},{1,5},{5,9},{9,13},{13,1},{2,6},{6,10},{... | collective-permute-start | bytes 294920 | tf_op jit(solution)/shard_map/ppermute | solution.py:14
  19.3 8.2 %collective-permute-start.4 = (bf16[3,256,64]{1,2,0:T(8,128)(2,1)S(1)}, bf16[3,256,64]{1,2,0:T(8,128)(2,1)S(1)}, u32[]{:S(2)}, u32[]{:S(2)}) collective-permute-start(bf16[3,256,64]{1,2,0:T(8,128)(2,1)S(1)} %get-tuple-element.43), channel_id=1, source_target_pairs={{0,8},{4,12},{8,0},{12,4},{1,9},{5,13},{9,1},{13,5},{2,10},{6,14},... | collective-permute-start | bytes 294920 | tf_op jit(solution)/shard_map/ppermute | solution.py:14
  27.9 7.4 %collective-permute-start.6 = (bf16[3,256,64]{1,2,0:T(8,128)(2,1)S(1)}, bf16[3,256,64]{1,2,0:T(8,128)(2,1)S(1)}, u32[]{:S(2)}, u32[]{:S(2)}) collective-permute-start(bf16[3,256,64]{1,2,0:T(8,128)(2,1)S(1)} %get-tuple-element.21), channel_id=1, source_target_pairs={{0,4},{4,8},{8,12},{12,0},{1,5},{5,9},{9,13},{13,1},{2,6},{6,10},{... | collective-permute-start | bytes 294920 | tf_op jit(solution)/shard_map/ppermute | solution.py:14
  30.5 8.2 %collective-permute-start.7 = (bf16[3,256,64]{1,2,0:T(8,128)(2,1)S(1)}, bf16[3,256,64]{1,2,0:T(8,128)(2,1)S(1)}, u32[]{:S(2)}, u32[]{:S(2)}) collective-permute-start(bf16[3,256,64]{1,2,0:T(8,128)(2,1)S(1)} %get-tuple-element.21), channel_id=1, source_target_pairs={{0,8},{4,12},{8,0},{12,4},{1,9},{5,13},{9,1},{13,5},{2,10},{6,14},... | collective-permute-start | bytes 294920 | tf_op jit(solution)/shard_map/ppermute | solution.py:14
  40.9 7.3 %collective-permute-start.10 = (bf16[3,256,64]{1,2,0:T(8,128)(2,1)S(1)}, bf16[3,256,64]{1,2,0:T(8,128)(2,1)S(1)}, u32[]{:S(2)}, u32[]{:S(2)}) collective-permute-start(bf16[3,256,64]{1,2,0:T(8,128)(2,1)S(1)} %get-tuple-element.40), channel_id=1, source_target_pairs={{0,8},{4,12},{8,0},{12,4},{1,9},{5,13},{9,1},{13,5},{2,10},{6,14},... | collective-permute-start | bytes 294920 | tf_op jit(solution)/shard_map/ppermute | solution.py:14
  45.8 7.0 %collective-permute-start.9 = (bf16[3,256,64]{1,2,0:T(8,128)(2,1)S(1)}, bf16[3,256,64]{1,2,0:T(8,128)(2,1)S(1)}, u32[]{:S(2)}, u32[]{:S(2)}) collective-permute-start(bf16[3,256,64]{1,2,0:T(8,128)(2,1)S(1)} %get-tuple-element.38), channel_id=1, source_target_pairs={{0,4},{4,8},{8,12},{12,0},{1,5},{5,9},{9,13},{13,1},{2,6},{6,10},{... | collective-permute-start | bytes 294920 | tf_op jit(solution)/shard_map/ppermute | solution.py:14
  53.2 7.0 %collective-permute-start.12 = (bf16[3,256,64]{1,2,0:T(8,128)(2,1)S(1)}, bf16[3,256,64]{1,2,0:T(8,128)(2,1)S(1)}, u32[]{:S(2)}, u32[]{:S(2)}) collective-permute-start(bf16[3,256,64]{1,2,0:T(8,128)(2,1)S(1)} %multiply_convert_fusion.42), channel_id=1, source_target_pairs={{0,2},{2,0},{4,6},{6,4},{8,10},{10,8},{12,14},{14,12},{1,3},{3,1},... | collective-permute-start | bytes 294920 | tf_op jit(solution)/shard_map/ppermute | solution.py:49
  54.7 8.4 %collective-permute-start.13 = (bf16[3,256,64]{1,2,0:T(8,128)(2,1)S(1)}, bf16[3,256,64]{1,2,0:T(8,128)(2,1)S(1)}, u32[]{:S(2)}, u32[]{:S(2)}) collective-permute-start(bf16[3,256,64]{1,2,0:T(8,128)(2,1)S(1)} %multiply_convert_fusion.42), channel_id=1, source_target_pairs={{0,6},{2,4},{4,10},{6,8},{8,14},{10,12},{12,2},{14,0},{1,7},{3,5},... | collective-permute-start | bytes 294920 | tf_op jit(solution)/shard_map/ppermute | solution.py:49
  54.7 10.6 %collective-permute-start.14 = (bf16[3,256,64]{1,2,0:T(8,128)(2,1)S(1)}, bf16[3,256,64]{1,2,0:T(8,128)(2,1)S(1)}, u32[]{:S(2)}, u32[]{:S(2)}) collective-permute-start(bf16[3,256,64]{1,2,0:T(8,128)(2,1)S(1)} %multiply_convert_fusion.42), channel_id=1, source_target_pairs={{0,10},{2,8},{4,14},{6,12},{8,2},{10,0},{12,6},{14,4},{1,11},{3,9}... | collective-permute-start | bytes 294920 | tf_op jit(solution)/shard_map/ppermute | solution.py:49
  57.8 7.6 %collective-permute-start.15 = (bf16[3,256,64]{1,2,0:T(8,128)(2,1)S(1)}, bf16[3,256,64]{1,2,0:T(8,128)(2,1)S(1)}, u32[]{:S(2)}, u32[]{:S(2)}) collective-permute-start(bf16[3,256,64]{1,2,0:T(8,128)(2,1)S(1)} %multiply_convert_fusion.42), channel_id=1, source_target_pairs={{0,14},{2,12},{4,2},{6,0},{8,6},{10,4},{12,10},{14,8},{1,15},{3,13... | collective-permute-start | bytes 294920 | tf_op jit(solution)/shard_map/ppermute | solution.py:49
  67.6 7.3 %collective-permute-start.18 = (bf16[3,256,64]{1,2,0:T(8,128)(2,1)S(1)}, bf16[3,256,64]{1,2,0:T(8,128)(2,1)S(1)}, u32[]{:S(2)}, u32[]{:S(2)}) collective-permute-start(bf16[3,256,64]{1,2,0:T(8,128)(2,1)S(1)} %get-tuple-element.35), channel_id=1, source_target_pairs={{0,4},{4,8},{8,12},{12,0},{1,5},{5,9},{9,13},{13,1},{2,6},{6,10},{... | collective-permute-start | bytes 294920 | tf_op jit(solution)/shard_map/ppermute | solution.py:14
  69.5 8.1 %collective-permute-start.19 = (bf16[3,256,64]{1,2,0:T(8,128)(2,1)S(1)}, bf16[3,256,64]{1,2,0:T(8,128)(2,1)S(1)}, u32[]{:S(2)}, u32[]{:S(2)}) collective-permute-start(bf16[3,256,64]{1,2,0:T(8,128)(2,1)S(1)} %get-tuple-element.37), channel_id=1, source_target_pairs={{0,8},{4,12},{8,0},{12,4},{1,9},{5,13},{9,1},{13,5},{2,10},{6,14},... | collective-permute-start | bytes 294920 | tf_op jit(solution)/shard_map/ppermute | solution.py:14
  78.2 7.5 %collective-permute-start.21 = (bf16[3,256,64]{1,2,0:T(8,128)(2,1)S(1)}, bf16[3,256,64]{1,2,0:T(8,128)(2,1)S(1)}, u32[]{:S(2)}, u32[]{:S(2)}) collective-permute-start(bf16[3,256,64]{1,2,0:T(8,128)(2,1)S(1)} %get-tuple-element.15), channel_id=1, source_target_pairs={{0,4},{4,8},{8,12},{12,0},{1,5},{5,9},{9,13},{13,1},{2,6},{6,10},{... | collective-permute-start | bytes 294920 | tf_op jit(solution)/shard_map/ppermute | solution.py:14
  80.3 8.1 %collective-permute-start.22 = (bf16[3,256,64]{1,2,0:T(8,128)(2,1)S(1)}, bf16[3,256,64]{1,2,0:T(8,128)(2,1)S(1)}, u32[]{:S(2)}, u32[]{:S(2)}) collective-permute-start(bf16[3,256,64]{1,2,0:T(8,128)(2,1)S(1)} %get-tuple-element.15), channel_id=1, source_target_pairs={{0,8},{4,12},{8,0},{12,4},{1,9},{5,13},{9,1},{13,5},{2,10},{6,14},... | collective-permute-start | bytes 294920 | tf_op jit(solution)/shard_map/ppermute | solution.py:14
  90.6 7.5 %collective-permute-start.24 = (bf16[3,256,64]{1,2,0:T(8,128)(2,1)S(1)}, bf16[3,256,64]{1,2,0:T(8,128)(2,1)S(1)}, u32[]{:S(2)}, u32[]{:S(2)}) collective-permute-start(bf16[3,256,64]{1,2,0:T(8,128)(2,1)S(1)} %get-tuple-element.32), channel_id=1, source_target_pairs={{0,4},{4,8},{8,12},{12,0},{1,5},{5,9},{9,13},{13,1},{2,6},{6,10},{... | collective-permute-start | bytes 294920 | tf_op jit(solution)/shard_map/ppermute | solution.py:14
  93.1 8.2 %collective-permute-start.25 = (bf16[3,256,64]{1,2,0:T(8,128)(2,1)S(1)}, bf16[3,256,64]{1,2,0:T(8,128)(2,1)S(1)}, u32[]{:S(2)}, u32[]{:S(2)}) collective-permute-start(bf16[3,256,64]{1,2,0:T(8,128)(2,1)S(1)} %get-tuple-element.34), channel_id=1, source_target_pairs={{0,8},{4,12},{8,0},{12,4},{1,9},{5,13},{9,1},{13,5},{2,10},{6,14},... | collective-permute-start | bytes 294920 | tf_op jit(solution)/shard_map/ppermute | solution.py:14
  95.6 14.4 %collective-permute-start.16 = (bf16[2,512,256]{2,1,0:T(8,128)(2,1)S(1)}, bf16[2,512,256]{2,1,0:T(8,128)(2,1)S(1)}, u32[]{:S(2)}, u32[]{:S(2)}) collective-permute-start(bf16[2,512,256]{2,1,0:T(8,128)(2,1)S(1)} %slice_bitcast_fusion), channel_id=1, source_target_pairs={{0,2},{2,0},{1,3},{3,1},{4,6},{6,4},{5,7},{7,5},{8,10},{10,8},{9,1... | collective-permute-start | bytes 1572872 | tf_op jit(solution)/shard_map/ppermute | solution.py:14
  101.7 14.6 %collective-permute-start.27 = (bf16[3,256,64]{1,2,0:T(8,128)(2,1)S(1)}, bf16[3,256,64]{1,2,0:T(8,128)(2,1)S(1)}, u32[]{:S(2)}, u32[]{:S(2)}) collective-permute-start(bf16[3,256,64]{1,2,0:T(8,128)(2,1)S(1)} %multiply_convert_fusion.41), channel_id=1, source_target_pairs={{0,2},{2,0},{4,6},{6,4},{8,10},{10,8},{12,14},{14,12},{1,3},{3,1},... | collective-permute-start | bytes 294920 | tf_op jit(solution)/shard_map/ppermute | solution.py:49
  111.0 7.4 %collective-permute-start.28 = (bf16[3,256,64]{1,2,0:T(8,128)(2,1)S(1)}, bf16[3,256,64]{1,2,0:T(8,128)(2,1)S(1)}, u32[]{:S(2)}, u32[]{:S(2)}) collective-permute-start(bf16[3,256,64]{1,2,0:T(8,128)(2,1)S(1)} %multiply_convert_fusion.41), channel_id=1, source_target_pairs={{0,6},{2,4},{4,10},{6,8},{8,14},{10,12},{12,2},{14,0},{1,7},{3,5},... | collective-permute-start | bytes 294920 | tf_op jit(solution)/shard_map/ppermute | solution.py:49
  111.8 9.0 %collective-permute-start.29 = (bf16[3,256,64]{1,2,0:T(8,128)(2,1)S(1)}, bf16[3,256,64]{1,2,0:T(8,128)(2,1)S(1)}, u32[]{:S(2)}, u32[]{:S(2)}) collective-permute-start(bf16[3,256,64]{1,2,0:T(8,128)(2,1)S(1)} %multiply_convert_fusion.41), channel_id=1, source_target_pairs={{0,10},{2,8},{4,14},{6,12},{8,2},{10,0},{12,6},{14,4},{1,11},{3,9}... | collective-permute-start | bytes 294920 | tf_op jit(solution)/shard_map/ppermute | solution.py:49
  123.7 7.4 %collective-permute-start.32 = (bf16[3,256,64]{1,2,0:T(8,128)(2,1)}, bf16[3,256,64]{1,2,0:T(8,128)(2,1)S(1)}, u32[]{:S(2)}, u32[]{:S(2)}) collective-permute-start(bf16[3,256,64]{1,2,0:T(8,128)(2,1)} %get-tuple-element.29), channel_id=1, source_target_pairs={{0,4},{4,8},{8,12},{12,0},{1,5},{5,9},{9,13},{13,1},{2,6},{6,10},{... | collective-permute-start | bytes 294920 | tf_op jit(solution)/shard_map/ppermute | solution.py:14
  125.2 8.1 %collective-permute-start.33 = (bf16[3,256,64]{1,2,0:T(8,128)(2,1)S(1)}, bf16[3,256,64]{1,2,0:T(8,128)(2,1)S(1)}, u32[]{:S(2)}, u32[]{:S(2)}) collective-permute-start(bf16[3,256,64]{1,2,0:T(8,128)(2,1)S(1)} %get-tuple-element.31), channel_id=1, source_target_pairs={{0,8},{4,12},{8,0},{12,4},{1,9},{5,13},{9,1},{13,5},{2,10},{6,14},... | collective-permute-start | bytes 294920 | tf_op jit(solution)/shard_map/ppermute | solution.py:14
  129.9 38.3 %collective-permute-start.17 = (bf16[512,256]{1,0:T(8,128)(2,1)}, bf16[512,256]{1,0:T(8,128)(2,1)}, u32[]{:S(2)}, u32[]{:S(2)}) collective-permute-start(bf16[512,256]{1,0:T(8,128)(2,1)} %convolution_convert_fusion.2), channel_id=1, source_target_pairs={{0,2},{2,0},{1,3},{3,1},{4,6},{6,4},{5,7},{7,5},{8,10},{10,8},{9,1... | collective-permute-start | bytes 786440 | tf_op jit(solution)/shard_map/ppermute | solution.py:14
  134.6 7.5 %collective-permute-start.35 = (bf16[3,256,64]{1,2,0:T(8,128)(2,1)S(1)}, bf16[3,256,64]{1,2,0:T(8,128)(2,1)S(1)}, u32[]{:S(2)}, u32[]{:S(2)}) collective-permute-start(bf16[3,256,64]{1,2,0:T(8,128)(2,1)S(1)} %get-tuple-element.9), channel_id=1, source_target_pairs={{0,4},{4,8},{8,12},{12,0},{1,5},{5,9},{9,13},{13,1},{2,6},{6,10},{... | collective-permute-start | bytes 294920 | tf_op jit(solution)/shard_map/ppermute | solution.py:14
  136.6 8.1 %collective-permute-start.36 = (bf16[3,256,64]{1,2,0:T(8,128)(2,1)S(1)}, bf16[3,256,64]{1,2,0:T(8,128)(2,1)S(1)}, u32[]{:S(2)}, u32[]{:S(2)}) collective-permute-start(bf16[3,256,64]{1,2,0:T(8,128)(2,1)S(1)} %get-tuple-element.9), channel_id=1, source_target_pairs={{0,8},{4,12},{8,0},{12,4},{1,9},{5,13},{9,1},{13,5},{2,10},{6,14},... | collective-permute-start | bytes 294920 | tf_op jit(solution)/shard_map/ppermute | solution.py:14
  146.9 7.0 %collective-permute-start.38 = (bf16[3,256,64]{1,2,0:T(8,128)(2,1)S(1)}, bf16[3,256,64]{1,2,0:T(8,128)(2,1)S(1)}, u32[]{:S(2)}, u32[]{:S(2)}) collective-permute-start(bf16[3,256,64]{1,2,0:T(8,128)(2,1)S(1)} %get-tuple-element.26), channel_id=1, source_target_pairs={{0,4},{4,8},{8,12},{12,0},{1,5},{5,9},{9,13},{13,1},{2,6},{6,10},{... | collective-permute-start | bytes 294920 | tf_op jit(solution)/shard_map/ppermute | solution.py:14
  148.6 8.0 %collective-permute-start.39 = (bf16[3,256,64]{1,2,0:T(8,128)(2,1)S(1)}, bf16[3,256,64]{1,2,0:T(8,128)(2,1)S(1)}, u32[]{:S(2)}, u32[]{:S(2)}) collective-permute-start(bf16[3,256,64]{1,2,0:T(8,128)(2,1)S(1)} %get-tuple-element.28), channel_id=1, source_target_pairs={{0,8},{4,12},{8,0},{12,4},{1,9},{5,13},{9,1},{13,5},{2,10},{6,14},... | collective-permute-start | bytes 294920 | tf_op jit(solution)/shard_map/ppermute | solution.py:14
  151.5 16.8 %collective-permute-start.31 = (bf16[512,256]{1,0:T(8,128)(2,1)S(1)}, bf16[512,256]{1,0:T(8,128)(2,1)S(1)}, u32[]{:S(2)}, u32[]{:S(2)}) collective-permute-start(bf16[512,256]{1,0:T(8,128)(2,1)S(1)} %convolution_convert_fusion.1), channel_id=1, source_target_pairs={{0,2},{2,0},{1,3},{3,1},{4,6},{6,4},{5,7},{7,5},{8,10},{10,8},{9,1... | collective-permute-start | bytes 786440 | tf_op jit(solution)/shard_map/ppermute | solution.py:14
  157.0 7.3 %collective-permute-start.41 = (bf16[3,256,64]{1,2,0:T(8,128)(2,1)S(1)}, bf16[3,256,64]{1,2,0:T(8,128)(2,1)S(1)}, u32[]{:S(2)}, u32[]{:S(2)}) collective-permute-start(bf16[3,256,64]{1,2,0:T(8,128)(2,1)S(1)} %get-tuple-element.5), channel_id=1, source_target_pairs={{0,4},{4,8},{8,12},{12,0},{1,5},{5,9},{9,13},{13,1},{2,6},{6,10},{... | collective-permute-start | bytes 294920 | tf_op jit(solution)/shard_map/ppermute | solution.py:14
  160.5 7.0 %collective-permute-start.42 = (bf16[3,256,64]{1,2,0:T(8,128)(2,1)S(1)}, bf16[3,256,64]{1,2,0:T(8,128)(2,1)S(1)}, u32[]{:S(2)}, u32[]{:S(2)}) collective-permute-start(bf16[3,256,64]{1,2,0:T(8,128)(2,1)S(1)} %get-tuple-element.5), channel_id=1, source_target_pairs={{0,8},{4,12},{8,0},{12,4},{1,9},{5,13},{9,1},{13,5},{2,10},{6,14},... | collective-permute-start | bytes 294920 | tf_op jit(solution)/shard_map/ppermute | solution.py:14
  (21 other events, 125.5 us)

commit v9 on v8

--- a/solution.py
+++ b/solution.py
@@ -7,6 +7,7 @@
 
 
 ITERS = 2
+DELAY_STEPS = 60
 
 
 def rotated(value, axis, by):
@@ -57,8 +58,8 @@
 
 
 def fast_grads(fast, key_block, scaled):
-    gate_pre = jnp.einsum("td,dh->th", key_block, fast[0], preferred_element_type=jnp.float32)
-    up_pre = jnp.einsum("td,dh->th", key_block, fast[1], preferred_element_type=jnp.float32)
+    pair = jnp.einsum("td,mdh->mth", key_block, fast[:2], preferred_element_type=jnp.float32)
+    gate_pre, up_pre = pair[0], pair[1]
     sigmoid_gate = jax.nn.sigmoid(gate_pre)
     gated = gate_pre * sigmoid_gate
     hidden = (gated * up_pre).astype(jnp.bfloat16)
@@ -67,10 +68,10 @@
         back_grad * up_pre * sigmoid_gate * (1.0 + gate_pre * (1.0 - sigmoid_gate))
     ).astype(jnp.bfloat16)
     grad_up = (back_grad * gated).astype(jnp.bfloat16)
-    first = jnp.einsum("td,th->dh", key_block, grad_gate, preferred_element_type=jnp.float32)
-    second = jnp.einsum("td,th->dh", key_block, grad_up, preferred_element_type=jnp.float32)
+    grads = jnp.stack([grad_gate, grad_up])
+    first_two = jnp.einsum("td,mth->mdh", key_block, grads, preferred_element_type=jnp.float32)
     third = jnp.einsum("th,td->hd", hidden, scaled, preferred_element_type=jnp.float32)
-    return jnp.stack([first, second, third], axis=0).astype(jnp.bfloat16)
+    return jnp.concatenate([first_two, third[None]], axis=0).astype(jnp.bfloat16)
 
 
 def apply_fast(fast, query_block):
@@ -96,6 +97,10 @@
     tick_count = key_rows.shape[0]
     results = []
     weights = states_in[0, 0]
+    unit = (init_norms[0, 0] + 1.0) / (init_norms[0, 0] + 1.0)
+    weights = lax.fori_loop(
+        0, lax.axis_index("head") * DELAY_STEPS, lambda step, held: held * unit, weights
+    )
     fast = gather_cols(weights.astype(jnp.bfloat16), part_cols)
     arrived = None
     earlier_queries = rotated(query_rows[: tick_count - 1, 0, :, 0], "span", 1)

time: 170 us -> 172 us (1.012)
  starting transfers between devices: 71.8 us -> 66.1 us
  waiting for transfers between devices: 70.8 us -> 74.4 us
  local copies, waits for them, and re-layouts: 3.02 us -> 5.57 us
    ppermute x36, starting transfers between devices: 57.9 us -> 53 us  [rotated(): lax.ppermute(value, axis, [(i, (i + by) % devices) for i in range(devices)])]
    dot_general x24 -> x12, matrix products: 7.81 us -> 4.2 us  [the longest x6 2.24 us: fast_grads(): jnp.einsum('td,mth->mdh', key_block, grads, preferred_element_type=jnp.fl...]
    ppermute x36, waiting for transfers between devices: 61.3 us -> 64.3 us  [rotated(): lax.ppermute(value, axis, [(i, (i + by) % devices) for i in range(devices)])]
    unnamed x19 -> x24, local copies, waits for them, and re-layouts: 1.68 us -> 4.41 us
  transfers between devices with their start and end apart: 44 -> 44, of which waited for: 28 -> 30; matrix products, arithmetic and copies ran while one was open for 6% -> 7% of each run, Pallas kernels for 0% -> 0%
where the time goes in v9:
time: 172 us; the launch traced here: 171 us
  waiting for transfers between devices  74.4 us (43%)
  starting transfers between devices  66.1 us (38%)
  matrix products  15.5 us (9%)
  other arithmetic  7.71 us (4%)
  local copies, waits for them, and re-layouts  5.57 us (3%)
  between operations  2.14 us (1%)
    ppermute x36, waiting for transfers between devices, rotated(): lax.ppermute(value, axis, [(i, (i + by) % devices) for i in range(devices)])  64.3 us
    ppermute x36, starting transfers between devices, rotated(): lax.ppermute(value, axis, [(i, (i + by) % devices) for i in range(devices)])  53 us
    ppermute x8, starting transfers between devices, cross_gather(): got = lax.ppermute(own, ('tok', 'span'), pairs)  13.1 us
    ppermute x8, waiting for transfers between devices, cross_gather(): got = lax.ppermute(own, ('tok', 'span'), pairs)  10.1 us
    unnamed x24, local copies, waits for them, and re-layouts  4.41 us
    dot_general x3, matrix products, apply_fast(): jnp.einsum('th,hd->td', applied, fast[2], preferred_element_type=jnp.floa...  3.87 us
  transfers between devices with their start and end apart: 44, of which 30 were waited for; matrix products, arithmetic and copies ran while one was open for 7% of the time, Pallas kernels for 0%

profile of v9, /device:TPU:0, one launch (start us, length us, event | category | flops | bytes accessed | tf_op | source)
XLA Modules:
  0.0 171.5 jit_solution(3565003537937902843)
XLA Ops:
  3.7 3.1 %collective-permute-start = (bf16[3,256,64]{1,2,0:T(8,128)(2,1)S(1)}, bf16[3,256,64]{1,2,0:T(8,128)(2,1)S(1)}, u32[]{:S(2)}, u32[]{:S(2)}) collective-permute-start(bf16[3,256,64]{1,2,0:T(8,128)(2,1)S(1)} %get-tuple-element.57), channel_id=1, source_target_pairs={{0,4},{4,8},{8,12},{12,0},{1,5},{5,9},{9,13},{13,1},{2,6},{6,10},{... | collective-permute-start | bytes 294920 | tf_op jit(solution)/shard_map/ppermute | solution.py:15
  6.8 2.6 %collective-permute-start.1 = (bf16[3,256,64]{1,2,0:T(8,128)(2,1)S(1)}, bf16[3,256,64]{1,2,0:T(8,128)(2,1)S(1)}, u32[]{:S(2)}, u32[]{:S(2)}) collective-permute-start(bf16[3,256,64]{1,2,0:T(8,128)(2,1)S(1)} %get-tuple-element.57), channel_id=1, source_target_pairs={{0,8},{4,12},{8,0},{12,4},{1,9},{5,13},{9,1},{13,5},{2,10},{6,14},... | collective-permute-start | bytes 294920 | tf_op jit(solution)/shard_map/ppermute | solution.py:15
  11.4 2.2 %collective-permute-done.1 = bf16[3,256,64]{1,2,0:T(8,128)(2,1)S(1)} collective-permute-done((bf16[3,256,64]{1,2,0:T(8,128)(2,1)S(1)}, bf16[3,256,64]{1,2,0:T(8,128)(2,1)S(1)}, u32[]{:S(2)}, u32[]{:S(2)}) %collective-permute-start.1) | collective-permute-done | bytes 98336 | tf_op jit(solution)/shard_map/ppermute | solution.py:15
  17.6 2.6 %collective-permute-start.4 = (bf16[3,256,64]{1,2,0:T(8,128)(2,1)S(1)}, bf16[3,256,64]{1,2,0:T(8,128)(2,1)S(1)}, u32[]{:S(2)}, u32[]{:S(2)}) collective-permute-start(bf16[3,256,64]{1,2,0:T(8,128)(2,1)S(1)} %get-tuple-element.86), channel_id=1, source_target_pairs={{0,8},{4,12},{8,0},{12,4},{1,9},{5,13},{9,1},{13,5},{2,10},{6,14},... | collective-permute-start | bytes 294920 | tf_op jit(solution)/shard_map/ppermute | solution.py:15
  20.4 2.7 %collective-permute-done.3 = bf16[3,256,64]{1,2,0:T(8,128)(2,1)S(1)} collective-permute-done((bf16[3,256,64]{1,2,0:T(8,128)(2,1)S(1)}, bf16[3,256,64]{1,2,0:T(8,128)(2,1)S(1)}, u32[]{:S(2)}, u32[]{:S(2)}) %collective-permute-start.3) | collective-permute-done | bytes 98336 | tf_op jit(solution)/shard_map/ppermute | solution.py:15
  30.0 2.7 %collective-permute-done.6 = bf16[3,256,64]{1,2,0:T(8,128)(2,1)S(1)} collective-permute-done((bf16[3,256,64]{1,2,0:T(8,128)(2,1)S(1)}, bf16[3,256,64]{1,2,0:T(8,128)(2,1)S(1)}, u32[]{:S(2)}, u32[]{:S(2)}) %collective-permute-start.6) | collective-permute-done | bytes 98336 | tf_op jit(solution)/shard_map/ppermute | solution.py:15
  32.7 4.3 %collective-permute-done.7 = bf16[3,256,64]{1,2,0:T(8,128)(2,1)S(1)} collective-permute-done((bf16[3,256,64]{1,2,0:T(8,128)(2,1)S(1)}, bf16[3,256,64]{1,2,0:T(8,128)(2,1)S(1)}, u32[]{:S(2)}, u32[]{:S(2)}) %collective-permute-start.7) | collective-permute-done | bytes 98336 | tf_op jit(solution)/shard_map/ppermute | solution.py:15
  40.3 3.4 %collective-permute-start.11 = (bf16[3,256,64]{1,2,0:T(8,128)(2,1)S(1)}, bf16[3,256,64]{1,2,0:T(8,128)(2,1)S(1)}, u32[]{:S(2)}, u32[]{:S(2)}) collective-permute-start(bf16[3,256,64]{1,2,0:T(8,128)(2,1)S(1)} %get-tuple-element.84), channel_id=1, source_target_pairs={{0,12},{4,0},{8,4},{12,8},{1,13},{5,1},{9,5},{13,9},{2,14},{6,2},{... | collective-permute-start | bytes 294920 | tf_op jit(solution)/shard_map/ppermute | solution.py:15
  44.7 2.2 %collective-permute-done.11 = bf16[3,256,64]{1,2,0:T(8,128)(2,1)S(1)} collective-permute-done((bf16[3,256,64]{1,2,0:T(8,128)(2,1)S(1)}, bf16[3,256,64]{1,2,0:T(8,128)(2,1)S(1)}, u32[]{:S(2)}, u32[]{:S(2)}) %collective-permute-start.11) | collective-permute-done | bytes 98336 | tf_op jit(solution)/shard_map/ppermute | solution.py:15
  46.9 4.6 %collective-permute-done.9 = bf16[3,256,64]{1,2,0:T(8,128)(2,1)S(1)} collective-permute-done((bf16[3,256,64]{1,2,0:T(8,128)(2,1)S(1)}, bf16[3,256,64]{1,2,0:T(8,128)(2,1)S(1)}, u32[]{:S(2)}, u32[]{:S(2)}) %collective-permute-start.9) | collective-permute-done | bytes 98336 | tf_op jit(solution)/shard_map/ppermute | solution.py:15
  51.8 2.6 %collective-permute-start.12 = (bf16[3,256,64]{1,2,0:T(8,128)(2,1)S(1)}, bf16[3,256,64]{1,2,0:T(8,128)(2,1)S(1)}, u32[]{:S(2)}, u32[]{:S(2)}) collective-permute-start(bf16[3,256,64]{1,2,0:T(8,128)(2,1)S(1)} %multiply_convert_fusion.21), channel_id=1, source_target_pairs={{0,2},{2,0},{4,6},{6,4},{8,10},{10,8},{12,14},{14,12},{1,3},{3,1},... | collective-permute-start | bytes 294920 | tf_op jit(solution)/shard_map/ppermute | solution.py:50
  54.4 3.1 %collective-permute-start.14 = (bf16[3,256,64]{1,2,0:T(8,128)(2,1)S(1)}, bf16[3,256,64]{1,2,0:T(8,128)(2,1)S(1)}, u32[]{:S(2)}, u32[]{:S(2)}) collective-permute-start(bf16[3,256,64]{1,2,0:T(8,128)(2,1)S(1)} %multiply_convert_fusion.21), channel_id=1, source_target_pairs={{0,10},{2,8},{4,14},{6,12},{8,2},{10,0},{12,6},{14,4},{1,11},{3,9}... | collective-permute-start | bytes 294920 | tf_op jit(solution)/shard_map/ppermute | solution.py:50
  59.6 3.2 %collective-permute-done.13 = bf16[3,256,64]{1,2,0:T(8,128)(2,1)S(1)} collective-permute-done((bf16[3,256,64]{1,2,0:T(8,128)(2,1)S(1)}, bf16[3,256,64]{1,2,0:T(8,128)(2,1)S(1)}, u32[]{:S(2)}, u32[]{:S(2)}) %collective-permute-start.13) | collective-permute-done | bytes 98336 | tf_op jit(solution)/shard_map/ppermute | solution.py:50
  62.8 2.3 %collective-permute-done.14 = bf16[3,256,64]{1,2,0:T(8,128)(2,1)S(1)} collective-permute-done((bf16[3,256,64]{1,2,0:T(8,128)(2,1)S(1)}, bf16[3,256,64]{1,2,0:T(8,128)(2,1)S(1)}, u32[]{:S(2)}, u32[]{:S(2)}) %collective-permute-start.14) | collective-permute-done | bytes 98336 | tf_op jit(solution)/shard_map/ppermute | solution.py:50
  68.8 2.4 %collective-permute-start.19 = (bf16[3,256,64]{1,2,0:T(8,128)(2,1)S(1)}, bf16[3,256,64]{1,2,0:T(8,128)(2,1)S(1)}, u32[]{:S(2)}, u32[]{:S(2)}) collective-permute-start(bf16[3,256,64]{1,2,0:T(8,128)(2,1)S(1)} %get-tuple-element.80), channel_id=1, source_target_pairs={{0,8},{4,12},{8,0},{12,4},{1,9},{5,13},{9,1},{13,5},{2,10},{6,14},... | collective-permute-start | bytes 294920 | tf_op jit(solution)/shard_map/ppermute | solution.py:15
  71.6 2.9 %collective-permute-done.18 = bf16[3,256,64]{1,2,0:T(8,128)(2,1)S(1)} collective-permute-done((bf16[3,256,64]{1,2,0:T(8,128)(2,1)S(1)}, bf16[3,256,64]{1,2,0:T(8,128)(2,1)S(1)}, u32[]{:S(2)}, u32[]{:S(2)}) %collective-permute-start.18) | collective-permute-done | bytes 98336 | tf_op jit(solution)/shard_map/ppermute | solution.py:15
  74.4 2.6 %collective-permute-done.19 = bf16[3,256,64]{1,2,0:T(8,128)(2,1)S(1)} collective-permute-done((bf16[3,256,64]{1,2,0:T(8,128)(2,1)S(1)}, bf16[3,256,64]{1,2,0:T(8,128)(2,1)S(1)}, u32[]{:S(2)}, u32[]{:S(2)}) %collective-permute-start.19) | collective-permute-done | bytes 98336 | tf_op jit(solution)/shard_map/ppermute | solution.py:15
  77.8 2.2 %collective-permute-start.21 = (bf16[3,256,64]{1,2,0:T(8,128)(2,1)S(1)}, bf16[3,256,64]{1,2,0:T(8,128)(2,1)S(1)}, u32[]{:S(2)}, u32[]{:S(2)}) collective-permute-start(bf16[3,256,64]{1,2,0:T(8,128)(2,1)S(1)} %get-tuple-element.47), channel_id=1, source_target_pairs={{0,4},{4,8},{8,12},{12,0},{1,5},{5,9},{9,13},{13,1},{2,6},{6,10},{... | collective-permute-start | bytes 294920 | tf_op jit(solution)/shard_map/ppermute | solution.py:15
  82.5 2.9 %collective-permute-done.21 = bf16[3,256,64]{1,2,0:T(8,128)(2,1)S(1)} collective-permute-done((bf16[3,256,64]{1,2,0:T(8,128)(2,1)S(1)}, bf16[3,256,64]{1,2,0:T(8,128)(2,1)S(1)}, u32[]{:S(2)}, u32[]{:S(2)}) %collective-permute-start.21) | collective-permute-done | bytes 98336 | tf_op jit(solution)/shard_map/ppermute | solution.py:15
  85.4 3.0 %collective-permute-done.22 = bf16[3,256,64]{1,2,0:T(8,128)(2,1)S(1)} collective-permute-done((bf16[3,256,64]{1,2,0:T(8,128)(2,1)S(1)}, bf16[3,256,64]{1,2,0:T(8,128)(2,1)S(1)}, u32[]{:S(2)}, u32[]{:S(2)}) %collective-permute-start.22) | collective-permute-done | bytes 98336 | tf_op jit(solution)/shard_map/ppermute | solution.py:15
  90.1 2.6 %collective-permute-start.24 = (bf16[3,256,64]{1,2,0:T(8,128)(2,1)S(1)}, bf16[3,256,64]{1,2,0:T(8,128)(2,1)S(1)}, u32[]{:S(2)}, u32[]{:S(2)}) collective-permute-start(bf16[3,256,64]{1,2,0:T(8,128)(2,1)S(1)} %get-tuple-element.76), channel_id=1, source_target_pairs={{0,4},{4,8},{8,12},{12,0},{1,5},{5,9},{9,13},{13,1},{2,6},{6,10},{... | collective-permute-start | bytes 294920 | tf_op jit(solution)/shard_map/ppermute | solution.py:15
  97.5 3.4 %collective-permute-done.25 = bf16[3,256,64]{1,2,0:T(8,128)(2,1)S(1)} collective-permute-done((bf16[3,256,64]{1,2,0:T(8,128)(2,1)S(1)}, bf16[3,256,64]{1,2,0:T(8,128)(2,1)S(1)}, u32[]{:S(2)}, u32[]{:S(2)}) %collective-permute-start.25) | collective-permute-done | bytes 98336 | tf_op jit(solution)/shard_map/ppermute | solution.py:15
  102.0 7.6 %collective-permute-done.16 = bf16[2,512,256]{2,1,0:T(8,128)(2,1)S(1)} collective-permute-done((bf16[2,512,256]{2,1,0:T(8,128)(2,1)S(1)}, bf16[2,512,256]{2,1,0:T(8,128)(2,1)S(1)}, u32[]{:S(2)}, u32[]{:S(2)}) %collective-permute-start.16) | collective-permute-done | bytes 524320 | tf_op jit(solution)/shard_map/ppermute | solution.py:15
  110.7 3.1 %collective-permute-start.29 = (bf16[3,256,64]{1,2,0:T(8,128)(2,1)S(1)}, bf16[3,256,64]{1,2,0:T(8,128)(2,1)S(1)}, u32[]{:S(2)}, u32[]{:S(2)}) collective-permute-start(bf16[3,256,64]{1,2,0:T(8,128)(2,1)S(1)} %multiply_convert_fusion.20), channel_id=1, source_target_pairs={{0,10},{2,8},{4,14},{6,12},{8,2},{10,0},{12,6},{14,4},{1,11},{3,9}... | collective-permute-start | bytes 294920 | tf_op jit(solution)/shard_map/ppermute | solution.py:50
  115.5 2.6 %collective-permute-done.28 = bf16[3,256,64]{1,2,0:T(8,128)(2,1)S(1)} collective-permute-done((bf16[3,256,64]{1,2,0:T(8,128)(2,1)S(1)}, bf16[3,256,64]{1,2,0:T(8,128)(2,1)S(1)}, u32[]{:S(2)}, u32[]{:S(2)}) %collective-permute-start.28) | collective-permute-done | bytes 98336 | tf_op jit(solution)/shard_map/ppermute | solution.py:50
  127.2 2.3 %convolution_convert_fusion.6 = bf16[512,256]{1,0:T(8,128)(2,1)} fusion(f32[512,256]{1,0:T(8,128)} %convolution_bitcast_fusion.10, bf16[2,512,256]{2,1,0:T(8,128)(2,1)} %copy-done.2, bf16[3,256,256]{1,2,0:T(8,128)(2,1)S(1)} %constant_dynamic-update-slice_fusion.16), kind=kOutput, calls=%fused_computation.19 | convolution fusion | flops 135135232 | bytes 1310720 | tf_op jit(solution)/shard_map/th,hd->td/dot_general | solution.py:81
  130.5 2.4 %collective-permute-done.33 = bf16[3,256,64]{1,2,0:T(8,128)(2,1)S(1)} collective-permute-done((bf16[3,256,64]{1,2,0:T(8,128)(2,1)}, bf16[3,256,64]{1,2,0:T(8,128)(2,1)S(1)}, u32[]{:S(2)}, u32[]{:S(2)}) %collective-permute-start.33) | collective-permute-done | bytes 98336 | tf_op jit(solution)/shard_map/ppermute | solution.py:15
  140.2 2.2 %collective-permute-done.35 = bf16[3,256,64]{1,2,0:T(8,128)(2,1)S(1)} collective-permute-done((bf16[3,256,64]{1,2,0:T(8,128)(2,1)S(1)}, bf16[3,256,64]{1,2,0:T(8,128)(2,1)S(1)}, u32[]{:S(2)}, u32[]{:S(2)}) %collective-permute-start.35) | collective-permute-done | bytes 98336 | tf_op jit(solution)/shard_map/ppermute | solution.py:15
  142.4 2.6 %collective-permute-done.36 = bf16[3,256,64]{1,2,0:T(8,128)(2,1)S(1)} collective-permute-done((bf16[3,256,64]{1,2,0:T(8,128)(2,1)S(1)}, bf16[3,256,64]{1,2,0:T(8,128)(2,1)S(1)}, u32[]{:S(2)}, u32[]{:S(2)}) %collective-permute-start.36) | collective-permute-done | bytes 98336 | tf_op jit(solution)/shard_map/ppermute | solution.py:15
  154.5 2.7 %collective-permute-done.39 = bf16[3,256,64]{1,2,0:T(8,128)(2,1)S(1)} collective-permute-done((bf16[3,256,64]{1,2,0:T(8,128)(2,1)S(1)}, bf16[3,256,64]{1,2,0:T(8,128)(2,1)S(1)}, u32[]{:S(2)}, u32[]{:S(2)}) %collective-permute-start.39) | collective-permute-done | bytes 98336 | tf_op jit(solution)/shard_map/ppermute | solution.py:15
  163.4 2.6 %collective-permute-done.41 = bf16[3,256,64]{1,2,0:T(8,128)(2,1)S(1)} collective-permute-done((bf16[3,256,64]{1,2,0:T(8,128)(2,1)S(1)}, bf16[3,256,64]{1,2,0:T(8,128)(2,1)S(1)}, u32[]{:S(2)}, u32[]{:S(2)}) %collective-permute-start.41) | collective-permute-done | bytes 98336 | tf_op jit(solution)/shard_map/ppermute | solution.py:15
  166.1 2.7 %collective-permute-done.42 = bf16[3,256,64]{1,2,0:T(8,128)(2,1)S(1)} collective-permute-done((bf16[3,256,64]{1,2,0:T(8,128)(2,1)S(1)}, bf16[3,256,64]{1,2,0:T(8,128)(2,1)S(1)}, u32[]{:S(2)}, u32[]{:S(2)}) %collective-permute-start.42) | collective-permute-done | bytes 98336 | tf_op jit(solution)/shard_map/ppermute | solution.py:15
  (176 shorter events, 75.0 us)
Async XLA Ops:
  3.7 7.7 %collective-permute-start = (bf16[3,256,64]{1,2,0:T(8,128)(2,1)S(1)}, bf16[3,256,64]{1,2,0:T(8,128)(2,1)S(1)}, u32[]{:S(2)}, u32[]{:S(2)}) collective-permute-start(bf16[3,256,64]{1,2,0:T(8,128)(2,1)S(1)} %get-tuple-element.57), channel_id=1, source_target_pairs={{0,4},{4,8},{8,12},{12,0},{1,5},{5,9},{9,13},{13,1},{2,6},{6,10},{... | collective-permute-start | bytes 294920 | tf_op jit(solution)/shard_map/ppermute | solution.py:15
  17.6 7.6 %collective-permute-start.4 = (bf16[3,256,64]{1,2,0:T(8,128)(2,1)S(1)}, bf16[3,256,64]{1,2,0:T(8,128)(2,1)S(1)}, u32[]{:S(2)}, u32[]{:S(2)}) collective-permute-start(bf16[3,256,64]{1,2,0:T(8,128)(2,1)S(1)} %get-tuple-element.86), channel_id=1, source_target_pairs={{0,8},{4,12},{8,0},{12,4},{1,9},{5,13},{9,1},{13,5},{2,10},{6,14},... | collective-permute-start | bytes 294920 | tf_op jit(solution)/shard_map/ppermute | solution.py:15
  27.1 9.9 %collective-permute-start.7 = (bf16[3,256,64]{1,2,0:T(8,128)(2,1)S(1)}, bf16[3,256,64]{1,2,0:T(8,128)(2,1)S(1)}, u32[]{:S(2)}, u32[]{:S(2)}) collective-permute-start(bf16[3,256,64]{1,2,0:T(8,128)(2,1)S(1)} %get-tuple-element.53), channel_id=1, source_target_pairs={{0,8},{4,12},{8,0},{12,4},{1,9},{5,13},{9,1},{13,5},{2,10},{6,14},... | collective-permute-start | bytes 294920 | tf_op jit(solution)/shard_map/ppermute | solution.py:15
  29.3 7.8 %collective-permute-start.8 = (bf16[3,256,64]{1,2,0:T(8,128)(2,1)S(1)}, bf16[3,256,64]{1,2,0:T(8,128)(2,1)S(1)}, u32[]{:S(2)}, u32[]{:S(2)}) collective-permute-start(bf16[3,256,64]{1,2,0:T(8,128)(2,1)S(1)} %get-tuple-element.53), channel_id=1, source_target_pairs={{0,12},{4,0},{8,4},{12,8},{1,13},{5,1},{9,5},{13,9},{2,14},{6,2},{... | collective-permute-start | bytes 294920 | tf_op jit(solution)/shard_map/ppermute | solution.py:15
  43.7 7.8 %collective-permute-start.9 = (bf16[3,256,64]{1,2,0:T(8,128)(2,1)S(1)}, bf16[3,256,64]{1,2,0:T(8,128)(2,1)S(1)}, u32[]{:S(2)}, u32[]{:S(2)}) collective-permute-start(bf16[3,256,64]{1,2,0:T(8,128)(2,1)S(1)} %get-tuple-element.82), channel_id=1, source_target_pairs={{0,4},{4,8},{8,12},{12,0},{1,5},{5,9},{9,13},{13,1},{2,6},{6,10},{... | collective-permute-start | bytes 294920 | tf_op jit(solution)/shard_map/ppermute | solution.py:15
  51.8 7.7 %collective-permute-start.12 = (bf16[3,256,64]{1,2,0:T(8,128)(2,1)S(1)}, bf16[3,256,64]{1,2,0:T(8,128)(2,1)S(1)}, u32[]{:S(2)}, u32[]{:S(2)}) collective-permute-start(bf16[3,256,64]{1,2,0:T(8,128)(2,1)S(1)} %multiply_convert_fusion.21), channel_id=1, source_target_pairs={{0,2},{2,0},{4,6},{6,4},{8,10},{10,8},{12,14},{14,12},{1,3},{3,1},... | collective-permute-start | bytes 294920 | tf_op jit(solution)/shard_map/ppermute | solution.py:50
  54.4 8.4 %collective-permute-start.13 = (bf16[3,256,64]{1,2,0:T(8,128)(2,1)S(1)}, bf16[3,256,64]{1,2,0:T(8,128)(2,1)S(1)}, u32[]{:S(2)}, u32[]{:S(2)}) collective-permute-start(bf16[3,256,64]{1,2,0:T(8,128)(2,1)S(1)} %multiply_convert_fusion.21), channel_id=1, source_target_pairs={{0,6},{2,4},{4,10},{6,8},{8,14},{10,12},{12,2},{14,0},{1,7},{3,5},... | collective-permute-start | bytes 294920 | tf_op jit(solution)/shard_map/ppermute | solution.py:50
  54.4 10.7 %collective-permute-start.14 = (bf16[3,256,64]{1,2,0:T(8,128)(2,1)S(1)}, bf16[3,256,64]{1,2,0:T(8,128)(2,1)S(1)}, u32[]{:S(2)}, u32[]{:S(2)}) collective-permute-start(bf16[3,256,64]{1,2,0:T(8,128)(2,1)S(1)} %multiply_convert_fusion.21), channel_id=1, source_target_pairs={{0,10},{2,8},{4,14},{6,12},{8,2},{10,0},{12,6},{14,4},{1,11},{3,9}... | collective-permute-start | bytes 294920 | tf_op jit(solution)/shard_map/ppermute | solution.py:50
  57.5 7.6 %collective-permute-start.15 = (bf16[3,256,64]{1,2,0:T(8,128)(2,1)S(1)}, bf16[3,256,64]{1,2,0:T(8,128)(2,1)S(1)}, u32[]{:S(2)}, u32[]{:S(2)}) collective-permute-start(bf16[3,256,64]{1,2,0:T(8,128)(2,1)S(1)} %multiply_convert_fusion.21), channel_id=1, source_target_pairs={{0,14},{2,12},{4,2},{6,0},{8,6},{10,4},{12,10},{14,8},{1,15},{3,13... | collective-permute-start | bytes 294920 | tf_op jit(solution)/shard_map/ppermute | solution.py:50
  66.8 7.6 %collective-permute-start.18 = (bf16[3,256,64]{1,2,0:T(8,128)(2,1)S(1)}, bf16[3,256,64]{1,2,0:T(8,128)(2,1)S(1)}, u32[]{:S(2)}, u32[]{:S(2)}) collective-permute-start(bf16[3,256,64]{1,2,0:T(8,128)(2,1)S(1)} %get-tuple-element.79), channel_id=1, source_target_pairs={{0,4},{4,8},{8,12},{12,0},{1,5},{5,9},{9,13},{13,1},{2,6},{6,10},{... | collective-permute-start | bytes 294920 | tf_op jit(solution)/shard_map/ppermute | solution.py:15
  68.8 8.3 %collective-permute-start.19 = (bf16[3,256,64]{1,2,0:T(8,128)(2,1)S(1)}, bf16[3,256,64]{1,2,0:T(8,128)(2,1)S(1)}, u32[]{:S(2)}, u32[]{:S(2)}) collective-permute-start(bf16[3,256,64]{1,2,0:T(8,128)(2,1)S(1)} %get-tuple-element.80), channel_id=1, source_target_pairs={{0,8},{4,12},{8,0},{12,4},{1,9},{5,13},{9,1},{13,5},{2,10},{6,14},... | collective-permute-start | bytes 294920 | tf_op jit(solution)/shard_map/ppermute | solution.py:15
  77.8 7.5 %collective-permute-start.21 = (bf16[3,256,64]{1,2,0:T(8,128)(2,1)S(1)}, bf16[3,256,64]{1,2,0:T(8,128)(2,1)S(1)}, u32[]{:S(2)}, u32[]{:S(2)}) collective-permute-start(bf16[3,256,64]{1,2,0:T(8,128)(2,1)S(1)} %get-tuple-element.47), channel_id=1, source_target_pairs={{0,4},{4,8},{8,12},{12,0},{1,5},{5,9},{9,13},{13,1},{2,6},{6,10},{... | collective-permute-start | bytes 294920 | tf_op jit(solution)/shard_map/ppermute | solution.py:15
  80.1 8.4 %collective-permute-start.22 = (bf16[3,256,64]{1,2,0:T(8,128)(2,1)S(1)}, bf16[3,256,64]{1,2,0:T(8,128)(2,1)S(1)}, u32[]{:S(2)}, u32[]{:S(2)}) collective-permute-start(bf16[3,256,64]{1,2,0:T(8,128)(2,1)S(1)} %get-tuple-element.47), channel_id=1, source_target_pairs={{0,8},{4,12},{8,0},{12,4},{1,9},{5,13},{9,1},{13,5},{2,10},{6,14},... | collective-permute-start | bytes 294920 | tf_op jit(solution)/shard_map/ppermute | solution.py:15
  81.5 7.0 %collective-permute-start.23 = (bf16[3,256,64]{1,2,0:T(8,128)(2,1)S(1)}, bf16[3,256,64]{1,2,0:T(8,128)(2,1)S(1)}, u32[]{:S(2)}, u32[]{:S(2)}) collective-permute-start(bf16[3,256,64]{1,2,0:T(8,128)(2,1)S(1)} %get-tuple-element.47), channel_id=1, source_target_pairs={{0,12},{4,0},{8,4},{12,8},{1,13},{5,1},{9,5},{13,9},{2,14},{6,2},{... | collective-permute-start | bytes 294920 | tf_op jit(solution)/shard_map/ppermute | solution.py:15
  90.1 7.4 %collective-permute-start.24 = (bf16[3,256,64]{1,2,0:T(8,128)(2,1)S(1)}, bf16[3,256,64]{1,2,0:T(8,128)(2,1)S(1)}, u32[]{:S(2)}, u32[]{:S(2)}) collective-permute-start(bf16[3,256,64]{1,2,0:T(8,128)(2,1)S(1)} %get-tuple-element.76), channel_id=1, source_target_pairs={{0,4},{4,8},{8,12},{12,0},{1,5},{5,9},{9,13},{13,1},{2,6},{6,10},{... | collective-permute-start | bytes 294920 | tf_op jit(solution)/shard_map/ppermute | solution.py:15
  92.7 8.2 %collective-permute-start.25 = (bf16[3,256,64]{1,2,0:T(8,128)(2,1)S(1)}, bf16[3,256,64]{1,2,0:T(8,128)(2,1)S(1)}, u32[]{:S(2)}, u32[]{:S(2)}) collective-permute-start(bf16[3,256,64]{1,2,0:T(8,128)(2,1)S(1)} %get-tuple-element.77), channel_id=1, source_target_pairs={{0,8},{4,12},{8,0},{12,4},{1,9},{5,13},{9,1},{13,5},{2,10},{6,14},... | collective-permute-start | bytes 294920 | tf_op jit(solution)/shard_map/ppermute | solution.py:15
  94.0 6.9 %collective-permute-start.26 = (bf16[3,256,64]{1,2,0:T(8,128)(2,1)S(1)}, bf16[3,256,64]{1,2,0:T(8,128)(2,1)S(1)}, u32[]{:S(2)}, u32[]{:S(2)}) collective-permute-start(bf16[3,256,64]{1,2,0:T(8,128)(2,1)S(1)} %get-tuple-element.78), channel_id=1, source_target_pairs={{0,12},{4,0},{8,4},{12,8},{1,13},{5,1},{9,5},{13,9},{2,14},{6,2},{... | collective-permute-start | bytes 294920 | tf_op jit(solution)/shard_map/ppermute | solution.py:15
  95.2 14.4 %collective-permute-start.16 = (bf16[2,512,256]{2,1,0:T(8,128)(2,1)S(1)}, bf16[2,512,256]{2,1,0:T(8,128)(2,1)S(1)}, u32[]{:S(2)}, u32[]{:S(2)}) collective-permute-start(bf16[2,512,256]{2,1,0:T(8,128)(2,1)S(1)} %slice_bitcast_fusion), channel_id=1, source_target_pairs={{0,2},{2,0},{1,3},{3,1},{4,6},{6,4},{5,7},{7,5},{8,10},{10,8},{9,1... | collective-permute-start | bytes 1572872 | tf_op jit(solution)/shard_map/ppermute | solution.py:15
  101.3 14.1 %collective-permute-start.27 = (bf16[3,256,64]{1,2,0:T(8,128)(2,1)S(1)}, bf16[3,256,64]{1,2,0:T(8,128)(2,1)S(1)}, u32[]{:S(2)}, u32[]{:S(2)}) collective-permute-start(bf16[3,256,64]{1,2,0:T(8,128)(2,1)S(1)} %multiply_convert_fusion.20), channel_id=1, source_target_pairs={{0,2},{2,0},{4,6},{6,4},{8,10},{10,8},{12,14},{14,12},{1,3},{3,1},... | collective-permute-start | bytes 294920 | tf_op jit(solution)/shard_map/ppermute | solution.py:50
  110.7 7.4 %collective-permute-start.28 = (bf16[3,256,64]{1,2,0:T(8,128)(2,1)S(1)}, bf16[3,256,64]{1,2,0:T(8,128)(2,1)S(1)}, u32[]{:S(2)}, u32[]{:S(2)}) collective-permute-start(bf16[3,256,64]{1,2,0:T(8,128)(2,1)S(1)} %multiply_convert_fusion.20), channel_id=1, source_target_pairs={{0,6},{2,4},{4,10},{6,8},{8,14},{10,12},{12,2},{14,0},{1,7},{3,5},... | collective-permute-start | bytes 294920 | tf_op jit(solution)/shard_map/ppermute | solution.py:50
  110.7 9.4 %collective-permute-start.29 = (bf16[3,256,64]{1,2,0:T(8,128)(2,1)S(1)}, bf16[3,256,64]{1,2,0:T(8,128)(2,1)S(1)}, u32[]{:S(2)}, u32[]{:S(2)}) collective-permute-start(bf16[3,256,64]{1,2,0:T(8,128)(2,1)S(1)} %multiply_convert_fusion.20), channel_id=1, source_target_pairs={{0,10},{2,8},{4,14},{6,12},{8,2},{10,0},{12,6},{14,4},{1,11},{3,9}... | collective-permute-start | bytes 294920 | tf_op jit(solution)/shard_map/ppermute | solution.py:50
  123.3 7.2 %collective-permute-start.32 = (bf16[3,256,64]{1,2,0:T(8,128)(2,1)}, bf16[3,256,64]{1,2,0:T(8,128)(2,1)S(1)}, u32[]{:S(2)}, u32[]{:S(2)}) collective-permute-start(bf16[3,256,64]{1,2,0:T(8,128)(2,1)} %get-tuple-element.73), channel_id=1, source_target_pairs={{0,4},{4,8},{8,12},{12,0},{1,5},{5,9},{9,13},{13,1},{2,6},{6,10},{... | collective-permute-start | bytes 294920 | tf_op jit(solution)/shard_map/ppermute | solution.py:15
  124.9 8.1 %collective-permute-start.33 = (bf16[3,256,64]{1,2,0:T(8,128)(2,1)}, bf16[3,256,64]{1,2,0:T(8,128)(2,1)S(1)}, u32[]{:S(2)}, u32[]{:S(2)}) collective-permute-start(bf16[3,256,64]{1,2,0:T(8,128)(2,1)} %get-tuple-element.74), channel_id=1, source_target_pairs={{0,8},{4,12},{8,0},{12,4},{1,9},{5,13},{9,1},{13,5},{2,10},{6,14},... | collective-permute-start | bytes 294920 | tf_op jit(solution)/shard_map/ppermute | solution.py:15
  126.4 7.2 %collective-permute-start.34 = (bf16[3,256,64]{1,2,0:T(8,128)(2,1)S(1)}, bf16[3,256,64]{1,2,0:T(8,128)(2,1)}, u32[]{:S(2)}, u32[]{:S(2)}) collective-permute-start(bf16[3,256,64]{1,2,0:T(8,128)(2,1)S(1)} %get-tuple-element.75), channel_id=1, source_target_pairs={{0,12},{4,0},{8,4},{12,8},{1,13},{5,1},{9,5},{13,9},{2,14},{6,2},{... | collective-permute-start | bytes 294920 | tf_op jit(solution)/shard_map/ppermute | solution.py:15
  129.5 40.0 %collective-permute-start.17 = (bf16[512,256]{1,0:T(8,128)(2,1)}, bf16[512,256]{1,0:T(8,128)(2,1)}, u32[]{:S(2)}, u32[]{:S(2)}) collective-permute-start(bf16[512,256]{1,0:T(8,128)(2,1)} %convolution_convert_fusion.6), channel_id=1, source_target_pairs={{0,2},{2,0},{1,3},{3,1},{4,6},{6,4},{5,7},{7,5},{8,10},{10,8},{9,1... | collective-permute-start | bytes 786440 | tf_op jit(solution)/shard_map/ppermute | solution.py:15
  134.9 7.5 %collective-permute-start.35 = (bf16[3,256,64]{1,2,0:T(8,128)(2,1)S(1)}, bf16[3,256,64]{1,2,0:T(8,128)(2,1)S(1)}, u32[]{:S(2)}, u32[]{:S(2)}) collective-permute-start(bf16[3,256,64]{1,2,0:T(8,128)(2,1)S(1)} %get-tuple-element.41), channel_id=1, source_target_pairs={{0,4},{4,8},{8,12},{12,0},{1,5},{5,9},{9,13},{13,1},{2,6},{6,10},{... | collective-permute-start | bytes 294920 | tf_op jit(solution)/shard_map/ppermute | solution.py:15
  137.1 8.0 %collective-permute-start.36 = (bf16[3,256,64]{1,2,0:T(8,128)(2,1)S(1)}, bf16[3,256,64]{1,2,0:T(8,128)(2,1)S(1)}, u32[]{:S(2)}, u32[]{:S(2)}) collective-permute-start(bf16[3,256,64]{1,2,0:T(8,128)(2,1)S(1)} %get-tuple-element.41), channel_id=1, source_target_pairs={{0,8},{4,12},{8,0},{12,4},{1,9},{5,13},{9,1},{13,5},{2,10},{6,14},... | collective-permute-start | bytes 294920 | tf_op jit(solution)/shard_map/ppermute | solution.py:15
  147.5 7.0 %collective-permute-start.38 = (bf16[3,256,64]{1,2,0:T(8,128)(2,1)S(1)}, bf16[3,256,64]{1,2,0:T(8,128)(2,1)S(1)}, u32[]{:S(2)}, u32[]{:S(2)}) collective-permute-start(bf16[3,256,64]{1,2,0:T(8,128)(2,1)S(1)} %get-tuple-element.70), channel_id=1, source_target_pairs={{0,4},{4,8},{8,12},{12,0},{1,5},{5,9},{9,13},{13,1},{2,6},{6,10},{... | collective-permute-start | bytes 294920 | tf_op jit(solution)/shard_map/ppermute | solution.py:15
  149.2 8.0 %collective-permute-start.39 = (bf16[3,256,64]{1,2,0:T(8,128)(2,1)S(1)}, bf16[3,256,64]{1,2,0:T(8,128)(2,1)S(1)}, u32[]{:S(2)}, u32[]{:S(2)}) collective-permute-start(bf16[3,256,64]{1,2,0:T(8,128)(2,1)S(1)} %get-tuple-element.71), channel_id=1, source_target_pairs={{0,8},{4,12},{8,0},{12,4},{1,9},{5,13},{9,1},{13,5},{2,10},{6,14},... | collective-permute-start | bytes 294920 | tf_op jit(solution)/shard_map/ppermute | solution.py:15
  152.8 16.7 %collective-permute-start.31 = (bf16[512,256]{1,0:T(8,128)(2,1)}, bf16[512,256]{1,0:T(8,128)(2,1)S(1)}, u32[]{:S(2)}, u32[]{:S(2)}) collective-permute-start(bf16[512,256]{1,0:T(8,128)(2,1)} %convolution_convert_fusion.3), channel_id=1, source_target_pairs={{0,2},{2,0},{1,3},{3,1},{4,6},{6,4},{5,7},{7,5},{8,10},{10,8},{9,1... | collective-permute-start | bytes 786440 | tf_op jit(solution)/shard_map/ppermute | solution.py:15
  158.5 7.6 %collective-permute-start.41 = (bf16[3,256,64]{1,2,0:T(8,128)(2,1)S(1)}, bf16[3,256,64]{1,2,0:T(8,128)(2,1)S(1)}, u32[]{:S(2)}, u32[]{:S(2)}) collective-permute-start(bf16[3,256,64]{1,2,0:T(8,128)(2,1)S(1)} %get-tuple-element.37), channel_id=1, source_target_pairs={{0,4},{4,8},{8,12},{12,0},{1,5},{5,9},{9,13},{13,1},{2,6},{6,10},{... | collective-permute-start | bytes 294920 | tf_op jit(solution)/shard_map/ppermute | solution.py:15
  161.0 7.7 %collective-permute-start.42 = (bf16[3,256,64]{1,2,0:T(8,128)(2,1)S(1)}, bf16[3,256,64]{1,2,0:T(8,128)(2,1)S(1)}, u32[]{:S(2)}, u32[]{:S(2)}) collective-permute-start(bf16[3,256,64]{1,2,0:T(8,128)(2,1)S(1)} %get-tuple-element.37), channel_id=1, source_target_pairs={{0,8},{4,12},{8,0},{12,4},{1,9},{5,13},{9,1},{13,5},{2,10},{6,14},... | collective-permute-start | bytes 294920 | tf_op jit(solution)/shard_map/ppermute | solution.py:15
  (23 other events, 115.0 us)

commit v10 on v8

--- a/solution.py
+++ b/solution.py
@@ -7,6 +7,7 @@
 
 
 ITERS = 2
+DELAY_STEPS = 60
 
 
 def rotated(value, axis, by):
@@ -96,6 +97,11 @@
     tick_count = key_rows.shape[0]
     results = []
     weights = states_in[0, 0]
+    anchor = jnp.abs(weights[0, 0, 0]) + 1.0
+    unit = anchor / anchor
+    weights = lax.fori_loop(
+        0, lax.axis_index("head") * DELAY_STEPS, lambda step, held: held * unit, weights
+    )
     fast = gather_cols(weights.astype(jnp.bfloat16), part_cols)
     arrived = None
     earlier_queries = rotated(query_rows[: tick_count - 1, 0, :, 0], "span", 1)

time: 170 us -> 169 us (level)
  starting transfers between devices: 71.8 us -> 68.7 us
    ppermute x36, starting transfers between devices: 57.9 us -> 55.6 us  [rotated(): lax.ppermute(value, axis, [(i, (i + by) % devices) for i in range(devices)])]
  transfers between devices with their start and end apart: 44 -> 44, of which waited for: 28 -> 29; matrix products, arithmetic and copies ran while one was open for 6% -> 6% of each run, Pallas kernels for 0% -> 0%
where the time goes in v10:
time: 169 us
  waiting for transfers between devices  71 us (42%)
  starting transfers between devices  68.7 us (41%)
  matrix products  16.8 us (10%)
  other arithmetic  6.22 us (4%)
  local copies, waits for them, and re-layouts  3.9 us (2%)
  between operations  2.27 us (1%)
    ppermute x36, waiting for transfers between devices, rotated(): lax.ppermute(value, axis, [(i, (i + by) % devices) for i in range(devices)])  60.5 us
    ppermute x36, starting transfers between devices, rotated(): lax.ppermute(value, axis, [(i, (i + by) % devices) for i in range(devices)])  55.6 us
    ppermute x8, starting transfers between devices, cross_gather(): got = lax.ppermute(own, ('tok', 'span'), pairs)  13.1 us
    ppermute x8, waiting for transfers between devices, cross_gather(): got = lax.ppermute(own, ('tok', 'span'), pairs)  10.5 us
  transfers between devices with their start and end apart: 44, of which 29 were waited for; matrix products, arithmetic and copies ran while one was open for 6% of the time, Pallas kernels for 0%

profile of v10, /device:TPU:0, one launch (start us, length us, event | category | flops | bytes accessed | tf_op | source)
XLA Modules:
  0.0 168.9 jit_solution(2620366956803780399)
XLA Ops:
  3.2 3.1 %collective-permute-start = (bf16[3,256,64]{1,2,0:T(8,128)(2,1)S(1)}, bf16[3,256,64]{1,2,0:T(8,128)(2,1)S(1)}, u32[]{:S(2)}, u32[]{:S(2)}) collective-permute-start(bf16[3,256,64]{1,2,0:T(8,128)(2,1)S(1)} %get-tuple-element.57), channel_id=1, source_target_pairs={{0,4},{4,8},{8,12},{12,0},{1,5},{5,9},{9,13},{13,1},{2,6},{6,10},{... | collective-permute-start | bytes 294920 | tf_op jit(solution)/shard_map/ppermute | solution.py:15
  6.3 2.6 %collective-permute-start.1 = (bf16[3,256,64]{1,2,0:T(8,128)(2,1)S(1)}, bf16[3,256,64]{1,2,0:T(8,128)(2,1)S(1)}, u32[]{:S(2)}, u32[]{:S(2)}) collective-permute-start(bf16[3,256,64]{1,2,0:T(8,128)(2,1)S(1)} %get-tuple-element.57), channel_id=1, source_target_pairs={{0,8},{4,12},{8,0},{12,4},{1,9},{5,13},{9,1},{13,5},{2,10},{6,14},... | collective-permute-start | bytes 294920 | tf_op jit(solution)/shard_map/ppermute | solution.py:15
  11.0 2.2 %collective-permute-done.1 = bf16[3,256,64]{1,2,0:T(8,128)(2,1)S(1)} collective-permute-done((bf16[3,256,64]{1,2,0:T(8,128)(2,1)S(1)}, bf16[3,256,64]{1,2,0:T(8,128)(2,1)S(1)}, u32[]{:S(2)}, u32[]{:S(2)}) %collective-permute-start.1) | collective-permute-done | bytes 98336 | tf_op jit(solution)/shard_map/ppermute | solution.py:15
  17.5 2.6 %collective-permute-start.4 = (bf16[3,256,64]{1,2,0:T(8,128)(2,1)S(1)}, bf16[3,256,64]{1,2,0:T(8,128)(2,1)S(1)}, u32[]{:S(2)}, u32[]{:S(2)}) collective-permute-start(bf16[3,256,64]{1,2,0:T(8,128)(2,1)S(1)} %get-tuple-element.75), channel_id=1, source_target_pairs={{0,8},{4,12},{8,0},{12,4},{1,9},{5,13},{9,1},{13,5},{2,10},{6,14},... | collective-permute-start | bytes 294920 | tf_op jit(solution)/shard_map/ppermute | solution.py:15
  20.5 2.5 %collective-permute-done.3 = bf16[3,256,64]{1,2,0:T(8,128)(2,1)S(1)} collective-permute-done((bf16[3,256,64]{1,2,0:T(8,128)(2,1)S(1)}, bf16[3,256,64]{1,2,0:T(8,128)(2,1)S(1)}, u32[]{:S(2)}, u32[]{:S(2)}) %collective-permute-start.3) | collective-permute-done | bytes 98336 | tf_op jit(solution)/shard_map/ppermute | solution.py:15
  23.0 2.1 %collective-permute-done.4 = bf16[3,256,64]{1,2,0:T(8,128)(2,1)S(1)} collective-permute-done((bf16[3,256,64]{1,2,0:T(8,128)(2,1)S(1)}, bf16[3,256,64]{1,2,0:T(8,128)(2,1)S(1)}, u32[]{:S(2)}, u32[]{:S(2)}) %collective-permute-start.4) | collective-permute-done | bytes 98336 | tf_op jit(solution)/shard_map/ppermute | solution.py:15
  27.0 2.1 %collective-permute-start.7 = (bf16[3,256,64]{1,2,0:T(8,128)(2,1)S(1)}, bf16[3,256,64]{1,2,0:T(8,128)(2,1)S(1)}, u32[]{:S(2)}, u32[]{:S(2)}) collective-permute-start(bf16[3,256,64]{1,2,0:T(8,128)(2,1)S(1)} %get-tuple-element.53), channel_id=1, source_target_pairs={{0,8},{4,12},{8,0},{12,4},{1,9},{5,13},{9,1},{13,5},{2,10},{6,14},... | collective-permute-start | bytes 294920 | tf_op jit(solution)/shard_map/ppermute | solution.py:15
  29.9 2.7 %collective-permute-done.6 = bf16[3,256,64]{1,2,0:T(8,128)(2,1)S(1)} collective-permute-done((bf16[3,256,64]{1,2,0:T(8,128)(2,1)S(1)}, bf16[3,256,64]{1,2,0:T(8,128)(2,1)S(1)}, u32[]{:S(2)}, u32[]{:S(2)}) %collective-permute-start.6) | collective-permute-done | bytes 98336 | tf_op jit(solution)/shard_map/ppermute | solution.py:15
  32.6 4.4 %collective-permute-done.7 = bf16[3,256,64]{1,2,0:T(8,128)(2,1)S(1)} collective-permute-done((bf16[3,256,64]{1,2,0:T(8,128)(2,1)S(1)}, bf16[3,256,64]{1,2,0:T(8,128)(2,1)S(1)}, u32[]{:S(2)}, u32[]{:S(2)}) %collective-permute-start.7) | collective-permute-done | bytes 98336 | tf_op jit(solution)/shard_map/ppermute | solution.py:15
  40.7 3.4 %collective-permute-start.11 = (bf16[3,256,64]{1,2,0:T(8,128)(2,1)S(1)}, bf16[3,256,64]{1,2,0:T(8,128)(2,1)S(1)}, u32[]{:S(2)}, u32[]{:S(2)}) collective-permute-start(bf16[3,256,64]{1,2,0:T(8,128)(2,1)S(1)} %get-tuple-element.71), channel_id=1, source_target_pairs={{0,12},{4,0},{8,4},{12,8},{1,13},{5,1},{9,5},{13,9},{2,14},{6,2},{... | collective-permute-start | bytes 294920 | tf_op jit(solution)/shard_map/ppermute | solution.py:15
  45.1 2.5 %collective-permute-done.11 = bf16[3,256,64]{1,2,0:T(8,128)(2,1)S(1)} collective-permute-done((bf16[3,256,64]{1,2,0:T(8,128)(2,1)S(1)}, bf16[3,256,64]{1,2,0:T(8,128)(2,1)S(1)}, u32[]{:S(2)}, u32[]{:S(2)}) %collective-permute-start.11) | collective-permute-done | bytes 98336 | tf_op jit(solution)/shard_map/ppermute | solution.py:15
  47.7 4.2 %collective-permute-done.9 = bf16[3,256,64]{1,2,0:T(8,128)(2,1)S(1)} collective-permute-done((bf16[3,256,64]{1,2,0:T(8,128)(2,1)S(1)}, bf16[3,256,64]{1,2,0:T(8,128)(2,1)S(1)}, u32[]{:S(2)}, u32[]{:S(2)}) %collective-permute-start.9) | collective-permute-done | bytes 98336 | tf_op jit(solution)/shard_map/ppermute | solution.py:15
  53.6 2.7 %collective-permute-start.14 = (bf16[3,256,64]{1,2,0:T(8,128)(2,1)S(1)}, bf16[3,256,64]{1,2,0:T(8,128)(2,1)S(1)}, u32[]{:S(2)}, u32[]{:S(2)}) collective-permute-start(bf16[3,256,64]{1,2,0:T(8,128)(2,1)S(1)} %multiply_convert_fusion.42), channel_id=1, source_target_pairs={{0,10},{2,8},{4,14},{6,12},{8,2},{10,0},{12,6},{14,4},{1,11},{3,9}... | collective-permute-start | bytes 294920 | tf_op jit(solution)/shard_map/ppermute | solution.py:50
  56.3 3.0 %collective-permute-start.15 = (bf16[3,256,64]{1,2,0:T(8,128)(2,1)S(1)}, bf16[3,256,64]{1,2,0:T(8,128)(2,1)S(1)}, u32[]{:S(2)}, u32[]{:S(2)}) collective-permute-start(bf16[3,256,64]{1,2,0:T(8,128)(2,1)S(1)} %multiply_convert_fusion.42), channel_id=1, source_target_pairs={{0,14},{2,12},{4,2},{6,0},{8,6},{10,4},{12,10},{14,8},{1,15},{3,13... | collective-permute-start | bytes 294920 | tf_op jit(solution)/shard_map/ppermute | solution.py:50
  59.4 2.6 %collective-permute-done.13 = bf16[3,256,64]{1,2,0:T(8,128)(2,1)S(1)} collective-permute-done((bf16[3,256,64]{1,2,0:T(8,128)(2,1)S(1)}, bf16[3,256,64]{1,2,0:T(8,128)(2,1)S(1)}, u32[]{:S(2)}, u32[]{:S(2)}) %collective-permute-start.13) | collective-permute-done | bytes 98336 | tf_op jit(solution)/shard_map/ppermute | solution.py:50
  62.0 3.1 %collective-permute-done.14 = bf16[3,256,64]{1,2,0:T(8,128)(2,1)S(1)} collective-permute-done((bf16[3,256,64]{1,2,0:T(8,128)(2,1)S(1)}, bf16[3,256,64]{1,2,0:T(8,128)(2,1)S(1)}, u32[]{:S(2)}, u32[]{:S(2)}) %collective-permute-start.14) | collective-permute-done | bytes 98336 | tf_op jit(solution)/shard_map/ppermute | solution.py:50
  71.9 2.9 %collective-permute-done.18 = bf16[3,256,64]{1,2,0:T(8,128)(2,1)S(1)} collective-permute-done((bf16[3,256,64]{1,2,0:T(8,128)(2,1)S(1)}, bf16[3,256,64]{1,2,0:T(8,128)(2,1)S(1)}, u32[]{:S(2)}, u32[]{:S(2)}) %collective-permute-start.18) | collective-permute-done | bytes 98336 | tf_op jit(solution)/shard_map/ppermute | solution.py:15
  74.8 2.7 %collective-permute-done.19 = bf16[3,256,64]{1,2,0:T(8,128)(2,1)S(1)} collective-permute-done((bf16[3,256,64]{1,2,0:T(8,128)(2,1)S(1)}, bf16[3,256,64]{1,2,0:T(8,128)(2,1)S(1)}, u32[]{:S(2)}, u32[]{:S(2)}) %collective-permute-start.19) | collective-permute-done | bytes 98336 | tf_op jit(solution)/shard_map/ppermute | solution.py:15
  77.9 2.4 %collective-permute-start.21 = (bf16[3,256,64]{1,2,0:T(8,128)(2,1)S(1)}, bf16[3,256,64]{1,2,0:T(8,128)(2,1)S(1)}, u32[]{:S(2)}, u32[]{:S(2)}) collective-permute-start(bf16[3,256,64]{1,2,0:T(8,128)(2,1)S(1)} %get-tuple-element.47), channel_id=1, source_target_pairs={{0,4},{4,8},{8,12},{12,0},{1,5},{5,9},{9,13},{13,1},{2,6},{6,10},{... | collective-permute-start | bytes 294920 | tf_op jit(solution)/shard_map/ppermute | solution.py:15
  82.8 2.7 %collective-permute-done.21 = bf16[3,256,64]{1,2,0:T(8,128)(2,1)S(1)} collective-permute-done((bf16[3,256,64]{1,2,0:T(8,128)(2,1)S(1)}, bf16[3,256,64]{1,2,0:T(8,128)(2,1)S(1)}, u32[]{:S(2)}, u32[]{:S(2)}) %collective-permute-start.21) | collective-permute-done | bytes 98336 | tf_op jit(solution)/shard_map/ppermute | solution.py:15
  85.5 3.1 %collective-permute-done.22 = bf16[3,256,64]{1,2,0:T(8,128)(2,1)S(1)} collective-permute-done((bf16[3,256,64]{1,2,0:T(8,128)(2,1)S(1)}, bf16[3,256,64]{1,2,0:T(8,128)(2,1)S(1)}, u32[]{:S(2)}, u32[]{:S(2)}) %collective-permute-start.22) | collective-permute-done | bytes 98336 | tf_op jit(solution)/shard_map/ppermute | solution.py:15
  90.7 2.6 %collective-permute-start.24 = (bf16[3,256,64]{1,2,0:T(8,128)(2,1)S(1)}, bf16[3,256,64]{1,2,0:T(8,128)(2,1)S(1)}, u32[]{:S(2)}, u32[]{:S(2)}) collective-permute-start(bf16[3,256,64]{1,2,0:T(8,128)(2,1)S(1)} %get-tuple-element.64), channel_id=1, source_target_pairs={{0,4},{4,8},{8,12},{12,0},{1,5},{5,9},{9,13},{13,1},{2,6},{6,10},{... | collective-permute-start | bytes 294920 | tf_op jit(solution)/shard_map/ppermute | solution.py:15
  98.1 3.4 %collective-permute-done.25 = bf16[3,256,64]{1,2,0:T(8,128)(2,1)S(1)} collective-permute-done((bf16[3,256,64]{1,2,0:T(8,128)(2,1)S(1)}, bf16[3,256,64]{1,2,0:T(8,128)(2,1)S(1)}, u32[]{:S(2)}, u32[]{:S(2)}) %collective-permute-start.25) | collective-permute-done | bytes 98336 | tf_op jit(solution)/shard_map/ppermute | solution.py:15
  103.0 7.2 %collective-permute-done.16 = bf16[2,512,256]{2,1,0:T(8,128)(2,1)S(1)} collective-permute-done((bf16[2,512,256]{2,1,0:T(8,128)(2,1)S(1)}, bf16[2,512,256]{2,1,0:T(8,128)(2,1)S(1)}, u32[]{:S(2)}, u32[]{:S(2)}) %collective-permute-start.16) | collective-permute-done | bytes 524320 | tf_op jit(solution)/shard_map/ppermute | solution.py:15
  111.8 2.6 %collective-permute-start.29 = (bf16[3,256,64]{1,2,0:T(8,128)(2,1)S(1)}, bf16[3,256,64]{1,2,0:T(8,128)(2,1)S(1)}, u32[]{:S(2)}, u32[]{:S(2)}) collective-permute-start(bf16[3,256,64]{1,2,0:T(8,128)(2,1)S(1)} %multiply_convert_fusion.41), channel_id=1, source_target_pairs={{0,10},{2,8},{4,14},{6,12},{8,2},{10,0},{12,6},{14,4},{1,11},{3,9}... | collective-permute-start | bytes 294920 | tf_op jit(solution)/shard_map/ppermute | solution.py:50
  116.2 2.5 %collective-permute-done.28 = bf16[3,256,64]{1,2,0:T(8,128)(2,1)S(1)} collective-permute-done((bf16[3,256,64]{1,2,0:T(8,128)(2,1)S(1)}, bf16[3,256,64]{1,2,0:T(8,128)(2,1)S(1)}, u32[]{:S(2)}, u32[]{:S(2)}) %collective-permute-start.28) | collective-permute-done | bytes 98336 | tf_op jit(solution)/shard_map/ppermute | solution.py:50
  118.7 2.3 %collective-permute-done.29 = bf16[3,256,64]{1,2,0:T(8,128)(2,1)S(1)} collective-permute-done((bf16[3,256,64]{1,2,0:T(8,128)(2,1)S(1)}, bf16[3,256,64]{1,2,0:T(8,128)(2,1)S(1)}, u32[]{:S(2)}, u32[]{:S(2)}) %collective-permute-start.29) | collective-permute-done | bytes 98336 | tf_op jit(solution)/shard_map/ppermute | solution.py:50
  127.8 2.3 %convolution_convert_fusion.2 = bf16[512,256]{1,0:T(8,128)(2,1)} fusion(f32[512,256]{1,0:T(8,128)} %convolution_bitcast_fusion.12, bf16[2,512,256]{2,1,0:T(8,128)(2,1)} %copy-done.4, bf16[3,256,256]{1,2,0:T(8,128)(2,1)S(1)} %constant_dynamic-update-slice_fusion.16), kind=kOutput, calls=%fused_computation.21 | convolution fusion | flops 135135232 | bytes 1310720 | tf_op jit(solution)/shard_map/th,hd->td/dot_general | solution.py:81
  141.4 2.6 %collective-permute-done.36 = bf16[3,256,64]{1,2,0:T(8,128)(2,1)S(1)} collective-permute-done((bf16[3,256,64]{1,2,0:T(8,128)(2,1)S(1)}, bf16[3,256,64]{1,2,0:T(8,128)(2,1)S(1)}, u32[]{:S(2)}, u32[]{:S(2)}) %collective-permute-start.36) | collective-permute-done | bytes 98336 | tf_op jit(solution)/shard_map/ppermute | solution.py:15
  152.8 2.7 %collective-permute-done.39 = bf16[3,256,64]{1,2,0:T(8,128)(2,1)S(1)} collective-permute-done((bf16[3,256,64]{1,2,0:T(8,128)(2,1)S(1)}, bf16[3,256,64]{1,2,0:T(8,128)(2,1)S(1)}, u32[]{:S(2)}, u32[]{:S(2)}) %collective-permute-start.39) | collective-permute-done | bytes 98336 | tf_op jit(solution)/shard_map/ppermute | solution.py:15
  155.9 2.7 %collective-permute-start.41 = (bf16[3,256,64]{1,2,0:T(8,128)(2,1)S(1)}, bf16[3,256,64]{1,2,0:T(8,128)(2,1)S(1)}, u32[]{:S(2)}, u32[]{:S(2)}) collective-permute-start(bf16[3,256,64]{1,2,0:T(8,128)(2,1)S(1)} %get-tuple-element.37), channel_id=1, source_target_pairs={{0,4},{4,8},{8,12},{12,0},{1,5},{5,9},{9,13},{13,1},{2,6},{6,10},{... | collective-permute-start | bytes 294920 | tf_op jit(solution)/shard_map/ppermute | solution.py:15
  163.5 2.7 %collective-permute-done.42 = bf16[3,256,64]{1,2,0:T(8,128)(2,1)S(1)} collective-permute-done((bf16[3,256,64]{1,2,0:T(8,128)(2,1)S(1)}, bf16[3,256,64]{1,2,0:T(8,128)(2,1)S(1)}, u32[]{:S(2)}, u32[]{:S(2)}) %collective-permute-start.42) | collective-permute-done | bytes 98336 | tf_op jit(solution)/shard_map/ppermute | solution.py:15
  (187 shorter events, 73.6 us)
Async XLA Ops:
  3.2 7.7 %collective-permute-start = (bf16[3,256,64]{1,2,0:T(8,128)(2,1)S(1)}, bf16[3,256,64]{1,2,0:T(8,128)(2,1)S(1)}, u32[]{:S(2)}, u32[]{:S(2)}) collective-permute-start(bf16[3,256,64]{1,2,0:T(8,128)(2,1)S(1)} %get-tuple-element.57), channel_id=1, source_target_pairs={{0,4},{4,8},{8,12},{12,0},{1,5},{5,9},{9,13},{13,1},{2,6},{6,10},{... | collective-permute-start | bytes 294920 | tf_op jit(solution)/shard_map/ppermute | solution.py:15
  6.3 6.8 %collective-permute-start.1 = (bf16[3,256,64]{1,2,0:T(8,128)(2,1)S(1)}, bf16[3,256,64]{1,2,0:T(8,128)(2,1)S(1)}, u32[]{:S(2)}, u32[]{:S(2)}) collective-permute-start(bf16[3,256,64]{1,2,0:T(8,128)(2,1)S(1)} %get-tuple-element.57), channel_id=1, source_target_pairs={{0,8},{4,12},{8,0},{12,4},{1,9},{5,13},{9,1},{13,5},{2,10},{6,14},... | collective-permute-start | bytes 294920 | tf_op jit(solution)/shard_map/ppermute | solution.py:15
  17.5 7.6 %collective-permute-start.4 = (bf16[3,256,64]{1,2,0:T(8,128)(2,1)S(1)}, bf16[3,256,64]{1,2,0:T(8,128)(2,1)S(1)}, u32[]{:S(2)}, u32[]{:S(2)}) collective-permute-start(bf16[3,256,64]{1,2,0:T(8,128)(2,1)S(1)} %get-tuple-element.75), channel_id=1, source_target_pairs={{0,8},{4,12},{8,0},{12,4},{1,9},{5,13},{9,1},{13,5},{2,10},{6,14},... | collective-permute-start | bytes 294920 | tf_op jit(solution)/shard_map/ppermute | solution.py:15
  27.0 9.9 %collective-permute-start.7 = (bf16[3,256,64]{1,2,0:T(8,128)(2,1)S(1)}, bf16[3,256,64]{1,2,0:T(8,128)(2,1)S(1)}, u32[]{:S(2)}, u32[]{:S(2)}) collective-permute-start(bf16[3,256,64]{1,2,0:T(8,128)(2,1)S(1)} %get-tuple-element.53), channel_id=1, source_target_pairs={{0,8},{4,12},{8,0},{12,4},{1,9},{5,13},{9,1},{13,5},{2,10},{6,14},... | collective-permute-start | bytes 294920 | tf_op jit(solution)/shard_map/ppermute | solution.py:15
  29.2 7.8 %collective-permute-start.8 = (bf16[3,256,64]{1,2,0:T(8,128)(2,1)S(1)}, bf16[3,256,64]{1,2,0:T(8,128)(2,1)S(1)}, u32[]{:S(2)}, u32[]{:S(2)}) collective-permute-start(bf16[3,256,64]{1,2,0:T(8,128)(2,1)S(1)} %get-tuple-element.53), channel_id=1, source_target_pairs={{0,12},{4,0},{8,4},{12,8},{1,13},{5,1},{9,5},{13,9},{2,14},{6,2},{... | collective-permute-start | bytes 294920 | tf_op jit(solution)/shard_map/ppermute | solution.py:15
  40.7 7.0 %collective-permute-start.11 = (bf16[3,256,64]{1,2,0:T(8,128)(2,1)S(1)}, bf16[3,256,64]{1,2,0:T(8,128)(2,1)S(1)}, u32[]{:S(2)}, u32[]{:S(2)}) collective-permute-start(bf16[3,256,64]{1,2,0:T(8,128)(2,1)S(1)} %get-tuple-element.71), channel_id=1, source_target_pairs={{0,12},{4,0},{8,4},{12,8},{1,13},{5,1},{9,5},{13,9},{2,14},{6,2},{... | collective-permute-start | bytes 294920 | tf_op jit(solution)/shard_map/ppermute | solution.py:15
  44.1 7.8 %collective-permute-start.9 = (bf16[3,256,64]{1,2,0:T(8,128)(2,1)S(1)}, bf16[3,256,64]{1,2,0:T(8,128)(2,1)S(1)}, u32[]{:S(2)}, u32[]{:S(2)}) collective-permute-start(bf16[3,256,64]{1,2,0:T(8,128)(2,1)S(1)} %get-tuple-element.70), channel_id=1, source_target_pairs={{0,4},{4,8},{8,12},{12,0},{1,5},{5,9},{9,13},{13,1},{2,6},{6,10},{... | collective-permute-start | bytes 294920 | tf_op jit(solution)/shard_map/ppermute | solution.py:15
  52.3 7.1 %collective-permute-start.12 = (bf16[3,256,64]{1,2,0:T(8,128)(2,1)S(1)}, bf16[3,256,64]{1,2,0:T(8,128)(2,1)S(1)}, u32[]{:S(2)}, u32[]{:S(2)}) collective-permute-start(bf16[3,256,64]{1,2,0:T(8,128)(2,1)S(1)} %multiply_convert_fusion.42), channel_id=1, source_target_pairs={{0,2},{2,0},{4,6},{6,4},{8,10},{10,8},{12,14},{14,12},{1,3},{3,1},... | collective-permute-start | bytes 294920 | tf_op jit(solution)/shard_map/ppermute | solution.py:50
  53.6 8.4 %collective-permute-start.13 = (bf16[3,256,64]{1,2,0:T(8,128)(2,1)S(1)}, bf16[3,256,64]{1,2,0:T(8,128)(2,1)S(1)}, u32[]{:S(2)}, u32[]{:S(2)}) collective-permute-start(bf16[3,256,64]{1,2,0:T(8,128)(2,1)S(1)} %multiply_convert_fusion.42), channel_id=1, source_target_pairs={{0,6},{2,4},{4,10},{6,8},{8,14},{10,12},{12,2},{14,0},{1,7},{3,5},... | collective-permute-start | bytes 294920 | tf_op jit(solution)/shard_map/ppermute | solution.py:50
  53.6 11.5 %collective-permute-start.14 = (bf16[3,256,64]{1,2,0:T(8,128)(2,1)S(1)}, bf16[3,256,64]{1,2,0:T(8,128)(2,1)S(1)}, u32[]{:S(2)}, u32[]{:S(2)}) collective-permute-start(bf16[3,256,64]{1,2,0:T(8,128)(2,1)S(1)} %multiply_convert_fusion.42), channel_id=1, source_target_pairs={{0,10},{2,8},{4,14},{6,12},{8,2},{10,0},{12,6},{14,4},{1,11},{3,9}... | collective-permute-start | bytes 294920 | tf_op jit(solution)/shard_map/ppermute | solution.py:50
  56.3 8.8 %collective-permute-start.15 = (bf16[3,256,64]{1,2,0:T(8,128)(2,1)S(1)}, bf16[3,256,64]{1,2,0:T(8,128)(2,1)S(1)}, u32[]{:S(2)}, u32[]{:S(2)}) collective-permute-start(bf16[3,256,64]{1,2,0:T(8,128)(2,1)S(1)} %multiply_convert_fusion.42), channel_id=1, source_target_pairs={{0,14},{2,12},{4,2},{6,0},{8,6},{10,4},{12,10},{14,8},{1,15},{3,13... | collective-permute-start | bytes 294920 | tf_op jit(solution)/shard_map/ppermute | solution.py:50
  67.4 7.4 %collective-permute-start.18 = (bf16[3,256,64]{1,2,0:T(8,128)(2,1)S(1)}, bf16[3,256,64]{1,2,0:T(8,128)(2,1)S(1)}, u32[]{:S(2)}, u32[]{:S(2)}) collective-permute-start(bf16[3,256,64]{1,2,0:T(8,128)(2,1)S(1)} %get-tuple-element.67), channel_id=1, source_target_pairs={{0,4},{4,8},{8,12},{12,0},{1,5},{5,9},{9,13},{13,1},{2,6},{6,10},{... | collective-permute-start | bytes 294920 | tf_op jit(solution)/shard_map/ppermute | solution.py:15
  69.5 8.1 %collective-permute-start.19 = (bf16[3,256,64]{1,2,0:T(8,128)(2,1)S(1)}, bf16[3,256,64]{1,2,0:T(8,128)(2,1)S(1)}, u32[]{:S(2)}, u32[]{:S(2)}) collective-permute-start(bf16[3,256,64]{1,2,0:T(8,128)(2,1)S(1)} %get-tuple-element.69), channel_id=1, source_target_pairs={{0,8},{4,12},{8,0},{12,4},{1,9},{5,13},{9,1},{13,5},{2,10},{6,14},... | collective-permute-start | bytes 294920 | tf_op jit(solution)/shard_map/ppermute | solution.py:15
  70.2 7.3 %collective-permute-start.20 = (bf16[3,256,64]{1,2,0:T(8,128)(2,1)S(1)}, bf16[3,256,64]{1,2,0:T(8,128)(2,1)S(1)}, u32[]{:S(2)}, u32[]{:S(2)}) collective-permute-start(bf16[3,256,64]{1,2,0:T(8,128)(2,1)S(1)} %get-tuple-element.68), channel_id=1, source_target_pairs={{0,12},{4,0},{8,4},{12,8},{1,13},{5,1},{9,5},{13,9},{2,14},{6,2},{... | collective-permute-start | bytes 294920 | tf_op jit(solution)/shard_map/ppermute | solution.py:15
  77.9 7.6 %collective-permute-start.21 = (bf16[3,256,64]{1,2,0:T(8,128)(2,1)S(1)}, bf16[3,256,64]{1,2,0:T(8,128)(2,1)S(1)}, u32[]{:S(2)}, u32[]{:S(2)}) collective-permute-start(bf16[3,256,64]{1,2,0:T(8,128)(2,1)S(1)} %get-tuple-element.47), channel_id=1, source_target_pairs={{0,4},{4,8},{8,12},{12,0},{1,5},{5,9},{9,13},{13,1},{2,6},{6,10},{... | collective-permute-start | bytes 294920 | tf_op jit(solution)/shard_map/ppermute | solution.py:15
  80.3 8.2 %collective-permute-start.22 = (bf16[3,256,64]{1,2,0:T(8,128)(2,1)S(1)}, bf16[3,256,64]{1,2,0:T(8,128)(2,1)S(1)}, u32[]{:S(2)}, u32[]{:S(2)}) collective-permute-start(bf16[3,256,64]{1,2,0:T(8,128)(2,1)S(1)} %get-tuple-element.47), channel_id=1, source_target_pairs={{0,8},{4,12},{8,0},{12,4},{1,9},{5,13},{9,1},{13,5},{2,10},{6,14},... | collective-permute-start | bytes 294920 | tf_op jit(solution)/shard_map/ppermute | solution.py:15
  81.6 6.9 %collective-permute-start.23 = (bf16[3,256,64]{1,2,0:T(8,128)(2,1)S(1)}, bf16[3,256,64]{1,2,0:T(8,128)(2,1)S(1)}, u32[]{:S(2)}, u32[]{:S(2)}) collective-permute-start(bf16[3,256,64]{1,2,0:T(8,128)(2,1)S(1)} %get-tuple-element.47), channel_id=1, source_target_pairs={{0,12},{4,0},{8,4},{12,8},{1,13},{5,1},{9,5},{13,9},{2,14},{6,2},{... | collective-permute-start | bytes 294920 | tf_op jit(solution)/shard_map/ppermute | solution.py:15
  90.7 7.4 %collective-permute-start.24 = (bf16[3,256,64]{1,2,0:T(8,128)(2,1)S(1)}, bf16[3,256,64]{1,2,0:T(8,128)(2,1)S(1)}, u32[]{:S(2)}, u32[]{:S(2)}) collective-permute-start(bf16[3,256,64]{1,2,0:T(8,128)(2,1)S(1)} %get-tuple-element.64), channel_id=1, source_target_pairs={{0,4},{4,8},{8,12},{12,0},{1,5},{5,9},{9,13},{13,1},{2,6},{6,10},{... | collective-permute-start | bytes 294920 | tf_op jit(solution)/shard_map/ppermute | solution.py:15
  93.3 8.2 %collective-permute-start.25 = (bf16[3,256,64]{1,2,0:T(8,128)(2,1)S(1)}, bf16[3,256,64]{1,2,0:T(8,128)(2,1)S(1)}, u32[]{:S(2)}, u32[]{:S(2)}) collective-permute-start(bf16[3,256,64]{1,2,0:T(8,128)(2,1)S(1)} %get-tuple-element.66), channel_id=1, source_target_pairs={{0,8},{4,12},{8,0},{12,4},{1,9},{5,13},{9,1},{13,5},{2,10},{6,14},... | collective-permute-start | bytes 294920 | tf_op jit(solution)/shard_map/ppermute | solution.py:15
  94.6 6.9 %collective-permute-start.26 = (bf16[3,256,64]{1,2,0:T(8,128)(2,1)S(1)}, bf16[3,256,64]{1,2,0:T(8,128)(2,1)S(1)}, u32[]{:S(2)}, u32[]{:S(2)}) collective-permute-start(bf16[3,256,64]{1,2,0:T(8,128)(2,1)S(1)} %get-tuple-element.65), channel_id=1, source_target_pairs={{0,12},{4,0},{8,4},{12,8},{1,13},{5,1},{9,5},{13,9},{2,14},{6,2},{... | collective-permute-start | bytes 294920 | tf_op jit(solution)/shard_map/ppermute | solution.py:15
  95.8 14.4 %collective-permute-start.16 = (bf16[2,512,256]{2,1,0:T(8,128)(2,1)S(1)}, bf16[2,512,256]{2,1,0:T(8,128)(2,1)S(1)}, u32[]{:S(2)}, u32[]{:S(2)}) collective-permute-start(bf16[2,512,256]{2,1,0:T(8,128)(2,1)S(1)} %slice_bitcast_fusion), channel_id=1, source_target_pairs={{0,2},{2,0},{1,3},{3,1},{4,6},{6,4},{5,7},{7,5},{8,10},{10,8},{9,1... | collective-permute-start | bytes 1572872 | tf_op jit(solution)/shard_map/ppermute | solution.py:15
  101.9 14.2 %collective-permute-start.27 = (bf16[3,256,64]{1,2,0:T(8,128)(2,1)S(1)}, bf16[3,256,64]{1,2,0:T(8,128)(2,1)S(1)}, u32[]{:S(2)}, u32[]{:S(2)}) collective-permute-start(bf16[3,256,64]{1,2,0:T(8,128)(2,1)S(1)} %multiply_convert_fusion.41), channel_id=1, source_target_pairs={{0,2},{2,0},{4,6},{6,4},{8,10},{10,8},{12,14},{14,12},{1,3},{3,1},... | collective-permute-start | bytes 294920 | tf_op jit(solution)/shard_map/ppermute | solution.py:50
  111.3 7.4 %collective-permute-start.28 = (bf16[3,256,64]{1,2,0:T(8,128)(2,1)S(1)}, bf16[3,256,64]{1,2,0:T(8,128)(2,1)S(1)}, u32[]{:S(2)}, u32[]{:S(2)}) collective-permute-start(bf16[3,256,64]{1,2,0:T(8,128)(2,1)S(1)} %multiply_convert_fusion.41), channel_id=1, source_target_pairs={{0,6},{2,4},{4,10},{6,8},{8,14},{10,12},{12,2},{14,0},{1,7},{3,5},... | collective-permute-start | bytes 294920 | tf_op jit(solution)/shard_map/ppermute | solution.py:50
  111.8 9.1 %collective-permute-start.29 = (bf16[3,256,64]{1,2,0:T(8,128)(2,1)S(1)}, bf16[3,256,64]{1,2,0:T(8,128)(2,1)S(1)}, u32[]{:S(2)}, u32[]{:S(2)}) collective-permute-start(bf16[3,256,64]{1,2,0:T(8,128)(2,1)S(1)} %multiply_convert_fusion.41), channel_id=1, source_target_pairs={{0,10},{2,8},{4,14},{6,12},{8,2},{10,0},{12,6},{14,4},{1,11},{3,9}... | collective-permute-start | bytes 294920 | tf_op jit(solution)/shard_map/ppermute | solution.py:50
  123.8 7.2 %collective-permute-start.32 = (bf16[3,256,64]{1,2,0:T(8,128)(2,1)}, bf16[3,256,64]{1,2,0:T(8,128)(2,1)S(1)}, u32[]{:S(2)}, u32[]{:S(2)}) collective-permute-start(bf16[3,256,64]{1,2,0:T(8,128)(2,1)} %get-tuple-element.61), channel_id=1, source_target_pairs={{0,4},{4,8},{8,12},{12,0},{1,5},{5,9},{9,13},{13,1},{2,6},{6,10},{... | collective-permute-start | bytes 294920 | tf_op jit(solution)/shard_map/ppermute | solution.py:15
  125.4 7.6 %collective-permute-start.33 = (bf16[3,256,64]{1,2,0:T(8,128)(2,1)S(1)}, bf16[3,256,64]{1,2,0:T(8,128)(2,1)S(1)}, u32[]{:S(2)}, u32[]{:S(2)}) collective-permute-start(bf16[3,256,64]{1,2,0:T(8,128)(2,1)S(1)} %get-tuple-element.63), channel_id=1, source_target_pairs={{0,8},{4,12},{8,0},{12,4},{1,9},{5,13},{9,1},{13,5},{2,10},{6,14},... | collective-permute-start | bytes 294920 | tf_op jit(solution)/shard_map/ppermute | solution.py:15
  130.1 36.9 %collective-permute-start.17 = (bf16[512,256]{1,0:T(8,128)(2,1)}, bf16[512,256]{1,0:T(8,128)(2,1)}, u32[]{:S(2)}, u32[]{:S(2)}) collective-permute-start(bf16[512,256]{1,0:T(8,128)(2,1)} %convolution_convert_fusion.2), channel_id=1, source_target_pairs={{0,2},{2,0},{1,3},{3,1},{4,6},{6,4},{5,7},{7,5},{8,10},{10,8},{9,1... | collective-permute-start | bytes 786440 | tf_op jit(solution)/shard_map/ppermute | solution.py:15
  134.3 7.1 %collective-permute-start.35 = (bf16[3,256,64]{1,2,0:T(8,128)(2,1)S(1)}, bf16[3,256,64]{1,2,0:T(8,128)(2,1)S(1)}, u32[]{:S(2)}, u32[]{:S(2)}) collective-permute-start(bf16[3,256,64]{1,2,0:T(8,128)(2,1)S(1)} %get-tuple-element.41), channel_id=1, source_target_pairs={{0,4},{4,8},{8,12},{12,0},{1,5},{5,9},{9,13},{13,1},{2,6},{6,10},{... | collective-permute-start | bytes 294920 | tf_op jit(solution)/shard_map/ppermute | solution.py:15
  136.4 7.7 %collective-permute-start.36 = (bf16[3,256,64]{1,2,0:T(8,128)(2,1)S(1)}, bf16[3,256,64]{1,2,0:T(8,128)(2,1)S(1)}, u32[]{:S(2)}, u32[]{:S(2)}) collective-permute-start(bf16[3,256,64]{1,2,0:T(8,128)(2,1)S(1)} %get-tuple-element.41), channel_id=1, source_target_pairs={{0,8},{4,12},{8,0},{12,4},{1,9},{5,13},{9,1},{13,5},{2,10},{6,14},... | collective-permute-start | bytes 294920 | tf_op jit(solution)/shard_map/ppermute | solution.py:15
  147.9 7.6 %collective-permute-start.39 = (bf16[3,256,64]{1,2,0:T(8,128)(2,1)S(1)}, bf16[3,256,64]{1,2,0:T(8,128)(2,1)S(1)}, u32[]{:S(2)}, u32[]{:S(2)}) collective-permute-start(bf16[3,256,64]{1,2,0:T(8,128)(2,1)S(1)} %get-tuple-element.60), channel_id=1, source_target_pairs={{0,8},{4,12},{8,0},{12,4},{1,9},{5,13},{9,1},{13,5},{2,10},{6,14},... | collective-permute-start | bytes 294920 | tf_op jit(solution)/shard_map/ppermute | solution.py:15
  150.8 16.2 %collective-permute-start.31 = (bf16[512,256]{1,0:T(8,128)(2,1)S(1)}, bf16[512,256]{1,0:T(8,128)(2,1)S(1)}, u32[]{:S(2)}, u32[]{:S(2)}) collective-permute-start(bf16[512,256]{1,0:T(8,128)(2,1)S(1)} %convolution_convert_fusion.1), channel_id=1, source_target_pairs={{0,2},{2,0},{1,3},{3,1},{4,6},{6,4},{5,7},{7,5},{8,10},{10,8},{9,1... | collective-permute-start | bytes 786440 | tf_op jit(solution)/shard_map/ppermute | solution.py:15
  155.9 7.5 %collective-permute-start.41 = (bf16[3,256,64]{1,2,0:T(8,128)(2,1)S(1)}, bf16[3,256,64]{1,2,0:T(8,128)(2,1)S(1)}, u32[]{:S(2)}, u32[]{:S(2)}) collective-permute-start(bf16[3,256,64]{1,2,0:T(8,128)(2,1)S(1)} %get-tuple-element.37), channel_id=1, source_target_pairs={{0,4},{4,8},{8,12},{12,0},{1,5},{5,9},{9,13},{13,1},{2,6},{6,10},{... | collective-permute-start | bytes 294920 | tf_op jit(solution)/shard_map/ppermute | solution.py:15
  (20 other events, 116.4 us)

commit v11 on v10

--- a/solution.py
+++ b/solution.py
@@ -18,10 +18,13 @@
 def scatter_sum(partial, part_cols):
     tok_count = lax.axis_size("tok")
     me = lax.axis_index("tok")
+    got = {}
+    for by in reversed(range(1, tok_count)):
+        chunk = lax.dynamic_slice_in_dim(partial, ((me + by) % tok_count) * part_cols, part_cols, 2)
+        got[by] = rotated(chunk, "tok", by)
     total = lax.dynamic_slice_in_dim(partial, me * part_cols, part_cols, 2).astype(jnp.float32)
     for by in range(1, tok_count):
-        chunk = lax.dynamic_slice_in_dim(partial, ((me + by) % tok_count) * part_cols, part_cols, 2)
-        total = total + rotated(chunk, "tok", by).astype(jnp.float32)
+        total = total + got[by].astype(jnp.float32)
     return total
 
 
@@ -30,7 +33,7 @@
     me = lax.axis_index("tok")
     full = jnp.zeros(own.shape[:2] + (part_cols * tok_count,), own.dtype)
     full = lax.dynamic_update_slice_in_dim(full, own, me * part_cols, 2)
-    for by in range(1, tok_count):
+    for by in reversed(range(1, tok_count)):
         got = rotated(own, "tok", by)
         full = lax.dynamic_update_slice_in_dim(full, got, ((me - by) % tok_count) * part_cols, 2)
     return full
@@ -97,8 +100,7 @@
     tick_count = key_rows.shape[0]
     results = []
     weights = states_in[0, 0]
-    anchor = jnp.abs(weights[0, 0, 0]) + 1.0
-    unit = anchor / anchor
+    unit = (init_norms[0, 0] + 1.0) / (init_norms[0, 0] + 1.0)
     weights = lax.fori_loop(
         0, lax.axis_index("head") * DELAY_STEPS, lambda step, held: held * unit, weights
     )

time: 169 us -> 177 us (1.047)
  waiting for transfers between devices: 71 us -> 83.6 us
  starting transfers between devices: 68.7 us -> 62.8 us
    ppermute x36, waiting for transfers between devices: 60.5 us -> 74.2 us  [rotated(): lax.ppermute(value, axis, [(i, (i + by) % devices) for i in range(devices)])]
    ppermute x36, starting transfers between devices: 55.6 us -> 49.4 us  [rotated(): lax.ppermute(value, axis, [(i, (i + by) % devices) for i in range(devices)])]
  transfers between devices with their start and end apart: 44 -> 44, of which waited for: 29 -> 27; matrix products, arithmetic and copies ran while one was open for 6% -> 6% of each run, Pallas kernels for 0% -> 0%
where the time goes in v11:
time: 177 us
  waiting for transfers between devices  83.6 us (47%)
  starting transfers between devices  62.8 us (35%)
  matrix products  17.7 us (10%)
  other arithmetic  6.22 us (4%)
  local copies, waits for them, and re-layouts  3.98 us (2%)
  between operations  2.25 us (1%)
    ppermute x36, waiting for transfers between devices, rotated(): lax.ppermute(value, axis, [(i, (i + by) % devices) for i in range(devices)])  74.2 us
    ppermute x36, starting transfers between devices, rotated(): lax.ppermute(value, axis, [(i, (i + by) % devices) for i in range(devices)])  49.4 us
    ppermute x8, starting transfers between devices, cross_gather(): got = lax.ppermute(own, ('tok', 'span'), pairs)  13.5 us
    ppermute x8, waiting for transfers between devices, cross_gather(): got = lax.ppermute(own, ('tok', 'span'), pairs)  9.36 us
  transfers between devices with their start and end apart: 44, of which 27 were waited for; matrix products, arithmetic and copies ran while one was open for 6% of the time, Pallas kernels for 0%

profile of v11, /device:TPU:0, one launch (start us, length us, event | category | flops | bytes accessed | tf_op | source)
XLA Modules:
  0.0 176.5 jit_solution(18024192237166058225)
XLA Ops:
  3.7 5.1 %collective-permute-start = (bf16[3,256,64]{1,2,0:T(8,128)(2,1)S(1)}, bf16[3,256,64]{1,2,0:T(8,128)(2,1)S(1)}, u32[]{:S(2)}, u32[]{:S(2)}) collective-permute-start(bf16[3,256,64]{1,2,0:T(8,128)(2,1)S(1)} %get-tuple-element.57), channel_id=1, source_target_pairs={{0,12},{4,0},{8,4},{12,8},{1,13},{5,1},{9,5},{13,9},{2,14},{6,2},{... | collective-permute-start | bytes 294920 | tf_op jit(solution)/shard_map/ppermute | solution.py:15
  11.0 4.4 %collective-permute-done.1 = bf16[3,256,64]{1,2,0:T(8,128)(2,1)S(1)} collective-permute-done((bf16[3,256,64]{1,2,0:T(8,128)(2,1)S(1)}, bf16[3,256,64]{1,2,0:T(8,128)(2,1)S(1)}, u32[]{:S(2)}, u32[]{:S(2)}) %collective-permute-start.1) | collective-permute-done | bytes 98336 | tf_op jit(solution)/shard_map/ppermute | solution.py:15
  20.3 2.5 %collective-permute-start.5 = (bf16[3,256,64]{1,2,0:T(8,128)(2,1)S(1)}, bf16[3,256,64]{1,2,0:T(8,128)(2,1)S(1)}, u32[]{:S(2)}, u32[]{:S(2)}) collective-permute-start(bf16[3,256,64]{1,2,0:T(8,128)(2,1)S(1)} %get-tuple-element.74), channel_id=1, source_target_pairs={{0,12},{4,0},{8,4},{12,8},{1,13},{5,1},{9,5},{13,9},{2,14},{6,2},{... | collective-permute-start | bytes 294920 | tf_op jit(solution)/shard_map/ppermute | solution.py:15
  22.8 2.1 %collective-permute-done.3 = bf16[3,256,64]{1,2,0:T(8,128)(2,1)S(1)} collective-permute-done((bf16[3,256,64]{1,2,0:T(8,128)(2,1)S(1)}, bf16[3,256,64]{1,2,0:T(8,128)(2,1)S(1)}, u32[]{:S(2)}, u32[]{:S(2)}) %collective-permute-start.3) | collective-permute-done | bytes 98336 | tf_op jit(solution)/shard_map/ppermute | solution.py:15
  26.4 4.4 %collective-permute-start.6 = (bf16[3,256,64]{1,2,0:T(8,128)(2,1)S(1)}, bf16[3,256,64]{1,2,0:T(8,128)(2,1)S(1)}, u32[]{:S(2)}, u32[]{:S(2)}) collective-permute-start(bf16[3,256,64]{1,2,0:T(8,128)(2,1)S(1)} %get-tuple-element.53), channel_id=1, source_target_pairs={{0,12},{4,0},{8,4},{12,8},{1,13},{5,1},{9,5},{13,9},{2,14},{6,2},{... | collective-permute-start | bytes 294920 | tf_op jit(solution)/shard_map/ppermute | solution.py:15
  33.0 7.5 %collective-permute-done.7 = bf16[3,256,64]{1,2,0:T(8,128)(2,1)S(1)} collective-permute-done((bf16[3,256,64]{1,2,0:T(8,128)(2,1)S(1)}, bf16[3,256,64]{1,2,0:T(8,128)(2,1)S(1)}, u32[]{:S(2)}, u32[]{:S(2)}) %collective-permute-start.7) | collective-permute-done | bytes 98336 | tf_op jit(solution)/shard_map/ppermute | solution.py:15
  46.2 4.7 %collective-permute-done.10 = bf16[3,256,64]{1,2,0:T(8,128)(2,1)S(1)} collective-permute-done((bf16[3,256,64]{1,2,0:T(8,128)(2,1)S(1)}, bf16[3,256,64]{1,2,0:T(8,128)(2,1)S(1)}, u32[]{:S(2)}, u32[]{:S(2)}) %collective-permute-start.10) | collective-permute-done | bytes 98336 | tf_op jit(solution)/shard_map/ppermute | solution.py:15
  50.9 2.6 %collective-permute-done.11 = bf16[3,256,64]{1,2,0:T(8,128)(2,1)S(1)} collective-permute-done((bf16[3,256,64]{1,2,0:T(8,128)(2,1)S(1)}, bf16[3,256,64]{1,2,0:T(8,128)(2,1)S(1)}, u32[]{:S(2)}, u32[]{:S(2)}) %collective-permute-start.11) | collective-permute-done | bytes 98336 | tf_op jit(solution)/shard_map/ppermute | solution.py:15
  57.2 3.2 %collective-permute-start.15 = (bf16[3,256,64]{1,2,0:T(8,128)(2,1)S(1)}, bf16[3,256,64]{1,2,0:T(8,128)(2,1)S(1)}, u32[]{:S(2)}, u32[]{:S(2)}) collective-permute-start(bf16[3,256,64]{1,2,0:T(8,128)(2,1)S(1)} %multiply_convert_fusion.42), channel_id=1, source_target_pairs={{0,14},{2,12},{4,2},{6,0},{8,6},{10,4},{12,10},{14,8},{1,15},{3,13... | collective-permute-start | bytes 294920 | tf_op jit(solution)/shard_map/ppermute | solution.py:53
  60.5 2.9 %collective-permute-done.13 = bf16[3,256,64]{1,2,0:T(8,128)(2,1)S(1)} collective-permute-done((bf16[3,256,64]{1,2,0:T(8,128)(2,1)S(1)}, bf16[3,256,64]{1,2,0:T(8,128)(2,1)S(1)}, u32[]{:S(2)}, u32[]{:S(2)}) %collective-permute-start.13) | collective-permute-done | bytes 98336 | tf_op jit(solution)/shard_map/ppermute | solution.py:53
  63.4 3.0 %collective-permute-done.14 = bf16[3,256,64]{1,2,0:T(8,128)(2,1)S(1)} collective-permute-done((bf16[3,256,64]{1,2,0:T(8,128)(2,1)S(1)}, bf16[3,256,64]{1,2,0:T(8,128)(2,1)S(1)}, u32[]{:S(2)}, u32[]{:S(2)}) %collective-permute-start.14) | collective-permute-done | bytes 98336 | tf_op jit(solution)/shard_map/ppermute | solution.py:53
  68.7 2.6 %collective-permute-start.18 = (bf16[3,256,64]{1,2,0:T(8,128)(2,1)S(1)}, bf16[3,256,64]{1,2,0:T(8,128)(2,1)S(1)}, u32[]{:S(2)}, u32[]{:S(2)}) collective-permute-start(bf16[3,256,64]{1,2,0:T(8,128)(2,1)S(1)} %get-tuple-element.67), channel_id=1, source_target_pairs={{0,4},{4,8},{8,12},{12,0},{1,5},{5,9},{9,13},{13,1},{2,6},{6,10},{... | collective-permute-start | bytes 294920 | tf_op jit(solution)/shard_map/ppermute | solution.py:15
  73.7 2.4 %collective-permute-done.18 = bf16[3,256,64]{1,2,0:T(8,128)(2,1)S(1)} collective-permute-done((bf16[3,256,64]{1,2,0:T(8,128)(2,1)S(1)}, bf16[3,256,64]{1,2,0:T(8,128)(2,1)S(1)}, u32[]{:S(2)}, u32[]{:S(2)}) %collective-permute-start.18) | collective-permute-done | bytes 98336 | tf_op jit(solution)/shard_map/ppermute | solution.py:15
  76.1 3.4 %collective-permute-done.19 = bf16[3,256,64]{1,2,0:T(8,128)(2,1)S(1)} collective-permute-done((bf16[3,256,64]{1,2,0:T(8,128)(2,1)S(1)}, bf16[3,256,64]{1,2,0:T(8,128)(2,1)S(1)}, u32[]{:S(2)}, u32[]{:S(2)}) %collective-permute-start.19) | collective-permute-done | bytes 98336 | tf_op jit(solution)/shard_map/ppermute | solution.py:15
  79.8 3.5 %collective-permute-start.21 = (bf16[3,256,64]{1,2,0:T(8,128)(2,1)S(1)}, bf16[3,256,64]{1,2,0:T(8,128)(2,1)S(1)}, u32[]{:S(2)}, u32[]{:S(2)}) collective-permute-start(bf16[3,256,64]{1,2,0:T(8,128)(2,1)S(1)} %get-tuple-element.47), channel_id=1, source_target_pairs={{0,12},{4,0},{8,4},{12,8},{1,13},{5,1},{9,5},{13,9},{2,14},{6,2},{... | collective-permute-start | bytes 294920 | tf_op jit(solution)/shard_map/ppermute | solution.py:15
  84.0 2.5 %collective-permute-done.21 = bf16[3,256,64]{1,2,0:T(8,128)(2,1)S(1)} collective-permute-done((bf16[3,256,64]{1,2,0:T(8,128)(2,1)S(1)}, bf16[3,256,64]{1,2,0:T(8,128)(2,1)S(1)}, u32[]{:S(2)}, u32[]{:S(2)}) %collective-permute-start.21) | collective-permute-done | bytes 98336 | tf_op jit(solution)/shard_map/ppermute | solution.py:15
  86.5 6.4 %collective-permute-done.22 = bf16[3,256,64]{1,2,0:T(8,128)(2,1)S(1)} collective-permute-done((bf16[3,256,64]{1,2,0:T(8,128)(2,1)S(1)}, bf16[3,256,64]{1,2,0:T(8,128)(2,1)S(1)}, u32[]{:S(2)}, u32[]{:S(2)}) %collective-permute-start.22) | collective-permute-done | bytes 98336 | tf_op jit(solution)/shard_map/ppermute | solution.py:15
  96.4 2.6 %collective-permute-start.26 = (bf16[3,256,64]{1,2,0:T(8,128)(2,1)S(1)}, bf16[3,256,64]{1,2,0:T(8,128)(2,1)S(1)}, u32[]{:S(2)}, u32[]{:S(2)}) collective-permute-start(bf16[3,256,64]{1,2,0:T(8,128)(2,1)S(1)} %get-tuple-element.65), channel_id=1, source_target_pairs={{0,12},{4,0},{8,4},{12,8},{1,13},{5,1},{9,5},{13,9},{2,14},{6,2},{... | collective-permute-start | bytes 294920 | tf_op jit(solution)/shard_map/ppermute | solution.py:15
  100.1 2.6 %collective-permute-done.24 = bf16[3,256,64]{1,2,0:T(8,128)(2,1)S(1)} collective-permute-done((bf16[3,256,64]{1,2,0:T(8,128)(2,1)S(1)}, bf16[3,256,64]{1,2,0:T(8,128)(2,1)S(1)}, u32[]{:S(2)}, u32[]{:S(2)}) %collective-permute-start.24) | collective-permute-done | bytes 98336 | tf_op jit(solution)/shard_map/ppermute | solution.py:15
  102.6 2.6 %collective-permute-done.25 = bf16[3,256,64]{1,2,0:T(8,128)(2,1)S(1)} collective-permute-done((bf16[3,256,64]{1,2,0:T(8,128)(2,1)S(1)}, bf16[3,256,64]{1,2,0:T(8,128)(2,1)S(1)}, u32[]{:S(2)}, u32[]{:S(2)}) %collective-permute-start.25) | collective-permute-done | bytes 98336 | tf_op jit(solution)/shard_map/ppermute | solution.py:15
  106.6 6.1 %collective-permute-done.16 = bf16[2,512,256]{2,1,0:T(8,128)(2,1)S(1)} collective-permute-done((bf16[2,512,256]{2,1,0:T(8,128)(2,1)S(1)}, bf16[2,512,256]{2,1,0:T(8,128)(2,1)S(1)}, u32[]{:S(2)}, u32[]{:S(2)}) %collective-permute-start.16) | collective-permute-done | bytes 524320 | tf_op jit(solution)/shard_map/ppermute | solution.py:15
  115.9 3.8 %collective-permute-start.30 = (bf16[3,256,64]{1,2,0:T(8,128)(2,1)S(1)}, bf16[3,256,64]{1,2,0:T(8,128)(2,1)S(1)}, u32[]{:S(2)}, u32[]{:S(2)}) collective-permute-start(bf16[3,256,64]{1,2,0:T(8,128)(2,1)S(1)} %multiply_convert_fusion.41), channel_id=1, source_target_pairs={{0,14},{2,12},{4,2},{6,0},{8,6},{10,4},{12,10},{14,8},{1,15},{3,13... | collective-permute-start | bytes 294920 | tf_op jit(solution)/shard_map/ppermute | solution.py:53
  121.2 2.0 %collective-permute-done.29 = bf16[3,256,64]{1,2,0:T(8,128)(2,1)S(1)} collective-permute-done((bf16[3,256,64]{1,2,0:T(8,128)(2,1)S(1)}, bf16[3,256,64]{1,2,0:T(8,128)(2,1)S(1)}, u32[]{:S(2)}, u32[]{:S(2)}) %collective-permute-start.29) | collective-permute-done | bytes 98336 | tf_op jit(solution)/shard_map/ppermute | solution.py:53
  127.6 2.4 %collective-permute-start.33 = (bf16[3,256,64]{1,2,0:T(8,128)(2,1)S(1)}, bf16[3,256,64]{1,2,0:T(8,128)(2,1)S(1)}, u32[]{:S(2)}, u32[]{:S(2)}) collective-permute-start(bf16[3,256,64]{1,2,0:T(8,128)(2,1)S(1)} %get-tuple-element.63), channel_id=1, source_target_pairs={{0,8},{4,12},{8,0},{12,4},{1,9},{5,13},{9,1},{13,5},{2,10},{6,14},... | collective-permute-start | bytes 294920 | tf_op jit(solution)/shard_map/ppermute | solution.py:15
  130.1 2.3 %convolution_convert_fusion.2 = bf16[512,256]{1,0:T(8,128)(2,1)} fusion(f32[512,256]{1,0:T(8,128)} %convolution_bitcast_fusion.12, bf16[2,512,256]{2,1,0:T(8,128)(2,1)} %copy-done.4, bf16[3,256,256]{1,2,0:T(8,128)(2,1)S(1)} %constant_dynamic-update-slice_fusion.16), kind=kOutput, calls=%fused_computation.21 | convolution fusion | flops 135135232 | bytes 1310720 | tf_op jit(solution)/shard_map/th,hd->td/dot_general | solution.py:84
  133.3 1.9 %collective-permute-done.33 = bf16[3,256,64]{1,2,0:T(8,128)(2,1)S(1)} collective-permute-done((bf16[3,256,64]{1,2,0:T(8,128)(2,1)S(1)}, bf16[3,256,64]{1,2,0:T(8,128)(2,1)S(1)}, u32[]{:S(2)}, u32[]{:S(2)}) %collective-permute-start.33) | collective-permute-done | bytes 98336 | tf_op jit(solution)/shard_map/ppermute | solution.py:15
  142.6 7.7 %collective-permute-done.36 = bf16[3,256,64]{1,2,0:T(8,128)(2,1)S(1)} collective-permute-done((bf16[3,256,64]{1,2,0:T(8,128)(2,1)S(1)}, bf16[3,256,64]{1,2,0:T(8,128)(2,1)S(1)}, u32[]{:S(2)}, u32[]{:S(2)}) %collective-permute-start.36) | collective-permute-done | bytes 98336 | tf_op jit(solution)/shard_map/ppermute | solution.py:15
  153.6 2.8 %collective-permute-start.40 = (bf16[3,256,64]{1,2,0:T(8,128)(2,1)S(1)}, bf16[3,256,64]{1,2,0:T(8,128)(2,1)S(1)}, u32[]{:S(2)}, u32[]{:S(2)}) collective-permute-start(bf16[3,256,64]{1,2,0:T(8,128)(2,1)S(1)} %get-tuple-element.59), channel_id=1, source_target_pairs={{0,12},{4,0},{8,4},{12,8},{1,13},{5,1},{9,5},{13,9},{2,14},{6,2},{... | collective-permute-start | bytes 294920 | tf_op jit(solution)/shard_map/ppermute | solution.py:15
  159.1 3.7 %collective-permute-done.39 = bf16[3,256,64]{1,2,0:T(8,128)(2,1)S(1)} collective-permute-done((bf16[3,256,64]{1,2,0:T(8,128)(2,1)S(1)}, bf16[3,256,64]{1,2,0:T(8,128)(2,1)S(1)}, u32[]{:S(2)}, u32[]{:S(2)}) %collective-permute-start.39) | collective-permute-done | bytes 98336 | tf_op jit(solution)/shard_map/ppermute | solution.py:15
  163.3 3.3 %collective-permute-start.41 = (bf16[3,256,64]{1,2,0:T(8,128)(2,1)S(1)}, bf16[3,256,64]{1,2,0:T(8,128)(2,1)S(1)}, u32[]{:S(2)}, u32[]{:S(2)}) collective-permute-start(bf16[3,256,64]{1,2,0:T(8,128)(2,1)S(1)} %get-tuple-element.37), channel_id=1, source_target_pairs={{0,12},{4,0},{8,4},{12,8},{1,13},{5,1},{9,5},{13,9},{2,14},{6,2},{... | collective-permute-start | bytes 294920 | tf_op jit(solution)/shard_map/ppermute | solution.py:15
  168.7 5.1 %collective-permute-done.42 = bf16[3,256,64]{1,2,0:T(8,128)(2,1)S(1)} collective-permute-done((bf16[3,256,64]{1,2,0:T(8,128)(2,1)S(1)}, bf16[3,256,64]{1,2,0:T(8,128)(2,1)S(1)}, u32[]{:S(2)}, u32[]{:S(2)}) %collective-permute-start.42) | collective-permute-done | bytes 98336 | tf_op jit(solution)/shard_map/ppermute | solution.py:15
  174.6 1.9 %maximum_bitcast_fusion = bf16[3,1,512,1,256]{4,2,3,1,0:T(8,128)(2,1)} fusion(bf16[1,512,256]{2,1,0:T(8,128)(2,1)S(1)} %fusion, bf16[1,512,256]{2,1,0:T(8,128)(2,1)S(1)} %bitcast.320, bf16[1,512,256]{2,1,0:T(8,128)(2,1)} %bitcast.34), kind=kLoop, calls=%fused_computation.59 | loop fusion | flops 786432 | bytes 1572864
  (190 shorter events, 60.3 us)
Async XLA Ops:
  3.7 7.3 %collective-permute-start = (bf16[3,256,64]{1,2,0:T(8,128)(2,1)S(1)}, bf16[3,256,64]{1,2,0:T(8,128)(2,1)S(1)}, u32[]{:S(2)}, u32[]{:S(2)}) collective-permute-start(bf16[3,256,64]{1,2,0:T(8,128)(2,1)S(1)} %get-tuple-element.57), channel_id=1, source_target_pairs={{0,12},{4,0},{8,4},{12,8},{1,13},{5,1},{9,5},{13,9},{2,14},{6,2},{... | collective-permute-start | bytes 294920 | tf_op jit(solution)/shard_map/ppermute | solution.py:15
  18.4 7.6 %collective-permute-start.4 = (bf16[3,256,64]{1,2,0:T(8,128)(2,1)S(1)}, bf16[3,256,64]{1,2,0:T(8,128)(2,1)S(1)}, u32[]{:S(2)}, u32[]{:S(2)}) collective-permute-start(bf16[3,256,64]{1,2,0:T(8,128)(2,1)S(1)} %get-tuple-element.75), channel_id=1, source_target_pairs={{0,8},{4,12},{8,0},{12,4},{1,9},{5,13},{9,1},{13,5},{2,10},{6,14},... | collective-permute-start | bytes 294920 | tf_op jit(solution)/shard_map/ppermute | solution.py:15
  30.8 9.7 %collective-permute-start.7 = (bf16[3,256,64]{1,2,0:T(8,128)(2,1)S(1)}, bf16[3,256,64]{1,2,0:T(8,128)(2,1)S(1)}, u32[]{:S(2)}, u32[]{:S(2)}) collective-permute-start(bf16[3,256,64]{1,2,0:T(8,128)(2,1)S(1)} %get-tuple-element.53), channel_id=1, source_target_pairs={{0,8},{4,12},{8,0},{12,4},{1,9},{5,13},{9,1},{13,5},{2,10},{6,14},... | collective-permute-start | bytes 294920 | tf_op jit(solution)/shard_map/ppermute | solution.py:15
  30.8 9.7 %collective-permute-start.8 = (bf16[3,256,64]{1,2,0:T(8,128)(2,1)S(1)}, bf16[3,256,64]{1,2,0:T(8,128)(2,1)S(1)}, u32[]{:S(2)}, u32[]{:S(2)}) collective-permute-start(bf16[3,256,64]{1,2,0:T(8,128)(2,1)S(1)} %get-tuple-element.53), channel_id=1, source_target_pairs={{0,4},{4,8},{8,12},{12,0},{1,5},{5,9},{9,13},{13,1},{2,6},{6,10},{... | collective-permute-start | bytes 294920 | tf_op jit(solution)/shard_map/ppermute | solution.py:15
  42.7 8.2 %collective-permute-start.10 = (bf16[3,256,64]{1,2,0:T(8,128)(2,1)S(1)}, bf16[3,256,64]{1,2,0:T(8,128)(2,1)S(1)}, u32[]{:S(2)}, u32[]{:S(2)}) collective-permute-start(bf16[3,256,64]{1,2,0:T(8,128)(2,1)S(1)} %get-tuple-element.72), channel_id=1, source_target_pairs={{0,8},{4,12},{8,0},{12,4},{1,9},{5,13},{9,1},{13,5},{2,10},{6,14},... | collective-permute-start | bytes 294920 | tf_op jit(solution)/shard_map/ppermute | solution.py:15
  44.1 9.3 %collective-permute-start.11 = (bf16[3,256,64]{1,2,0:T(8,128)(2,1)S(1)}, bf16[3,256,64]{1,2,0:T(8,128)(2,1)S(1)}, u32[]{:S(2)}, u32[]{:S(2)}) collective-permute-start(bf16[3,256,64]{1,2,0:T(8,128)(2,1)S(1)} %get-tuple-element.71), channel_id=1, source_target_pairs={{0,12},{4,0},{8,4},{12,8},{1,13},{5,1},{9,5},{13,9},{2,14},{6,2},{... | collective-permute-start | bytes 294920 | tf_op jit(solution)/shard_map/ppermute | solution.py:15
  44.6 8.9 %collective-permute-start.9 = (bf16[3,256,64]{1,2,0:T(8,128)(2,1)S(1)}, bf16[3,256,64]{1,2,0:T(8,128)(2,1)S(1)}, u32[]{:S(2)}, u32[]{:S(2)}) collective-permute-start(bf16[3,256,64]{1,2,0:T(8,128)(2,1)S(1)} %get-tuple-element.70), channel_id=1, source_target_pairs={{0,4},{4,8},{8,12},{12,0},{1,5},{5,9},{9,13},{13,1},{2,6},{6,10},{... | collective-permute-start | bytes 294920 | tf_op jit(solution)/shard_map/ppermute | solution.py:15
  55.4 8.0 %collective-permute-start.13 = (bf16[3,256,64]{1,2,0:T(8,128)(2,1)S(1)}, bf16[3,256,64]{1,2,0:T(8,128)(2,1)S(1)}, u32[]{:S(2)}, u32[]{:S(2)}) collective-permute-start(bf16[3,256,64]{1,2,0:T(8,128)(2,1)S(1)} %multiply_convert_fusion.42), channel_id=1, source_target_pairs={{0,6},{2,4},{4,10},{6,8},{8,14},{10,12},{12,2},{14,0},{1,7},{3,5},... | collective-permute-start | bytes 294920 | tf_op jit(solution)/shard_map/ppermute | solution.py:53
  57.0 9.4 %collective-permute-start.14 = (bf16[3,256,64]{1,2,0:T(8,128)(2,1)S(1)}, bf16[3,256,64]{1,2,0:T(8,128)(2,1)S(1)}, u32[]{:S(2)}, u32[]{:S(2)}) collective-permute-start(bf16[3,256,64]{1,2,0:T(8,128)(2,1)S(1)} %multiply_convert_fusion.42), channel_id=1, source_target_pairs={{0,10},{2,8},{4,14},{6,12},{8,2},{10,0},{12,6},{14,4},{1,11},{3,9}... | collective-permute-start | bytes 294920 | tf_op jit(solution)/shard_map/ppermute | solution.py:53
  57.2 9.2 %collective-permute-start.15 = (bf16[3,256,64]{1,2,0:T(8,128)(2,1)S(1)}, bf16[3,256,64]{1,2,0:T(8,128)(2,1)S(1)}, u32[]{:S(2)}, u32[]{:S(2)}) collective-permute-start(bf16[3,256,64]{1,2,0:T(8,128)(2,1)S(1)} %multiply_convert_fusion.42), channel_id=1, source_target_pairs={{0,14},{2,12},{4,2},{6,0},{8,6},{10,4},{12,10},{14,8},{1,15},{3,13... | collective-permute-start | bytes 294920 | tf_op jit(solution)/shard_map/ppermute | solution.py:53
  68.7 7.4 %collective-permute-start.18 = (bf16[3,256,64]{1,2,0:T(8,128)(2,1)S(1)}, bf16[3,256,64]{1,2,0:T(8,128)(2,1)S(1)}, u32[]{:S(2)}, u32[]{:S(2)}) collective-permute-start(bf16[3,256,64]{1,2,0:T(8,128)(2,1)S(1)} %get-tuple-element.67), channel_id=1, source_target_pairs={{0,4},{4,8},{8,12},{12,0},{1,5},{5,9},{9,13},{13,1},{2,6},{6,10},{... | collective-permute-start | bytes 294920 | tf_op jit(solution)/shard_map/ppermute | solution.py:15
  71.3 8.2 %collective-permute-start.19 = (bf16[3,256,64]{1,2,0:T(8,128)(2,1)S(1)}, bf16[3,256,64]{1,2,0:T(8,128)(2,1)S(1)}, u32[]{:S(2)}, u32[]{:S(2)}) collective-permute-start(bf16[3,256,64]{1,2,0:T(8,128)(2,1)S(1)} %get-tuple-element.69), channel_id=1, source_target_pairs={{0,8},{4,12},{8,0},{12,4},{1,9},{5,13},{9,1},{13,5},{2,10},{6,14},... | collective-permute-start | bytes 294920 | tf_op jit(solution)/shard_map/ppermute | solution.py:15
  72.2 7.2 %collective-permute-start.20 = (bf16[3,256,64]{1,2,0:T(8,128)(2,1)S(1)}, bf16[3,256,64]{1,2,0:T(8,128)(2,1)S(1)}, u32[]{:S(2)}, u32[]{:S(2)}) collective-permute-start(bf16[3,256,64]{1,2,0:T(8,128)(2,1)S(1)} %get-tuple-element.68), channel_id=1, source_target_pairs={{0,12},{4,0},{8,4},{12,8},{1,13},{5,1},{9,5},{13,9},{2,14},{6,2},{... | collective-permute-start | bytes 294920 | tf_op jit(solution)/shard_map/ppermute | solution.py:15
  79.8 6.7 %collective-permute-start.21 = (bf16[3,256,64]{1,2,0:T(8,128)(2,1)S(1)}, bf16[3,256,64]{1,2,0:T(8,128)(2,1)S(1)}, u32[]{:S(2)}, u32[]{:S(2)}) collective-permute-start(bf16[3,256,64]{1,2,0:T(8,128)(2,1)S(1)} %get-tuple-element.47), channel_id=1, source_target_pairs={{0,12},{4,0},{8,4},{12,8},{1,13},{5,1},{9,5},{13,9},{2,14},{6,2},{... | collective-permute-start | bytes 294920 | tf_op jit(solution)/shard_map/ppermute | solution.py:15
  83.3 9.6 %collective-permute-start.22 = (bf16[3,256,64]{1,2,0:T(8,128)(2,1)S(1)}, bf16[3,256,64]{1,2,0:T(8,128)(2,1)S(1)}, u32[]{:S(2)}, u32[]{:S(2)}) collective-permute-start(bf16[3,256,64]{1,2,0:T(8,128)(2,1)S(1)} %get-tuple-element.47), channel_id=1, source_target_pairs={{0,8},{4,12},{8,0},{12,4},{1,9},{5,13},{9,1},{13,5},{2,10},{6,14},... | collective-permute-start | bytes 294920 | tf_op jit(solution)/shard_map/ppermute | solution.py:15
  83.9 9.0 %collective-permute-start.23 = (bf16[3,256,64]{1,2,0:T(8,128)(2,1)S(1)}, bf16[3,256,64]{1,2,0:T(8,128)(2,1)S(1)}, u32[]{:S(2)}, u32[]{:S(2)}) collective-permute-start(bf16[3,256,64]{1,2,0:T(8,128)(2,1)S(1)} %get-tuple-element.47), channel_id=1, source_target_pairs={{0,4},{4,8},{8,12},{12,0},{1,5},{5,9},{9,13},{13,1},{2,6},{6,10},{... | collective-permute-start | bytes 294920 | tf_op jit(solution)/shard_map/ppermute | solution.py:15
  95.1 7.5 %collective-permute-start.24 = (bf16[3,256,64]{1,2,0:T(8,128)(2,1)S(1)}, bf16[3,256,64]{1,2,0:T(8,128)(2,1)S(1)}, u32[]{:S(2)}, u32[]{:S(2)}) collective-permute-start(bf16[3,256,64]{1,2,0:T(8,128)(2,1)S(1)} %get-tuple-element.64), channel_id=1, source_target_pairs={{0,4},{4,8},{8,12},{12,0},{1,5},{5,9},{9,13},{13,1},{2,6},{6,10},{... | collective-permute-start | bytes 294920 | tf_op jit(solution)/shard_map/ppermute | solution.py:15
  95.2 10.1 %collective-permute-start.25 = (bf16[3,256,64]{1,2,0:T(8,128)(2,1)S(1)}, bf16[3,256,64]{1,2,0:T(8,128)(2,1)S(1)}, u32[]{:S(2)}, u32[]{:S(2)}) collective-permute-start(bf16[3,256,64]{1,2,0:T(8,128)(2,1)S(1)} %get-tuple-element.66), channel_id=1, source_target_pairs={{0,8},{4,12},{8,0},{12,4},{1,9},{5,13},{9,1},{13,5},{2,10},{6,14},... | collective-permute-start | bytes 294920 | tf_op jit(solution)/shard_map/ppermute | solution.py:15
  96.4 8.8 %collective-permute-start.26 = (bf16[3,256,64]{1,2,0:T(8,128)(2,1)S(1)}, bf16[3,256,64]{1,2,0:T(8,128)(2,1)S(1)}, u32[]{:S(2)}, u32[]{:S(2)}) collective-permute-start(bf16[3,256,64]{1,2,0:T(8,128)(2,1)S(1)} %get-tuple-element.65), channel_id=1, source_target_pairs={{0,12},{4,0},{8,4},{12,8},{1,13},{5,1},{9,5},{13,9},{2,14},{6,2},{... | collective-permute-start | bytes 294920 | tf_op jit(solution)/shard_map/ppermute | solution.py:15
  99.1 13.6 %collective-permute-start.16 = (bf16[2,512,256]{2,1,0:T(8,128)(2,1)S(1)}, bf16[2,512,256]{2,1,0:T(8,128)(2,1)S(1)}, u32[]{:S(2)}, u32[]{:S(2)}) collective-permute-start(bf16[2,512,256]{2,1,0:T(8,128)(2,1)S(1)} %slice_bitcast_fusion), channel_id=1, source_target_pairs={{0,2},{2,0},{1,3},{3,1},{4,6},{6,4},{5,7},{7,5},{8,10},{10,8},{9,1... | collective-permute-start | bytes 1572872 | tf_op jit(solution)/shard_map/ppermute | solution.py:15
  105.6 14.0 %collective-permute-start.27 = (bf16[3,256,64]{1,2,0:T(8,128)(2,1)S(1)}, bf16[3,256,64]{1,2,0:T(8,128)(2,1)S(1)}, u32[]{:S(2)}, u32[]{:S(2)}) collective-permute-start(bf16[3,256,64]{1,2,0:T(8,128)(2,1)S(1)} %multiply_convert_fusion.41), channel_id=1, source_target_pairs={{0,2},{2,0},{4,6},{6,4},{8,10},{10,8},{12,14},{14,12},{1,3},{3,1},... | collective-permute-start | bytes 294920 | tf_op jit(solution)/shard_map/ppermute | solution.py:53
  113.7 7.4 %collective-permute-start.28 = (bf16[3,256,64]{1,2,0:T(8,128)(2,1)S(1)}, bf16[3,256,64]{1,2,0:T(8,128)(2,1)S(1)}, u32[]{:S(2)}, u32[]{:S(2)}) collective-permute-start(bf16[3,256,64]{1,2,0:T(8,128)(2,1)S(1)} %multiply_convert_fusion.41), channel_id=1, source_target_pairs={{0,6},{2,4},{4,10},{6,8},{8,14},{10,12},{12,2},{14,0},{1,7},{3,5},... | collective-permute-start | bytes 294920 | tf_op jit(solution)/shard_map/ppermute | solution.py:53
  114.7 8.5 %collective-permute-start.29 = (bf16[3,256,64]{1,2,0:T(8,128)(2,1)S(1)}, bf16[3,256,64]{1,2,0:T(8,128)(2,1)S(1)}, u32[]{:S(2)}, u32[]{:S(2)}) collective-permute-start(bf16[3,256,64]{1,2,0:T(8,128)(2,1)S(1)} %multiply_convert_fusion.41), channel_id=1, source_target_pairs={{0,10},{2,8},{4,14},{6,12},{8,2},{10,0},{12,6},{14,4},{1,11},{3,9}... | collective-permute-start | bytes 294920 | tf_op jit(solution)/shard_map/ppermute | solution.py:53
  115.9 7.3 %collective-permute-start.30 = (bf16[3,256,64]{1,2,0:T(8,128)(2,1)S(1)}, bf16[3,256,64]{1,2,0:T(8,128)(2,1)S(1)}, u32[]{:S(2)}, u32[]{:S(2)}) collective-permute-start(bf16[3,256,64]{1,2,0:T(8,128)(2,1)S(1)} %multiply_convert_fusion.41), channel_id=1, source_target_pairs={{0,14},{2,12},{4,2},{6,0},{8,6},{10,4},{12,10},{14,8},{1,15},{3,13... | collective-permute-start | bytes 294920 | tf_op jit(solution)/shard_map/ppermute | solution.py:53
  126.1 7.2 %collective-permute-start.32 = (bf16[3,256,64]{1,2,0:T(8,128)(2,1)}, bf16[3,256,64]{1,2,0:T(8,128)(2,1)S(1)}, u32[]{:S(2)}, u32[]{:S(2)}) collective-permute-start(bf16[3,256,64]{1,2,0:T(8,128)(2,1)} %get-tuple-element.61), channel_id=1, source_target_pairs={{0,4},{4,8},{8,12},{12,0},{1,5},{5,9},{9,13},{13,1},{2,6},{6,10},{... | collective-permute-start | bytes 294920 | tf_op jit(solution)/shard_map/ppermute | solution.py:15
  127.6 7.5 %collective-permute-start.33 = (bf16[3,256,64]{1,2,0:T(8,128)(2,1)S(1)}, bf16[3,256,64]{1,2,0:T(8,128)(2,1)S(1)}, u32[]{:S(2)}, u32[]{:S(2)}) collective-permute-start(bf16[3,256,64]{1,2,0:T(8,128)(2,1)S(1)} %get-tuple-element.63), channel_id=1, source_target_pairs={{0,8},{4,12},{8,0},{12,4},{1,9},{5,13},{9,1},{13,5},{2,10},{6,14},... | collective-permute-start | bytes 294920 | tf_op jit(solution)/shard_map/ppermute | solution.py:15
  132.4 42.3 %collective-permute-start.17 = (bf16[512,256]{1,0:T(8,128)(2,1)}, bf16[512,256]{1,0:T(8,128)(2,1)}, u32[]{:S(2)}, u32[]{:S(2)}) collective-permute-start(bf16[512,256]{1,0:T(8,128)(2,1)} %convolution_convert_fusion.2), channel_id=1, source_target_pairs={{0,2},{2,0},{1,3},{3,1},{4,6},{6,4},{5,7},{7,5},{8,10},{10,8},{9,1... | collective-permute-start | bytes 786440 | tf_op jit(solution)/shard_map/ppermute | solution.py:15
  140.0 10.3 %collective-permute-start.36 = (bf16[3,256,64]{1,2,0:T(8,128)(2,1)S(1)}, bf16[3,256,64]{1,2,0:T(8,128)(2,1)S(1)}, u32[]{:S(2)}, u32[]{:S(2)}) collective-permute-start(bf16[3,256,64]{1,2,0:T(8,128)(2,1)S(1)} %get-tuple-element.41), channel_id=1, source_target_pairs={{0,8},{4,12},{8,0},{12,4},{1,9},{5,13},{9,1},{13,5},{2,10},{6,14},... | collective-permute-start | bytes 294920 | tf_op jit(solution)/shard_map/ppermute | solution.py:15
  141.4 8.9 %collective-permute-start.37 = (bf16[3,256,64]{1,2,0:T(8,128)(2,1)S(1)}, bf16[3,256,64]{1,2,0:T(8,128)(2,1)S(1)}, u32[]{:S(2)}, u32[]{:S(2)}) collective-permute-start(bf16[3,256,64]{1,2,0:T(8,128)(2,1)S(1)} %get-tuple-element.41), channel_id=1, source_target_pairs={{0,4},{4,8},{8,12},{12,0},{1,5},{5,9},{9,13},{13,1},{2,6},{6,10},{... | collective-permute-start | bytes 294920 | tf_op jit(solution)/shard_map/ppermute | solution.py:15
  152.5 10.3 %collective-permute-start.39 = (bf16[3,256,64]{1,2,0:T(8,128)(2,1)S(1)}, bf16[3,256,64]{1,2,0:T(8,128)(2,1)S(1)}, u32[]{:S(2)}, u32[]{:S(2)}) collective-permute-start(bf16[3,256,64]{1,2,0:T(8,128)(2,1)S(1)} %get-tuple-element.60), channel_id=1, source_target_pairs={{0,8},{4,12},{8,0},{12,4},{1,9},{5,13},{9,1},{13,5},{2,10},{6,14},... | collective-permute-start | bytes 294920 | tf_op jit(solution)/shard_map/ppermute | solution.py:15
  153.6 9.2 %collective-permute-start.40 = (bf16[3,256,64]{1,2,0:T(8,128)(2,1)S(1)}, bf16[3,256,64]{1,2,0:T(8,128)(2,1)S(1)}, u32[]{:S(2)}, u32[]{:S(2)}) collective-permute-start(bf16[3,256,64]{1,2,0:T(8,128)(2,1)S(1)} %get-tuple-element.59), channel_id=1, source_target_pairs={{0,12},{4,0},{8,4},{12,8},{1,13},{5,1},{9,5},{13,9},{2,14},{6,2},{... | collective-permute-start | bytes 294920 | tf_op jit(solution)/shard_map/ppermute | solution.py:15
  156.9 17.7 %collective-permute-start.31 = (bf16[512,256]{1,0:T(8,128)(2,1)S(1)}, bf16[512,256]{1,0:T(8,128)(2,1)S(1)}, u32[]{:S(2)}, u32[]{:S(2)}) collective-permute-start(bf16[512,256]{1,0:T(8,128)(2,1)S(1)} %convolution_convert_fusion.1), channel_id=1, source_target_pairs={{0,2},{2,0},{1,3},{3,1},{4,6},{6,4},{5,7},{7,5},{8,10},{10,8},{9,1... | collective-permute-start | bytes 786440 | tf_op jit(solution)/shard_map/ppermute | solution.py:15
  (21 other events, 123.5 us)

commit v12 on v10

--- a/solution.py
+++ b/solution.py
@@ -7,7 +7,7 @@
 
 
 ITERS = 2
-DELAY_STEPS = 60
+DELAY_STEPS = 80
 
 
 def rotated(value, axis, by):
@@ -97,8 +97,7 @@
     tick_count = key_rows.shape[0]
     results = []
     weights = states_in[0, 0]
-    anchor = jnp.abs(weights[0, 0, 0]) + 1.0
-    unit = anchor / anchor
+    unit = (init_norms[0, 0] + 1.0) / (init_norms[0, 0] + 1.0)
     weights = lax.fori_loop(
         0, lax.axis_index("head") * DELAY_STEPS, lambda step, held: held * unit, weights
     )

time: 169 us -> 170 us (level)
  starting transfers between devices: 68.7 us -> 72 us
  waiting for transfers between devices: 71 us -> 67.9 us
    ppermute x36, starting transfers between devices: 55.6 us -> 58 us  [rotated(): lax.ppermute(value, axis, [(i, (i + by) % devices) for i in range(devices)])]
    ppermute x8, waiting for transfers between devices: 10.5 us -> 8.41 us  [cross_gather(): got = lax.ppermute(own, ('tok', 'span'), pairs)]
where the time goes in v12:
time: 170 us
  starting transfers between devices  72 us (42%)
  waiting for transfers between devices  67.9 us (40%)
  matrix products  17.7 us (10%)
  other arithmetic  6.22 us (4%)
  local copies, waits for them, and re-layouts  3.97 us (2%)
  between operations  2.21 us (1%)
    ppermute x36, waiting for transfers between devices, rotated(): lax.ppermute(value, axis, [(i, (i + by) % devices) for i in range(devices)])  59.5 us
    ppermute x36, starting transfers between devices, rotated(): lax.ppermute(value, axis, [(i, (i + by) % devices) for i in range(devices)])  58 us
    ppermute x8, starting transfers between devices, cross_gather(): got = lax.ppermute(own, ('tok', 'span'), pairs)  14 us
    ppermute x8, waiting for transfers between devices, cross_gather(): got = lax.ppermute(own, ('tok', 'span'), pairs)  8.41 us
  transfers between devices with their start and end apart: 44, of which 29 were waited for; matrix products, arithmetic and copies ran while one was open for 6% of the time, Pallas kernels for 0%

profile of v12, /device:TPU:0, one launch (start us, length us, event | category | flops | bytes accessed | tf_op | source)
XLA Modules:
  0.0 170.0 jit_solution(254235687717507292)
XLA Ops:
  3.7 3.1 %collective-permute-start = (bf16[3,256,64]{1,2,0:T(8,128)(2,1)S(1)}, bf16[3,256,64]{1,2,0:T(8,128)(2,1)S(1)}, u32[]{:S(2)}, u32[]{:S(2)}) collective-permute-start(bf16[3,256,64]{1,2,0:T(8,128)(2,1)S(1)} %get-tuple-element.57), channel_id=1, source_target_pairs={{0,4},{4,8},{8,12},{12,0},{1,5},{5,9},{9,13},{13,1},{2,6},{6,10},{... | collective-permute-start | bytes 294920 | tf_op jit(solution)/shard_map/ppermute | solution.py:15
  6.8 2.6 %collective-permute-start.1 = (bf16[3,256,64]{1,2,0:T(8,128)(2,1)S(1)}, bf16[3,256,64]{1,2,0:T(8,128)(2,1)S(1)}, u32[]{:S(2)}, u32[]{:S(2)}) collective-permute-start(bf16[3,256,64]{1,2,0:T(8,128)(2,1)S(1)} %get-tuple-element.57), channel_id=1, source_target_pairs={{0,8},{4,12},{8,0},{12,4},{1,9},{5,13},{9,1},{13,5},{2,10},{6,14},... | collective-permute-start | bytes 294920 | tf_op jit(solution)/shard_map/ppermute | solution.py:15
  11.4 2.2 %collective-permute-done.1 = bf16[3,256,64]{1,2,0:T(8,128)(2,1)S(1)} collective-permute-done((bf16[3,256,64]{1,2,0:T(8,128)(2,1)S(1)}, bf16[3,256,64]{1,2,0:T(8,128)(2,1)S(1)}, u32[]{:S(2)}, u32[]{:S(2)}) %collective-permute-start.1) | collective-permute-done | bytes 98336 | tf_op jit(solution)/shard_map/ppermute | solution.py:15
  18.0 2.6 %collective-permute-start.4 = (bf16[3,256,64]{1,2,0:T(8,128)(2,1)S(1)}, bf16[3,256,64]{1,2,0:T(8,128)(2,1)S(1)}, u32[]{:S(2)}, u32[]{:S(2)}) collective-permute-start(bf16[3,256,64]{1,2,0:T(8,128)(2,1)S(1)} %get-tuple-element.75), channel_id=1, source_target_pairs={{0,8},{4,12},{8,0},{12,4},{1,9},{5,13},{9,1},{13,5},{2,10},{6,14},... | collective-permute-start | bytes 294920 | tf_op jit(solution)/shard_map/ppermute | solution.py:15
  20.7 2.7 %collective-permute-done.3 = bf16[3,256,64]{1,2,0:T(8,128)(2,1)S(1)} collective-permute-done((bf16[3,256,64]{1,2,0:T(8,128)(2,1)S(1)}, bf16[3,256,64]{1,2,0:T(8,128)(2,1)S(1)}, u32[]{:S(2)}, u32[]{:S(2)}) %collective-permute-start.3) | collective-permute-done | bytes 98336 | tf_op jit(solution)/shard_map/ppermute | solution.py:15
  23.4 2.2 %collective-permute-done.4 = bf16[3,256,64]{1,2,0:T(8,128)(2,1)S(1)} collective-permute-done((bf16[3,256,64]{1,2,0:T(8,128)(2,1)S(1)}, bf16[3,256,64]{1,2,0:T(8,128)(2,1)S(1)}, u32[]{:S(2)}, u32[]{:S(2)}) %collective-permute-start.4) | collective-permute-done | bytes 98336 | tf_op jit(solution)/shard_map/ppermute | solution.py:15
  30.4 2.7 %collective-permute-done.6 = bf16[3,256,64]{1,2,0:T(8,128)(2,1)S(1)} collective-permute-done((bf16[3,256,64]{1,2,0:T(8,128)(2,1)S(1)}, bf16[3,256,64]{1,2,0:T(8,128)(2,1)S(1)}, u32[]{:S(2)}, u32[]{:S(2)}) %collective-permute-start.6) | collective-permute-done | bytes 98336 | tf_op jit(solution)/shard_map/ppermute | solution.py:15
  33.1 3.0 %collective-permute-done.7 = bf16[3,256,64]{1,2,0:T(8,128)(2,1)S(1)} collective-permute-done((bf16[3,256,64]{1,2,0:T(8,128)(2,1)S(1)}, bf16[3,256,64]{1,2,0:T(8,128)(2,1)S(1)}, u32[]{:S(2)}, u32[]{:S(2)}) %collective-permute-start.7) | collective-permute-done | bytes 98336 | tf_op jit(solution)/shard_map/ppermute | solution.py:15
  39.1 3.2 %collective-permute-start.11 = (bf16[3,256,64]{1,2,0:T(8,128)(2,1)S(1)}, bf16[3,256,64]{1,2,0:T(8,128)(2,1)S(1)}, u32[]{:S(2)}, u32[]{:S(2)}) collective-permute-start(bf16[3,256,64]{1,2,0:T(8,128)(2,1)S(1)} %get-tuple-element.71), channel_id=1, source_target_pairs={{0,12},{4,0},{8,4},{12,8},{1,13},{5,1},{9,5},{13,9},{2,14},{6,2},{... | collective-permute-start | bytes 294920 | tf_op jit(solution)/shard_map/ppermute | solution.py:15
  42.3 2.8 %collective-permute-done.10 = bf16[3,256,64]{1,2,0:T(8,128)(2,1)S(1)} collective-permute-done((bf16[3,256,64]{1,2,0:T(8,128)(2,1)S(1)}, bf16[3,256,64]{1,2,0:T(8,128)(2,1)S(1)}, u32[]{:S(2)}, u32[]{:S(2)}) %collective-permute-start.10) | collective-permute-done | bytes 98336 | tf_op jit(solution)/shard_map/ppermute | solution.py:15
  45.1 3.7 %collective-permute-done.9 = bf16[3,256,64]{1,2,0:T(8,128)(2,1)S(1)} collective-permute-done((bf16[3,256,64]{1,2,0:T(8,128)(2,1)S(1)}, bf16[3,256,64]{1,2,0:T(8,128)(2,1)S(1)}, u32[]{:S(2)}, u32[]{:S(2)}) %collective-permute-start.9) | collective-permute-done | bytes 98336 | tf_op jit(solution)/shard_map/ppermute | solution.py:15
  52.2 3.4 %collective-permute-start.15 = (bf16[3,256,64]{1,2,0:T(8,128)(2,1)S(1)}, bf16[3,256,64]{1,2,0:T(8,128)(2,1)S(1)}, u32[]{:S(2)}, u32[]{:S(2)}) collective-permute-start(bf16[3,256,64]{1,2,0:T(8,128)(2,1)S(1)} %multiply_convert_fusion.42), channel_id=1, source_target_pairs={{0,14},{2,12},{4,2},{6,0},{8,6},{10,4},{12,10},{14,8},{1,15},{3,13... | collective-permute-start | bytes 294920 | tf_op jit(solution)/shard_map/ppermute | solution.py:50
  55.6 2.8 %collective-permute-done.13 = bf16[3,256,64]{1,2,0:T(8,128)(2,1)S(1)} collective-permute-done((bf16[3,256,64]{1,2,0:T(8,128)(2,1)S(1)}, bf16[3,256,64]{1,2,0:T(8,128)(2,1)S(1)}, u32[]{:S(2)}, u32[]{:S(2)}) %collective-permute-start.13) | collective-permute-done | bytes 98336 | tf_op jit(solution)/shard_map/ppermute | solution.py:50
  61.8 5.1 %collective-permute-start.18 = (bf16[3,256,64]{1,2,0:T(8,128)(2,1)S(1)}, bf16[3,256,64]{1,2,0:T(8,128)(2,1)S(1)}, u32[]{:S(2)}, u32[]{:S(2)}) collective-permute-start(bf16[3,256,64]{1,2,0:T(8,128)(2,1)S(1)} %get-tuple-element.67), channel_id=1, source_target_pairs={{0,4},{4,8},{8,12},{12,0},{1,5},{5,9},{9,13},{13,1},{2,6},{6,10},{... | collective-permute-start | bytes 294920 | tf_op jit(solution)/shard_map/ppermute | solution.py:15
  66.9 2.4 %collective-permute-start.20 = (bf16[3,256,64]{1,2,0:T(8,128)(2,1)S(1)}, bf16[3,256,64]{1,2,0:T(8,128)(2,1)S(1)}, u32[]{:S(2)}, u32[]{:S(2)}) collective-permute-start(bf16[3,256,64]{1,2,0:T(8,128)(2,1)S(1)} %get-tuple-element.68), channel_id=1, source_target_pairs={{0,12},{4,0},{8,4},{12,8},{1,13},{5,1},{9,5},{13,9},{2,14},{6,2},{... | collective-permute-start | bytes 294920 | tf_op jit(solution)/shard_map/ppermute | solution.py:15
  70.1 5.2 %collective-permute-done.19 = bf16[3,256,64]{1,2,0:T(8,128)(2,1)S(1)} collective-permute-done((bf16[3,256,64]{1,2,0:T(8,128)(2,1)S(1)}, bf16[3,256,64]{1,2,0:T(8,128)(2,1)S(1)}, u32[]{:S(2)}, u32[]{:S(2)}) %collective-permute-start.19) | collective-permute-done | bytes 98336 | tf_op jit(solution)/shard_map/ppermute | solution.py:15
  75.6 2.6 %collective-permute-start.21 = (bf16[3,256,64]{1,2,0:T(8,128)(2,1)S(1)}, bf16[3,256,64]{1,2,0:T(8,128)(2,1)S(1)}, u32[]{:S(2)}, u32[]{:S(2)}) collective-permute-start(bf16[3,256,64]{1,2,0:T(8,128)(2,1)S(1)} %get-tuple-element.47), channel_id=1, source_target_pairs={{0,4},{4,8},{8,12},{12,0},{1,5},{5,9},{9,13},{13,1},{2,6},{6,10},{... | collective-permute-start | bytes 294920 | tf_op jit(solution)/shard_map/ppermute | solution.py:15
  80.7 2.5 %collective-permute-done.21 = bf16[3,256,64]{1,2,0:T(8,128)(2,1)S(1)} collective-permute-done((bf16[3,256,64]{1,2,0:T(8,128)(2,1)S(1)}, bf16[3,256,64]{1,2,0:T(8,128)(2,1)S(1)}, u32[]{:S(2)}, u32[]{:S(2)}) %collective-permute-start.21) | collective-permute-done | bytes 98336 | tf_op jit(solution)/shard_map/ppermute | solution.py:15
  83.2 3.5 %collective-permute-done.22 = bf16[3,256,64]{1,2,0:T(8,128)(2,1)S(1)} collective-permute-done((bf16[3,256,64]{1,2,0:T(8,128)(2,1)S(1)}, bf16[3,256,64]{1,2,0:T(8,128)(2,1)S(1)}, u32[]{:S(2)}, u32[]{:S(2)}) %collective-permute-start.22) | collective-permute-done | bytes 98336 | tf_op jit(solution)/shard_map/ppermute | solution.py:15
  88.9 2.6 %collective-permute-start.24 = (bf16[3,256,64]{1,2,0:T(8,128)(2,1)S(1)}, bf16[3,256,64]{1,2,0:T(8,128)(2,1)S(1)}, u32[]{:S(2)}, u32[]{:S(2)}) collective-permute-start(bf16[3,256,64]{1,2,0:T(8,128)(2,1)S(1)} %get-tuple-element.64), channel_id=1, source_target_pairs={{0,4},{4,8},{8,12},{12,0},{1,5},{5,9},{9,13},{13,1},{2,6},{6,10},{... | collective-permute-start | bytes 294920 | tf_op jit(solution)/shard_map/ppermute | solution.py:15
  94.0 2.2 %collective-permute-start.16 = (bf16[2,512,256]{2,1,0:T(8,128)(2,1)S(1)}, bf16[2,512,256]{2,1,0:T(8,128)(2,1)S(1)}, u32[]{:S(2)}, u32[]{:S(2)}) collective-permute-start(bf16[2,512,256]{2,1,0:T(8,128)(2,1)S(1)} %slice_bitcast_fusion), channel_id=1, source_target_pairs={{0,2},{2,0},{1,3},{3,1},{4,6},{6,4},{5,7},{7,5},{8,10},{10,8},{9,1... | collective-permute-start | bytes 1572872 | tf_op jit(solution)/shard_map/ppermute | solution.py:15
  96.3 3.3 %collective-permute-done.25 = bf16[3,256,64]{1,2,0:T(8,128)(2,1)S(1)} collective-permute-done((bf16[3,256,64]{1,2,0:T(8,128)(2,1)S(1)}, bf16[3,256,64]{1,2,0:T(8,128)(2,1)S(1)}, u32[]{:S(2)}, u32[]{:S(2)}) %collective-permute-start.25) | collective-permute-done | bytes 98336 | tf_op jit(solution)/shard_map/ppermute | solution.py:15
  100.1 2.2 %collective-permute-start.27 = (bf16[3,256,64]{1,2,0:T(8,128)(2,1)S(1)}, bf16[3,256,64]{1,2,0:T(8,128)(2,1)S(1)}, u32[]{:S(2)}, u32[]{:S(2)}) collective-permute-start(bf16[3,256,64]{1,2,0:T(8,128)(2,1)S(1)} %multiply_convert_fusion.41), channel_id=1, source_target_pairs={{0,2},{2,0},{4,6},{6,4},{8,10},{10,8},{12,14},{14,12},{1,3},{3,1},... | collective-permute-start | bytes 294920 | tf_op jit(solution)/shard_map/ppermute | solution.py:50
  102.2 6.5 %collective-permute-done.16 = bf16[2,512,256]{2,1,0:T(8,128)(2,1)S(1)} collective-permute-done((bf16[2,512,256]{2,1,0:T(8,128)(2,1)S(1)}, bf16[2,512,256]{2,1,0:T(8,128)(2,1)S(1)}, u32[]{:S(2)}, u32[]{:S(2)}) %collective-permute-start.16) | collective-permute-done | bytes 524320 | tf_op jit(solution)/shard_map/ppermute | solution.py:15
  112.9 2.4 %collective-permute-start.30 = (bf16[3,256,64]{1,2,0:T(8,128)(2,1)S(1)}, bf16[3,256,64]{1,2,0:T(8,128)(2,1)S(1)}, u32[]{:S(2)}, u32[]{:S(2)}) collective-permute-start(bf16[3,256,64]{1,2,0:T(8,128)(2,1)S(1)} %multiply_convert_fusion.41), channel_id=1, source_target_pairs={{0,14},{2,12},{4,2},{6,0},{8,6},{10,4},{12,10},{14,8},{1,15},{3,13... | collective-permute-start | bytes 294920 | tf_op jit(solution)/shard_map/ppermute | solution.py:50
  117.2 2.6 %collective-permute-done.29 = bf16[3,256,64]{1,2,0:T(8,128)(2,1)S(1)} collective-permute-done((bf16[3,256,64]{1,2,0:T(8,128)(2,1)S(1)}, bf16[3,256,64]{1,2,0:T(8,128)(2,1)S(1)}, u32[]{:S(2)}, u32[]{:S(2)}) %collective-permute-start.29) | collective-permute-done | bytes 98336 | tf_op jit(solution)/shard_map/ppermute | solution.py:50
  126.6 2.3 %convolution_convert_fusion.2 = bf16[512,256]{1,0:T(8,128)(2,1)} fusion(f32[512,256]{1,0:T(8,128)} %convolution_bitcast_fusion.12, bf16[2,512,256]{2,1,0:T(8,128)(2,1)} %copy-done.4, bf16[3,256,256]{1,2,0:T(8,128)(2,1)S(1)} %constant_dynamic-update-slice_fusion.16), kind=kOutput, calls=%fused_computation.21 | convolution fusion | flops 135135232 | bytes 1310720 | tf_op jit(solution)/shard_map/th,hd->td/dot_general | solution.py:81
  130.1 2.2 %collective-permute-done.33 = bf16[3,256,64]{1,2,0:T(8,128)(2,1)S(1)} collective-permute-done((bf16[3,256,64]{1,2,0:T(8,128)(2,1)S(1)}, bf16[3,256,64]{1,2,0:T(8,128)(2,1)S(1)}, u32[]{:S(2)}, u32[]{:S(2)}) %collective-permute-start.33) | collective-permute-done | bytes 98336 | tf_op jit(solution)/shard_map/ppermute | solution.py:15
  141.1 3.0 %collective-permute-done.36 = bf16[3,256,64]{1,2,0:T(8,128)(2,1)S(1)} collective-permute-done((bf16[3,256,64]{1,2,0:T(8,128)(2,1)S(1)}, bf16[3,256,64]{1,2,0:T(8,128)(2,1)S(1)}, u32[]{:S(2)}, u32[]{:S(2)}) %collective-permute-start.36) | collective-permute-done | bytes 98336 | tf_op jit(solution)/shard_map/ppermute | solution.py:15
  153.9 2.5 %collective-permute-done.39 = bf16[3,256,64]{1,2,0:T(8,128)(2,1)S(1)} collective-permute-done((bf16[3,256,64]{1,2,0:T(8,128)(2,1)S(1)}, bf16[3,256,64]{1,2,0:T(8,128)(2,1)S(1)}, u32[]{:S(2)}, u32[]{:S(2)}) %collective-permute-start.39) | collective-permute-done | bytes 98336 | tf_op jit(solution)/shard_map/ppermute | solution.py:15
  161.9 2.4 %collective-permute-done.41 = bf16[3,256,64]{1,2,0:T(8,128)(2,1)S(1)} collective-permute-done((bf16[3,256,64]{1,2,0:T(8,128)(2,1)S(1)}, bf16[3,256,64]{1,2,0:T(8,128)(2,1)S(1)}, u32[]{:S(2)}, u32[]{:S(2)}) %collective-permute-start.41) | collective-permute-done | bytes 98336 | tf_op jit(solution)/shard_map/ppermute | solution.py:15
  164.3 3.0 %collective-permute-done.42 = bf16[3,256,64]{1,2,0:T(8,128)(2,1)S(1)} collective-permute-done((bf16[3,256,64]{1,2,0:T(8,128)(2,1)S(1)}, bf16[3,256,64]{1,2,0:T(8,128)(2,1)S(1)}, u32[]{:S(2)}, u32[]{:S(2)}) %collective-permute-start.42) | collective-permute-done | bytes 98336 | tf_op jit(solution)/shard_map/ppermute | solution.py:15
  (190 shorter events, 72.4 us)
Async XLA Ops:
  3.7 7.7 %collective-permute-start = (bf16[3,256,64]{1,2,0:T(8,128)(2,1)S(1)}, bf16[3,256,64]{1,2,0:T(8,128)(2,1)S(1)}, u32[]{:S(2)}, u32[]{:S(2)}) collective-permute-start(bf16[3,256,64]{1,2,0:T(8,128)(2,1)S(1)} %get-tuple-element.57), channel_id=1, source_target_pairs={{0,4},{4,8},{8,12},{12,0},{1,5},{5,9},{9,13},{13,1},{2,6},{6,10},{... | collective-permute-start | bytes 294920 | tf_op jit(solution)/shard_map/ppermute | solution.py:15
  18.0 7.6 %collective-permute-start.4 = (bf16[3,256,64]{1,2,0:T(8,128)(2,1)S(1)}, bf16[3,256,64]{1,2,0:T(8,128)(2,1)S(1)}, u32[]{:S(2)}, u32[]{:S(2)}) collective-permute-start(bf16[3,256,64]{1,2,0:T(8,128)(2,1)S(1)} %get-tuple-element.75), channel_id=1, source_target_pairs={{0,8},{4,12},{8,0},{12,4},{1,9},{5,13},{9,1},{13,5},{2,10},{6,14},... | collective-permute-start | bytes 294920 | tf_op jit(solution)/shard_map/ppermute | solution.py:15
  27.6 8.5 %collective-permute-start.7 = (bf16[3,256,64]{1,2,0:T(8,128)(2,1)S(1)}, bf16[3,256,64]{1,2,0:T(8,128)(2,1)S(1)}, u32[]{:S(2)}, u32[]{:S(2)}) collective-permute-start(bf16[3,256,64]{1,2,0:T(8,128)(2,1)S(1)} %get-tuple-element.53), channel_id=1, source_target_pairs={{0,8},{4,12},{8,0},{12,4},{1,9},{5,13},{9,1},{13,5},{2,10},{6,14},... | collective-permute-start | bytes 294920 | tf_op jit(solution)/shard_map/ppermute | solution.py:15
  38.3 6.8 %collective-permute-start.10 = (bf16[3,256,64]{1,2,0:T(8,128)(2,1)S(1)}, bf16[3,256,64]{1,2,0:T(8,128)(2,1)S(1)}, u32[]{:S(2)}, u32[]{:S(2)}) collective-permute-start(bf16[3,256,64]{1,2,0:T(8,128)(2,1)S(1)} %get-tuple-element.72), channel_id=1, source_target_pairs={{0,8},{4,12},{8,0},{12,4},{1,9},{5,13},{9,1},{13,5},{2,10},{6,14},... | collective-permute-start | bytes 294920 | tf_op jit(solution)/shard_map/ppermute | solution.py:15
  50.8 7.6 %collective-permute-start.13 = (bf16[3,256,64]{1,2,0:T(8,128)(2,1)S(1)}, bf16[3,256,64]{1,2,0:T(8,128)(2,1)S(1)}, u32[]{:S(2)}, u32[]{:S(2)}) collective-permute-start(bf16[3,256,64]{1,2,0:T(8,128)(2,1)S(1)} %multiply_convert_fusion.42), channel_id=1, source_target_pairs={{0,6},{2,4},{4,10},{6,8},{8,14},{10,12},{12,2},{14,0},{1,7},{3,5},... | collective-permute-start | bytes 294920 | tf_op jit(solution)/shard_map/ppermute | solution.py:50
  50.8 8.7 %collective-permute-start.14 = (bf16[3,256,64]{1,2,0:T(8,128)(2,1)S(1)}, bf16[3,256,64]{1,2,0:T(8,128)(2,1)S(1)}, u32[]{:S(2)}, u32[]{:S(2)}) collective-permute-start(bf16[3,256,64]{1,2,0:T(8,128)(2,1)S(1)} %multiply_convert_fusion.42), channel_id=1, source_target_pairs={{0,10},{2,8},{4,14},{6,12},{8,2},{10,0},{12,6},{14,4},{1,11},{3,9}... | collective-permute-start | bytes 294920 | tf_op jit(solution)/shard_map/ppermute | solution.py:50
  52.2 7.3 %collective-permute-start.15 = (bf16[3,256,64]{1,2,0:T(8,128)(2,1)S(1)}, bf16[3,256,64]{1,2,0:T(8,128)(2,1)S(1)}, u32[]{:S(2)}, u32[]{:S(2)}) collective-permute-start(bf16[3,256,64]{1,2,0:T(8,128)(2,1)S(1)} %multiply_convert_fusion.42), channel_id=1, source_target_pairs={{0,14},{2,12},{4,2},{6,0},{8,6},{10,4},{12,10},{14,8},{1,15},{3,13... | collective-permute-start | bytes 294920 | tf_op jit(solution)/shard_map/ppermute | solution.py:50
  61.8 8.3 %collective-permute-start.18 = (bf16[3,256,64]{1,2,0:T(8,128)(2,1)S(1)}, bf16[3,256,64]{1,2,0:T(8,128)(2,1)S(1)}, u32[]{:S(2)}, u32[]{:S(2)}) collective-permute-start(bf16[3,256,64]{1,2,0:T(8,128)(2,1)S(1)} %get-tuple-element.67), channel_id=1, source_target_pairs={{0,4},{4,8},{8,12},{12,0},{1,5},{5,9},{9,13},{13,1},{2,6},{6,10},{... | collective-permute-start | bytes 294920 | tf_op jit(solution)/shard_map/ppermute | solution.py:15
  66.9 8.4 %collective-permute-start.19 = (bf16[3,256,64]{1,2,0:T(8,128)(2,1)S(1)}, bf16[3,256,64]{1,2,0:T(8,128)(2,1)S(1)}, u32[]{:S(2)}, u32[]{:S(2)}) collective-permute-start(bf16[3,256,64]{1,2,0:T(8,128)(2,1)S(1)} %get-tuple-element.69), channel_id=1, source_target_pairs={{0,8},{4,12},{8,0},{12,4},{1,9},{5,13},{9,1},{13,5},{2,10},{6,14},... | collective-permute-start | bytes 294920 | tf_op jit(solution)/shard_map/ppermute | solution.py:15
  66.9 8.4 %collective-permute-start.20 = (bf16[3,256,64]{1,2,0:T(8,128)(2,1)S(1)}, bf16[3,256,64]{1,2,0:T(8,128)(2,1)S(1)}, u32[]{:S(2)}, u32[]{:S(2)}) collective-permute-start(bf16[3,256,64]{1,2,0:T(8,128)(2,1)S(1)} %get-tuple-element.68), channel_id=1, source_target_pairs={{0,12},{4,0},{8,4},{12,8},{1,13},{5,1},{9,5},{13,9},{2,14},{6,2},{... | collective-permute-start | bytes 294920 | tf_op jit(solution)/shard_map/ppermute | solution.py:15
  75.6 7.6 %collective-permute-start.21 = (bf16[3,256,64]{1,2,0:T(8,128)(2,1)S(1)}, bf16[3,256,64]{1,2,0:T(8,128)(2,1)S(1)}, u32[]{:S(2)}, u32[]{:S(2)}) collective-permute-start(bf16[3,256,64]{1,2,0:T(8,128)(2,1)S(1)} %get-tuple-element.47), channel_id=1, source_target_pairs={{0,4},{4,8},{8,12},{12,0},{1,5},{5,9},{9,13},{13,1},{2,6},{6,10},{... | collective-permute-start | bytes 294920 | tf_op jit(solution)/shard_map/ppermute | solution.py:15
  78.2 8.5 %collective-permute-start.22 = (bf16[3,256,64]{1,2,0:T(8,128)(2,1)S(1)}, bf16[3,256,64]{1,2,0:T(8,128)(2,1)S(1)}, u32[]{:S(2)}, u32[]{:S(2)}) collective-permute-start(bf16[3,256,64]{1,2,0:T(8,128)(2,1)S(1)} %get-tuple-element.47), channel_id=1, source_target_pairs={{0,8},{4,12},{8,0},{12,4},{1,9},{5,13},{9,1},{13,5},{2,10},{6,14},... | collective-permute-start | bytes 294920 | tf_op jit(solution)/shard_map/ppermute | solution.py:15
  79.9 6.8 %collective-permute-start.23 = (bf16[3,256,64]{1,2,0:T(8,128)(2,1)S(1)}, bf16[3,256,64]{1,2,0:T(8,128)(2,1)S(1)}, u32[]{:S(2)}, u32[]{:S(2)}) collective-permute-start(bf16[3,256,64]{1,2,0:T(8,128)(2,1)S(1)} %get-tuple-element.47), channel_id=1, source_target_pairs={{0,12},{4,0},{8,4},{12,8},{1,13},{5,1},{9,5},{13,9},{2,14},{6,2},{... | collective-permute-start | bytes 294920 | tf_op jit(solution)/shard_map/ppermute | solution.py:15
  88.9 7.4 %collective-permute-start.24 = (bf16[3,256,64]{1,2,0:T(8,128)(2,1)S(1)}, bf16[3,256,64]{1,2,0:T(8,128)(2,1)S(1)}, u32[]{:S(2)}, u32[]{:S(2)}) collective-permute-start(bf16[3,256,64]{1,2,0:T(8,128)(2,1)S(1)} %get-tuple-element.64), channel_id=1, source_target_pairs={{0,4},{4,8},{8,12},{12,0},{1,5},{5,9},{9,13},{13,1},{2,6},{6,10},{... | collective-permute-start | bytes 294920 | tf_op jit(solution)/shard_map/ppermute | solution.py:15
  91.5 8.2 %collective-permute-start.25 = (bf16[3,256,64]{1,2,0:T(8,128)(2,1)S(1)}, bf16[3,256,64]{1,2,0:T(8,128)(2,1)S(1)}, u32[]{:S(2)}, u32[]{:S(2)}) collective-permute-start(bf16[3,256,64]{1,2,0:T(8,128)(2,1)S(1)} %get-tuple-element.66), channel_id=1, source_target_pairs={{0,8},{4,12},{8,0},{12,4},{1,9},{5,13},{9,1},{13,5},{2,10},{6,14},... | collective-permute-start | bytes 294920 | tf_op jit(solution)/shard_map/ppermute | solution.py:15
  92.7 7.0 %collective-permute-start.26 = (bf16[3,256,64]{1,2,0:T(8,128)(2,1)S(1)}, bf16[3,256,64]{1,2,0:T(8,128)(2,1)S(1)}, u32[]{:S(2)}, u32[]{:S(2)}) collective-permute-start(bf16[3,256,64]{1,2,0:T(8,128)(2,1)S(1)} %get-tuple-element.65), channel_id=1, source_target_pairs={{0,12},{4,0},{8,4},{12,8},{1,13},{5,1},{9,5},{13,9},{2,14},{6,2},{... | collective-permute-start | bytes 294920 | tf_op jit(solution)/shard_map/ppermute | solution.py:15
  94.0 14.8 %collective-permute-start.16 = (bf16[2,512,256]{2,1,0:T(8,128)(2,1)S(1)}, bf16[2,512,256]{2,1,0:T(8,128)(2,1)S(1)}, u32[]{:S(2)}, u32[]{:S(2)}) collective-permute-start(bf16[2,512,256]{2,1,0:T(8,128)(2,1)S(1)} %slice_bitcast_fusion), channel_id=1, source_target_pairs={{0,2},{2,0},{1,3},{3,1},{4,6},{6,4},{5,7},{7,5},{8,10},{10,8},{9,1... | collective-permute-start | bytes 1572872 | tf_op jit(solution)/shard_map/ppermute | solution.py:15
  100.1 15.2 %collective-permute-start.27 = (bf16[3,256,64]{1,2,0:T(8,128)(2,1)S(1)}, bf16[3,256,64]{1,2,0:T(8,128)(2,1)S(1)}, u32[]{:S(2)}, u32[]{:S(2)}) collective-permute-start(bf16[3,256,64]{1,2,0:T(8,128)(2,1)S(1)} %multiply_convert_fusion.41), channel_id=1, source_target_pairs={{0,2},{2,0},{4,6},{6,4},{8,10},{10,8},{12,14},{14,12},{1,3},{3,1},... | collective-permute-start | bytes 294920 | tf_op jit(solution)/shard_map/ppermute | solution.py:50
  109.8 7.4 %collective-permute-start.28 = (bf16[3,256,64]{1,2,0:T(8,128)(2,1)S(1)}, bf16[3,256,64]{1,2,0:T(8,128)(2,1)S(1)}, u32[]{:S(2)}, u32[]{:S(2)}) collective-permute-start(bf16[3,256,64]{1,2,0:T(8,128)(2,1)S(1)} %multiply_convert_fusion.41), channel_id=1, source_target_pairs={{0,6},{2,4},{4,10},{6,8},{8,14},{10,12},{12,2},{14,0},{1,7},{3,5},... | collective-permute-start | bytes 294920 | tf_op jit(solution)/shard_map/ppermute | solution.py:50
  111.2 8.6 %collective-permute-start.29 = (bf16[3,256,64]{1,2,0:T(8,128)(2,1)S(1)}, bf16[3,256,64]{1,2,0:T(8,128)(2,1)S(1)}, u32[]{:S(2)}, u32[]{:S(2)}) collective-permute-start(bf16[3,256,64]{1,2,0:T(8,128)(2,1)S(1)} %multiply_convert_fusion.41), channel_id=1, source_target_pairs={{0,10},{2,8},{4,14},{6,12},{8,2},{10,0},{12,6},{14,4},{1,11},{3,9}... | collective-permute-start | bytes 294920 | tf_op jit(solution)/shard_map/ppermute | solution.py:50
  112.9 7.0 %collective-permute-start.30 = (bf16[3,256,64]{1,2,0:T(8,128)(2,1)S(1)}, bf16[3,256,64]{1,2,0:T(8,128)(2,1)S(1)}, u32[]{:S(2)}, u32[]{:S(2)}) collective-permute-start(bf16[3,256,64]{1,2,0:T(8,128)(2,1)S(1)} %multiply_convert_fusion.41), channel_id=1, source_target_pairs={{0,14},{2,12},{4,2},{6,0},{8,6},{10,4},{12,10},{14,8},{1,15},{3,13... | collective-permute-start | bytes 294920 | tf_op jit(solution)/shard_map/ppermute | solution.py:50
  122.8 7.3 %collective-permute-start.32 = (bf16[3,256,64]{1,2,0:T(8,128)(2,1)}, bf16[3,256,64]{1,2,0:T(8,128)(2,1)S(1)}, u32[]{:S(2)}, u32[]{:S(2)}) collective-permute-start(bf16[3,256,64]{1,2,0:T(8,128)(2,1)} %get-tuple-element.61), channel_id=1, source_target_pairs={{0,4},{4,8},{8,12},{12,0},{1,5},{5,9},{9,13},{13,1},{2,6},{6,10},{... | collective-permute-start | bytes 294920 | tf_op jit(solution)/shard_map/ppermute | solution.py:15
  124.2 8.1 %collective-permute-start.33 = (bf16[3,256,64]{1,2,0:T(8,128)(2,1)S(1)}, bf16[3,256,64]{1,2,0:T(8,128)(2,1)S(1)}, u32[]{:S(2)}, u32[]{:S(2)}) collective-permute-start(bf16[3,256,64]{1,2,0:T(8,128)(2,1)S(1)} %get-tuple-element.63), channel_id=1, source_target_pairs={{0,8},{4,12},{8,0},{12,4},{1,9},{5,13},{9,1},{13,5},{2,10},{6,14},... | collective-permute-start | bytes 294920 | tf_op jit(solution)/shard_map/ppermute | solution.py:15
  128.9 39.2 %collective-permute-start.17 = (bf16[512,256]{1,0:T(8,128)(2,1)}, bf16[512,256]{1,0:T(8,128)(2,1)}, u32[]{:S(2)}, u32[]{:S(2)}) collective-permute-start(bf16[512,256]{1,0:T(8,128)(2,1)} %convolution_convert_fusion.2), channel_id=1, source_target_pairs={{0,2},{2,0},{1,3},{3,1},{4,6},{6,4},{5,7},{7,5},{8,10},{10,8},{9,1... | collective-permute-start | bytes 786440 | tf_op jit(solution)/shard_map/ppermute | solution.py:15
  133.5 7.6 %collective-permute-start.35 = (bf16[3,256,64]{1,2,0:T(8,128)(2,1)S(1)}, bf16[3,256,64]{1,2,0:T(8,128)(2,1)S(1)}, u32[]{:S(2)}, u32[]{:S(2)}) collective-permute-start(bf16[3,256,64]{1,2,0:T(8,128)(2,1)S(1)} %get-tuple-element.41), channel_id=1, source_target_pairs={{0,4},{4,8},{8,12},{12,0},{1,5},{5,9},{9,13},{13,1},{2,6},{6,10},{... | collective-permute-start | bytes 294920 | tf_op jit(solution)/shard_map/ppermute | solution.py:15
  136.4 7.8 %collective-permute-start.36 = (bf16[3,256,64]{1,2,0:T(8,128)(2,1)S(1)}, bf16[3,256,64]{1,2,0:T(8,128)(2,1)S(1)}, u32[]{:S(2)}, u32[]{:S(2)}) collective-permute-start(bf16[3,256,64]{1,2,0:T(8,128)(2,1)S(1)} %get-tuple-element.41), channel_id=1, source_target_pairs={{0,8},{4,12},{8,0},{12,4},{1,9},{5,13},{9,1},{13,5},{2,10},{6,14},... | collective-permute-start | bytes 294920 | tf_op jit(solution)/shard_map/ppermute | solution.py:15
  146.3 7.6 %collective-permute-start.38 = (bf16[3,256,64]{1,2,0:T(8,128)(2,1)S(1)}, bf16[3,256,64]{1,2,0:T(8,128)(2,1)S(1)}, u32[]{:S(2)}, u32[]{:S(2)}) collective-permute-start(bf16[3,256,64]{1,2,0:T(8,128)(2,1)S(1)} %get-tuple-element.58), channel_id=1, source_target_pairs={{0,4},{4,8},{8,12},{12,0},{1,5},{5,9},{9,13},{13,1},{2,6},{6,10},{... | collective-permute-start | bytes 294920 | tf_op jit(solution)/shard_map/ppermute | solution.py:15
  148.1 8.3 %collective-permute-start.39 = (bf16[3,256,64]{1,2,0:T(8,128)(2,1)S(1)}, bf16[3,256,64]{1,2,0:T(8,128)(2,1)S(1)}, u32[]{:S(2)}, u32[]{:S(2)}) collective-permute-start(bf16[3,256,64]{1,2,0:T(8,128)(2,1)S(1)} %get-tuple-element.60), channel_id=1, source_target_pairs={{0,8},{4,12},{8,0},{12,4},{1,9},{5,13},{9,1},{13,5},{2,10},{6,14},... | collective-permute-start | bytes 294920 | tf_op jit(solution)/shard_map/ppermute | solution.py:15
  149.2 7.2 %collective-permute-start.40 = (bf16[3,256,64]{1,2,0:T(8,128)(2,1)S(1)}, bf16[3,256,64]{1,2,0:T(8,128)(2,1)S(1)}, u32[]{:S(2)}, u32[]{:S(2)}) collective-permute-start(bf16[3,256,64]{1,2,0:T(8,128)(2,1)S(1)} %get-tuple-element.59), channel_id=1, source_target_pairs={{0,12},{4,0},{8,4},{12,8},{1,13},{5,1},{9,5},{13,9},{2,14},{6,2},{... | collective-permute-start | bytes 294920 | tf_op jit(solution)/shard_map/ppermute | solution.py:15
  151.0 17.1 %collective-permute-start.31 = (bf16[512,256]{1,0:T(8,128)(2,1)S(1)}, bf16[512,256]{1,0:T(8,128)(2,1)S(1)}, u32[]{:S(2)}, u32[]{:S(2)}) collective-permute-start(bf16[512,256]{1,0:T(8,128)(2,1)S(1)} %convolution_convert_fusion.1), channel_id=1, source_target_pairs={{0,2},{2,0},{1,3},{3,1},{4,6},{6,4},{5,7},{7,5},{8,10},{10,8},{9,1... | collective-permute-start | bytes 786440 | tf_op jit(solution)/shard_map/ppermute | solution.py:15
  156.8 7.5 %collective-permute-start.41 = (bf16[3,256,64]{1,2,0:T(8,128)(2,1)S(1)}, bf16[3,256,64]{1,2,0:T(8,128)(2,1)S(1)}, u32[]{:S(2)}, u32[]{:S(2)}) collective-permute-start(bf16[3,256,64]{1,2,0:T(8,128)(2,1)S(1)} %get-tuple-element.37), channel_id=1, source_target_pairs={{0,4},{4,8},{8,12},{12,0},{1,5},{5,9},{9,13},{13,1},{2,6},{6,10},{... | collective-permute-start | bytes 294920 | tf_op jit(solution)/shard_map/ppermute | solution.py:15
  159.5 7.8 %collective-permute-start.42 = (bf16[3,256,64]{1,2,0:T(8,128)(2,1)S(1)}, bf16[3,256,64]{1,2,0:T(8,128)(2,1)S(1)}, u32[]{:S(2)}, u32[]{:S(2)}) collective-permute-start(bf16[3,256,64]{1,2,0:T(8,128)(2,1)S(1)} %get-tuple-element.37), channel_id=1, source_target_pairs={{0,8},{4,12},{8,0},{12,4},{1,9},{5,13},{9,1},{13,5},{2,10},{6,14},... | collective-permute-start | bytes 294920 | tf_op jit(solution)/shard_map/ppermute | solution.py:15
  (21 other events, 124.0 us)
